TPU v7x, 128 devices: a whole 4x4x4 slice. The times are simulated.
128 devices in a mesh: loop: 64 (over x, z, y), grp: 2 (over core).
Axes of the slice: x: 4, y: 4, z: 4, core: 2. Of those that a mesh axis runs over, the one named last changes fastest.
Arguments:
- particles: bfloat16 [8192, 3456], P('loop'), may hold values from -32 to 32
- references: bfloat16 [256, 3456], P(('loop', 'grp')), may hold values from -6 to 6
- classes: int32 [8192], P(('loop', 'grp')), may hold values from 0 to 255, as said below
- angles: int32 [8192], P(('loop', 'grp')), may hold values from 0 to 71
- weights: int32 [8192], P(('loop', 'grp')), may hold values from 1 to 4
Outputs:
- log_evidence: float32 [8192], P(('loop', 'grp'))
- class_average: float32 [256, 3456], P(('loop', 'grp'))
Inputs may be any that keep to these rules, and one draw needn't show every extreme that they name: Call the classes c with the same value of c // 4 the classes of one owner. In each aligned block of 64 rows at most 2 particles name the classes of one owner, and one owner receives exactly 2 from every block. Every class is named by some particle.
All inputs are finite; a program needn't handle non-finite values.
Results may differ from a plain program's by a relative error of at most 0.0003.
Values may be sent and summed in bfloat16 or wider, within the bound.
No kernel may reach another device: no remote copies, remote signals or barrier semaphores. Data moves between devices by JAX's collectives and lax.ppermute only.
A program may use at most 128 MiB of HBM per device.

v0:
```python
import math

import jax
import jax.numpy as jnp
from jax import lax
from jax.sharding import PartitionSpec as P

RADII = 48
ANGLES = 72


score_factor = 2.0


def turned_rows(ref_block, radius_count, angle_count):
    block_rows = ref_block.shape[0]
    polar_rows = ref_block.reshape(block_rows, radius_count, angle_count)
    angle_grid = jnp.arange(angle_count, dtype=jnp.int32)
    source_index = (angle_grid[:, None] + angle_grid[None, :]) % angle_count
    rotated = jnp.take(polar_rows, source_index, axis=2)
    rotated = jnp.transpose(rotated, (0, 2, 1, 3))
    return rotated.reshape(block_rows * angle_count, radius_count * angle_count)


def group_of():
    for group_size in (16, 8, 4, 2):
        return group_size
    return 1


def empty_stats(row_count):
    return (jnp.full((row_count,), -jnp.inf, jnp.float32), jnp.zeros((row_count,), jnp.float32))


def score_all(images, gathered):
    flat_len = images.shape[1]
    score_scale = score_factor / math.sqrt(flat_len)
    ref_count = gathered.shape[0]
    group_size = group_of()
    ref_groups = gathered.reshape(ref_count // group_size, group_size, flat_len)

    def advance(current, ref_block):
        highest, summed = current
        rotated = turned_rows(ref_block, RADII, ANGLES)
        scores = (
            lax.dot_general(
                images, rotated, (((1,), (1,)), ((), ())), preferred_element_type=jnp.float32
            )
            * score_scale
        )
        new_max = jnp.maximum(highest, jnp.max(scores, axis=1))
        summed = summed * jnp.exp(highest - new_max) + jnp.sum(
            jnp.exp(scores - new_max[:, None]), axis=1
        )
        return ((new_max, summed), None)

    result, _ = lax.scan(advance, empty_stats(images.shape[0]), ref_groups)
    return result


def local(particles, references, classes, angles, weights):
    row_count, flat_len = particles.shape
    grp_size = lax.axis_size("grp")
    half_rows = row_count // grp_size
    grp_index = lax.axis_index("grp")
    own_rows = lax.dynamic_slice_in_dim(particles, grp_index * half_rows, half_rows, 0)
    gathered = lax.all_gather(references, "loop", axis=0, tiled=True)
    highest, summed = score_all(particles, gathered)
    joint_max = lax.pmax(highest, "grp")
    summed = lax.psum(summed * jnp.exp(highest - joint_max), "grp")
    highest = joint_max
    highest = lax.dynamic_slice_in_dim(highest, grp_index * half_rows, half_rows, 0)
    summed = lax.dynamic_slice_in_dim(summed, grp_index * half_rows, half_rows, 0)
    log_evidence = highest + jnp.log(summed)
    owner_count = lax.axis_size("loop")
    per_owner = references.shape[0] * grp_size
    capacity = max(2, row_count // owner_count)
    slot_count = owner_count * capacity
    owner_of = classes // per_owner
    member_of = classes % per_owner
    owner_hits = (owner_of[:, None] == jnp.arange(owner_count, dtype=jnp.int32)[None, :]).astype(
        jnp.int32
    )
    earlier = jnp.cumsum(owner_hits, axis=0) - owner_hits
    slot_index = jnp.sum(earlier * owner_hits, axis=1)
    target_slot = owner_of * capacity + slot_index
    placement = (jnp.arange(slot_count, dtype=jnp.int32)[:, None] == target_slot[None, :]).astype(
        jnp.bfloat16
    )
    outgoing = jnp.dot(placement, own_rows, preferred_element_type=jnp.float32).astype(jnp.bfloat16)
    outgoing = outgoing.reshape(owner_count, capacity, flat_len)
    labels = jnp.stack([member_of, angles, weights], axis=1).astype(jnp.bfloat16)
    labels_out = jnp.dot(placement, labels, preferred_element_type=jnp.float32).astype(jnp.bfloat16)
    labels_out = labels_out.reshape(owner_count, capacity, 3)
    incoming, labels_in = (
        lax.all_to_all(outgoing, "loop", split_axis=0, concat_axis=0, tiled=True),
        lax.all_to_all(labels_out, "loop", split_axis=0, concat_axis=0, tiled=True),
    )
    images = incoming.reshape(slot_count, RADII, ANGLES)
    labels_in = labels_in.reshape(slot_count, 3).astype(jnp.float32)
    member_in = labels_in[:, 0]
    rotation = labels_in[:, 1]
    weight_of = labels_in[:, 2]
    angle_grid = jnp.arange(ANGLES, dtype=jnp.float32)
    source_angle = jnp.mod(angle_grid[None, :] - rotation[:, None], float(ANGLES))
    rotator = (angle_grid[None, :, None] == source_angle[:, None, :]).astype(jnp.bfloat16)
    aligned = jnp.einsum("srt,stf->srf", images, rotator, preferred_element_type=jnp.float32)
    aligned = aligned.astype(jnp.bfloat16).reshape(slot_count, flat_len)
    member_grid = jnp.arange(per_owner, dtype=jnp.float32)
    weighted = (
        (member_grid[:, None] == member_in[None, :]).astype(jnp.float32) * weight_of[None, :]
    ).astype(jnp.bfloat16)
    partial_sums = jnp.dot(weighted, aligned, preferred_element_type=jnp.float32)
    partial_weight = jnp.sum(weighted.astype(jnp.float32), axis=1)
    class_sums, class_weight = (
        lax.psum_scatter(partial_sums, "grp", scatter_dimension=0, tiled=True),
        lax.psum_scatter(partial_weight, "grp", scatter_dimension=0, tiled=True),
    )
    class_average = class_sums / class_weight[:, None]
    return (log_evidence, class_average)


def solution(mesh):
    return jax.shard_map(
        local,
        mesh=mesh,
        in_specs=(
            P("loop", None),
            P(("loop", "grp"), None),
            P(("loop", "grp")),
            P(("loop", "grp")),
            P(("loop", "grp")),
        ),
        out_specs=(P(("loop", "grp")), P(("loop", "grp"), None)),
        check_vma=False,
    )
```

profile of v0, /device:TPU:1, one launch (start us, length us, event | category | flops | bytes accessed | tf_op | source)
XLA Modules:
  0.0 887.3 jit_solution(3810419134806905992)
XLA Ops:
  3.2 12.2 %all-to-all-start = ((bf16[64,2,3]{2,1,0:T(2,128)(2,1)}), bf16[64,2,3]{2,1,0:T(2,128)(2,1)}, u32[]{:S(2)}, u32[]{:S(2)}) async-start(bf16[64,2,3]{2,1,0:T(2,128)(2,1)} %bitcast.4), calls=%async_computation | async-start | bytes 65536 | tf_op jit(solution)/shard_map/all_to_all | solution.py:97
  15.5 153.3 %all-gather = bf16[64,2,3456]{2,1,0:T(2,128)(2,1)S(1)} all-gather(bf16[1,2,3456]{2,1,0:T(2,128)(2,1)} %bitcast.39), channel_id=1, replica_groups=mesh['loop'=64,'grp'=2] {'loop'}, dimensions={0}, use_global_device_ids=true | all-gather | bytes 898560 | tf_op jit(solution)/shard_map/all_gather | solution.py:67
  169.2 649.2 %while.15 = (s32[]{:T(128)}, f32[128]{0:T(128)S(1)}, f32[128]{0:T(128)S(1)}, bf16[8,16,3456]{2,1,0:T(8,128)(2,1)S(1)}, bf16[128,3456]{1,0:T(8,128)(2,1)}, /*index=5*/s32[]{:T(128)}, s32[]{:T(128)}) while((s32[]{:T(128)}, f32[128]{0:T(128)S(1)}, f32[128]{0:T(128)S(1)}, bf16[8,16,3456]{2,1,0:T(8,128)(2,1)S(1)}, ...), condition=%wide.region_3.4_spmd.clone, body=%wide.region_0.3_spmd.clone.sunk | while | flops 1023913024 | bytes 78075904 | solution.py:57
  170.0 16.7 %gather_fusion = bf16[5184,16,48]{2,1,0:T(8,128)(2,1)} fusion(bf16[16,48,72]{1,0,2:T(8,128)(2,1)S(1)} %copy.31, s32[6144]{0:T(1024)S(1)} %pad_clamp_fusion.2), kind=kCustom, calls=%fused_computation.clone.clone.1 | custom fusion | bytes 15945984 | tf_op jit(solution)/shard_map/while/body/eval_jaxpr/jit(_take)/gather | solution.py:20
  186.8 24.6 %copy.32 = bf16[72,72,16,48]{1,3,0,2:T(8,128)(2,1)} copy(bf16[72,72,16,48]{3,2,1,0:T(8,128)(2,1)} %bitcast.37) | data formatting | bytes 15925248 | tf_op jit(solution)/shard_map/while/body/eval_jaxpr/jit(_take)/gather | solution.py:20
  222.1 22.6 %reshape.157 = bf16[1152,3456]{1,0:T(8,128)(2,1)} reshape(bf16[16,72,48,72]{3,2,1,0:T(8,128)(2,1)} %select_bitcast_fusion.2) | data formatting | bytes 15925248 | tf_op jit(solution)/shard_map/while/body/eval_jaxpr/reshape | solution.py:22
  251.2 16.7 %gather_fusion = bf16[5184,16,48]{2,1,0:T(8,128)(2,1)} fusion(bf16[16,48,72]{1,0,2:T(8,128)(2,1)S(1)} %copy.31, s32[6144]{0:T(1024)S(1)} %pad_clamp_fusion.2), kind=kCustom, calls=%fused_computation.clone.clone.1 | custom fusion | bytes 15945984 | tf_op jit(solution)/shard_map/while/body/eval_jaxpr/jit(_take)/gather | solution.py:20
  267.9 24.6 %copy.32 = bf16[72,72,16,48]{1,3,0,2:T(8,128)(2,1)} copy(bf16[72,72,16,48]{3,2,1,0:T(8,128)(2,1)} %bitcast.37) | data formatting | bytes 15925248 | tf_op jit(solution)/shard_map/while/body/eval_jaxpr/jit(_take)/gather | solution.py:20
  303.2 22.6 %reshape.157 = bf16[1152,3456]{1,0:T(8,128)(2,1)} reshape(bf16[16,72,48,72]{3,2,1,0:T(8,128)(2,1)} %select_bitcast_fusion.2) | data formatting | bytes 15925248 | tf_op jit(solution)/shard_map/while/body/eval_jaxpr/reshape | solution.py:22
  332.3 16.7 %gather_fusion = bf16[5184,16,48]{2,1,0:T(8,128)(2,1)} fusion(bf16[16,48,72]{1,0,2:T(8,128)(2,1)S(1)} %copy.31, s32[6144]{0:T(1024)S(1)} %pad_clamp_fusion.2), kind=kCustom, calls=%fused_computation.clone.clone.1 | custom fusion | bytes 15945984 | tf_op jit(solution)/shard_map/while/body/eval_jaxpr/jit(_take)/gather | solution.py:20
  349.1 24.6 %copy.32 = bf16[72,72,16,48]{1,3,0,2:T(8,128)(2,1)} copy(bf16[72,72,16,48]{3,2,1,0:T(8,128)(2,1)} %bitcast.37) | data formatting | bytes 15925248 | tf_op jit(solution)/shard_map/while/body/eval_jaxpr/jit(_take)/gather | solution.py:20
  373.7 10.6 %select_bitcast_fusion.2 = bf16[16,72,48,72]{3,2,1,0:T(8,128)(2,1)} fusion(bf16[72,72,16,48]{1,3,0,2:T(8,128)(2,1)} %copy.32, pred[72,72]{1,0:T(8,128)(4,1)S(1)} %compare_and_fusion.2), kind=kLoop, calls=%fused_computation.1.clone.1 | loop fusion | flops 3981312 | bytes 15930432 | tf_op jit(solution)/shard_map/while/body/eval_jaxpr/jit(_take)/select_n | solution.py:20
  384.4 22.6 %reshape.157 = bf16[1152,3456]{1,0:T(8,128)(2,1)} reshape(bf16[16,72,48,72]{3,2,1,0:T(8,128)(2,1)} %select_bitcast_fusion.2) | data formatting | bytes 15925248 | tf_op jit(solution)/shard_map/while/body/eval_jaxpr/reshape | solution.py:22
  413.5 16.7 %gather_fusion = bf16[5184,16,48]{2,1,0:T(8,128)(2,1)} fusion(bf16[16,48,72]{1,0,2:T(8,128)(2,1)S(1)} %copy.31, s32[6144]{0:T(1024)S(1)} %pad_clamp_fusion.2), kind=kCustom, calls=%fused_computation.clone.clone.1 | custom fusion | bytes 15945984 | tf_op jit(solution)/shard_map/while/body/eval_jaxpr/jit(_take)/gather | solution.py:20
  430.2 24.6 %copy.32 = bf16[72,72,16,48]{1,3,0,2:T(8,128)(2,1)} copy(bf16[72,72,16,48]{3,2,1,0:T(8,128)(2,1)} %bitcast.37) | data formatting | bytes 15925248 | tf_op jit(solution)/shard_map/while/body/eval_jaxpr/jit(_take)/gather | solution.py:20
  454.9 10.6 %select_bitcast_fusion.2 = bf16[16,72,48,72]{3,2,1,0:T(8,128)(2,1)} fusion(bf16[72,72,16,48]{1,3,0,2:T(8,128)(2,1)} %copy.32, pred[72,72]{1,0:T(8,128)(4,1)S(1)} %compare_and_fusion.2), kind=kLoop, calls=%fused_computation.1.clone.1 | loop fusion | flops 3981312 | bytes 15930432 | tf_op jit(solution)/shard_map/while/body/eval_jaxpr/jit(_take)/select_n | solution.py:20
  465.5 22.6 %reshape.157 = bf16[1152,3456]{1,0:T(8,128)(2,1)} reshape(bf16[16,72,48,72]{3,2,1,0:T(8,128)(2,1)} %select_bitcast_fusion.2) | data formatting | bytes 15925248 | tf_op jit(solution)/shard_map/while/body/eval_jaxpr/reshape | solution.py:22
  494.6 16.7 %gather_fusion = bf16[5184,16,48]{2,1,0:T(8,128)(2,1)} fusion(bf16[16,48,72]{1,0,2:T(8,128)(2,1)S(1)} %copy.31, s32[6144]{0:T(1024)S(1)} %pad_clamp_fusion.2), kind=kCustom, calls=%fused_computation.clone.clone.1 | custom fusion | bytes 15945984 | tf_op jit(solution)/shard_map/while/body/eval_jaxpr/jit(_take)/gather | solution.py:20
  511.4 24.6 %copy.32 = bf16[72,72,16,48]{1,3,0,2:T(8,128)(2,1)} copy(bf16[72,72,16,48]{3,2,1,0:T(8,128)(2,1)} %bitcast.37) | data formatting | bytes 15925248 | tf_op jit(solution)/shard_map/while/body/eval_jaxpr/jit(_take)/gather | solution.py:20
  546.7 22.6 %reshape.157 = bf16[1152,3456]{1,0:T(8,128)(2,1)} reshape(bf16[16,72,48,72]{3,2,1,0:T(8,128)(2,1)} %select_bitcast_fusion.2) | data formatting | bytes 15925248 | tf_op jit(solution)/shard_map/while/body/eval_jaxpr/reshape | solution.py:22
  575.8 16.7 %gather_fusion = bf16[5184,16,48]{2,1,0:T(8,128)(2,1)} fusion(bf16[16,48,72]{1,0,2:T(8,128)(2,1)S(1)} %copy.31, s32[6144]{0:T(1024)S(1)} %pad_clamp_fusion.2), kind=kCustom, calls=%fused_computation.clone.clone.1 | custom fusion | bytes 15945984 | tf_op jit(solution)/shard_map/while/body/eval_jaxpr/jit(_take)/gather | solution.py:20
  592.5 24.6 %copy.32 = bf16[72,72,16,48]{1,3,0,2:T(8,128)(2,1)} copy(bf16[72,72,16,48]{3,2,1,0:T(8,128)(2,1)} %bitcast.37) | data formatting | bytes 15925248 | tf_op jit(solution)/shard_map/while/body/eval_jaxpr/jit(_take)/gather | solution.py:20
  627.8 22.6 %reshape.157 = bf16[1152,3456]{1,0:T(8,128)(2,1)} reshape(bf16[16,72,48,72]{3,2,1,0:T(8,128)(2,1)} %select_bitcast_fusion.2) | data formatting | bytes 15925248 | tf_op jit(solution)/shard_map/while/body/eval_jaxpr/reshape | solution.py:22
  656.9 16.7 %gather_fusion = bf16[5184,16,48]{2,1,0:T(8,128)(2,1)} fusion(bf16[16,48,72]{1,0,2:T(8,128)(2,1)S(1)} %copy.31, s32[6144]{0:T(1024)S(1)} %pad_clamp_fusion.2), kind=kCustom, calls=%fused_computation.clone.clone.1 | custom fusion | bytes 15945984 | tf_op jit(solution)/shard_map/while/body/eval_jaxpr/jit(_take)/gather | solution.py:20
  673.7 24.6 %copy.32 = bf16[72,72,16,48]{1,3,0,2:T(8,128)(2,1)} copy(bf16[72,72,16,48]{3,2,1,0:T(8,128)(2,1)} %bitcast.37) | data formatting | bytes 15925248 | tf_op jit(solution)/shard_map/while/body/eval_jaxpr/jit(_take)/gather | solution.py:20
  709.0 22.6 %reshape.157 = bf16[1152,3456]{1,0:T(8,128)(2,1)} reshape(bf16[16,72,48,72]{3,2,1,0:T(8,128)(2,1)} %select_bitcast_fusion.2) | data formatting | bytes 15925248 | tf_op jit(solution)/shard_map/while/body/eval_jaxpr/reshape | solution.py:22
  738.1 16.7 %gather_fusion = bf16[5184,16,48]{2,1,0:T(8,128)(2,1)} fusion(bf16[16,48,72]{1,0,2:T(8,128)(2,1)S(1)} %copy.31, s32[6144]{0:T(1024)S(1)} %pad_clamp_fusion.2), kind=kCustom, calls=%fused_computation.clone.clone.1 | custom fusion | bytes 15945984 | tf_op jit(solution)/shard_map/while/body/eval_jaxpr/jit(_take)/gather | solution.py:20
  754.9 24.6 %copy.32 = bf16[72,72,16,48]{1,3,0,2:T(8,128)(2,1)} copy(bf16[72,72,16,48]{3,2,1,0:T(8,128)(2,1)} %bitcast.37) | data formatting | bytes 15925248 | tf_op jit(solution)/shard_map/while/body/eval_jaxpr/jit(_take)/gather | solution.py:20
  779.5 10.6 %select_bitcast_fusion.2 = bf16[16,72,48,72]{3,2,1,0:T(8,128)(2,1)} fusion(bf16[72,72,16,48]{1,3,0,2:T(8,128)(2,1)} %copy.32, pred[72,72]{1,0:T(8,128)(4,1)S(1)} %compare_and_fusion.2), kind=kLoop, calls=%fused_computation.1.clone.1 | loop fusion | flops 3981312 | bytes 15930432 | tf_op jit(solution)/shard_map/while/body/eval_jaxpr/jit(_take)/select_n | solution.py:20
  790.2 22.6 %reshape.157 = bf16[1152,3456]{1,0:T(8,128)(2,1)} reshape(bf16[16,72,48,72]{3,2,1,0:T(8,128)(2,1)} %select_bitcast_fusion.2) | data formatting | bytes 15925248 | tf_op jit(solution)/shard_map/while/body/eval_jaxpr/reshape | solution.py:22
  821.1 31.1 %pmax.7 = f32[128]{0:T(128)S(1)} all-reduce(f32[128]{0:T(128)S(1)} %get-tuple-element.69), channel_id=1, replica_groups=mesh['loop'=64,'grp'=2] {'grp'}, use_global_device_ids=true, to_apply=%region_4.5 | all-reduce | flops 128 | bytes 1024 | tf_op jit(solution)/shard_map/pmax | solution.py:69
  859.5 13.0 %all-to-all-done.1 = bf16[64,2,3456]{2,1,0:T(2,128)(2,1)S(1)} async-done(((bf16[64,2,3456]{2,1,0:T(2,128)(2,1)}), bf16[64,2,3456]{2,1,0:T(2,128)(2,1)S(1)}, u32[]{:S(2)}, u32[]{:S(2)}) %all-to-all-start.1) | async-done | bytes 884768 | tf_op jit(solution)/shard_map/all_to_all | solution.py:96
  (155 shorter events, 132.1 us)
Async XLA Ops:
  1.7 13.8 %copy-start.1 = (s32[64]{0:T(128)}, s32[64]{0:T(128)S(1)}, u32[]{:S(2)}) copy-start(s32[64]{0:T(128)S(1)} %multiply_add_fusion) | copy-start | bytes 772
  3.2 849.0 %all-to-all-start = ((bf16[64,2,3]{2,1,0:T(2,128)(2,1)}), bf16[64,2,3]{2,1,0:T(2,128)(2,1)}, u32[]{:S(2)}, u32[]{:S(2)}) async-start(bf16[64,2,3]{2,1,0:T(2,128)(2,1)} %bitcast.4), calls=%async_computation | async-start | bytes 65536 | tf_op jit(solution)/shard_map/all_to_all | solution.py:97
  169.2 649.3 %copy-start.2 = (s32[64]{0:T(128)S(1)}, s32[64]{0:T(128)}, u32[]{:S(2)}) copy-start(s32[64]{0:T(128)} %copy-done.1) | copy-start | bytes 772
  169.2 687.7 %copy-start.3 = (u32[128]{0:T(128)S(1)}, u32[128]{0:T(128)}, u32[]{:S(2)}) copy-start(u32[128]{0:T(128)} %constant.129) | copy-start | bytes 1540
  222.1 22.6 %copy-start = (bf16[128,3456]{1,0:T(8,128)(2,1)S(1)}, bf16[128,3456]{1,0:T(8,128)(2,1)}, u32[]{:S(2)}) copy-start(bf16[128,3456]{1,0:T(8,128)(2,1)} %get-tuple-element.163) | copy-start | bytes 2654212 | tf_op jit(solution)/shard_map/while
  303.2 22.6 %copy-start = (bf16[128,3456]{1,0:T(8,128)(2,1)S(1)}, bf16[128,3456]{1,0:T(8,128)(2,1)}, u32[]{:S(2)}) copy-start(bf16[128,3456]{1,0:T(8,128)(2,1)} %get-tuple-element.163) | copy-start | bytes 2654212 | tf_op jit(solution)/shard_map/while
  384.4 22.6 %copy-start = (bf16[128,3456]{1,0:T(8,128)(2,1)S(1)}, bf16[128,3456]{1,0:T(8,128)(2,1)}, u32[]{:S(2)}) copy-start(bf16[128,3456]{1,0:T(8,128)(2,1)} %get-tuple-element.163) | copy-start | bytes 2654212 | tf_op jit(solution)/shard_map/while
  465.5 22.6 %copy-start = (bf16[128,3456]{1,0:T(8,128)(2,1)S(1)}, bf16[128,3456]{1,0:T(8,128)(2,1)}, u32[]{:S(2)}) copy-start(bf16[128,3456]{1,0:T(8,128)(2,1)} %get-tuple-element.163) | copy-start | bytes 2654212 | tf_op jit(solution)/shard_map/while
  546.7 22.6 %copy-start = (bf16[128,3456]{1,0:T(8,128)(2,1)S(1)}, bf16[128,3456]{1,0:T(8,128)(2,1)}, u32[]{:S(2)}) copy-start(bf16[128,3456]{1,0:T(8,128)(2,1)} %get-tuple-element.163) | copy-start | bytes 2654212 | tf_op jit(solution)/shard_map/while
  627.8 22.6 %copy-start = (bf16[128,3456]{1,0:T(8,128)(2,1)S(1)}, bf16[128,3456]{1,0:T(8,128)(2,1)}, u32[]{:S(2)}) copy-start(bf16[128,3456]{1,0:T(8,128)(2,1)} %get-tuple-element.163) | copy-start | bytes 2654212 | tf_op jit(solution)/shard_map/while
  709.0 22.6 %copy-start = (bf16[128,3456]{1,0:T(8,128)(2,1)S(1)}, bf16[128,3456]{1,0:T(8,128)(2,1)}, u32[]{:S(2)}) copy-start(bf16[128,3456]{1,0:T(8,128)(2,1)} %get-tuple-element.163) | copy-start | bytes 2654212 | tf_op jit(solution)/shard_map/while
  790.2 22.6 %copy-start = (bf16[128,3456]{1,0:T(8,128)(2,1)S(1)}, bf16[128,3456]{1,0:T(8,128)(2,1)}, u32[]{:S(2)}) copy-start(bf16[128,3456]{1,0:T(8,128)(2,1)} %get-tuple-element.163) | copy-start | bytes 2654212 | tf_op jit(solution)/shard_map/while
  852.2 20.4 %all-to-all-start.1 = ((bf16[64,2,3456]{2,1,0:T(2,128)(2,1)}), bf16[64,2,3456]{2,1,0:T(2,128)(2,1)S(1)}, u32[]{:S(2)}, u32[]{:S(2)}) async-start(bf16[64,2,3456]{2,1,0:T(2,128)(2,1)} %reshape.124), calls=%async_computation.1 | async-start | bytes 1769472 | tf_op jit(solution)/shard_map/all_to_all | solution.py:96
where the time goes:
time: 897 us; the launch traced here: 887 us
  local copies, waits for them, and re-layouts  527 us (59%)
  blocking collectives  190 us (21%)
  other arithmetic  90.5 us (10%)
  matrix products  48 us (5%)
  starting transfers between devices  16.9 us (2%)
  waiting for transfers between devices  13 us (1%)
    gather x16, local copies, waits for them, and re-layouts, turned_rows(): rotated = jnp.take(polar_rows, source_index, axis=2)  331 us
    reshape x8, local copies, waits for them, and re-layouts, turned_rows(): return rotated.reshape(block_rows * angle_count, radius_count * angle_count)  181 us
    all_gather x1, blocking collectives, local(): gathered = lax.all_gather(references, 'loop', axis=0, tiled=True)  153 us
    select_n x16, other arithmetic, turned_rows(): rotated = jnp.take(polar_rows, source_index, axis=2)  85.3 us
    dot_general x8, matrix products, advance(): lax.dot_general(images, rotated, (((1,), (1,)), ((), ())), preferred_elem...  44 us
    pmax x1, blocking collectives, local(): joint_max = lax.pmax(highest, 'grp')  31.1 us
  transfers between devices with their start and end apart: 2, of which 1 were waited for; matrix products, arithmetic and copies ran while one was open for 74% of the time, Pallas kernels for 0%

commit v1 on v0

--- a/solution.py
+++ b/solution.py
@@ -1,8 +1,11 @@
+import functools
 import math
 
 import jax
 import jax.numpy as jnp
 from jax import lax
+from jax.experimental import pallas as pl
+from jax.experimental.pallas import tpu as pltpu
 from jax.sharding import PartitionSpec as P
 
 RADII = 48
@@ -12,50 +15,50 @@
 score_factor = 2.0
 
 
-def turned_rows(ref_block, radius_count, angle_count):
-    block_rows = ref_block.shape[0]
-    polar_rows = ref_block.reshape(block_rows, radius_count, angle_count)
-    angle_grid = jnp.arange(angle_count, dtype=jnp.int32)
-    source_index = (angle_grid[:, None] + angle_grid[None, :]) % angle_count
-    rotated = jnp.take(polar_rows, source_index, axis=2)
-    rotated = jnp.transpose(rotated, (0, 2, 1, 3))
-    return rotated.reshape(block_rows * angle_count, radius_count * angle_count)
+def angle_major(rows):
+    count = rows.shape[0]
+    return rows.reshape(count, RADII, ANGLES).transpose(0, 2, 1).reshape(count, RADII * ANGLES)
 
 
-def group_of():
-    for group_size in (16, 8, 4, 2):
-        return group_size
-    return 1
+def score_kernel(p_ref, r_ref, max_ref, sum_ref, s_scr, *, scale):
+    flat_len = p_ref.shape[1]
+    images = p_ref[...]
 
+    def shift_scores(s, carry):
+        start = pl.multiple_of(s * RADII, 16)
+        turned = r_ref[pl.ds(start, flat_len), :]
+        scores = jnp.dot(images, turned, preferred_element_type=jnp.float32) * scale
+        s_scr[s] = scores
+        return jnp.maximum(carry, scores)
 
-def empty_stats(row_count):
-    return (jnp.full((row_count,), -jnp.inf, jnp.float32), jnp.zeros((row_count,), jnp.float32))
+    first = jnp.full(s_scr.shape[1:], -jnp.inf, jnp.float32)
+    lane_max = lax.fori_loop(0, ANGLES, shift_scores, first)
+    highest = jnp.max(lane_max, axis=1, keepdims=True)
+
+    def shift_sum(s, carry):
+        return carry + jnp.exp(s_scr[s] - highest)
+
+    lane_sum = lax.fori_loop(0, ANGLES, shift_sum, jnp.zeros(s_scr.shape[1:], jnp.float32))
+    max_ref[...] = highest
+    sum_ref[...] = jnp.sum(lane_sum, axis=1, keepdims=True)
 
 
 def score_all(images, gathered):
-    flat_len = images.shape[1]
-    score_scale = score_factor / math.sqrt(flat_len)
+    row_count, flat_len = images.shape
     ref_count = gathered.shape[0]
-    group_size = group_of()
-    ref_groups = gathered.reshape(ref_count // group_size, group_size, flat_len)
-
-    def advance(current, ref_block):
-        highest, summed = current
-        rotated = turned_rows(ref_block, RADII, ANGLES)
-        scores = (
-            lax.dot_general(
-                images, rotated, (((1,), (1,)), ((), ())), preferred_element_type=jnp.float32
-            )
-            * score_scale
-        )
-        new_max = jnp.maximum(highest, jnp.max(scores, axis=1))
-        summed = summed * jnp.exp(highest - new_max) + jnp.sum(
-            jnp.exp(scores - new_max[:, None]), axis=1
-        )
-        return ((new_max, summed), None)
-
-    result, _ = lax.scan(advance, empty_stats(images.shape[0]), ref_groups)
-    return result
+    scale = score_factor / math.sqrt(flat_len)
+    lhs = angle_major(images)
+    rhs = angle_major(gathered).T
+    rhs = jnp.concatenate([rhs, rhs], axis=0)
+    highest, summed = pl.pallas_call(
+        functools.partial(score_kernel, scale=scale),
+        out_shape=(
+            jax.ShapeDtypeStruct((row_count, 1), jnp.float32),
+            jax.ShapeDtypeStruct((row_count, 1), jnp.float32),
+        ),
+        scratch_shapes=[pltpu.VMEM((ANGLES, row_count, ref_count), jnp.float32)],
+    )(lhs, rhs)
+    return highest[:, 0], summed[:, 0]
 
 
 def local(particles, references, classes, angles, weights):

time: 897 us -> 282 us (0.31)
  local copies, waits for them, and re-layouts: 527 us -> 16.9 us
  other arithmetic: 90.5 us -> 6.45 us
  matrix products: 48 us -> 2.98 us
  Pallas kernels: 0 us -> 32.9 us
    gather x16 -> x0, local copies, waits for them, and re-layouts: 331 us -> none  [turned_rows(): rotated = jnp.take(polar_rows, source_index, axis=2)]
    reshape x25 -> x2, local copies, waits for them, and re-layouts: 186 us -> 5.02 us  [angle_major(): rows.reshape(count, RADII, ANGLES).transpose(0, 2, 1)]
    select_n x16 -> x0, other arithmetic: 85.3 us -> none  [turned_rows(): rotated = jnp.take(polar_rows, source_index, axis=2)]
    dot_general x8 -> x0, matrix products: 44 us -> none  [advance(): lax.dot_general(images, rotated, (((1,), (1,)), ((), ())), preferred_elem...]
    pallas_call x0 -> x1, Pallas kernels: none -> 32.9 us  [score_all(): pl.pallas_call(functools.partial(score_kernel, scale=scale), out_shape=(j...]
  transfers between devices with their start and end apart: 2 -> 2, of which waited for: 1 -> 1; matrix products, arithmetic and copies ran while one was open for 74% -> 5% of each run, Pallas kernels for 0% -> 12%
where the time goes in v1:
time: 282 us; the launch traced here: 281 us
  blocking collectives  190 us (67%)
  Pallas kernels  32.9 us (12%)
  local copies, waits for them, and re-layouts  16.9 us (6%)
  starting transfers between devices  16.6 us (6%)
  waiting for transfers between devices  13.8 us (5%)
  other arithmetic  6.45 us (2%)
  matrix products  2.98 us (1%)
    all_gather x1, blocking collectives, local(): gathered = lax.all_gather(references, 'loop', axis=0, tiled=True)  153 us
    pallas_call x1, Pallas kernels, score_all(): pl.pallas_call(functools.partial(score_kernel, scale=scale), out_shape=(j...  32.9 us
    pmax x1, blocking collectives, local(): joint_max = lax.pmax(highest, 'grp')  31.1 us
    all_to_all x1, waiting for transfers between devices, local(): lax.all_to_all(outgoing, 'loop', split_axis=0, concat_axis=0, tiled=True)  13.8 us
    all_to_all x1, starting transfers between devices, local(): lax.all_to_all(labels_out, 'loop', split_axis=0, concat_axis=0, tiled=True)  12 us
  transfers between devices with their start and end apart: 2, of which 1 were waited for; matrix products, arithmetic and copies ran while one was open for 5% of the time, Pallas kernels for 12%

profile of v1, /device:TPU:1, one launch (start us, length us, event | category | flops | bytes accessed | tf_op | source)
XLA Modules:
  0.0 281.0 jit_solution(5525094729728338233)
XLA Ops:
  0.6 0.7 fusion.20
  1.5 0.2 select_reduce_fusion
  1.7 0.7 convert_bitcast_fusion
  2.3 0.1 convolution_convert_fusion.1
  2.5 0.7 copy.36
  3.2 12.0 %all-to-all-start = ((bf16[64,2,3]{2,1,0:T(2,128)(2,1)}), bf16[64,2,3]{2,1,0:T(2,128)(2,1)S(1)}, u32[]{:S(2)}, u32[]{:S(2)}) async-start(bf16[64,2,3]{2,1,0:T(2,128)(2,1)} %bitcast.10), calls=%async_computation | async-start | bytes 65536 | tf_op jit(solution)/shard_map/all_to_all | solution.py:100
  15.2 1.9 copy.28
  17.2 1.6 copy.31.p_ref
  18.9 153.2 %all-gather = bf16[64,2,3456]{2,1,0:T(2,128)(2,1)S(1)} all-gather(bf16[1,2,3456]{2,1,0:T(2,128)(2,1)S(1)} %bitcast.33), channel_id=1, replica_groups=mesh['loop'=64,'grp'=2] {'loop'}, dimensions={0}, use_global_device_ids=true | all-gather | bytes 898560 | tf_op jit(solution)/shard_map/all_gather | solution.py:70
  172.1 3.4 %reshape.62 = bf16[128,48,72]{2,1,0:T(8,128)(2,1)S(1)} reshape(bf16[64,2,3456]{2,1,0:T(2,128)(2,1)S(1)} %all-gather) | data formatting | bytes 1769472 | tf_op jit(solution)/shard_map/reshape | solution.py:20
  175.5 1.3 copy.30
  176.8 1.3 pad_maximum_fusion.r_ref
  178.1 0.1 copy-done
  178.3 0.4 convolution_convert_fusion
  178.6 32.9 %shard_map.68 = (f32[128,1]{1,0:T(8,128)}, f32[128,1]{1,0:T(8,128)}) custom-call(bf16[128,3456]{1,0:T(8,128)(2,1)} %copy.31.p_ref, bf16[6912,128]{1,0:T(8,128)(2,1)} %pad_maximum_fusion.r_ref), custom_call_target="tpu_custom_call" | custom-call | tf_op jit(solution)/shard_map/pallas_call | solution.py:53
  211.6 0.9 reduce.1
  212.5 1.0 reduce
  213.5 1.3 reshape.65
  214.8 31.1 %pmax.7 = f32[128]{0:T(128)S(1)} all-reduce(f32[128]{0:T(128)S(1)} %reduce), channel_id=1, replica_groups=mesh['loop'=64,'grp'=2] {'grp'}, use_global_device_ids=true, to_apply=%region_0.0 | all-reduce | flops 128 | bytes 1024 | tf_op jit(solution)/shard_map/pmax | solution.py:72
  245.9 4.6 %all-to-all-start.1 = ((bf16[64,2,3456]{2,1,0:T(2,128)(2,1)}), bf16[64,2,3456]{2,1,0:T(2,128)(2,1)S(1)}, u32[]{:S(2)}, u32[]{:S(2)}) async-start(bf16[64,2,3456]{2,1,0:T(2,128)(2,1)} %reshape.65), calls=%async_computation.1 | async-start | bytes 1769472 | tf_op jit(solution)/shard_map/all_to_all | solution.py:99
  250.6 0.6 dynamic-slice
  251.9 0.1 copy.34
  252.0 0.1 reshape.68
  252.2 0.1 convert_reduce_fusion
  252.4 13.8 %all-to-all-done.1 = bf16[64,2,3456]{2,1,0:T(2,128)(2,1)S(1)} async-done(((bf16[64,2,3456]{2,1,0:T(2,128)(2,1)}), bf16[64,2,3456]{2,1,0:T(2,128)(2,1)S(1)}, u32[]{:S(2)}, u32[]{:S(2)}) %all-to-all-start.1) | async-done | bytes 884768 | tf_op jit(solution)/shard_map/all_to_all | solution.py:99
  266.2 3.4 %reshape.66 = bf16[128,48,72]{2,1,0:T(8,128)(2,1)S(1)} reshape(bf16[64,2,3456]{2,1,0:T(2,128)(2,1)S(1)} %all-to-all-done.1) | data formatting | bytes 1769472 | tf_op jit(solution)/shard_map/reshape | solution.py:102
  269.6 2.1 fusion.2
  271.7 2.0 copy.35
  273.8 0.3 fusion.10
  274.1 5.5 %all-reduce.2 = (f32[128]{0:T(128)S(1)}, f32[4,3456]{1,0:T(4,128)S(1)}, f32[4]{0:T(128)S(1)}) all-reduce(f32[128]{0:T(128)S(1)} %exponential_multiply_fusion, f32[4,3456]{1,0:T(4,128)S(1)} %fusion.10, f32[4]{0:T(128)S(1)} %convert_reduce_fusion), channel_id=1, replica_groups=mesh['loop'=64,'grp'=2] {'grp'}, use_global_device_ids=true, to_apply=%region_1.0 | all-reduce | flops 13956 | bytes 111648 | tf_op jit(solution)/shard_map/psum | solution.py:73
  279.6 0.6 log_add_fusion
  280.3 0.7 dynamic-slice_divide_fusion
  (16 shorter events, 0.6 us)
Async XLA Ops:
  3.2 242.6 %all-to-all-start = ((bf16[64,2,3]{2,1,0:T(2,128)(2,1)}), bf16[64,2,3]{2,1,0:T(2,128)(2,1)S(1)}, u32[]{:S(2)}, u32[]{:S(2)}) async-start(bf16[64,2,3]{2,1,0:T(2,128)(2,1)} %bitcast.10), calls=%async_computation | async-start | bytes 65536 | tf_op jit(solution)/shard_map/all_to_all | solution.py:100
  17.1 1.8 copy-start.1
  176.8 1.5 copy-start
  213.5 37.1 %copy-start.2 = (u32[128]{0:T(128)S(1)}, u32[128]{0:T(128)}, u32[]{:S(2)}) copy-start(u32[128]{0:T(128)} %constant.58) | copy-start | bytes 1540
  245.9 20.4 %all-to-all-start.1 = ((bf16[64,2,3456]{2,1,0:T(2,128)(2,1)}), bf16[64,2,3456]{2,1,0:T(2,128)(2,1)S(1)}, u32[]{:S(2)}, u32[]{:S(2)}) async-start(bf16[64,2,3456]{2,1,0:T(2,128)(2,1)} %reshape.65), calls=%async_computation.1 | async-start | bytes 1769472 | tf_op jit(solution)/shard_map/all_to_all | solution.py:99

commit v2 on v1

--- a/solution.py
+++ b/solution.py
@@ -61,13 +61,38 @@
     return highest[:, 0], summed[:, 0]
 
 
+def ring_factors(count):
+    factors = []
+    while count > 1:
+        factor = 4 if count % 4 == 0 else count
+        factors.append(factor)
+        count //= factor
+    return factors
+
+
+def staged_gather(rows, axis):
+    count = lax.axis_size(axis)
+    stride = 1
+    for factor in ring_factors(count):
+        parts = [rows]
+        for step in range(1, factor):
+            pairs = []
+            for source in range(count):
+                digit = (source // stride) % factor
+                pairs.append((source, source + ((digit + step) % factor - digit) * stride))
+            parts.append(lax.ppermute(rows, axis, pairs))
+        rows = jnp.concatenate(parts, axis=0)
+        stride *= factor
+    return rows
+
+
 def local(particles, references, classes, angles, weights):
     row_count, flat_len = particles.shape
     grp_size = lax.axis_size("grp")
     half_rows = row_count // grp_size
     grp_index = lax.axis_index("grp")
     own_rows = lax.dynamic_slice_in_dim(particles, grp_index * half_rows, half_rows, 0)
-    gathered = lax.all_gather(references, "loop", axis=0, tiled=True)
+    gathered = staged_gather(references, "loop")
     highest, summed = score_all(particles, gathered)
     joint_max = lax.pmax(highest, "grp")
     summed = lax.psum(summed * jnp.exp(highest - joint_max), "grp")

time: 282 us -> 129 us (0.46)
  blocking collectives: 190 us -> 8.32 us
  starting transfers between devices: 16.6 us -> 33.3 us
  local copies, waits for them, and re-layouts: 16.9 us -> 32.5 us
  waiting for transfers between devices: 13.8 us -> 10.6 us
    all_gather x1 -> x0, blocking collectives: 153 us -> none  [local(): gathered = lax.all_gather(references, 'loop', axis=0, tiled=True)]
    pmax x1, blocking collectives: 31.1 us -> 4.57 us  [local(): joint_max = lax.pmax(highest, 'grp')]
    ppermute x0 -> x9, starting transfers between devices: none -> 15.4 us  [staged_gather(): parts.append(lax.ppermute(rows, axis, pairs))]
    all_to_all x1, waiting for transfers between devices: 13.8 us -> 0.01 us  [local(): lax.all_to_all(outgoing, 'loop', split_axis=0, concat_axis=0, tiled=True)]
    ppermute x0 -> x9, local copies, waits for them, and re-layouts: none -> 9.94 us  [staged_gather(): parts.append(lax.ppermute(rows, axis, pairs))]
    ppermute x0 -> x9, waiting for transfers between devices: none -> 9.84 us  [staged_gather(): parts.append(lax.ppermute(rows, axis, pairs))]
    concatenate x0 -> x2, local copies, waits for them, and re-layouts: none -> 8.83 us  [staged_gather(): rows = jnp.concatenate(parts, axis=0)]
    all_to_all x1, starting transfers between devices: 4.65 us -> 9.3 us  [local(): lax.all_to_all(outgoing, 'loop', split_axis=0, concat_axis=0, tiled=True)]
  transfers between devices with their start and end apart: 2 -> 11, of which waited for: 1 -> 2; matrix products, arithmetic and copies ran while one was open for 5% -> 26% of each run, Pallas kernels for 12% -> 26%
where the time goes in v2:
time: 129 us; the launch traced here: 128 us
  starting transfers between devices  33.3 us (26%)
  Pallas kernels  32.9 us (26%)
  local copies, waits for them, and re-layouts  32.5 us (25%)
  waiting for transfers between devices  10.6 us (8%)
  blocking collectives  8.32 us (6%)
  other arithmetic  7.18 us (6%)
  matrix products  1.83 us (1%)
  between operations  1.54 us (1%)
    pallas_call x1, Pallas kernels, score_all(): pl.pallas_call(functools.partial(score_kernel, scale=scale), out_shape=(j...  32.9 us
    ppermute x9, starting transfers between devices, staged_gather(): parts.append(lax.ppermute(rows, axis, pairs))  15.4 us
    ppermute x9, local copies, waits for them, and re-layouts, staged_gather(): parts.append(lax.ppermute(rows, axis, pairs))  9.94 us
    ppermute x9, waiting for transfers between devices, staged_gather(): parts.append(lax.ppermute(rows, axis, pairs))  9.84 us
    all_to_all x1, starting transfers between devices, local(): lax.all_to_all(outgoing, 'loop', split_axis=0, concat_axis=0, tiled=True)  9.3 us
    concatenate x2, local copies, waits for them, and re-layouts, staged_gather(): rows = jnp.concatenate(parts, axis=0)  8.83 us
    all_to_all x1, starting transfers between devices, local(): lax.all_to_all(labels_out, 'loop', split_axis=0, concat_axis=0, tiled=True)  8.62 us
    reshape x1, local copies, waits for them, and re-layouts, local(): images = incoming.reshape(slot_count, RADII, ANGLES)  4.83 us
  transfers between devices with their start and end apart: 11, of which 2 were waited for; matrix products, arithmetic and copies ran while one was open for 26% of the time, Pallas kernels for 26%

profile of v2, /device:TPU:1, one launch (start us, length us, event | category | flops | bytes accessed | tf_op | source)
XLA Modules:
  0.0 128.2 jit_solution(1935263101039808382)
XLA Ops:
  0.6 2.2 %collective-permute-start = (bf16[2,3456]{1,0:T(2,128)(2,1)}, bf16[2,3456]{1,0:T(2,128)(2,1)S(1)}, u32[]{:S(2)}, u32[]{:S(2)}) collective-permute-start(bf16[2,3456]{1,0:T(2,128)(2,1)} %param.6), channel_id=1, source_target_pairs={{0,2},{2,4},{4,6},{6,0},{8,10},{10,12},{12,14},{14,8},{16,18},{18,... | collective-permute-start | bytes 41480 | tf_op jit(solution)/shard_map/ppermute | solution.py:83
  2.8 2.6 %collective-permute-start.1 = (bf16[2,3456]{1,0:T(2,128)(2,1)}, bf16[2,3456]{1,0:T(2,128)(2,1)S(1)}, u32[]{:S(2)}, u32[]{:S(2)}) collective-permute-start(bf16[2,3456]{1,0:T(2,128)(2,1)} %param.6), channel_id=1, source_target_pairs={{0,4},{2,6},{4,0},{6,2},{8,12},{10,14},{12,8},{14,10},{16,20},{18,... | collective-permute-start | bytes 41480 | tf_op jit(solution)/shard_map/ppermute | solution.py:83
  5.5 1.1 collective-permute-start.2
  9.1 8.6 %all-to-all-start = ((bf16[64,2,3]{2,1,0:T(2,128)(2,1)}), bf16[64,2,3]{2,1,0:T(2,128)(2,1)S(1)}, u32[]{:S(2)}, u32[]{:S(2)}) async-start(bf16[64,2,3]{2,1,0:T(2,128)(2,1)} %bitcast.10), calls=%async_computation | async-start | bytes 65536 | tf_op jit(solution)/shard_map/all_to_all | solution.py:125
  17.7 2.0 %copy.56 = bf16[2,3456]{0,1:T(8,128)(2,1)} copy(bf16[2,3456]{1,0:T(2,128)(2,1)} %param.6) | data formatting | bytes 27648 | tf_op args[1]
  19.8 1.0 copy.54
  21.3 1.7 %copy.67.p_ref = bf16[128,3456]{1,0:T(8,128)(2,1)} copy(bf16[128,3456]{0,1:T(8,128)(2,1)S(1)} %bitcast.32) | data formatting | bytes 1769472 | tf_op jit(solution)/shard_map/reshape | solution.py:20
  22.9 1.2 reshape.65
  26.1 9.3 %all-to-all-start.1 = ((bf16[64,2,3456]{2,1,0:T(2,128)(2,1)}), bf16[64,2,3456]{2,1,0:T(2,128)(2,1)}, u32[]{:S(2)}, u32[]{:S(2)}) async-start(bf16[64,2,3456]{2,1,0:T(2,128)(2,1)} %reshape.65), calls=%async_computation.1 | async-start | bytes 1769472 | tf_op jit(solution)/shard_map/all_to_all | solution.py:124
  36.0 1.0 collective-permute-start.3
  37.0 2.4 %collective-permute-start.4 = (bf16[8,3456]{1,0:T(8,128)(2,1)S(1)}, bf16[8,3456]{1,0:T(8,128)(2,1)S(1)}, u32[]{:S(2)}, u32[]{:S(2)}) collective-permute-start(bf16[8,3456]{1,0:T(8,128)(2,1)S(1)} %pad_maximum_fusion.1), channel_id=1, source_target_pairs={{0,16},{2,18},{4,20},{6,22},{8,24},{10,26},{12,28},{14,30},{16,0},... | collective-permute-start | bytes 165896 | tf_op jit(solution)/shard_map/ppermute | solution.py:83
  39.4 1.2 collective-permute-start.5
  40.7 9.8 %collective-permute-done.4 = bf16[8,3456]{1,0:T(8,128)(2,1)S(1)} collective-permute-done((bf16[8,3456]{1,0:T(8,128)(2,1)S(1)}, bf16[8,3456]{1,0:T(8,128)(2,1)S(1)}, u32[]{:S(2)}, u32[]{:S(2)}) %collective-permute-start.4) | collective-permute-done | bytes 55328 | tf_op jit(solution)/shard_map/ppermute | solution.py:83
  50.6 1.9 %collective-permute-start.6 = (bf16[32,3456]{1,0:T(8,128)(2,1)S(1)}, bf16[32,3456]{1,0:T(8,128)(2,1)}, u32[]{:S(2)}, u32[]{:S(2)}) collective-permute-start(bf16[32,3456]{1,0:T(8,128)(2,1)S(1)} %concatenate.15), channel_id=1, source_target_pairs={{0,32},{2,34},{4,36},{6,38},{8,40},{10,42},{12,44},{14,46},{16,48}... | collective-permute-start | bytes 663560 | tf_op jit(solution)/shard_map/ppermute | solution.py:83
  52.6 2.0 %collective-permute-start.7 = (bf16[32,3456]{1,0:T(8,128)(2,1)S(1)}, bf16[32,3456]{1,0:T(8,128)(2,1)S(1)}, u32[]{:S(2)}, u32[]{:S(2)}) collective-permute-start(bf16[32,3456]{1,0:T(8,128)(2,1)S(1)} %concatenate.15), channel_id=1, source_target_pairs={{0,64},{2,66},{4,68},{6,70},{8,72},{10,74},{12,76},{14,78},{16,80}... | collective-permute-start | bytes 663560 | tf_op jit(solution)/shard_map/ppermute | solution.py:83
  54.6 0.9 collective-permute-start.8
  56.3 1.3 %copy.57 = bf16[2,3456]{0,1:T(8,128)(2,1)} copy(bf16[2,3456]{1,0:T(2,128)(2,1)S(1)} %collective-permute-done) | data formatting | bytes 27648 | tf_op jit(solution)/shard_map/ppermute | solution.py:83
  57.6 1.3 %copy.58 = bf16[2,3456]{0,1:T(8,128)(2,1)} copy(bf16[2,3456]{1,0:T(2,128)(2,1)S(1)} %collective-permute-done.1) | data formatting | bytes 27648 | tf_op jit(solution)/shard_map/ppermute | solution.py:83
  58.9 1.3 %copy.59 = bf16[2,3456]{0,1:T(8,128)(2,1)} copy(bf16[2,3456]{1,0:T(2,128)(2,1)S(1)} %collective-permute-done.2) | data formatting | bytes 27648 | tf_op jit(solution)/shard_map/ppermute | solution.py:83
  61.5 2.2 %copy.63 = bf16[32,3456]{0,1:T(8,128)(2,1)} copy(bf16[32,3456]{1,0:T(8,128)(2,1)} %collective-permute-done.6) | data formatting | bytes 442368 | tf_op jit(solution)/shard_map/ppermute | solution.py:83
  63.7 1.2 copy.64
  64.9 1.3 %copy.65 = bf16[32,3456]{0,1:T(8,128)(2,1)} copy(bf16[32,3456]{1,0:T(8,128)(2,1)S(1)} %collective-permute-done.8) | data formatting | bytes 442368 | tf_op jit(solution)/shard_map/ppermute | solution.py:83
  66.2 8.7 %concatenate.16 = bf16[128,3456]{0,1:T(8,128)(2,1)S(1)} concatenate(bf16[2,3456]{0,1:T(8,128)(2,1)} %copy.56, bf16[2,3456]{0,1:T(8,128)(2,1)} %copy.57, bf16[2,3456]{0,1:T(8,128)(2,1)} %copy.58, bf16[2,3456]{0,1:T(8,128)(2,1)} %copy.59, bf16[8,3456]{0,1:T(8,128)(2,1)S(1)} %copy.60, bf16[8,3456]{0,1:T(8,128)(2,1)S(1)} %copy.61, bf16[8,3456]{0,1:T(8,128)(2,1)S(1)} %copy.62, ...), dimensions={0} | concatenate | bytes 1769472 | tf_op jit(solution)/shard_map/concatenate | solution.py:84
  75.1 1.3 %pad_maximum_fusion.r_ref = bf16[6912,128]{1,0:T(8,128)(2,1)} fusion(bf16[3456,128]{1,0:T(8,128)(2,1)S(1)} %bitcast.33), kind=kLoop, calls=%fused_computation.4 | loop fusion | flops 3538944 | bytes 2654208 | tf_op jit(solution)/shard_map/concatenate | solution.py:52
  76.4 32.9 %shard_map.68 = (f32[128,1]{1,0:T(8,128)}, f32[128,1]{1,0:T(8,128)}) custom-call(bf16[128,3456]{1,0:T(8,128)(2,1)} %copy.67.p_ref, bf16[6912,128]{1,0:T(8,128)(2,1)} %pad_maximum_fusion.r_ref), custom_call_target="tpu_custom_call" | custom-call | tf_op jit(solution)/shard_map/pallas_call | solution.py:53
  109.3 1.0 reduce
  110.3 1.0 reduce.1
  111.3 4.6 %pmax.7 = f32[128]{0:T(128)S(1)} all-reduce(f32[128]{0:T(128)S(1)} %reduce), channel_id=1, replica_groups=mesh['loop'=64,'grp'=2] {'grp'}, use_global_device_ids=true, to_apply=%region_0.0 | all-reduce | flops 128 | bytes 1024 | tf_op jit(solution)/shard_map/pmax | solution.py:97
  115.9 4.8 %reshape.66 = bf16[128,48,72]{2,1,0:T(8,128)(2,1)S(1)} reshape(bf16[64,2,3456]{2,1,0:T(2,128)(2,1)} %all-to-all-done.1) | data formatting | bytes 1769472 | tf_op jit(solution)/shard_map/reshape | solution.py:127
  120.7 1.0 fusion.2
  121.7 1.0 copy.71
  123.1 3.7 %all-reduce.2 = (f32[128]{0:T(128)S(1)}, f32[4,3456]{1,0:T(4,128)S(1)}, f32[4]{0:T(128)S(1)}) all-reduce(f32[128]{0:T(128)S(1)} %exponential_multiply_fusion, f32[4,3456]{1,0:T(4,128)S(1)} %fusion.10, f32[4]{0:T(128)S(1)} %convert_reduce_fusion), channel_id=1, replica_groups=mesh['loop'=64,'grp'=2] {'grp'}, use_global_device_ids=true, to_apply=%region_1.0 | all-reduce | flops 13956 | bytes 111648 | tf_op jit(solution)/shard_map/psum | solution.py:98
  (47 shorter events, 9.0 us)
Async XLA Ops:
  0.6 19.1 %copy-start = (bf16[128,3456]{1,0:T(8,128)(2,1)S(1)}, bf16[128,3456]{1,0:T(8,128)(2,1)}, u32[]{:S(2)}) copy-start(bf16[128,3456]{1,0:T(8,128)(2,1)} %param.5) | copy-start | bytes 2654212
  0.6 35.2 %collective-permute-start = (bf16[2,3456]{1,0:T(2,128)(2,1)}, bf16[2,3456]{1,0:T(2,128)(2,1)S(1)}, u32[]{:S(2)}, u32[]{:S(2)}) collective-permute-start(bf16[2,3456]{1,0:T(2,128)(2,1)} %param.6), channel_id=1, source_target_pairs={{0,2},{2,4},{4,6},{6,0},{8,10},{10,12},{12,14},{14,8},{16,18},{18,... | collective-permute-start | bytes 41480 | tf_op jit(solution)/shard_map/ppermute | solution.py:83
  2.8 33.0 %collective-permute-start.1 = (bf16[2,3456]{1,0:T(2,128)(2,1)}, bf16[2,3456]{1,0:T(2,128)(2,1)S(1)}, u32[]{:S(2)}, u32[]{:S(2)}) collective-permute-start(bf16[2,3456]{1,0:T(2,128)(2,1)} %param.6), channel_id=1, source_target_pairs={{0,4},{2,6},{4,0},{6,2},{8,12},{10,14},{12,8},{14,10},{16,20},{18,... | collective-permute-start | bytes 41480 | tf_op jit(solution)/shard_map/ppermute | solution.py:83
  5.5 30.4 %collective-permute-start.2 = (bf16[2,3456]{1,0:T(2,128)(2,1)}, bf16[2,3456]{1,0:T(2,128)(2,1)S(1)}, u32[]{:S(2)}, u32[]{:S(2)}) collective-permute-start(bf16[2,3456]{1,0:T(2,128)(2,1)} %param.6), channel_id=1, source_target_pairs={{0,6},{2,0},{4,2},{6,4},{8,14},{10,8},{12,10},{14,12},{16,22},{18,... | collective-permute-start | bytes 41480 | tf_op jit(solution)/shard_map/ppermute | solution.py:83
  9.1 17.0 %all-to-all-start = ((bf16[64,2,3]{2,1,0:T(2,128)(2,1)}), bf16[64,2,3]{2,1,0:T(2,128)(2,1)S(1)}, u32[]{:S(2)}, u32[]{:S(2)}) async-start(bf16[64,2,3]{2,1,0:T(2,128)(2,1)} %bitcast.10), calls=%async_computation | async-start | bytes 65536 | tf_op jit(solution)/shard_map/all_to_all | solution.py:125
  21.3 2.9 %copy-start.3 = (u32[128]{0:T(128)S(1)}, u32[128]{0:T(128)}, u32[]{:S(2)}) copy-start(u32[128]{0:T(128)} %constant.58) | copy-start | bytes 1540
  22.9 13.0 %copy-start.1 = (bf16[2,3456]{1,0:T(2,128)(2,1)S(1)}, bf16[2,3456]{1,0:T(2,128)(2,1)}, u32[]{:S(2)}) copy-start(bf16[2,3456]{1,0:T(2,128)(2,1)} %param.6) | copy-start | bytes 41476
  26.1 89.7 %all-to-all-start.1 = ((bf16[64,2,3456]{2,1,0:T(2,128)(2,1)}), bf16[64,2,3456]{2,1,0:T(2,128)(2,1)}, u32[]{:S(2)}, u32[]{:S(2)}) async-start(bf16[64,2,3456]{2,1,0:T(2,128)(2,1)} %reshape.65), calls=%async_computation.1 | async-start | bytes 1769472 | tf_op jit(solution)/shard_map/all_to_all | solution.py:124
  36.0 4.7 %collective-permute-start.3 = (bf16[8,3456]{1,0:T(8,128)(2,1)S(1)}, bf16[8,3456]{1,0:T(8,128)(2,1)S(1)}, u32[]{:S(2)}, u32[]{:S(2)}) collective-permute-start(bf16[8,3456]{1,0:T(8,128)(2,1)S(1)} %pad_maximum_fusion.1), channel_id=1, source_target_pairs={{0,8},{2,10},{4,12},{6,14},{8,16},{10,18},{12,20},{14,22},{16,24},... | collective-permute-start | bytes 165896 | tf_op jit(solution)/shard_map/ppermute | solution.py:83
  37.0 13.5 %collective-permute-start.4 = (bf16[8,3456]{1,0:T(8,128)(2,1)S(1)}, bf16[8,3456]{1,0:T(8,128)(2,1)S(1)}, u32[]{:S(2)}, u32[]{:S(2)}) collective-permute-start(bf16[8,3456]{1,0:T(8,128)(2,1)S(1)} %pad_maximum_fusion.1), channel_id=1, source_target_pairs={{0,16},{2,18},{4,20},{6,22},{8,24},{10,26},{12,28},{14,30},{16,0},... | collective-permute-start | bytes 165896 | tf_op jit(solution)/shard_map/ppermute | solution.py:83
  39.4 11.1 %collective-permute-start.5 = (bf16[8,3456]{1,0:T(8,128)(2,1)S(1)}, bf16[8,3456]{1,0:T(8,128)(2,1)S(1)}, u32[]{:S(2)}, u32[]{:S(2)}) collective-permute-start(bf16[8,3456]{1,0:T(8,128)(2,1)S(1)} %pad_maximum_fusion.1), channel_id=1, source_target_pairs={{0,24},{2,26},{4,28},{6,30},{8,0},{10,2},{12,4},{14,6},{16,8},{18,... | collective-permute-start | bytes 165896 | tf_op jit(solution)/shard_map/ppermute | solution.py:83
  50.6 10.9 %collective-permute-start.6 = (bf16[32,3456]{1,0:T(8,128)(2,1)S(1)}, bf16[32,3456]{1,0:T(8,128)(2,1)}, u32[]{:S(2)}, u32[]{:S(2)}) collective-permute-start(bf16[32,3456]{1,0:T(8,128)(2,1)S(1)} %concatenate.15), channel_id=1, source_target_pairs={{0,32},{2,34},{4,36},{6,38},{8,40},{10,42},{12,44},{14,46},{16,48}... | collective-permute-start | bytes 663560 | tf_op jit(solution)/shard_map/ppermute | solution.py:83
  52.6 11.1 %collective-permute-start.7 = (bf16[32,3456]{1,0:T(8,128)(2,1)S(1)}, bf16[32,3456]{1,0:T(8,128)(2,1)S(1)}, u32[]{:S(2)}, u32[]{:S(2)}) collective-permute-start(bf16[32,3456]{1,0:T(8,128)(2,1)S(1)} %concatenate.15), channel_id=1, source_target_pairs={{0,64},{2,66},{4,68},{6,70},{8,72},{10,74},{12,76},{14,78},{16,80}... | collective-permute-start | bytes 663560 | tf_op jit(solution)/shard_map/ppermute | solution.py:83
  54.6 10.3 %collective-permute-start.8 = (bf16[32,3456]{1,0:T(8,128)(2,1)S(1)}, bf16[32,3456]{1,0:T(8,128)(2,1)S(1)}, u32[]{:S(2)}, u32[]{:S(2)}) collective-permute-start(bf16[32,3456]{1,0:T(8,128)(2,1)S(1)} %concatenate.15), channel_id=1, source_target_pairs={{0,96},{2,98},{4,100},{6,102},{8,104},{10,106},{12,108},{14,110},{... | collective-permute-start | bytes 663560 | tf_op jit(solution)/shard_map/ppermute | solution.py:83
  109.3 11.4 %copy-start.2 = (f32[128,72]{1,0:T(8,128)S(1)}, f32[128,72]{1,0:T(8,128)}, u32[]{:S(2)}) copy-start(f32[128,72]{1,0:T(8,128)} %add_select_fusion) | copy-start | bytes 110596

commit v3 on v2

--- a/solution.py
+++ b/solution.py
@@ -20,13 +20,16 @@
     return rows.reshape(count, RADII, ANGLES).transpose(0, 2, 1).reshape(count, RADII * ANGLES)
 
 
-def score_kernel(p_ref, r_ref, max_ref, sum_ref, s_scr, *, scale):
+def score_kernel(p_ref, g_ref, max_ref, sum_ref, r_scr, s_scr, *, scale):
     flat_len = p_ref.shape[1]
+    columns = g_ref[...].T
+    r_scr[pl.ds(0, flat_len), :] = columns
+    r_scr[pl.ds(flat_len, flat_len), :] = columns
     images = p_ref[...]
 
     def shift_scores(s, carry):
         start = pl.multiple_of(s * RADII, 16)
-        turned = r_ref[pl.ds(start, flat_len), :]
+        turned = r_scr[pl.ds(start, flat_len), :]
         scores = jnp.dot(images, turned, preferred_element_type=jnp.float32) * scale
         s_scr[s] = scores
         return jnp.maximum(carry, scores)
@@ -43,21 +46,21 @@
     sum_ref[...] = jnp.sum(lane_sum, axis=1, keepdims=True)
 
 
-def score_all(images, gathered):
-    row_count, flat_len = images.shape
+def score_all(lhs, gathered):
+    row_count, flat_len = lhs.shape
     ref_count = gathered.shape[0]
     scale = score_factor / math.sqrt(flat_len)
-    lhs = angle_major(images)
-    rhs = angle_major(gathered).T
-    rhs = jnp.concatenate([rhs, rhs], axis=0)
     highest, summed = pl.pallas_call(
         functools.partial(score_kernel, scale=scale),
         out_shape=(
             jax.ShapeDtypeStruct((row_count, 1), jnp.float32),
             jax.ShapeDtypeStruct((row_count, 1), jnp.float32),
         ),
-        scratch_shapes=[pltpu.VMEM((ANGLES, row_count, ref_count), jnp.float32)],
-    )(lhs, rhs)
+        scratch_shapes=[
+            pltpu.VMEM((2 * flat_len, ref_count), jnp.bfloat16),
+            pltpu.VMEM((ANGLES, row_count, ref_count), jnp.float32),
+        ],
+    )(lhs, gathered)
     return highest[:, 0], summed[:, 0]
 
 
@@ -92,8 +95,8 @@
     half_rows = row_count // grp_size
     grp_index = lax.axis_index("grp")
     own_rows = lax.dynamic_slice_in_dim(particles, grp_index * half_rows, half_rows, 0)
-    gathered = staged_gather(references, "loop")
-    highest, summed = score_all(particles, gathered)
+    gathered = staged_gather(angle_major(references), "loop")
+    highest, summed = score_all(angle_major(particles), gathered)
     joint_max = lax.pmax(highest, "grp")
     summed = lax.psum(summed * jnp.exp(highest - joint_max), "grp")
     highest = joint_max
@@ -115,15 +118,16 @@
     placement = (jnp.arange(slot_count, dtype=jnp.int32)[:, None] == target_slot[None, :]).astype(
         jnp.bfloat16
     )
+    labels = jnp.stack([member_of, angles, weights], axis=1).astype(jnp.bfloat16)
+    label_lanes = 128
+    labels = jnp.pad(labels, ((0, 0), (0, label_lanes - labels.shape[1])))
+    own_rows = jnp.concatenate([own_rows, labels], axis=1)
     outgoing = jnp.dot(placement, own_rows, preferred_element_type=jnp.float32).astype(jnp.bfloat16)
-    outgoing = outgoing.reshape(owner_count, capacity, flat_len)
-    labels = jnp.stack([member_of, angles, weights], axis=1).astype(jnp.bfloat16)
-    labels_out = jnp.dot(placement, labels, preferred_element_type=jnp.float32).astype(jnp.bfloat16)
-    labels_out = labels_out.reshape(owner_count, capacity, 3)
-    incoming, labels_in = (
-        lax.all_to_all(outgoing, "loop", split_axis=0, concat_axis=0, tiled=True),
-        lax.all_to_all(labels_out, "loop", split_axis=0, concat_axis=0, tiled=True),
-    )
+    outgoing = outgoing.reshape(owner_count, capacity, flat_len + label_lanes)
+    incoming = lax.all_to_all(outgoing, "loop", split_axis=0, concat_axis=0, tiled=True)
+    incoming = incoming.reshape(slot_count, flat_len + label_lanes)
+    labels_in = incoming[:, flat_len : flat_len + 3]
+    incoming = incoming[:, :flat_len]
     images = incoming.reshape(slot_count, RADII, ANGLES)
     labels_in = labels_in.reshape(slot_count, 3).astype(jnp.float32)
     member_in = labels_in[:, 0]

time: 129 us -> 109 us (0.84)
  local copies, waits for them, and re-layouts: 32.5 us -> 19 us
  starting transfers between devices: 33.3 us -> 24.1 us
  waiting for transfers between devices: 10.6 us -> 14.4 us
  other arithmetic: 7.18 us -> 5.21 us
    ppermute x9 -> x0, local copies, waits for them, and re-layouts: 9.94 us -> none  [staged_gather(): parts.append(lax.ppermute(rows, axis, pairs))]
    all_to_all x1 -> x0, starting transfers between devices: 8.62 us -> none  [local(): lax.all_to_all(labels_out, 'loop', split_axis=0, concat_axis=0, tiled=True)]
    ppermute x9, waiting for transfers between devices: 9.84 us -> 14.4 us  [staged_gather(): parts.append(lax.ppermute(rows, axis, pairs))]
    reshape x1, local copies, waits for them, and re-layouts: 4.83 us -> 0.99 us  [local(): images = incoming.reshape(slot_count, RADII, ANGLES)]
    unnamed x12 -> x16, local copies, waits for them, and re-layouts: 3.66 us -> 1.78 us
    concatenate x2, local copies, waits for them, and re-layouts: 8.83 us -> 7.37 us  [staged_gather(): rows = jnp.concatenate(parts, axis=0)]
    concatenate x1 -> x0, other arithmetic: 1.34 us -> none  [score_all(): rhs = jnp.concatenate([rhs, rhs], axis=0)]
    reshape x1 -> x4, local copies, waits for them, and re-layouts: 1.66 us -> 2.77 us  [angle_major(): rows.reshape(count, RADII, ANGLES).transpose(0, 2, 1)]
  transfers between devices with their start and end apart: 11 -> 10, of which waited for: 2 -> 3; matrix products, arithmetic and copies ran while one was open for 26% -> 16% of each run, Pallas kernels for 26% -> 30%
where the time goes in v3:
time: 109 us; the launch traced here: 108 us
  Pallas kernels  32.9 us (30%)
  starting transfers between devices  24.1 us (22%)
  local copies, waits for them, and re-layouts  19 us (17%)
  waiting for transfers between devices  14.4 us (13%)
  blocking collectives  8.23 us (8%)
  other arithmetic  5.21 us (5%)
  matrix products  2.85 us (3%)
  between operations  1.53 us (1%)
    pallas_call x1, Pallas kernels, score_all(): pl.pallas_call(functools.partial(score_kernel, scale=scale), out_shape=(j...  32.9 us
    ppermute x9, starting transfers between devices, staged_gather(): parts.append(lax.ppermute(rows, axis, pairs))  15.4 us
    ppermute x9, waiting for transfers between devices, staged_gather(): parts.append(lax.ppermute(rows, axis, pairs))  14.4 us
    all_to_all x1, starting transfers between devices, local(): lax.all_to_all(outgoing, 'loop', split_axis=0, concat_axis=0, tiled=True)  8.74 us
    concatenate x2, local copies, waits for them, and re-layouts, staged_gather(): rows = jnp.concatenate(parts, axis=0)  7.37 us
    pmax x1, blocking collectives, local(): joint_max = lax.pmax(highest, 'grp')  4.48 us
    psum x1, blocking collectives, local(): summed = lax.psum(summed * jnp.exp(highest - joint_max), 'grp')  3.75 us
    reshape x4, local copies, waits for them, and re-layouts, angle_major(): rows.reshape(count, RADII, ANGLES).transpose(0, 2, 1)  2.77 us
  transfers between devices with their start and end apart: 10, of which 3 were waited for; matrix products, arithmetic and copies ran while one was open for 16% of the time, Pallas kernels for 30%

profile of v3, /device:TPU:1, one launch (start us, length us, event | category | flops | bytes accessed | tf_op | source)
XLA Modules:
  0.0 108.2 jit_solution(16871687900261475111)
XLA Ops:
  0.6 0.8 reshape.59
  1.7 2.2 %collective-permute-start = (bf16[2,3456]{1,0:T(2,128)(2,1)S(1)}, bf16[2,3456]{1,0:T(2,128)(2,1)S(1)}, u32[]{:S(2)}, u32[]{:S(2)}) collective-permute-start(bf16[2,3456]{1,0:T(2,128)(2,1)S(1)} %reshape.60), channel_id=1, source_target_pairs={{0,2},{2,4},{4,6},{6,0},{8,10},{10,12},{12,14},{14,8},{16,18},{18,... | collective-permute-start | bytes 41480 | tf_op jit(solution)/shard_map/ppermute | solution.py:86
  3.9 2.6 %collective-permute-start.1 = (bf16[2,3456]{1,0:T(2,128)(2,1)S(1)}, bf16[2,3456]{1,0:T(2,128)(2,1)S(1)}, u32[]{:S(2)}, u32[]{:S(2)}) collective-permute-start(bf16[2,3456]{1,0:T(2,128)(2,1)S(1)} %reshape.60), channel_id=1, source_target_pairs={{0,4},{2,6},{4,0},{6,2},{8,12},{10,14},{12,8},{14,10},{16,20},{18,... | collective-permute-start | bytes 41480 | tf_op jit(solution)/shard_map/ppermute | solution.py:86
  6.5 1.1 collective-permute-start.2
  7.6 0.7 and_select_fusion.1
  8.6 0.7 convert_bitcast_fusion
  9.4 1.0 constant_dynamic-slice_fusion
  10.8 1.3 %reshape.61 = bf16[64,2,3584]{2,1,0:T(2,128)(2,1)} reshape(bf16[128,3584]{1,0:T(8,128)(2,1)S(1)} %convolution_convert_fusion) | data formatting | bytes 1835008 | tf_op jit(solution)/shard_map/reshape | solution.py:126
  12.1 8.7 %all-to-all-start = ((bf16[64,2,3584]{2,1,0:T(2,128)(2,1)}), bf16[64,2,3584]{2,1,0:T(2,128)(2,1)S(1)}, u32[]{:S(2)}, u32[]{:S(2)}) async-start(bf16[64,2,3584]{2,1,0:T(2,128)(2,1)} %reshape.61), calls=%async_computation | async-start | bytes 1835008 | tf_op jit(solution)/shard_map/all_to_all | solution.py:127
  21.0 1.1 collective-permute-start.3
  22.1 2.4 %collective-permute-start.4 = (bf16[8,3456]{1,0:T(8,128)(2,1)S(1)}, bf16[8,3456]{1,0:T(8,128)(2,1)S(1)}, u32[]{:S(2)}, u32[]{:S(2)}) collective-permute-start(bf16[8,3456]{1,0:T(8,128)(2,1)S(1)} %pad_maximum_fusion), channel_id=1, source_target_pairs={{0,16},{2,18},{4,20},{6,22},{8,24},{10,26},{12,28},{14,30},{16,0},... | collective-permute-start | bytes 165896 | tf_op jit(solution)/shard_map/ppermute | solution.py:86
  24.5 1.2 %collective-permute-start.5 = (bf16[8,3456]{1,0:T(8,128)(2,1)S(1)}, bf16[8,3456]{1,0:T(8,128)(2,1)S(1)}, u32[]{:S(2)}, u32[]{:S(2)}) collective-permute-start(bf16[8,3456]{1,0:T(8,128)(2,1)S(1)} %pad_maximum_fusion), channel_id=1, source_target_pairs={{0,24},{2,26},{4,28},{6,30},{8,0},{10,2},{12,4},{14,6},{16,8},{18,... | collective-permute-start | bytes 165896 | tf_op jit(solution)/shard_map/ppermute | solution.py:86
  25.7 10.2 %collective-permute-done.4 = bf16[8,3456]{1,0:T(8,128)(2,1)S(1)} collective-permute-done((bf16[8,3456]{1,0:T(8,128)(2,1)S(1)}, bf16[8,3456]{1,0:T(8,128)(2,1)S(1)}, u32[]{:S(2)}, u32[]{:S(2)}) %collective-permute-start.4) | collective-permute-done | bytes 55328 | tf_op jit(solution)/shard_map/ppermute | solution.py:86
  36.2 2.6 %concatenate.15 = bf16[32,3456]{1,0:T(8,128)(2,1)} concatenate(bf16[2,3456]{1,0:T(2,128)(2,1)S(1)} %reshape.60, bf16[2,3456]{1,0:T(2,128)(2,1)S(1)} %collective-permute-done, bf16[2,3456]{1,0:T(2,128)(2,1)S(1)} %collective-permute-done.1, bf16[2,3456]{1,0:T(2,128)(2,1)S(1)} %collective-permute-done.2, bf16[8,3456]{1,0:T(8,128)(2,1)S(1)} %collective-permute-done.3, ...), dimensions={0} | concatenate | bytes 442368 | tf_op jit(solution)/shard_map/concatenate | solution.py:87
  38.7 0.8 collective-permute-start.6
  39.6 3.0 %collective-permute-start.7 = (bf16[32,3456]{1,0:T(8,128)(2,1)}, bf16[32,3456]{1,0:T(8,128)(2,1)S(1)}, u32[]{:S(2)}, u32[]{:S(2)}) collective-permute-start(bf16[32,3456]{1,0:T(8,128)(2,1)} %concatenate.15), channel_id=1, source_target_pairs={{0,64},{2,66},{4,68},{6,70},{8,72},{10,74},{12,76},{14,78},{16,80}... | collective-permute-start | bytes 663560 | tf_op jit(solution)/shard_map/ppermute | solution.py:86
  42.6 1.0 collective-permute-start.8
  43.6 1.0 copy.36
  44.7 1.7 %copy.39.p_ref = bf16[128,3456]{1,0:T(8,128)(2,1)} copy(bf16[128,3456]{0,1:T(8,128)(2,1)S(1)} %bitcast.18) | data formatting | bytes 1769472 | tf_op jit(solution)/shard_map/reshape | solution.py:20
  47.7 3.9 %collective-permute-done.7 = bf16[32,3456]{1,0:T(8,128)(2,1)S(1)} collective-permute-done((bf16[32,3456]{1,0:T(8,128)(2,1)}, bf16[32,3456]{1,0:T(8,128)(2,1)S(1)}, u32[]{:S(2)}, u32[]{:S(2)}) %collective-permute-start.7) | collective-permute-done | bytes 221216 | tf_op jit(solution)/shard_map/ppermute | solution.py:86
  51.6 4.8 %concatenate.16.g_ref = bf16[128,3456]{1,0:T(8,128)(2,1)} concatenate(bf16[2,3456]{1,0:T(2,128)(2,1)S(1)} %reshape.60, bf16[2,3456]{1,0:T(2,128)(2,1)S(1)} %collective-permute-done, bf16[2,3456]{1,0:T(2,128)(2,1)S(1)} %copy-done.2, bf16[2,3456]{1,0:T(2,128)(2,1)S(1)} %copy-done.4, bf16[8,3456]{1,0:T(8,128)(2,1)S(1)} %collective-permute-done.3, ...), dimensions={0} | concatenate | bytes 1769472 | tf_op jit(solution)/shard_map/concatenate | solution.py:87
  56.4 32.9 %shard_map.68 = (f32[128,1]{1,0:T(8,128)}, f32[128,1]{1,0:T(8,128)}) custom-call(bf16[128,3456]{1,0:T(8,128)(2,1)} %copy.39.p_ref, bf16[128,3456]{1,0:T(8,128)(2,1)} %concatenate.16.g_ref), custom_call_target="tpu_custom_call" | custom-call | tf_op jit(solution)/shard_map/pallas_call | solution.py:53
  89.3 0.9 reduce
  90.2 1.0 reduce.1
  91.2 4.5 %pmax.7 = f32[128]{0:T(128)S(1)} all-reduce(f32[128]{0:T(128)S(1)} %reduce), channel_id=1, replica_groups=mesh['loop'=64,'grp'=2] {'grp'}, use_global_device_ids=true, to_apply=%region_0.0 | all-reduce | flops 128 | bytes 1024 | tf_op jit(solution)/shard_map/pmax | solution.py:100
  96.4 1.0 copy.41
  97.4 1.0 copy.42
  98.4 2.1 %fusion.2 = bf16[128,48,72]{2,1,0:T(8,128)(2,1)} fusion(bf16[128,48,72]{2,1,0:T(8,128)(2,1)S(1)} %copy.42, f32[128,72]{1,0:T(8,128)S(1)} %add_select_fusion), kind=kOutput, calls=%fused_computation.4 | convolution fusion | flops 64806912 | bytes 1806336 | tf_op jit(solution)/shard_map/srt,stf->srf/dot_general | solution.py:139
  100.6 2.0 %copy.43 = bf16[128,48,72]{0,2,1:T(8,128)(2,1)S(1)} copy(bf16[128,48,72]{2,1,0:T(8,128)(2,1)} %fusion.2) | data formatting | bytes 1769472 | tf_op jit(solution)/shard_map/convert_element_type | solution.py:140
  103.0 3.7 %all-reduce.3 = (f32[128]{0:T(128)S(1)}, f32[4,3456]{1,0:T(4,128)S(1)}, f32[4]{0:T(128)S(1)}) all-reduce(f32[128]{0:T(128)S(1)} %exponential_multiply_fusion, f32[4,3456]{1,0:T(4,128)S(1)} %fusion.15, f32[4]{0:T(128)S(1)} %convert_reduce_fusion), channel_id=1, replica_groups=mesh['loop'=64,'grp'=2] {'grp'}, use_global_device_ids=true, to_apply=%region_1.0 | all-reduce | flops 13956 | bytes 111648 | tf_op jit(solution)/shard_map/psum | solution.py:101
  106.8 0.6 log_add_fusion
  107.5 0.7 dynamic-slice_divide_fusion
  (41 shorter events, 3.4 us)
Async XLA Ops:
  1.7 19.2 %collective-permute-start = (bf16[2,3456]{1,0:T(2,128)(2,1)S(1)}, bf16[2,3456]{1,0:T(2,128)(2,1)S(1)}, u32[]{:S(2)}, u32[]{:S(2)}) collective-permute-start(bf16[2,3456]{1,0:T(2,128)(2,1)S(1)} %reshape.60), channel_id=1, source_target_pairs={{0,2},{2,4},{4,6},{6,0},{8,10},{10,12},{12,14},{14,8},{16,18},{18,... | collective-permute-start | bytes 41480 | tf_op jit(solution)/shard_map/ppermute | solution.py:86
  3.9 17.0 %collective-permute-start.1 = (bf16[2,3456]{1,0:T(2,128)(2,1)S(1)}, bf16[2,3456]{1,0:T(2,128)(2,1)S(1)}, u32[]{:S(2)}, u32[]{:S(2)}) collective-permute-start(bf16[2,3456]{1,0:T(2,128)(2,1)S(1)} %reshape.60), channel_id=1, source_target_pairs={{0,4},{2,6},{4,0},{6,2},{8,12},{10,14},{12,8},{14,10},{16,20},{18,... | collective-permute-start | bytes 41480 | tf_op jit(solution)/shard_map/ppermute | solution.py:86
  6.5 14.4 %collective-permute-start.2 = (bf16[2,3456]{1,0:T(2,128)(2,1)S(1)}, bf16[2,3456]{1,0:T(2,128)(2,1)S(1)}, u32[]{:S(2)}, u32[]{:S(2)}) collective-permute-start(bf16[2,3456]{1,0:T(2,128)(2,1)S(1)} %reshape.60), channel_id=1, source_target_pairs={{0,6},{2,0},{4,2},{6,4},{8,14},{10,8},{12,10},{14,12},{16,22},{18,... | collective-permute-start | bytes 41480 | tf_op jit(solution)/shard_map/ppermute | solution.py:86
  12.1 31.5 %copy-start = (bf16[128,3456]{1,0:T(8,128)(2,1)S(1)}, bf16[128,3456]{1,0:T(8,128)(2,1)}, u32[]{:S(2)}) copy-start(bf16[128,3456]{1,0:T(8,128)(2,1)} %param.5) | copy-start | bytes 2654212
  12.1 83.5 %all-to-all-start = ((bf16[64,2,3584]{2,1,0:T(2,128)(2,1)}), bf16[64,2,3584]{2,1,0:T(2,128)(2,1)S(1)}, u32[]{:S(2)}, u32[]{:S(2)}) async-start(bf16[64,2,3584]{2,1,0:T(2,128)(2,1)} %reshape.61), calls=%async_computation | async-start | bytes 1835008 | tf_op jit(solution)/shard_map/all_to_all | solution.py:127
  20.9 15.3 %copy-start.1 = (bf16[2,3456]{1,0:T(2,128)(2,1)}, bf16[2,3456]{1,0:T(2,128)(2,1)S(1)}, u32[]{:S(2)}) copy-start(bf16[2,3456]{1,0:T(2,128)(2,1)S(1)} %collective-permute-done.1) | copy-start | bytes 41476
  20.9 15.2 %copy-start.3 = (bf16[2,3456]{1,0:T(2,128)(2,1)}, bf16[2,3456]{1,0:T(2,128)(2,1)S(1)}, u32[]{:S(2)}) copy-start(bf16[2,3456]{1,0:T(2,128)(2,1)S(1)} %collective-permute-done.2) | copy-start | bytes 41476
  21.0 4.7 %collective-permute-start.3 = (bf16[8,3456]{1,0:T(8,128)(2,1)S(1)}, bf16[8,3456]{1,0:T(8,128)(2,1)S(1)}, u32[]{:S(2)}, u32[]{:S(2)}) collective-permute-start(bf16[8,3456]{1,0:T(8,128)(2,1)S(1)} %pad_maximum_fusion), channel_id=1, source_target_pairs={{0,8},{2,10},{4,12},{6,14},{8,16},{10,18},{12,20},{14,22},{16,24},... | collective-permute-start | bytes 165896 | tf_op jit(solution)/shard_map/ppermute | solution.py:86
  22.1 13.8 %collective-permute-start.4 = (bf16[8,3456]{1,0:T(8,128)(2,1)S(1)}, bf16[8,3456]{1,0:T(8,128)(2,1)S(1)}, u32[]{:S(2)}, u32[]{:S(2)}) collective-permute-start(bf16[8,3456]{1,0:T(8,128)(2,1)S(1)} %pad_maximum_fusion), channel_id=1, source_target_pairs={{0,16},{2,18},{4,20},{6,22},{8,24},{10,26},{12,28},{14,30},{16,0},... | collective-permute-start | bytes 165896 | tf_op jit(solution)/shard_map/ppermute | solution.py:86
  24.5 11.7 %collective-permute-start.5 = (bf16[8,3456]{1,0:T(8,128)(2,1)S(1)}, bf16[8,3456]{1,0:T(8,128)(2,1)S(1)}, u32[]{:S(2)}, u32[]{:S(2)}) collective-permute-start(bf16[8,3456]{1,0:T(8,128)(2,1)S(1)} %pad_maximum_fusion), channel_id=1, source_target_pairs={{0,24},{2,26},{4,28},{6,30},{8,0},{10,2},{12,4},{14,6},{16,8},{18,... | collective-permute-start | bytes 165896 | tf_op jit(solution)/shard_map/ppermute | solution.py:86
  38.7 9.0 %collective-permute-start.6 = (bf16[32,3456]{1,0:T(8,128)(2,1)}, bf16[32,3456]{1,0:T(8,128)(2,1)S(1)}, u32[]{:S(2)}, u32[]{:S(2)}) collective-permute-start(bf16[32,3456]{1,0:T(8,128)(2,1)} %concatenate.15), channel_id=1, source_target_pairs={{0,32},{2,34},{4,36},{6,38},{8,40},{10,42},{12,44},{14,46},{16,48}... | collective-permute-start | bytes 663560 | tf_op jit(solution)/shard_map/ppermute | solution.py:86
  39.6 12.0 %collective-permute-start.7 = (bf16[32,3456]{1,0:T(8,128)(2,1)}, bf16[32,3456]{1,0:T(8,128)(2,1)S(1)}, u32[]{:S(2)}, u32[]{:S(2)}) collective-permute-start(bf16[32,3456]{1,0:T(8,128)(2,1)} %concatenate.15), channel_id=1, source_target_pairs={{0,64},{2,66},{4,68},{6,70},{8,72},{10,74},{12,76},{14,78},{16,80}... | collective-permute-start | bytes 663560 | tf_op jit(solution)/shard_map/ppermute | solution.py:86
  42.6 9.0 %collective-permute-start.8 = (bf16[32,3456]{1,0:T(8,128)(2,1)}, bf16[32,3456]{1,0:T(8,128)(2,1)S(1)}, u32[]{:S(2)}, u32[]{:S(2)}) collective-permute-start(bf16[32,3456]{1,0:T(8,128)(2,1)} %concatenate.15), channel_id=1, source_target_pairs={{0,96},{2,98},{4,100},{6,102},{8,104},{10,106},{12,108},{14,110},{... | collective-permute-start | bytes 663560 | tf_op jit(solution)/shard_map/ppermute | solution.py:86
  44.7 1.8 %copy-start.5 = (u32[128]{0:T(128)S(1)}, u32[128]{0:T(128)}, u32[]{:S(2)}) copy-start(u32[128]{0:T(128)} %constant.62) | copy-start | bytes 1540
  44.7 6.9 %copy-start.2 = (bf16[2,3456]{1,0:T(2,128)(2,1)S(1)}, bf16[2,3456]{1,0:T(2,128)(2,1)}, u32[]{:S(2)}) copy-start(bf16[2,3456]{1,0:T(2,128)(2,1)} %copy-done.1) | copy-start | bytes 41476
  44.7 6.9 %copy-start.4 = (bf16[2,3456]{1,0:T(2,128)(2,1)S(1)}, bf16[2,3456]{1,0:T(2,128)(2,1)}, u32[]{:S(2)}) copy-start(bf16[2,3456]{1,0:T(2,128)(2,1)} %copy-done.3) | copy-start | bytes 41476

commit v4 on v3

--- a/solution.py
+++ b/solution.py
@@ -26,24 +26,31 @@
     r_scr[pl.ds(0, flat_len), :] = columns
     r_scr[pl.ds(flat_len, flat_len), :] = columns
     images = p_ref[...]
+    half = ANGLES // 2
 
     def shift_scores(s, carry):
-        start = pl.multiple_of(s * RADII, 16)
-        turned = r_scr[pl.ds(start, flat_len), :]
+        turned = jnp.concatenate(
+            [
+                r_scr[pl.ds(pl.multiple_of(s * RADII, 16), flat_len), :],
+                r_scr[pl.ds(pl.multiple_of((s + half) * RADII, 16), flat_len), :],
+            ],
+            axis=1,
+        )
         scores = jnp.dot(images, turned, preferred_element_type=jnp.float32) * scale
         s_scr[s] = scores
         return jnp.maximum(carry, scores)
 
     first = jnp.full(s_scr.shape[1:], -jnp.inf, jnp.float32)
-    lane_max = lax.fori_loop(0, ANGLES, shift_scores, first)
-    highest = jnp.max(lane_max, axis=1, keepdims=True)
+    lane_max = lax.fori_loop(0, half, shift_scores, first, unroll=4)
+    highest = jnp.max(lane_max.T, axis=0, keepdims=True)
+    highest_col = jnp.max(lane_max, axis=1, keepdims=True)
 
     def shift_sum(s, carry):
-        return carry + jnp.exp(s_scr[s] - highest)
+        return carry + jnp.exp(s_scr[s] - highest_col)
 
-    lane_sum = lax.fori_loop(0, ANGLES, shift_sum, jnp.zeros(s_scr.shape[1:], jnp.float32))
+    lane_sum = lax.fori_loop(0, half, shift_sum, jnp.zeros(s_scr.shape[1:], jnp.float32))
     max_ref[...] = highest
-    sum_ref[...] = jnp.sum(lane_sum, axis=1, keepdims=True)
+    sum_ref[...] = jnp.sum(lane_sum.T, axis=0, keepdims=True)
 
 
 def score_all(lhs, gathered):
@@ -53,15 +60,15 @@
     highest, summed = pl.pallas_call(
         functools.partial(score_kernel, scale=scale),
         out_shape=(
-            jax.ShapeDtypeStruct((row_count, 1), jnp.float32),
-            jax.ShapeDtypeStruct((row_count, 1), jnp.float32),
+            jax.ShapeDtypeStruct((1, row_count), jnp.float32),
+            jax.ShapeDtypeStruct((1, row_count), jnp.float32),
         ),
         scratch_shapes=[
             pltpu.VMEM((2 * flat_len, ref_count), jnp.bfloat16),
-            pltpu.VMEM((ANGLES, row_count, ref_count), jnp.float32),
+            pltpu.VMEM((ANGLES // 2, row_count, 2 * ref_count), jnp.float32),
         ],
     )(lhs, gathered)
-    return highest[:, 0], summed[:, 0]
+    return highest[0], summed[0]
 
 
 def ring_factors(count):
@@ -97,11 +104,10 @@
     own_rows = lax.dynamic_slice_in_dim(particles, grp_index * half_rows, half_rows, 0)
     gathered = staged_gather(angle_major(references), "loop")
     highest, summed = score_all(angle_major(particles), gathered)
-    joint_max = lax.pmax(highest, "grp")
-    summed = lax.psum(summed * jnp.exp(highest - joint_max), "grp")
-    highest = joint_max
-    highest = lax.dynamic_slice_in_dim(highest, grp_index * half_rows, half_rows, 0)
-    summed = lax.dynamic_slice_in_dim(summed, grp_index * half_rows, half_rows, 0)
+    stats = lax.all_gather(jnp.stack([highest, summed], axis=0), "grp", axis=0, tiled=False)
+    stats = lax.dynamic_slice_in_dim(stats, grp_index * half_rows, half_rows, 2)
+    highest = jnp.max(stats[:, 0], axis=0)
+    summed = jnp.sum(stats[:, 1] * jnp.exp(stats[:, 0] - highest[None, :]), axis=0)
     log_evidence = highest + jnp.log(summed)
     owner_count = lax.axis_size("loop")
     per_owner = references.shape[0] * grp_size

time: 109 us -> 88.1 us (0.81)
  Pallas kernels: 32.9 us -> 14.3 us
  other arithmetic: 5.21 us -> 4.04 us
    pallas_call x1, Pallas kernels: 32.9 us -> 14.3 us  [score_all(): pl.pallas_call(functools.partial(score_kernel, scale=scale), out_shape=(j...]
    pmax x1 -> x0, blocking collectives: 4.48 us -> none  [local(): joint_max = lax.pmax(highest, 'grp')]
    all_gather x0 -> x1, blocking collectives: none -> 3.8 us  [local(): lax.all_gather(jnp.stack([highest, summed], axis=0), 'grp', axis=0, tiled...]
    psum x1 -> x0, blocking collectives: 3.75 us -> none  [local(): summed = lax.psum(summed * jnp.exp(highest - joint_max), 'grp')]
    unnamed x0 -> x1, blocking collectives: none -> 3.72 us
    pallas_call x2 -> x0, other arithmetic: 1.89 us -> none  [score_all(): pl.pallas_call(functools.partial(score_kernel, scale=scale), out_shape=(j...]
  transfers between devices with their start and end apart: 10 -> 10, of which waited for: 3 -> 3; matrix products, arithmetic and copies ran while one was open for 16% -> 19% of each run, Pallas kernels for 30% -> 16%
where the time goes in v4:
time: 88.1 us; the launch traced here: 87.7 us
  starting transfers between devices  24.1 us (27%)
  local copies, waits for them, and re-layouts  19 us (22%)
  waiting for transfers between devices  14.4 us (16%)
  Pallas kernels  14.3 us (16%)
  blocking collectives  7.53 us (9%)
  other arithmetic  4.04 us (5%)
  matrix products  2.85 us (3%)
  between operations  1.51 us (2%)
    ppermute x9, starting transfers between devices, staged_gather(): parts.append(lax.ppermute(rows, axis, pairs))  15.4 us
    ppermute x9, waiting for transfers between devices, staged_gather(): parts.append(lax.ppermute(rows, axis, pairs))  14.4 us
    pallas_call x1, Pallas kernels, score_all(): pl.pallas_call(functools.partial(score_kernel, scale=scale), out_shape=(j...  14.3 us
    all_to_all x1, starting transfers between devices, local(): lax.all_to_all(outgoing, 'loop', split_axis=0, concat_axis=0, tiled=True)  8.74 us
    concatenate x2, local copies, waits for them, and re-layouts, staged_gather(): rows = jnp.concatenate(parts, axis=0)  7.37 us
    all_gather x1, blocking collectives, local(): lax.all_gather(jnp.stack([highest, summed], axis=0), 'grp', axis=0, tiled...  3.8 us
    unnamed x1, blocking collectives  3.72 us
    reshape x4, local copies, waits for them, and re-layouts, angle_major(): rows.reshape(count, RADII, ANGLES).transpose(0, 2, 1)  2.77 us
  transfers between devices with their start and end apart: 10, of which 3 were waited for; matrix products, arithmetic and copies ran while one was open for 19% of the time, Pallas kernels for 16%

profile of v4, /device:TPU:1, one launch (start us, length us, event | category | flops | bytes accessed | tf_op | source)
XLA Modules:
  0.0 87.7 jit_solution(7990590000302699940)
XLA Ops:
  0.6 0.8 reshape.60
  1.7 2.2 %collective-permute-start = (bf16[2,3456]{1,0:T(2,128)(2,1)S(1)}, bf16[2,3456]{1,0:T(2,128)(2,1)S(1)}, u32[]{:S(2)}, u32[]{:S(2)}) collective-permute-start(bf16[2,3456]{1,0:T(2,128)(2,1)S(1)} %reshape.61), channel_id=1, source_target_pairs={{0,2},{2,4},{4,6},{6,0},{8,10},{10,12},{12,14},{14,8},{16,18},{18,... | collective-permute-start | bytes 41480 | tf_op jit(solution)/shard_map/ppermute | solution.py:93
  3.9 2.6 %collective-permute-start.1 = (bf16[2,3456]{1,0:T(2,128)(2,1)S(1)}, bf16[2,3456]{1,0:T(2,128)(2,1)S(1)}, u32[]{:S(2)}, u32[]{:S(2)}) collective-permute-start(bf16[2,3456]{1,0:T(2,128)(2,1)S(1)} %reshape.61), channel_id=1, source_target_pairs={{0,4},{2,6},{4,0},{6,2},{8,12},{10,14},{12,8},{14,10},{16,20},{18,... | collective-permute-start | bytes 41480 | tf_op jit(solution)/shard_map/ppermute | solution.py:93
  6.5 1.1 %collective-permute-start.2 = (bf16[2,3456]{1,0:T(2,128)(2,1)S(1)}, bf16[2,3456]{1,0:T(2,128)(2,1)S(1)}, u32[]{:S(2)}, u32[]{:S(2)}) collective-permute-start(bf16[2,3456]{1,0:T(2,128)(2,1)S(1)} %reshape.61), channel_id=1, source_target_pairs={{0,6},{2,0},{4,2},{6,4},{8,14},{10,8},{12,10},{14,12},{16,22},{18,... | collective-permute-start | bytes 41480 | tf_op jit(solution)/shard_map/ppermute | solution.py:93
  7.6 0.7 and_select_fusion.1
  8.6 0.7 convert_bitcast_fusion
  9.4 1.0 %constant_dynamic-slice_fusion.1 = bf16[64,3456]{1,0:T(8,128)(2,1)S(1)} fusion(bf16[128,3456]{1,0:T(8,128)(2,1)} %param.5, s32[]{:T(128)S(6)} %select_n.24), kind=kLoop, calls=%fused_computation.44 | loop fusion | bytes 884740 | tf_op jit(solution)/shard_map/dynamic_slice | solution.py:104
  10.8 1.3 %reshape.62 = bf16[64,2,3584]{2,1,0:T(2,128)(2,1)} reshape(bf16[128,3584]{1,0:T(8,128)(2,1)S(1)} %convolution_convert_fusion) | data formatting | bytes 1835008 | tf_op jit(solution)/shard_map/reshape | solution.py:132
  12.1 8.7 %all-to-all-start = ((bf16[64,2,3584]{2,1,0:T(2,128)(2,1)}), bf16[64,2,3584]{2,1,0:T(2,128)(2,1)S(1)}, u32[]{:S(2)}, u32[]{:S(2)}) async-start(bf16[64,2,3584]{2,1,0:T(2,128)(2,1)} %reshape.62), calls=%async_computation | async-start | bytes 1835008 | tf_op jit(solution)/shard_map/all_to_all | solution.py:133
  21.0 1.1 %collective-permute-start.3 = (bf16[8,3456]{1,0:T(8,128)(2,1)S(1)}, bf16[8,3456]{1,0:T(8,128)(2,1)S(1)}, u32[]{:S(2)}, u32[]{:S(2)}) collective-permute-start(bf16[8,3456]{1,0:T(8,128)(2,1)S(1)} %pad_maximum_fusion), channel_id=1, source_target_pairs={{0,8},{2,10},{4,12},{6,14},{8,16},{10,18},{12,20},{14,22},{16,24},... | collective-permute-start | bytes 165896 | tf_op jit(solution)/shard_map/ppermute | solution.py:93
  22.1 2.4 %collective-permute-start.4 = (bf16[8,3456]{1,0:T(8,128)(2,1)S(1)}, bf16[8,3456]{1,0:T(8,128)(2,1)S(1)}, u32[]{:S(2)}, u32[]{:S(2)}) collective-permute-start(bf16[8,3456]{1,0:T(8,128)(2,1)S(1)} %pad_maximum_fusion), channel_id=1, source_target_pairs={{0,16},{2,18},{4,20},{6,22},{8,24},{10,26},{12,28},{14,30},{16,0},... | collective-permute-start | bytes 165896 | tf_op jit(solution)/shard_map/ppermute | solution.py:93
  24.5 1.2 %collective-permute-start.5 = (bf16[8,3456]{1,0:T(8,128)(2,1)S(1)}, bf16[8,3456]{1,0:T(8,128)(2,1)S(1)}, u32[]{:S(2)}, u32[]{:S(2)}) collective-permute-start(bf16[8,3456]{1,0:T(8,128)(2,1)S(1)} %pad_maximum_fusion), channel_id=1, source_target_pairs={{0,24},{2,26},{4,28},{6,30},{8,0},{10,2},{12,4},{14,6},{16,8},{18,... | collective-permute-start | bytes 165896 | tf_op jit(solution)/shard_map/ppermute | solution.py:93
  25.7 10.2 %collective-permute-done.4 = bf16[8,3456]{1,0:T(8,128)(2,1)S(1)} collective-permute-done((bf16[8,3456]{1,0:T(8,128)(2,1)S(1)}, bf16[8,3456]{1,0:T(8,128)(2,1)S(1)}, u32[]{:S(2)}, u32[]{:S(2)}) %collective-permute-start.4) | collective-permute-done | bytes 55328 | tf_op jit(solution)/shard_map/ppermute | solution.py:93
  36.2 2.6 %concatenate.15 = bf16[32,3456]{1,0:T(8,128)(2,1)} concatenate(bf16[2,3456]{1,0:T(2,128)(2,1)S(1)} %reshape.61, bf16[2,3456]{1,0:T(2,128)(2,1)S(1)} %collective-permute-done, bf16[2,3456]{1,0:T(2,128)(2,1)S(1)} %collective-permute-done.1, bf16[2,3456]{1,0:T(2,128)(2,1)S(1)} %collective-permute-done.2, bf16[8,3456]{1,0:T(8,128)(2,1)S(1)} %collective-permute-done.3, ...), dimensions={0} | concatenate | bytes 442368 | tf_op jit(solution)/shard_map/concatenate | solution.py:94
  38.7 0.8 collective-permute-start.6
  39.6 3.0 %collective-permute-start.7 = (bf16[32,3456]{1,0:T(8,128)(2,1)}, bf16[32,3456]{1,0:T(8,128)(2,1)S(1)}, u32[]{:S(2)}, u32[]{:S(2)}) collective-permute-start(bf16[32,3456]{1,0:T(8,128)(2,1)} %concatenate.15), channel_id=1, source_target_pairs={{0,64},{2,66},{4,68},{6,70},{8,72},{10,74},{12,76},{14,78},{16,80}... | collective-permute-start | bytes 663560 | tf_op jit(solution)/shard_map/ppermute | solution.py:93
  42.6 1.0 %collective-permute-start.8 = (bf16[32,3456]{1,0:T(8,128)(2,1)}, bf16[32,3456]{1,0:T(8,128)(2,1)S(1)}, u32[]{:S(2)}, u32[]{:S(2)}) collective-permute-start(bf16[32,3456]{1,0:T(8,128)(2,1)} %concatenate.15), channel_id=1, source_target_pairs={{0,96},{2,98},{4,100},{6,102},{8,104},{10,106},{12,108},{14,110},{... | collective-permute-start | bytes 663560 | tf_op jit(solution)/shard_map/ppermute | solution.py:93
  43.6 1.0 %copy.36 = bf16[128,3456]{0,1:T(8,128)(2,1)S(1)} copy(bf16[128,3456]{1,0:T(8,128)(2,1)S(1)} %copy-done) | data formatting | bytes 1769472 | tf_op args[0]
  44.7 1.7 %copy.39.p_ref = bf16[128,3456]{1,0:T(8,128)(2,1)} copy(bf16[128,3456]{0,1:T(8,128)(2,1)S(1)} %bitcast.21) | data formatting | bytes 1769472 | tf_op jit(solution)/shard_map/reshape | solution.py:20
  46.5 0.6 dynamic-slice.1
  47.7 3.9 %collective-permute-done.7 = bf16[32,3456]{1,0:T(8,128)(2,1)S(1)} collective-permute-done((bf16[32,3456]{1,0:T(8,128)(2,1)}, bf16[32,3456]{1,0:T(8,128)(2,1)S(1)}, u32[]{:S(2)}, u32[]{:S(2)}) %collective-permute-start.7) | collective-permute-done | bytes 221216 | tf_op jit(solution)/shard_map/ppermute | solution.py:93
  51.6 4.8 %concatenate.16.g_ref = bf16[128,3456]{1,0:T(8,128)(2,1)} concatenate(bf16[2,3456]{1,0:T(2,128)(2,1)S(1)} %reshape.61, bf16[2,3456]{1,0:T(2,128)(2,1)S(1)} %collective-permute-done, bf16[2,3456]{1,0:T(2,128)(2,1)S(1)} %copy-done.2, bf16[2,3456]{1,0:T(2,128)(2,1)S(1)} %copy-done.4, bf16[8,3456]{1,0:T(8,128)(2,1)S(1)} %collective-permute-done.3, ...), dimensions={0} | concatenate | bytes 1769472 | tf_op jit(solution)/shard_map/concatenate | solution.py:94
  56.4 14.3 %shard_map.68 = (f32[1,128]{1,0:T(1,128)}, f32[1,128]{1,0:T(1,128)}) custom-call(bf16[128,3456]{1,0:T(8,128)(2,1)} %copy.39.p_ref, bf16[128,3456]{1,0:T(8,128)(2,1)} %concatenate.16.g_ref), custom_call_target="tpu_custom_call" | custom-call | tf_op jit(solution)/shard_map/pallas_call | solution.py:60
  70.7 0.7 maximum_bitcast_fusion
  71.4 3.8 %all-gather.1 = f32[2,2,128]{2,1,0:T(2,128)S(1)} all-gather(f32[1,2,128]{2,1,0:T(2,128)S(1)} %maximum_bitcast_fusion), channel_id=2, replica_groups=mesh['loop'=64,'grp'=2] {'grp'}, dimensions={0}, use_global_device_ids=true | all-gather | bytes 3072 | tf_op jit(solution)/shard_map/all_gather | solution.py:107
  75.3 0.5 log_add_fusion
  76.6 1.0 %copy.41 = bf16[128,3456]{0,1:T(8,128)(2,1)S(1)} copy(bf16[128,3456]{1,0:T(8,128)(2,1)S(1)} %slice.32) | data formatting | bytes 1769472 | tf_op jit(solution)/shard_map/slice | solution.py:136
  77.6 1.0 %copy.42 = bf16[128,48,72]{2,1,0:T(8,128)(2,1)S(1)} copy(bf16[128,48,72]{0,2,1:T(8,128)(2,1)S(1)} %bitcast.22) | data formatting | bytes 1769472 | tf_op jit(solution)/shard_map/reshape | solution.py:137
  78.6 2.1 %fusion.2 = bf16[128,48,72]{2,1,0:T(8,128)(2,1)} fusion(bf16[128,48,72]{2,1,0:T(8,128)(2,1)S(1)} %copy.42, f32[128,72]{1,0:T(8,128)S(1)} %add_select_fusion), kind=kOutput, calls=%fused_computation.4 | convolution fusion | flops 64806912 | bytes 1806336 | tf_op jit(solution)/shard_map/srt,stf->srf/dot_general | solution.py:145
  80.7 2.0 %copy.43 = bf16[128,48,72]{0,2,1:T(8,128)(2,1)S(1)} copy(bf16[128,48,72]{2,1,0:T(8,128)(2,1)} %fusion.2) | data formatting | bytes 1769472 | tf_op jit(solution)/shard_map/convert_element_type | solution.py:146
  83.2 3.7 %all-reduce.3 = (f32[4,3456]{1,0:T(4,128)S(1)}, f32[4]{0:T(128)S(1)}) all-reduce(f32[4,3456]{1,0:T(4,128)S(1)} %fusion.15, f32[4]{0:T(128)S(1)} %convert_reduce_fusion), channel_id=3, replica_groups=mesh['loop'=64,'grp'=2] {'grp'}, use_global_device_ids=true, to_apply=%region_4.5.clone | all-reduce | flops 13828 | bytes 110624
  87.0 0.7 dynamic-slice_divide_fusion
  (41 shorter events, 3.0 us)
Async XLA Ops:
  1.7 19.2 %collective-permute-start = (bf16[2,3456]{1,0:T(2,128)(2,1)S(1)}, bf16[2,3456]{1,0:T(2,128)(2,1)S(1)}, u32[]{:S(2)}, u32[]{:S(2)}) collective-permute-start(bf16[2,3456]{1,0:T(2,128)(2,1)S(1)} %reshape.61), channel_id=1, source_target_pairs={{0,2},{2,4},{4,6},{6,0},{8,10},{10,12},{12,14},{14,8},{16,18},{18,... | collective-permute-start | bytes 41480 | tf_op jit(solution)/shard_map/ppermute | solution.py:93
  3.9 17.0 %collective-permute-start.1 = (bf16[2,3456]{1,0:T(2,128)(2,1)S(1)}, bf16[2,3456]{1,0:T(2,128)(2,1)S(1)}, u32[]{:S(2)}, u32[]{:S(2)}) collective-permute-start(bf16[2,3456]{1,0:T(2,128)(2,1)S(1)} %reshape.61), channel_id=1, source_target_pairs={{0,4},{2,6},{4,0},{6,2},{8,12},{10,14},{12,8},{14,10},{16,20},{18,... | collective-permute-start | bytes 41480 | tf_op jit(solution)/shard_map/ppermute | solution.py:93
  6.5 14.4 %collective-permute-start.2 = (bf16[2,3456]{1,0:T(2,128)(2,1)S(1)}, bf16[2,3456]{1,0:T(2,128)(2,1)S(1)}, u32[]{:S(2)}, u32[]{:S(2)}) collective-permute-start(bf16[2,3456]{1,0:T(2,128)(2,1)S(1)} %reshape.61), channel_id=1, source_target_pairs={{0,6},{2,0},{4,2},{6,4},{8,14},{10,8},{12,10},{14,12},{16,22},{18,... | collective-permute-start | bytes 41480 | tf_op jit(solution)/shard_map/ppermute | solution.py:93
  12.1 31.5 %copy-start = (bf16[128,3456]{1,0:T(8,128)(2,1)S(1)}, bf16[128,3456]{1,0:T(8,128)(2,1)}, u32[]{:S(2)}) copy-start(bf16[128,3456]{1,0:T(8,128)(2,1)} %param.5) | copy-start | bytes 2654212
  12.1 63.7 %all-to-all-start = ((bf16[64,2,3584]{2,1,0:T(2,128)(2,1)}), bf16[64,2,3584]{2,1,0:T(2,128)(2,1)S(1)}, u32[]{:S(2)}, u32[]{:S(2)}) async-start(bf16[64,2,3584]{2,1,0:T(2,128)(2,1)} %reshape.62), calls=%async_computation | async-start | bytes 1835008 | tf_op jit(solution)/shard_map/all_to_all | solution.py:133
  20.9 15.3 %copy-start.1 = (bf16[2,3456]{1,0:T(2,128)(2,1)}, bf16[2,3456]{1,0:T(2,128)(2,1)S(1)}, u32[]{:S(2)}) copy-start(bf16[2,3456]{1,0:T(2,128)(2,1)S(1)} %collective-permute-done.1) | copy-start | bytes 41476
  20.9 15.2 %copy-start.3 = (bf16[2,3456]{1,0:T(2,128)(2,1)}, bf16[2,3456]{1,0:T(2,128)(2,1)S(1)}, u32[]{:S(2)}) copy-start(bf16[2,3456]{1,0:T(2,128)(2,1)S(1)} %collective-permute-done.2) | copy-start | bytes 41476
  21.0 4.7 %collective-permute-start.3 = (bf16[8,3456]{1,0:T(8,128)(2,1)S(1)}, bf16[8,3456]{1,0:T(8,128)(2,1)S(1)}, u32[]{:S(2)}, u32[]{:S(2)}) collective-permute-start(bf16[8,3456]{1,0:T(8,128)(2,1)S(1)} %pad_maximum_fusion), channel_id=1, source_target_pairs={{0,8},{2,10},{4,12},{6,14},{8,16},{10,18},{12,20},{14,22},{16,24},... | collective-permute-start | bytes 165896 | tf_op jit(solution)/shard_map/ppermute | solution.py:93
  22.1 13.8 %collective-permute-start.4 = (bf16[8,3456]{1,0:T(8,128)(2,1)S(1)}, bf16[8,3456]{1,0:T(8,128)(2,1)S(1)}, u32[]{:S(2)}, u32[]{:S(2)}) collective-permute-start(bf16[8,3456]{1,0:T(8,128)(2,1)S(1)} %pad_maximum_fusion), channel_id=1, source_target_pairs={{0,16},{2,18},{4,20},{6,22},{8,24},{10,26},{12,28},{14,30},{16,0},... | collective-permute-start | bytes 165896 | tf_op jit(solution)/shard_map/ppermute | solution.py:93
  24.5 11.7 %collective-permute-start.5 = (bf16[8,3456]{1,0:T(8,128)(2,1)S(1)}, bf16[8,3456]{1,0:T(8,128)(2,1)S(1)}, u32[]{:S(2)}, u32[]{:S(2)}) collective-permute-start(bf16[8,3456]{1,0:T(8,128)(2,1)S(1)} %pad_maximum_fusion), channel_id=1, source_target_pairs={{0,24},{2,26},{4,28},{6,30},{8,0},{10,2},{12,4},{14,6},{16,8},{18,... | collective-permute-start | bytes 165896 | tf_op jit(solution)/shard_map/ppermute | solution.py:93
  38.7 8.9 %collective-permute-start.6 = (bf16[32,3456]{1,0:T(8,128)(2,1)}, bf16[32,3456]{1,0:T(8,128)(2,1)S(1)}, u32[]{:S(2)}, u32[]{:S(2)}) collective-permute-start(bf16[32,3456]{1,0:T(8,128)(2,1)} %concatenate.15), channel_id=1, source_target_pairs={{0,32},{2,34},{4,36},{6,38},{8,40},{10,42},{12,44},{14,46},{16,48}... | collective-permute-start | bytes 663560 | tf_op jit(solution)/shard_map/ppermute | solution.py:93
  39.6 12.0 %collective-permute-start.7 = (bf16[32,3456]{1,0:T(8,128)(2,1)}, bf16[32,3456]{1,0:T(8,128)(2,1)S(1)}, u32[]{:S(2)}, u32[]{:S(2)}) collective-permute-start(bf16[32,3456]{1,0:T(8,128)(2,1)} %concatenate.15), channel_id=1, source_target_pairs={{0,64},{2,66},{4,68},{6,70},{8,72},{10,74},{12,76},{14,78},{16,80}... | collective-permute-start | bytes 663560 | tf_op jit(solution)/shard_map/ppermute | solution.py:93
  42.6 9.0 %collective-permute-start.8 = (bf16[32,3456]{1,0:T(8,128)(2,1)}, bf16[32,3456]{1,0:T(8,128)(2,1)S(1)}, u32[]{:S(2)}, u32[]{:S(2)}) collective-permute-start(bf16[32,3456]{1,0:T(8,128)(2,1)} %concatenate.15), channel_id=1, source_target_pairs={{0,96},{2,98},{4,100},{6,102},{8,104},{10,106},{12,108},{14,110},{... | collective-permute-start | bytes 663560 | tf_op jit(solution)/shard_map/ppermute | solution.py:93
  44.7 1.8 %copy-start.5 = (u32[128]{0:T(128)S(1)}, u32[128]{0:T(128)}, u32[]{:S(2)}) copy-start(u32[128]{0:T(128)} %constant.65) | copy-start | bytes 1540
  44.7 6.9 %copy-start.2 = (bf16[2,3456]{1,0:T(2,128)(2,1)S(1)}, bf16[2,3456]{1,0:T(2,128)(2,1)}, u32[]{:S(2)}) copy-start(bf16[2,3456]{1,0:T(2,128)(2,1)} %copy-done.1) | copy-start | bytes 41476
  44.7 6.9 %copy-start.4 = (bf16[2,3456]{1,0:T(2,128)(2,1)S(1)}, bf16[2,3456]{1,0:T(2,128)(2,1)}, u32[]{:S(2)}) copy-start(bf16[2,3456]{1,0:T(2,128)(2,1)} %copy-done.3) | copy-start | bytes 41476

commit v5 on v4

--- a/solution.py
+++ b/solution.py
@@ -20,9 +20,11 @@
     return rows.reshape(count, RADII, ANGLES).transpose(0, 2, 1).reshape(count, RADII * ANGLES)
 
 
-def score_kernel(p_ref, g_ref, max_ref, sum_ref, r_scr, s_scr, *, scale):
+def score_kernel(*refs, scale):
+    p_ref, piece_refs = refs[0], refs[1:-4]
+    max_ref, sum_ref, r_scr, s_scr = refs[-4:]
     flat_len = p_ref.shape[1]
-    columns = g_ref[...].T
+    columns = jnp.concatenate([piece[...] for piece in piece_refs], axis=0).T
     r_scr[pl.ds(0, flat_len), :] = columns
     r_scr[pl.ds(flat_len, flat_len), :] = columns
     images = p_ref[...]
@@ -53,9 +55,9 @@
     sum_ref[...] = jnp.sum(lane_sum.T, axis=0, keepdims=True)
 
 
-def score_all(lhs, gathered):
+def score_all(lhs, pieces):
     row_count, flat_len = lhs.shape
-    ref_count = gathered.shape[0]
+    ref_count = sum(piece.shape[0] for piece in pieces)
     scale = score_factor / math.sqrt(flat_len)
     highest, summed = pl.pallas_call(
         functools.partial(score_kernel, scale=scale),
@@ -67,7 +69,7 @@
             pltpu.VMEM((2 * flat_len, ref_count), jnp.bfloat16),
             pltpu.VMEM((ANGLES // 2, row_count, 2 * ref_count), jnp.float32),
         ],
-    )(lhs, gathered)
+    )(lhs, *pieces)
     return highest[0], summed[0]
 
 
@@ -93,7 +95,7 @@
             parts.append(lax.ppermute(rows, axis, pairs))
         rows = jnp.concatenate(parts, axis=0)
         stride *= factor
-    return rows
+    return parts
 
 
 def local(particles, references, classes, angles, weights):
@@ -102,13 +104,7 @@
     half_rows = row_count // grp_size
     grp_index = lax.axis_index("grp")
     own_rows = lax.dynamic_slice_in_dim(particles, grp_index * half_rows, half_rows, 0)
-    gathered = staged_gather(angle_major(references), "loop")
-    highest, summed = score_all(angle_major(particles), gathered)
-    stats = lax.all_gather(jnp.stack([highest, summed], axis=0), "grp", axis=0, tiled=False)
-    stats = lax.dynamic_slice_in_dim(stats, grp_index * half_rows, half_rows, 2)
-    highest = jnp.max(stats[:, 0], axis=0)
-    summed = jnp.sum(stats[:, 1] * jnp.exp(stats[:, 0] - highest[None, :]), axis=0)
-    log_evidence = highest + jnp.log(summed)
+    pieces = staged_gather(angle_major(references), "loop")
     owner_count = lax.axis_size("loop")
     per_owner = references.shape[0] * grp_size
     capacity = max(2, row_count // owner_count)
@@ -155,6 +151,13 @@
         lax.psum_scatter(partial_weight, "grp", scatter_dimension=0, tiled=True),
     )
     class_average = class_sums / class_weight[:, None]
+    class_average, pieces = lax.optimization_barrier((class_average, pieces))
+    highest, summed = score_all(angle_major(particles), pieces)
+    stats = lax.all_gather(jnp.stack([highest, summed], axis=0), "grp", axis=0, tiled=False)
+    stats = lax.dynamic_slice_in_dim(stats, grp_index * half_rows, half_rows, 2)
+    highest = jnp.max(stats[:, 0], axis=0)
+    summed = jnp.sum(stats[:, 1] * jnp.exp(stats[:, 0] - highest[None, :]), axis=0)
+    log_evidence = highest + jnp.log(summed)
     return (log_evidence, class_average)
 
 

time: 88.1 us -> 79.2 us (0.90)
  waiting for transfers between devices: 14.4 us -> 4.05 us
  starting transfers between devices: 24.1 us -> 30.9 us
  local copies, waits for them, and re-layouts: 19 us -> 13.4 us
    ppermute x9, waiting for transfers between devices: 14.4 us -> 4.05 us  [staged_gather(): parts.append(lax.ppermute(rows, axis, pairs))]
    concatenate x2 -> x1, local copies, waits for them, and re-layouts: 7.37 us -> 2.57 us  [staged_gather(): rows = jnp.concatenate(parts, axis=0)]
    ppermute x9, starting transfers between devices: 15.4 us -> 19 us  [staged_gather(): parts.append(lax.ppermute(rows, axis, pairs))]
    all_to_all x1, starting transfers between devices: 8.74 us -> 12 us  [local(): lax.all_to_all(outgoing, 'loop', split_axis=0, concat_axis=0, tiled=True)]
    unnamed x1, blocking collectives: 3.72 us -> 5.88 us
    all_gather x1, blocking collectives: 3.8 us -> 1.77 us  [local(): lax.all_gather(jnp.stack([highest, summed], axis=0), 'grp', axis=0, tiled...]
    unnamed x16 -> x10, local copies, waits for them, and re-layouts: 1.79 us -> 1.78 us
  transfers between devices with their start and end apart: 10 -> 10, of which waited for: 3 -> 3; matrix products, arithmetic and copies ran while one was open for 19% -> 18% of each run, Pallas kernels for 16% -> 0%
where the time goes in v5:
time: 79.2 us; the launch traced here: 78.9 us
  starting transfers between devices  30.9 us (39%)
  Pallas kernels  14.4 us (18%)
  local copies, waits for them, and re-layouts  13.4 us (17%)
  blocking collectives  7.66 us (10%)
  other arithmetic  4.05 us (5%)
  waiting for transfers between devices  4.05 us (5%)
  matrix products  2.85 us (4%)
  between operations  1.5 us (2%)
    ppermute x9, starting transfers between devices, staged_gather(): parts.append(lax.ppermute(rows, axis, pairs))  19 us
    pallas_call x1, Pallas kernels, score_all(): pl.pallas_call(functools.partial(score_kernel, scale=scale), out_shape=(j...  14.4 us
    all_to_all x1, starting transfers between devices, local(): lax.all_to_all(outgoing, 'loop', split_axis=0, concat_axis=0, tiled=True)  12 us
    unnamed x1, blocking collectives  5.88 us
    ppermute x9, waiting for transfers between devices, staged_gather(): parts.append(lax.ppermute(rows, axis, pairs))  4.05 us
    concatenate x1, local copies, waits for them, and re-layouts, staged_gather(): rows = jnp.concatenate(parts, axis=0)  2.57 us
    dot_general x1, matrix products, local(): jnp.einsum('srt,stf->srf', images, rotator, preferred_element_type=jnp.fl...  2.14 us
    convert_element_type x1, local copies, waits for them, and re-layouts, local(): aligned = aligned.astype(jnp.bfloat16).reshape(slot_count, flat_len)  2.02 us
  transfers between devices with their start and end apart: 10, of which 3 were waited for; matrix products, arithmetic and copies ran while one was open for 18% of the time, Pallas kernels for 0%

profile of v5, /device:TPU:1, one launch (start us, length us, event | category | flops | bytes accessed | tf_op | source)
XLA Modules:
  0.0 78.9 jit_solution(11809593950858119800)
XLA Ops:
  0.6 0.7 and_select_fusion.1
  1.7 0.7 convert_bitcast_fusion
  2.5 1.0 %constant_dynamic-slice_fusion.2 = bf16[64,3456]{1,0:T(8,128)(2,1)S(1)} fusion(bf16[128,3456]{1,0:T(8,128)(2,1)} %param.5, s32[]{:T(128)S(6)} %select_n.25), kind=kLoop, calls=%fused_computation.45 | loop fusion | bytes 884740 | tf_op jit(solution)/shard_map/dynamic_slice | solution.py:106
  3.5 0.4 convolution_convert_fusion
  3.9 1.3 %reshape.60 = bf16[64,2,3584]{2,1,0:T(2,128)(2,1)} reshape(bf16[128,3584]{1,0:T(8,128)(2,1)S(1)} %convolution_convert_fusion) | data formatting | bytes 1835008 | tf_op jit(solution)/shard_map/reshape | solution.py:128
  5.2 12.0 %all-to-all-start = ((bf16[64,2,3584]{2,1,0:T(2,128)(2,1)}), bf16[64,2,3584]{2,1,0:T(2,128)(2,1)S(1)}, u32[]{:S(2)}, u32[]{:S(2)}) async-start(bf16[64,2,3584]{2,1,0:T(2,128)(2,1)} %reshape.60), calls=%async_computation | async-start | bytes 1835008 | tf_op jit(solution)/shard_map/all_to_all | solution.py:129
  17.5 1.1 %collective-permute-start = (bf16[2,3456]{1,0:T(2,128)(2,1)S(1)}, bf16[2,3456]{1,0:T(2,128)(2,1)S(1)}, u32[]{:S(2)}, u32[]{:S(2)}) collective-permute-start(bf16[2,3456]{1,0:T(2,128)(2,1)S(1)} %reshape.65), channel_id=1, source_target_pairs={{0,2},{2,4},{4,6},{6,0},{8,10},{10,12},{12,14},{14,8},{16,18},{18,... | collective-permute-start | bytes 41480 | tf_op jit(solution)/shard_map/ppermute | solution.py:95
  18.6 2.4 %collective-permute-start.1 = (bf16[2,3456]{1,0:T(2,128)(2,1)S(1)}, bf16[2,3456]{1,0:T(2,128)(2,1)S(1)}, u32[]{:S(2)}, u32[]{:S(2)}) collective-permute-start(bf16[2,3456]{1,0:T(2,128)(2,1)S(1)} %reshape.65), channel_id=1, source_target_pairs={{0,4},{2,6},{4,0},{6,2},{8,12},{10,14},{12,8},{14,10},{16,20},{18,... | collective-permute-start | bytes 41480 | tf_op jit(solution)/shard_map/ppermute | solution.py:95
  21.0 1.2 %collective-permute-start.2 = (bf16[2,3456]{1,0:T(2,128)(2,1)S(1)}, bf16[2,3456]{1,0:T(2,128)(2,1)S(1)}, u32[]{:S(2)}, u32[]{:S(2)}) collective-permute-start(bf16[2,3456]{1,0:T(2,128)(2,1)S(1)} %reshape.65), channel_id=1, source_target_pairs={{0,6},{2,0},{4,2},{6,4},{8,14},{10,8},{12,10},{14,12},{16,22},{18,... | collective-permute-start | bytes 41480 | tf_op jit(solution)/shard_map/ppermute | solution.py:95
  22.3 1.3 %collective-permute-done.1 = bf16[2,3456]{1,0:T(2,128)(2,1)S(1)} collective-permute-done((bf16[2,3456]{1,0:T(2,128)(2,1)S(1)}, bf16[2,3456]{1,0:T(2,128)(2,1)S(1)}, u32[]{:S(2)}, u32[]{:S(2)}) %collective-permute-start.1) | collective-permute-done | bytes 13856 | tf_op jit(solution)/shard_map/ppermute | solution.py:95
  23.6 2.6 %collective-permute-done.2 = bf16[2,3456]{1,0:T(2,128)(2,1)S(1)} collective-permute-done((bf16[2,3456]{1,0:T(2,128)(2,1)S(1)}, bf16[2,3456]{1,0:T(2,128)(2,1)S(1)}, u32[]{:S(2)}, u32[]{:S(2)}) %collective-permute-start.2) | collective-permute-done | bytes 13856 | tf_op jit(solution)/shard_map/ppermute | solution.py:95
  26.4 2.0 %collective-permute-start.4 = (bf16[8,3456]{1,0:T(8,128)(2,1)S(1)}, bf16[8,3456]{1,0:T(8,128)(2,1)S(1)}, u32[]{:S(2)}, u32[]{:S(2)}) collective-permute-start(bf16[8,3456]{1,0:T(8,128)(2,1)S(1)} %pad_maximum_fusion), channel_id=1, source_target_pairs={{0,16},{2,18},{4,20},{6,22},{8,24},{10,26},{12,28},{14,30},{16,0},... | collective-permute-start | bytes 165896 | tf_op jit(solution)/shard_map/ppermute | solution.py:95
  28.4 1.0 %collective-permute-start.5 = (bf16[8,3456]{1,0:T(8,128)(2,1)S(1)}, bf16[8,3456]{1,0:T(8,128)(2,1)S(1)}, u32[]{:S(2)}, u32[]{:S(2)}) collective-permute-start(bf16[8,3456]{1,0:T(8,128)(2,1)S(1)} %pad_maximum_fusion), channel_id=1, source_target_pairs={{0,24},{2,26},{4,28},{6,30},{8,0},{10,2},{12,4},{14,6},{16,8},{18,... | collective-permute-start | bytes 165896 | tf_op jit(solution)/shard_map/ppermute | solution.py:95
  29.4 1.0 %copy.36 = bf16[128,3456]{0,1:T(8,128)(2,1)S(1)} copy(bf16[128,3456]{1,0:T(8,128)(2,1)S(1)} %copy-done) | data formatting | bytes 1769472 | tf_op args[0]
  30.6 1.7 %copy.43.refs_0_ = bf16[128,3456]{1,0:T(8,128)(2,1)} copy(bf16[128,3456]{0,1:T(8,128)(2,1)S(1)} %bitcast.21) | data formatting | bytes 1769472 | tf_op jit(solution)/shard_map/reshape | solution.py:20
  32.2 0.6 dynamic-slice.1
  33.5 2.6 %concatenate.12.refs_1_ = bf16[32,3456]{1,0:T(8,128)(2,1)} concatenate(bf16[2,3456]{1,0:T(2,128)(2,1)S(1)} %reshape.65, bf16[2,3456]{1,0:T(2,128)(2,1)S(1)} %collective-permute-done, bf16[2,3456]{1,0:T(2,128)(2,1)S(1)} %collective-permute-done.1, bf16[2,3456]{1,0:T(2,128)(2,1)S(1)} %collective-permute-done.2, bf16[8,3456]{1,0:T(8,128)(2,1)S(1)} %collective-permute-done.3, ...), dimensions={0} | concatenate | bytes 442368 | tf_op jit(solution)/shard_map/concatenate | solution.py:96
  36.1 5.5 %collective-permute-start.6 = (bf16[32,3456]{1,0:T(8,128)(2,1)}, bf16[32,3456]{1,0:T(8,128)(2,1)}, u32[]{:S(2)}, u32[]{:S(2)}) collective-permute-start(bf16[32,3456]{1,0:T(8,128)(2,1)} %concatenate.12.refs_1_), channel_id=1, source_target_pairs={{0,32},{2,34},{4,36},{6,38},{8,40},{10,42},{12,44},{14,46},{16,48}... | collective-permute-start | bytes 663560 | tf_op jit(solution)/shard_map/ppermute | solution.py:95
  41.5 3.8 %collective-permute-start.7 = (bf16[32,3456]{1,0:T(8,128)(2,1)}, bf16[32,3456]{1,0:T(8,128)(2,1)}, u32[]{:S(2)}, u32[]{:S(2)}) collective-permute-start(bf16[32,3456]{1,0:T(8,128)(2,1)} %concatenate.12.refs_1_), channel_id=1, source_target_pairs={{0,64},{2,66},{4,68},{6,70},{8,72},{10,74},{12,76},{14,78},{16,80}... | collective-permute-start | bytes 663560 | tf_op jit(solution)/shard_map/ppermute | solution.py:95
  45.4 1.9 %collective-permute-start.8 = (bf16[32,3456]{1,0:T(8,128)(2,1)}, bf16[32,3456]{1,0:T(8,128)(2,1)}, u32[]{:S(2)}, u32[]{:S(2)}) collective-permute-start(bf16[32,3456]{1,0:T(8,128)(2,1)} %concatenate.12.refs_1_), channel_id=1, source_target_pairs={{0,96},{2,98},{4,100},{6,102},{8,104},{10,106},{12,108},{14,110},{... | collective-permute-start | bytes 663560 | tf_op jit(solution)/shard_map/ppermute | solution.py:95
  47.3 0.3 reshape.61
  48.0 1.0 %copy.39 = bf16[128,3456]{0,1:T(8,128)(2,1)S(1)} copy(bf16[128,3456]{1,0:T(8,128)(2,1)S(1)} %slice.32) | data formatting | bytes 1769472 | tf_op jit(solution)/shard_map/slice | solution.py:132
  49.0 1.0 %copy.40 = bf16[128,48,72]{2,1,0:T(8,128)(2,1)S(1)} copy(bf16[128,48,72]{0,2,1:T(8,128)(2,1)S(1)} %bitcast.22) | data formatting | bytes 1769472 | tf_op jit(solution)/shard_map/reshape | solution.py:133
  50.0 2.1 %fusion.2 = bf16[128,48,72]{2,1,0:T(8,128)(2,1)} fusion(bf16[128,48,72]{2,1,0:T(8,128)(2,1)S(1)} %copy.40, f32[128,72]{1,0:T(8,128)S(1)} %add_select_fusion), kind=kOutput, calls=%fused_computation.4 | convolution fusion | flops 64806912 | bytes 1806336 | tf_op jit(solution)/shard_map/srt,stf->srf/dot_general | solution.py:141
  52.2 2.0 %copy.41 = bf16[128,48,72]{0,2,1:T(8,128)(2,1)S(1)} copy(bf16[128,48,72]{2,1,0:T(8,128)(2,1)} %fusion.2) | data formatting | bytes 1769472 | tf_op jit(solution)/shard_map/convert_element_type | solution.py:142
  54.3 0.3 fusion.15
  54.6 5.9 %all-reduce.3 = (f32[4,3456]{1,0:T(4,128)S(1)}, f32[4]{0:T(128)S(1)}) all-reduce(f32[4,3456]{1,0:T(4,128)S(1)} %fusion.15, f32[4]{0:T(128)S(1)} %convert_reduce_fusion), channel_id=3, replica_groups=mesh['loop'=64,'grp'=2] {'grp'}, use_global_device_ids=true, to_apply=%region_2.3.clone | all-reduce | flops 13828 | bytes 110624
  60.6 0.7 dynamic-slice_divide_fusion
  61.3 14.4 %shard_map.68 = (f32[1,128]{1,0:T(1,128)}, f32[1,128]{1,0:T(1,128)}) custom-call(bf16[128,3456]{1,0:T(8,128)(2,1)} %copy.43.refs_0_, bf16[32,3456]{1,0:T(8,128)(2,1)} %concatenate.12.refs_1_, bf16[32,3456]{1,0:T(8,128)(2,1)} %collective-permute-done.6.refs_2_, bf16[32,3456]{1,0:T(8,128)(2,1)} %collective-permute-done.7.refs_3_, ...), custom_call_target="tpu_custom_call" | custom-call | tf_op jit(solution)/shard_map/pallas_call | solution.py:62
  75.8 0.7 maximum_bitcast_fusion
  76.5 1.8 %all-gather.1 = f32[2,2,128]{2,1,0:T(2,128)S(1)} all-gather(f32[1,2,128]{2,1,0:T(2,128)S(1)} %maximum_bitcast_fusion), channel_id=2, replica_groups=mesh['loop'=64,'grp'=2] {'grp'}, dimensions={0}, use_global_device_ids=true | all-gather | bytes 3072 | tf_op jit(solution)/shard_map/all_gather | solution.py:156
  78.4 0.5 log_add_fusion
  (34 shorter events, 1.9 us)
Async XLA Ops:
  3.9 13.3 %copy-start.1 = (bf16[2,3456]{1,0:T(2,128)(2,1)S(1)}, bf16[2,3456]{1,0:T(2,128)(2,1)}, u32[]{:S(2)}) copy-start(bf16[2,3456]{1,0:T(2,128)(2,1)} %param.6) | copy-start | bytes 41476
  3.9 25.5 %copy-start = (bf16[128,3456]{1,0:T(8,128)(2,1)S(1)}, bf16[128,3456]{1,0:T(8,128)(2,1)}, u32[]{:S(2)}) copy-start(bf16[128,3456]{1,0:T(8,128)(2,1)} %param.5) | copy-start | bytes 2654212
  5.2 42.1 %all-to-all-start = ((bf16[64,2,3584]{2,1,0:T(2,128)(2,1)}), bf16[64,2,3584]{2,1,0:T(2,128)(2,1)S(1)}, u32[]{:S(2)}, u32[]{:S(2)}) async-start(bf16[64,2,3584]{2,1,0:T(2,128)(2,1)} %reshape.60), calls=%async_computation | async-start | bytes 1835008 | tf_op jit(solution)/shard_map/all_to_all | solution.py:129
  17.5 4.8 %collective-permute-start = (bf16[2,3456]{1,0:T(2,128)(2,1)S(1)}, bf16[2,3456]{1,0:T(2,128)(2,1)S(1)}, u32[]{:S(2)}, u32[]{:S(2)}) collective-permute-start(bf16[2,3456]{1,0:T(2,128)(2,1)S(1)} %reshape.65), channel_id=1, source_target_pairs={{0,2},{2,4},{4,6},{6,0},{8,10},{10,12},{12,14},{14,8},{16,18},{18,... | collective-permute-start | bytes 41480 | tf_op jit(solution)/shard_map/ppermute | solution.py:95
  18.6 5.0 %collective-permute-start.1 = (bf16[2,3456]{1,0:T(2,128)(2,1)S(1)}, bf16[2,3456]{1,0:T(2,128)(2,1)S(1)}, u32[]{:S(2)}, u32[]{:S(2)}) collective-permute-start(bf16[2,3456]{1,0:T(2,128)(2,1)S(1)} %reshape.65), channel_id=1, source_target_pairs={{0,4},{2,6},{4,0},{6,2},{8,12},{10,14},{12,8},{14,10},{16,20},{18,... | collective-permute-start | bytes 41480 | tf_op jit(solution)/shard_map/ppermute | solution.py:95
  21.0 5.2 %collective-permute-start.2 = (bf16[2,3456]{1,0:T(2,128)(2,1)S(1)}, bf16[2,3456]{1,0:T(2,128)(2,1)S(1)}, u32[]{:S(2)}, u32[]{:S(2)}) collective-permute-start(bf16[2,3456]{1,0:T(2,128)(2,1)S(1)} %reshape.65), channel_id=1, source_target_pairs={{0,6},{2,0},{4,2},{6,4},{8,14},{10,8},{12,10},{14,12},{16,22},{18,... | collective-permute-start | bytes 41480 | tf_op jit(solution)/shard_map/ppermute | solution.py:95
  26.3 7.2 %collective-permute-start.3 = (bf16[8,3456]{1,0:T(8,128)(2,1)S(1)}, bf16[8,3456]{1,0:T(8,128)(2,1)S(1)}, u32[]{:S(2)}, u32[]{:S(2)}) collective-permute-start(bf16[8,3456]{1,0:T(8,128)(2,1)S(1)} %pad_maximum_fusion), channel_id=1, source_target_pairs={{0,8},{2,10},{4,12},{6,14},{8,16},{10,18},{12,20},{14,22},{16,24},... | collective-permute-start | bytes 165896 | tf_op jit(solution)/shard_map/ppermute | solution.py:95
  26.4 7.1 %collective-permute-start.4 = (bf16[8,3456]{1,0:T(8,128)(2,1)S(1)}, bf16[8,3456]{1,0:T(8,128)(2,1)S(1)}, u32[]{:S(2)}, u32[]{:S(2)}) collective-permute-start(bf16[8,3456]{1,0:T(8,128)(2,1)S(1)} %pad_maximum_fusion), channel_id=1, source_target_pairs={{0,16},{2,18},{4,20},{6,22},{8,24},{10,26},{12,28},{14,30},{16,0},... | collective-permute-start | bytes 165896 | tf_op jit(solution)/shard_map/ppermute | solution.py:95
  28.4 5.1 %collective-permute-start.5 = (bf16[8,3456]{1,0:T(8,128)(2,1)S(1)}, bf16[8,3456]{1,0:T(8,128)(2,1)S(1)}, u32[]{:S(2)}, u32[]{:S(2)}) collective-permute-start(bf16[8,3456]{1,0:T(8,128)(2,1)S(1)} %pad_maximum_fusion), channel_id=1, source_target_pairs={{0,24},{2,26},{4,28},{6,30},{8,0},{10,2},{12,4},{14,6},{16,8},{18,... | collective-permute-start | bytes 165896 | tf_op jit(solution)/shard_map/ppermute | solution.py:95
  30.4 1.8 %copy-start.2 = (u32[128]{0:T(128)S(1)}, u32[128]{0:T(128)}, u32[]{:S(2)}) copy-start(u32[128]{0:T(128)} %constant.65) | copy-start | bytes 1540
  36.1 25.3 %collective-permute-start.6 = (bf16[32,3456]{1,0:T(8,128)(2,1)}, bf16[32,3456]{1,0:T(8,128)(2,1)}, u32[]{:S(2)}, u32[]{:S(2)}) collective-permute-start(bf16[32,3456]{1,0:T(8,128)(2,1)} %concatenate.12.refs_1_), channel_id=1, source_target_pairs={{0,32},{2,34},{4,36},{6,38},{8,40},{10,42},{12,44},{14,46},{16,48}... | collective-permute-start | bytes 663560 | tf_op jit(solution)/shard_map/ppermute | solution.py:95
  41.5 19.8 %collective-permute-start.7 = (bf16[32,3456]{1,0:T(8,128)(2,1)}, bf16[32,3456]{1,0:T(8,128)(2,1)}, u32[]{:S(2)}, u32[]{:S(2)}) collective-permute-start(bf16[32,3456]{1,0:T(8,128)(2,1)} %concatenate.12.refs_1_), channel_id=1, source_target_pairs={{0,64},{2,66},{4,68},{6,70},{8,72},{10,74},{12,76},{14,78},{16,80}... | collective-permute-start | bytes 663560 | tf_op jit(solution)/shard_map/ppermute | solution.py:95
  45.4 15.9 %collective-permute-start.8 = (bf16[32,3456]{1,0:T(8,128)(2,1)}, bf16[32,3456]{1,0:T(8,128)(2,1)}, u32[]{:S(2)}, u32[]{:S(2)}) collective-permute-start(bf16[32,3456]{1,0:T(8,128)(2,1)} %concatenate.12.refs_1_), channel_id=1, source_target_pairs={{0,96},{2,98},{4,100},{6,102},{8,104},{10,106},{12,108},{14,110},{... | collective-permute-start | bytes 663560 | tf_op jit(solution)/shard_map/ppermute | solution.py:95

commit v6 on v5

--- a/solution.py
+++ b/solution.py
@@ -43,14 +43,14 @@
         return jnp.maximum(carry, scores)
 
     first = jnp.full(s_scr.shape[1:], -jnp.inf, jnp.float32)
-    lane_max = lax.fori_loop(0, half, shift_scores, first, unroll=4)
+    lane_max = lax.fori_loop(0, half, shift_scores, first, unroll=9)
     highest = jnp.max(lane_max.T, axis=0, keepdims=True)
     highest_col = jnp.max(lane_max, axis=1, keepdims=True)
 
     def shift_sum(s, carry):
         return carry + jnp.exp(s_scr[s] - highest_col)
 
-    lane_sum = lax.fori_loop(0, half, shift_sum, jnp.zeros(s_scr.shape[1:], jnp.float32))
+    lane_sum = lax.fori_loop(0, half, shift_sum, jnp.zeros(s_scr.shape[1:], jnp.float32), unroll=4)
     max_ref[...] = highest
     sum_ref[...] = jnp.sum(lane_sum.T, axis=0, keepdims=True)
 

time: 79.2 us -> 78.2 us (0.987)
  Pallas kernels: 14.4 us -> 13.2 us
    pallas_call x1, Pallas kernels: 14.4 us -> 13.2 us  [score_all(): pl.pallas_call(functools.partial(score_kernel, scale=scale), out_shape=(j...]
  transfers between devices with their start and end apart: 10 -> 10, of which waited for: 3 -> 3; matrix products, arithmetic and copies ran while one was open for 18% -> 19% of each run, Pallas kernels for 0% -> 0%
where the time goes in v6:
time: 78.2 us; the launch traced here: 77.8 us
  starting transfers between devices  31 us (40%)
  local copies, waits for them, and re-layouts  13.4 us (17%)
  Pallas kernels  13.2 us (17%)
  blocking collectives  7.83 us (10%)
  other arithmetic  4.05 us (5%)
  waiting for transfers between devices  4.04 us (5%)
  matrix products  2.86 us (4%)
  between operations  1.5 us (2%)
    ppermute x9, starting transfers between devices, staged_gather(): parts.append(lax.ppermute(rows, axis, pairs))  19 us
    pallas_call x1, Pallas kernels, score_all(): pl.pallas_call(functools.partial(score_kernel, scale=scale), out_shape=(j...  13.2 us
    all_to_all x1, starting transfers between devices, local(): lax.all_to_all(outgoing, 'loop', split_axis=0, concat_axis=0, tiled=True)  12 us
    unnamed x1, blocking collectives  6.06 us
    ppermute x9, waiting for transfers between devices, staged_gather(): parts.append(lax.ppermute(rows, axis, pairs))  4.04 us
    concatenate x1, local copies, waits for them, and re-layouts, staged_gather(): rows = jnp.concatenate(parts, axis=0)  2.57 us
    dot_general x1, matrix products, local(): jnp.einsum('srt,stf->srf', images, rotator, preferred_element_type=jnp.fl...  2.14 us
    convert_element_type x1, local copies, waits for them, and re-layouts, local(): aligned = aligned.astype(jnp.bfloat16).reshape(slot_count, flat_len)  2.02 us
  transfers between devices with their start and end apart: 10, of which 3 were waited for; matrix products, arithmetic and copies ran while one was open for 19% of the time, Pallas kernels for 0%

profile of v6, /device:TPU:1, one launch (start us, length us, event | category | flops | bytes accessed | tf_op | source)
XLA Modules:
  0.0 77.8 jit_solution(14619316809173136841)
XLA Ops:
  0.6 0.7 and_select_fusion.1
  1.7 0.7 convert_bitcast_fusion
  2.5 1.0 %constant_dynamic-slice_fusion.2 = bf16[64,3456]{1,0:T(8,128)(2,1)S(1)} fusion(bf16[128,3456]{1,0:T(8,128)(2,1)} %param.5, s32[]{:T(128)S(6)} %select_n.25), kind=kLoop, calls=%fused_computation.45 | loop fusion | bytes 884740 | tf_op jit(solution)/shard_map/dynamic_slice | solution.py:106
  3.5 0.4 convolution_convert_fusion
  3.9 1.3 %reshape.60 = bf16[64,2,3584]{2,1,0:T(2,128)(2,1)} reshape(bf16[128,3584]{1,0:T(8,128)(2,1)S(1)} %convolution_convert_fusion) | data formatting | bytes 1835008 | tf_op jit(solution)/shard_map/reshape | solution.py:128
  5.2 12.0 %all-to-all-start = ((bf16[64,2,3584]{2,1,0:T(2,128)(2,1)}), bf16[64,2,3584]{2,1,0:T(2,128)(2,1)S(1)}, u32[]{:S(2)}, u32[]{:S(2)}) async-start(bf16[64,2,3584]{2,1,0:T(2,128)(2,1)} %reshape.60), calls=%async_computation | async-start | bytes 1835008 | tf_op jit(solution)/shard_map/all_to_all | solution.py:129
  17.5 1.1 %collective-permute-start = (bf16[2,3456]{1,0:T(2,128)(2,1)S(1)}, bf16[2,3456]{1,0:T(2,128)(2,1)S(1)}, u32[]{:S(2)}, u32[]{:S(2)}) collective-permute-start(bf16[2,3456]{1,0:T(2,128)(2,1)S(1)} %reshape.65), channel_id=1, source_target_pairs={{0,2},{2,4},{4,6},{6,0},{8,10},{10,12},{12,14},{14,8},{16,18},{18,... | collective-permute-start | bytes 41480 | tf_op jit(solution)/shard_map/ppermute | solution.py:95
  18.6 2.4 %collective-permute-start.1 = (bf16[2,3456]{1,0:T(2,128)(2,1)S(1)}, bf16[2,3456]{1,0:T(2,128)(2,1)S(1)}, u32[]{:S(2)}, u32[]{:S(2)}) collective-permute-start(bf16[2,3456]{1,0:T(2,128)(2,1)S(1)} %reshape.65), channel_id=1, source_target_pairs={{0,4},{2,6},{4,0},{6,2},{8,12},{10,14},{12,8},{14,10},{16,20},{18,... | collective-permute-start | bytes 41480 | tf_op jit(solution)/shard_map/ppermute | solution.py:95
  21.0 1.2 %collective-permute-start.2 = (bf16[2,3456]{1,0:T(2,128)(2,1)S(1)}, bf16[2,3456]{1,0:T(2,128)(2,1)S(1)}, u32[]{:S(2)}, u32[]{:S(2)}) collective-permute-start(bf16[2,3456]{1,0:T(2,128)(2,1)S(1)} %reshape.65), channel_id=1, source_target_pairs={{0,6},{2,0},{4,2},{6,4},{8,14},{10,8},{12,10},{14,12},{16,22},{18,... | collective-permute-start | bytes 41480 | tf_op jit(solution)/shard_map/ppermute | solution.py:95
  22.3 1.3 %collective-permute-done.1 = bf16[2,3456]{1,0:T(2,128)(2,1)S(1)} collective-permute-done((bf16[2,3456]{1,0:T(2,128)(2,1)S(1)}, bf16[2,3456]{1,0:T(2,128)(2,1)S(1)}, u32[]{:S(2)}, u32[]{:S(2)}) %collective-permute-start.1) | collective-permute-done | bytes 13856 | tf_op jit(solution)/shard_map/ppermute | solution.py:95
  23.6 2.6 %collective-permute-done.2 = bf16[2,3456]{1,0:T(2,128)(2,1)S(1)} collective-permute-done((bf16[2,3456]{1,0:T(2,128)(2,1)S(1)}, bf16[2,3456]{1,0:T(2,128)(2,1)S(1)}, u32[]{:S(2)}, u32[]{:S(2)}) %collective-permute-start.2) | collective-permute-done | bytes 13856 | tf_op jit(solution)/shard_map/ppermute | solution.py:95
  26.4 2.0 %collective-permute-start.4 = (bf16[8,3456]{1,0:T(8,128)(2,1)S(1)}, bf16[8,3456]{1,0:T(8,128)(2,1)S(1)}, u32[]{:S(2)}, u32[]{:S(2)}) collective-permute-start(bf16[8,3456]{1,0:T(8,128)(2,1)S(1)} %pad_maximum_fusion), channel_id=1, source_target_pairs={{0,16},{2,18},{4,20},{6,22},{8,24},{10,26},{12,28},{14,30},{16,0},... | collective-permute-start | bytes 165896 | tf_op jit(solution)/shard_map/ppermute | solution.py:95
  28.4 1.0 %collective-permute-start.5 = (bf16[8,3456]{1,0:T(8,128)(2,1)S(1)}, bf16[8,3456]{1,0:T(8,128)(2,1)S(1)}, u32[]{:S(2)}, u32[]{:S(2)}) collective-permute-start(bf16[8,3456]{1,0:T(8,128)(2,1)S(1)} %pad_maximum_fusion), channel_id=1, source_target_pairs={{0,24},{2,26},{4,28},{6,30},{8,0},{10,2},{12,4},{14,6},{16,8},{18,... | collective-permute-start | bytes 165896 | tf_op jit(solution)/shard_map/ppermute | solution.py:95
  29.4 1.0 %copy.36 = bf16[128,3456]{0,1:T(8,128)(2,1)S(1)} copy(bf16[128,3456]{1,0:T(8,128)(2,1)S(1)} %copy-done) | data formatting | bytes 1769472 | tf_op args[0]
  30.6 1.7 %copy.43.refs_0_ = bf16[128,3456]{1,0:T(8,128)(2,1)} copy(bf16[128,3456]{0,1:T(8,128)(2,1)S(1)} %bitcast.21) | data formatting | bytes 1769472 | tf_op jit(solution)/shard_map/reshape | solution.py:20
  32.2 0.6 dynamic-slice.1
  33.5 2.6 %concatenate.12.refs_1_ = bf16[32,3456]{1,0:T(8,128)(2,1)} concatenate(bf16[2,3456]{1,0:T(2,128)(2,1)S(1)} %reshape.65, bf16[2,3456]{1,0:T(2,128)(2,1)S(1)} %collective-permute-done, bf16[2,3456]{1,0:T(2,128)(2,1)S(1)} %collective-permute-done.1, bf16[2,3456]{1,0:T(2,128)(2,1)S(1)} %collective-permute-done.2, bf16[8,3456]{1,0:T(8,128)(2,1)S(1)} %collective-permute-done.3, ...), dimensions={0} | concatenate | bytes 442368 | tf_op jit(solution)/shard_map/concatenate | solution.py:96
  36.1 5.5 %collective-permute-start.6 = (bf16[32,3456]{1,0:T(8,128)(2,1)}, bf16[32,3456]{1,0:T(8,128)(2,1)}, u32[]{:S(2)}, u32[]{:S(2)}) collective-permute-start(bf16[32,3456]{1,0:T(8,128)(2,1)} %concatenate.12.refs_1_), channel_id=1, source_target_pairs={{0,32},{2,34},{4,36},{6,38},{8,40},{10,42},{12,44},{14,46},{16,48}... | collective-permute-start | bytes 663560 | tf_op jit(solution)/shard_map/ppermute | solution.py:95
  41.5 3.9 %collective-permute-start.7 = (bf16[32,3456]{1,0:T(8,128)(2,1)}, bf16[32,3456]{1,0:T(8,128)(2,1)}, u32[]{:S(2)}, u32[]{:S(2)}) collective-permute-start(bf16[32,3456]{1,0:T(8,128)(2,1)} %concatenate.12.refs_1_), channel_id=1, source_target_pairs={{0,64},{2,66},{4,68},{6,70},{8,72},{10,74},{12,76},{14,78},{16,80}... | collective-permute-start | bytes 663560 | tf_op jit(solution)/shard_map/ppermute | solution.py:95
  45.4 1.9 %collective-permute-start.8 = (bf16[32,3456]{1,0:T(8,128)(2,1)}, bf16[32,3456]{1,0:T(8,128)(2,1)}, u32[]{:S(2)}, u32[]{:S(2)}) collective-permute-start(bf16[32,3456]{1,0:T(8,128)(2,1)} %concatenate.12.refs_1_), channel_id=1, source_target_pairs={{0,96},{2,98},{4,100},{6,102},{8,104},{10,106},{12,108},{14,110},{... | collective-permute-start | bytes 663560 | tf_op jit(solution)/shard_map/ppermute | solution.py:95
  47.3 0.3 reshape.61
  48.0 1.0 %copy.39 = bf16[128,3456]{0,1:T(8,128)(2,1)S(1)} copy(bf16[128,3456]{1,0:T(8,128)(2,1)S(1)} %slice.32) | data formatting | bytes 1769472 | tf_op jit(solution)/shard_map/slice | solution.py:132
  49.0 1.0 %copy.40 = bf16[128,48,72]{2,1,0:T(8,128)(2,1)S(1)} copy(bf16[128,48,72]{0,2,1:T(8,128)(2,1)S(1)} %bitcast.22) | data formatting | bytes 1769472 | tf_op jit(solution)/shard_map/reshape | solution.py:133
  50.0 2.1 %fusion.2 = bf16[128,48,72]{2,1,0:T(8,128)(2,1)} fusion(bf16[128,48,72]{2,1,0:T(8,128)(2,1)S(1)} %copy.40, f32[128,72]{1,0:T(8,128)S(1)} %add_select_fusion), kind=kOutput, calls=%fused_computation.4 | convolution fusion | flops 64806912 | bytes 1806336 | tf_op jit(solution)/shard_map/srt,stf->srf/dot_general | solution.py:141
  52.2 2.0 %copy.41 = bf16[128,48,72]{0,2,1:T(8,128)(2,1)S(1)} copy(bf16[128,48,72]{2,1,0:T(8,128)(2,1)} %fusion.2) | data formatting | bytes 1769472 | tf_op jit(solution)/shard_map/convert_element_type | solution.py:142
  54.3 0.3 fusion.15
  54.7 6.1 %all-reduce.3 = (f32[4,3456]{1,0:T(4,128)S(1)}, f32[4]{0:T(128)S(1)}) all-reduce(f32[4,3456]{1,0:T(4,128)S(1)} %fusion.15, f32[4]{0:T(128)S(1)} %convert_reduce_fusion), channel_id=3, replica_groups=mesh['loop'=64,'grp'=2] {'grp'}, use_global_device_ids=true, to_apply=%region_2.3.clone | all-reduce | flops 13828 | bytes 110624
  60.8 0.7 dynamic-slice_divide_fusion
  61.5 13.2 %shard_map.68 = (f32[1,128]{1,0:T(1,128)}, f32[1,128]{1,0:T(1,128)}) custom-call(bf16[128,3456]{1,0:T(8,128)(2,1)} %copy.43.refs_0_, bf16[32,3456]{1,0:T(8,128)(2,1)} %concatenate.12.refs_1_, bf16[32,3456]{1,0:T(8,128)(2,1)} %collective-permute-done.6.refs_2_, bf16[32,3456]{1,0:T(8,128)(2,1)} %collective-permute-done.7.refs_3_, ...), custom_call_target="tpu_custom_call" | custom-call | tf_op jit(solution)/shard_map/pallas_call | solution.py:62
  74.7 0.7 maximum_bitcast_fusion
  75.4 1.8 %all-gather.1 = f32[2,2,128]{2,1,0:T(2,128)S(1)} all-gather(f32[1,2,128]{2,1,0:T(2,128)S(1)} %maximum_bitcast_fusion), channel_id=2, replica_groups=mesh['loop'=64,'grp'=2] {'grp'}, dimensions={0}, use_global_device_ids=true | all-gather | bytes 3072 | tf_op jit(solution)/shard_map/all_gather | solution.py:156
  77.3 0.5 log_add_fusion
  (34 shorter events, 1.9 us)
Async XLA Ops:
  3.9 13.3 %copy-start.1 = (bf16[2,3456]{1,0:T(2,128)(2,1)S(1)}, bf16[2,3456]{1,0:T(2,128)(2,1)}, u32[]{:S(2)}) copy-start(bf16[2,3456]{1,0:T(2,128)(2,1)} %param.6) | copy-start | bytes 41476
  3.9 25.5 %copy-start = (bf16[128,3456]{1,0:T(8,128)(2,1)S(1)}, bf16[128,3456]{1,0:T(8,128)(2,1)}, u32[]{:S(2)}) copy-start(bf16[128,3456]{1,0:T(8,128)(2,1)} %param.5) | copy-start | bytes 2654212
  5.2 42.1 %all-to-all-start = ((bf16[64,2,3584]{2,1,0:T(2,128)(2,1)}), bf16[64,2,3584]{2,1,0:T(2,128)(2,1)S(1)}, u32[]{:S(2)}, u32[]{:S(2)}) async-start(bf16[64,2,3584]{2,1,0:T(2,128)(2,1)} %reshape.60), calls=%async_computation | async-start | bytes 1835008 | tf_op jit(solution)/shard_map/all_to_all | solution.py:129
  17.5 4.8 %collective-permute-start = (bf16[2,3456]{1,0:T(2,128)(2,1)S(1)}, bf16[2,3456]{1,0:T(2,128)(2,1)S(1)}, u32[]{:S(2)}, u32[]{:S(2)}) collective-permute-start(bf16[2,3456]{1,0:T(2,128)(2,1)S(1)} %reshape.65), channel_id=1, source_target_pairs={{0,2},{2,4},{4,6},{6,0},{8,10},{10,12},{12,14},{14,8},{16,18},{18,... | collective-permute-start | bytes 41480 | tf_op jit(solution)/shard_map/ppermute | solution.py:95
  18.6 5.0 %collective-permute-start.1 = (bf16[2,3456]{1,0:T(2,128)(2,1)S(1)}, bf16[2,3456]{1,0:T(2,128)(2,1)S(1)}, u32[]{:S(2)}, u32[]{:S(2)}) collective-permute-start(bf16[2,3456]{1,0:T(2,128)(2,1)S(1)} %reshape.65), channel_id=1, source_target_pairs={{0,4},{2,6},{4,0},{6,2},{8,12},{10,14},{12,8},{14,10},{16,20},{18,... | collective-permute-start | bytes 41480 | tf_op jit(solution)/shard_map/ppermute | solution.py:95
  21.0 5.2 %collective-permute-start.2 = (bf16[2,3456]{1,0:T(2,128)(2,1)S(1)}, bf16[2,3456]{1,0:T(2,128)(2,1)S(1)}, u32[]{:S(2)}, u32[]{:S(2)}) collective-permute-start(bf16[2,3456]{1,0:T(2,128)(2,1)S(1)} %reshape.65), channel_id=1, source_target_pairs={{0,6},{2,0},{4,2},{6,4},{8,14},{10,8},{12,10},{14,12},{16,22},{18,... | collective-permute-start | bytes 41480 | tf_op jit(solution)/shard_map/ppermute | solution.py:95
  26.3 7.2 %collective-permute-start.3 = (bf16[8,3456]{1,0:T(8,128)(2,1)S(1)}, bf16[8,3456]{1,0:T(8,128)(2,1)S(1)}, u32[]{:S(2)}, u32[]{:S(2)}) collective-permute-start(bf16[8,3456]{1,0:T(8,128)(2,1)S(1)} %pad_maximum_fusion), channel_id=1, source_target_pairs={{0,8},{2,10},{4,12},{6,14},{8,16},{10,18},{12,20},{14,22},{16,24},... | collective-permute-start | bytes 165896 | tf_op jit(solution)/shard_map/ppermute | solution.py:95
  26.4 7.1 %collective-permute-start.4 = (bf16[8,3456]{1,0:T(8,128)(2,1)S(1)}, bf16[8,3456]{1,0:T(8,128)(2,1)S(1)}, u32[]{:S(2)}, u32[]{:S(2)}) collective-permute-start(bf16[8,3456]{1,0:T(8,128)(2,1)S(1)} %pad_maximum_fusion), channel_id=1, source_target_pairs={{0,16},{2,18},{4,20},{6,22},{8,24},{10,26},{12,28},{14,30},{16,0},... | collective-permute-start | bytes 165896 | tf_op jit(solution)/shard_map/ppermute | solution.py:95
  28.4 5.1 %collective-permute-start.5 = (bf16[8,3456]{1,0:T(8,128)(2,1)S(1)}, bf16[8,3456]{1,0:T(8,128)(2,1)S(1)}, u32[]{:S(2)}, u32[]{:S(2)}) collective-permute-start(bf16[8,3456]{1,0:T(8,128)(2,1)S(1)} %pad_maximum_fusion), channel_id=1, source_target_pairs={{0,24},{2,26},{4,28},{6,30},{8,0},{10,2},{12,4},{14,6},{16,8},{18,... | collective-permute-start | bytes 165896 | tf_op jit(solution)/shard_map/ppermute | solution.py:95
  30.4 1.8 %copy-start.2 = (u32[128]{0:T(128)S(1)}, u32[128]{0:T(128)}, u32[]{:S(2)}) copy-start(u32[128]{0:T(128)} %constant.65) | copy-start | bytes 1540
  36.1 25.4 %collective-permute-start.6 = (bf16[32,3456]{1,0:T(8,128)(2,1)}, bf16[32,3456]{1,0:T(8,128)(2,1)}, u32[]{:S(2)}, u32[]{:S(2)}) collective-permute-start(bf16[32,3456]{1,0:T(8,128)(2,1)} %concatenate.12.refs_1_), channel_id=1, source_target_pairs={{0,32},{2,34},{4,36},{6,38},{8,40},{10,42},{12,44},{14,46},{16,48}... | collective-permute-start | bytes 663560 | tf_op jit(solution)/shard_map/ppermute | solution.py:95
  41.5 20.0 %collective-permute-start.7 = (bf16[32,3456]{1,0:T(8,128)(2,1)}, bf16[32,3456]{1,0:T(8,128)(2,1)}, u32[]{:S(2)}, u32[]{:S(2)}) collective-permute-start(bf16[32,3456]{1,0:T(8,128)(2,1)} %concatenate.12.refs_1_), channel_id=1, source_target_pairs={{0,64},{2,66},{4,68},{6,70},{8,72},{10,74},{12,76},{14,78},{16,80}... | collective-permute-start | bytes 663560 | tf_op jit(solution)/shard_map/ppermute | solution.py:95
  45.4 16.1 %collective-permute-start.8 = (bf16[32,3456]{1,0:T(8,128)(2,1)}, bf16[32,3456]{1,0:T(8,128)(2,1)}, u32[]{:S(2)}, u32[]{:S(2)}) collective-permute-start(bf16[32,3456]{1,0:T(8,128)(2,1)} %concatenate.12.refs_1_), channel_id=1, source_target_pairs={{0,96},{2,98},{4,100},{6,102},{8,104},{10,106},{12,108},{14,110},{... | collective-permute-start | bytes 663560 | tf_op jit(solution)/shard_map/ppermute | solution.py:95

commit v7 on v6

--- a/solution.py
+++ b/solution.py
@@ -73,6 +73,15 @@
     return highest[0], summed[0]
 
 
+def average_kernel(w_ref, x_ref, o_ref, s_scr):
+    block = o_ref.shape[0]
+    s_scr[...] = jnp.dot(w_ref[...], x_ref[...], preferred_element_type=jnp.float32)
+    total = s_scr[pl.ds(0, block), :]
+    for angle in range(1, ANGLES):
+        total = total + pltpu.roll(s_scr[pl.ds(angle * block, block), :], angle * RADII, 1)
+    o_ref[...] = total
+
+
 def ring_factors(count):
     factors = []
     while count > 1:
@@ -103,8 +112,9 @@
     grp_size = lax.axis_size("grp")
     half_rows = row_count // grp_size
     grp_index = lax.axis_index("grp")
-    own_rows = lax.dynamic_slice_in_dim(particles, grp_index * half_rows, half_rows, 0)
     pieces = staged_gather(angle_major(references), "loop")
+    particle_rows = angle_major(particles)
+    own_rows = lax.dynamic_slice_in_dim(particle_rows, grp_index * half_rows, half_rows, 0)
     owner_count = lax.axis_size("loop")
     per_owner = references.shape[0] * grp_size
     capacity = max(2, row_count // owner_count)
@@ -130,29 +140,34 @@
     incoming = incoming.reshape(slot_count, flat_len + label_lanes)
     labels_in = incoming[:, flat_len : flat_len + 3]
     incoming = incoming[:, :flat_len]
-    images = incoming.reshape(slot_count, RADII, ANGLES)
-    labels_in = labels_in.reshape(slot_count, 3).astype(jnp.float32)
+    labels_in = labels_in.astype(jnp.float32)
     member_in = labels_in[:, 0]
     rotation = labels_in[:, 1]
     weight_of = labels_in[:, 2]
+    block = -(-per_owner // 8) * 8
     angle_grid = jnp.arange(ANGLES, dtype=jnp.float32)
-    source_angle = jnp.mod(angle_grid[None, :] - rotation[:, None], float(ANGLES))
-    rotator = (angle_grid[None, :, None] == source_angle[:, None, :]).astype(jnp.bfloat16)
-    aligned = jnp.einsum("srt,stf->srf", images, rotator, preferred_element_type=jnp.float32)
-    aligned = aligned.astype(jnp.bfloat16).reshape(slot_count, flat_len)
-    member_grid = jnp.arange(per_owner, dtype=jnp.float32)
-    weighted = (
-        (member_grid[:, None] == member_in[None, :]).astype(jnp.float32) * weight_of[None, :]
-    ).astype(jnp.bfloat16)
-    partial_sums = jnp.dot(weighted, aligned, preferred_element_type=jnp.float32)
-    partial_weight = jnp.sum(weighted.astype(jnp.float32), axis=1)
+    member_grid = jnp.arange(block, dtype=jnp.float32)
+    chosen = (angle_grid[:, None, None] == rotation[None, None, :]) & (
+        member_grid[None, :, None] == member_in[None, None, :]
+    )
+    by_angle = jnp.where(chosen, weight_of[None, None, :], 0.0).astype(jnp.bfloat16)
+    by_angle = by_angle.reshape(ANGLES * block, slot_count)
+    partial_sums = pl.pallas_call(
+        average_kernel,
+        out_shape=jax.ShapeDtypeStruct((block, flat_len), jnp.float32),
+        scratch_shapes=[pltpu.VMEM((ANGLES * block, flat_len), jnp.float32)],
+    )(by_angle, incoming)
+    partial_sums = partial_sums[:per_owner].reshape(per_owner, ANGLES, RADII).transpose(0, 2, 1)
+    partial_sums = partial_sums.reshape(per_owner, flat_len)
+    weighted = (member_grid[:per_owner, None] == member_in[None, :]).astype(jnp.float32) * weight_of[None, :]
+    partial_weight = jnp.sum(weighted, axis=1)
     class_sums, class_weight = (
         lax.psum_scatter(partial_sums, "grp", scatter_dimension=0, tiled=True),
         lax.psum_scatter(partial_weight, "grp", scatter_dimension=0, tiled=True),
     )
     class_average = class_sums / class_weight[:, None]
     class_average, pieces = lax.optimization_barrier((class_average, pieces))
-    highest, summed = score_all(angle_major(particles), pieces)
+    highest, summed = score_all(particle_rows, pieces)
     stats = lax.all_gather(jnp.stack([highest, summed], axis=0), "grp", axis=0, tiled=False)
     stats = lax.dynamic_slice_in_dim(stats, grp_index * half_rows, half_rows, 2)
     highest = jnp.max(stats[:, 0], axis=0)

time: 78.2 us -> 77.6 us (level)
  Pallas kernels: 13.2 us -> 17.2 us
  matrix products: 2.86 us -> 0.42 us
  local copies, waits for them, and re-layouts: 13.4 us -> 11 us
  waiting for transfers between devices: 4.04 us -> 4.91 us
    pallas_call x0 -> x1, Pallas kernels: none -> 3.97 us  [local(): pl.pallas_call(average_kernel, out_shape=jax.ShapeDtypeStruct((block, fla...]
    unnamed x10 -> x19, local copies, waits for them, and re-layouts: 1.78 us -> 4.34 us
    dot_general x2 -> x0, matrix products: 2.47 us -> none  [the longest x1 2.14 us: local(): jnp.einsum('srt,stf->srf', images, rotator, preferred_element_type=jnp.fl...]
    concatenate x1, local copies, waits for them, and re-layouts: 2.57 us -> 0.14 us  [staged_gather(): rows = jnp.concatenate(parts, axis=0)]
    convert_element_type x1 -> x0, local copies, waits for them, and re-layouts: 2.02 us -> none  [local(): aligned = aligned.astype(jnp.bfloat16).reshape(slot_count, flat_len)]
    slice x1 -> x2, local copies, waits for them, and re-layouts: 0.19 us -> 1.12 us  [the longest x1 0.9 us: local(): partial_sums[:per_owner].reshape(per_owner, ANGLES, RADII)]
    ppermute x9, waiting for transfers between devices: 4.04 us -> 4.91 us  [staged_gather(): parts.append(lax.ppermute(rows, axis, pairs))]
  transfers between devices with their start and end apart: 10 -> 10, of which waited for: 3 -> 4; matrix products, arithmetic and copies ran while one was open for 19% -> 9% of each run, Pallas kernels for 0% -> 5%
where the time goes in v7:
time: 77.6 us; the launch traced here: 77.2 us
  starting transfers between devices  30.3 us (39%)
  Pallas kernels  17.2 us (22%)
  local copies, waits for them, and re-layouts  11 us (14%)
  blocking collectives  7.83 us (10%)
  waiting for transfers between devices  4.91 us (6%)
  other arithmetic  4.07 us (5%)
  between operations  1.5 us (2%)
    ppermute x9, starting transfers between devices, staged_gather(): parts.append(lax.ppermute(rows, axis, pairs))  18.2 us
    pallas_call x1, Pallas kernels, score_all(): pl.pallas_call(functools.partial(score_kernel, scale=scale), out_shape=(j...  13.2 us
    all_to_all x1, starting transfers between devices, local(): lax.all_to_all(outgoing, 'loop', split_axis=0, concat_axis=0, tiled=True)  12.1 us
    unnamed x1, blocking collectives  6.05 us
    ppermute x9, waiting for transfers between devices, staged_gather(): parts.append(lax.ppermute(rows, axis, pairs))  4.91 us
    unnamed x19, local copies, waits for them, and re-layouts  4.34 us
    pallas_call x1, Pallas kernels, local(): pl.pallas_call(average_kernel, out_shape=jax.ShapeDtypeStruct((block, fla...  3.97 us
    reshape x4, local copies, waits for them, and re-layouts, angle_major(): rows.reshape(count, RADII, ANGLES).transpose(0, 2, 1)  1.97 us
  transfers between devices with their start and end apart: 10, of which 4 were waited for; matrix products, arithmetic and copies ran while one was open for 9% of the time, Pallas kernels for 5%

profile of v7, /device:TPU:1, one launch (start us, length us, event | category | flops | bytes accessed | tf_op | source)
XLA Modules:
  0.0 77.2 jit_solution(5821734812157773772)
XLA Ops:
  0.6 0.7 and_select_fusion.1
  1.7 1.9 %copy.27 = bf16[128,3456]{0,1:T(8,128)(2,1)S(1)} copy(bf16[128,3456]{1,0:T(8,128)(2,1)} %param.5) | data formatting | bytes 1769472 | tf_op args[0]
  4.0 0.3 copy-done.5
  4.4 0.4 convolution_convert_fusion
  4.8 1.3 %reshape.94 = bf16[64,2,3584]{2,1,0:T(2,128)(2,1)} reshape(bf16[128,3584]{1,0:T(8,128)(2,1)S(1)} %convolution_convert_fusion) | data formatting | bytes 1835008 | tf_op jit(solution)/shard_map/reshape | solution.py:138
  6.1 12.1 %all-to-all-start = ((bf16[64,2,3584]{2,1,0:T(2,128)(2,1)}), bf16[64,2,3584]{2,1,0:T(2,128)(2,1)S(1)}, u32[]{:S(2)}, u32[]{:S(2)}) async-start(bf16[64,2,3584]{2,1,0:T(2,128)(2,1)} %reshape.94), calls=%async_computation | async-start | bytes 1835008 | tf_op jit(solution)/shard_map/all_to_all | solution.py:139
  18.6 1.1 %collective-permute-start = (bf16[2,3456]{1,0:T(2,128)(2,1)S(1)}, bf16[2,3456]{1,0:T(2,128)(2,1)S(1)}, u32[]{:S(2)}, u32[]{:S(2)}) collective-permute-start(bf16[2,3456]{1,0:T(2,128)(2,1)S(1)} %reshape.99), channel_id=1, source_target_pairs={{0,2},{2,4},{4,6},{6,0},{8,10},{10,12},{12,14},{14,8},{16,18},{18,... | collective-permute-start | bytes 41480 | tf_op jit(solution)/shard_map/ppermute | solution.py:104
  19.7 2.4 %collective-permute-start.1 = (bf16[2,3456]{1,0:T(2,128)(2,1)S(1)}, bf16[2,3456]{1,0:T(2,128)(2,1)S(1)}, u32[]{:S(2)}, u32[]{:S(2)}) collective-permute-start(bf16[2,3456]{1,0:T(2,128)(2,1)S(1)} %reshape.99), channel_id=1, source_target_pairs={{0,4},{2,6},{4,0},{6,2},{8,12},{10,14},{12,8},{14,10},{16,20},{18,... | collective-permute-start | bytes 41480 | tf_op jit(solution)/shard_map/ppermute | solution.py:104
  22.1 1.2 %collective-permute-start.2 = (bf16[2,3456]{1,0:T(2,128)(2,1)S(1)}, bf16[2,3456]{1,0:T(2,128)(2,1)S(1)}, u32[]{:S(2)}, u32[]{:S(2)}) collective-permute-start(bf16[2,3456]{1,0:T(2,128)(2,1)S(1)} %reshape.99), channel_id=1, source_target_pairs={{0,6},{2,0},{4,2},{6,4},{8,14},{10,8},{12,10},{14,12},{16,22},{18,... | collective-permute-start | bytes 41480 | tf_op jit(solution)/shard_map/ppermute | solution.py:104
  23.4 1.3 %collective-permute-done.1 = bf16[2,3456]{1,0:T(2,128)(2,1)S(1)} collective-permute-done((bf16[2,3456]{1,0:T(2,128)(2,1)S(1)}, bf16[2,3456]{1,0:T(2,128)(2,1)S(1)}, u32[]{:S(2)}, u32[]{:S(2)}) %collective-permute-start.1) | collective-permute-done | bytes 13856 | tf_op jit(solution)/shard_map/ppermute | solution.py:104
  24.7 2.6 %collective-permute-done.2 = bf16[2,3456]{1,0:T(2,128)(2,1)S(1)} collective-permute-done((bf16[2,3456]{1,0:T(2,128)(2,1)S(1)}, bf16[2,3456]{1,0:T(2,128)(2,1)S(1)}, u32[]{:S(2)}, u32[]{:S(2)}) %collective-permute-start.2) | collective-permute-done | bytes 13856 | tf_op jit(solution)/shard_map/ppermute | solution.py:104
  27.4 2.0 %collective-permute-start.4 = (bf16[8,3456]{1,0:T(8,128)(2,1)S(1)}, bf16[8,3456]{1,0:T(8,128)(2,1)S(1)}, u32[]{:S(2)}, u32[]{:S(2)}) collective-permute-start(bf16[8,3456]{1,0:T(8,128)(2,1)S(1)} %pad_maximum_fusion), channel_id=1, source_target_pairs={{0,16},{2,18},{4,20},{6,22},{8,24},{10,26},{12,28},{14,30},{16,0},... | collective-permute-start | bytes 165896 | tf_op jit(solution)/shard_map/ppermute | solution.py:104
  29.5 1.0 %collective-permute-start.5 = (bf16[8,3456]{1,0:T(8,128)(2,1)S(1)}, bf16[8,3456]{1,0:T(8,128)(2,1)S(1)}, u32[]{:S(2)}, u32[]{:S(2)}) collective-permute-start(bf16[8,3456]{1,0:T(8,128)(2,1)S(1)} %pad_maximum_fusion), channel_id=1, source_target_pairs={{0,24},{2,26},{4,28},{6,30},{8,0},{10,2},{12,4},{14,6},{16,8},{18,... | collective-permute-start | bytes 165896 | tf_op jit(solution)/shard_map/ppermute | solution.py:104
  30.5 1.6 %copy.31.refs_0_ = bf16[128,3456]{1,0:T(8,128)(2,1)} copy(bf16[128,3456]{0,1:T(8,128)(2,1)S(1)} %bitcast.21) | data formatting | bytes 1769472 | tf_op jit(solution)/shard_map/reshape | solution.py:20
  32.1 0.6 dynamic-slice.1
  33.4 0.9 %collective-permute-done.3 = bf16[8,3456]{1,0:T(8,128)(2,1)S(1)} collective-permute-done((bf16[8,3456]{1,0:T(8,128)(2,1)S(1)}, bf16[8,3456]{1,0:T(8,128)(2,1)S(1)}, u32[]{:S(2)}, u32[]{:S(2)}) %collective-permute-start.3) | collective-permute-done | bytes 55328 | tf_op jit(solution)/shard_map/ppermute | solution.py:104
  34.4 4.7 %collective-permute-start.6 = (bf16[32,3456]{1,0:T(8,128)(2,1)S(1)}, bf16[32,3456]{1,0:T(8,128)(2,1)S(1)}, u32[]{:S(2)}, u32[]{:S(2)}) collective-permute-start(bf16[32,3456]{1,0:T(8,128)(2,1)S(1)} %concatenate.12.refs_1_), channel_id=1, source_target_pairs={{0,32},{2,34},{4,36},{6,38},{8,40},{10,42},{12,44},{14,46},{16,48}... | collective-permute-start | bytes 663560 | tf_op jit(solution)/shard_map/ppermute | solution.py:104
  39.1 3.9 %collective-permute-start.7 = (bf16[32,3456]{1,0:T(8,128)(2,1)S(1)}, bf16[32,3456]{1,0:T(8,128)(2,1)S(1)}, u32[]{:S(2)}, u32[]{:S(2)}) collective-permute-start(bf16[32,3456]{1,0:T(8,128)(2,1)S(1)} %concatenate.12.refs_1_), channel_id=1, source_target_pairs={{0,64},{2,66},{4,68},{6,70},{8,72},{10,74},{12,76},{14,78},{16,80}... | collective-permute-start | bytes 663560 | tf_op jit(solution)/shard_map/ppermute | solution.py:104
  43.0 1.9 %collective-permute-start.8 = (bf16[32,3456]{1,0:T(8,128)(2,1)S(1)}, bf16[32,3456]{1,0:T(8,128)(2,1)S(1)}, u32[]{:S(2)}, u32[]{:S(2)}) collective-permute-start(bf16[32,3456]{1,0:T(8,128)(2,1)S(1)} %concatenate.12.refs_1_), channel_id=1, source_target_pairs={{0,96},{2,98},{4,100},{6,102},{8,104},{10,106},{12,108},{14,110},{... | collective-permute-start | bytes 663560 | tf_op jit(solution)/shard_map/ppermute | solution.py:104
  44.8 0.3 reshape.95
  45.2 1.0 %slice.41.x_ref = bf16[128,3456]{1,0:T(8,128)(2,1)} slice(bf16[128,3584]{1,0:T(8,128)(2,1)S(1)} %reshape.95), slice={[0:128], [0:3456]} | slice | bytes 1769472 | tf_op jit(solution)/shard_map/slice | solution.py:142
  46.5 0.7 select_convert_fusion.w_ref
  47.2 4.0 %shard_map.68 = f32[8,3456]{1,0:T(8,128)} custom-call(bf16[576,128]{1,0:T(8,128)(2,1)} %select_convert_fusion.w_ref, bf16[128,3456]{1,0:T(8,128)(2,1)} %slice.41.x_ref), custom_call_target="tpu_custom_call" | custom-call | tf_op jit(solution)/shard_map/pallas_call | solution.py:155
  51.2 0.9 %slice.42 = f32[4,3456]{1,0:T(4,128)S(1)} slice(f32[8,3456]{1,0:T(8,128)} %shard_map.68), slice={[0:4], [0:3456]} | slice | bytes 110592 | tf_op jit(solution)/shard_map/slice | solution.py:160
  52.6 6.1 %all-reduce.3 = (f32[4,3456]{1,0:T(4,128)S(1)}, f32[4]{0:T(128)S(1)}) all-reduce(f32[4,3456]{1,0:T(4,128)S(1)} %reshape.97, f32[4]{0:T(128)S(1)} %select_reduce_fusion.1), channel_id=3, replica_groups=mesh['loop'=64,'grp'=2] {'grp'}, use_global_device_ids=true, to_apply=%region_2.3.clone | all-reduce | flops 13828 | bytes 110624
  58.7 0.7 dynamic-slice_divide_fusion
  59.5 0.7 copy-done.1
  60.2 0.7 copy-done.3
  60.9 13.2 %shard_map.69 = (f32[1,128]{1,0:T(1,128)}, f32[1,128]{1,0:T(1,128)}) custom-call(bf16[128,3456]{1,0:T(8,128)(2,1)} %copy.31.refs_0_, bf16[32,3456]{1,0:T(8,128)(2,1)} %copy-done, bf16[32,3456]{1,0:T(8,128)(2,1)} %copy-done.1, bf16[32,3456]{1,0:T(8,128)(2,1)} %copy-done.2, bf16[32,3456]{1,0:T(8,128)(2,1)} %copy-done.3), custom_call_target="tpu_custom_call" | custom-call | tf_op jit(solution)/shard_map/pallas_call | solution.py:62
  74.1 0.7 maximum_bitcast_fusion
  74.8 1.8 %all-gather.1 = f32[2,2,128]{2,1,0:T(2,128)S(1)} all-gather(f32[1,2,128]{2,1,0:T(2,128)S(1)} %maximum_bitcast_fusion), channel_id=2, replica_groups=mesh['loop'=64,'grp'=2] {'grp'}, dimensions={0}, use_global_device_ids=true | all-gather | bytes 3072 | tf_op jit(solution)/shard_map/all_gather | solution.py:171
  76.7 0.5 log_add_fusion
  (46 shorter events, 2.6 us)
Async XLA Ops:
  3.7 0.7 copy-start.5
  3.7 0.7 copy-start.6
  6.1 12.1 %copy-start.4 = (bf16[2,3456]{1,0:T(2,128)(2,1)S(1)}, bf16[2,3456]{1,0:T(2,128)(2,1)}, u32[]{:S(2)}) copy-start(bf16[2,3456]{1,0:T(2,128)(2,1)} %param.6) | copy-start | bytes 41476
  6.1 38.7 %all-to-all-start = ((bf16[64,2,3584]{2,1,0:T(2,128)(2,1)}), bf16[64,2,3584]{2,1,0:T(2,128)(2,1)S(1)}, u32[]{:S(2)}, u32[]{:S(2)}) async-start(bf16[64,2,3584]{2,1,0:T(2,128)(2,1)} %reshape.94), calls=%async_computation | async-start | bytes 1835008 | tf_op jit(solution)/shard_map/all_to_all | solution.py:139
  18.6 4.8 %collective-permute-start = (bf16[2,3456]{1,0:T(2,128)(2,1)S(1)}, bf16[2,3456]{1,0:T(2,128)(2,1)S(1)}, u32[]{:S(2)}, u32[]{:S(2)}) collective-permute-start(bf16[2,3456]{1,0:T(2,128)(2,1)S(1)} %reshape.99), channel_id=1, source_target_pairs={{0,2},{2,4},{4,6},{6,0},{8,10},{10,12},{12,14},{14,8},{16,18},{18,... | collective-permute-start | bytes 41480 | tf_op jit(solution)/shard_map/ppermute | solution.py:104
  19.7 5.0 %collective-permute-start.1 = (bf16[2,3456]{1,0:T(2,128)(2,1)S(1)}, bf16[2,3456]{1,0:T(2,128)(2,1)S(1)}, u32[]{:S(2)}, u32[]{:S(2)}) collective-permute-start(bf16[2,3456]{1,0:T(2,128)(2,1)S(1)} %reshape.99), channel_id=1, source_target_pairs={{0,4},{2,6},{4,0},{6,2},{8,12},{10,14},{12,8},{14,10},{16,20},{18,... | collective-permute-start | bytes 41480 | tf_op jit(solution)/shard_map/ppermute | solution.py:104
  22.1 5.2 %collective-permute-start.2 = (bf16[2,3456]{1,0:T(2,128)(2,1)S(1)}, bf16[2,3456]{1,0:T(2,128)(2,1)S(1)}, u32[]{:S(2)}, u32[]{:S(2)}) collective-permute-start(bf16[2,3456]{1,0:T(2,128)(2,1)S(1)} %reshape.99), channel_id=1, source_target_pairs={{0,6},{2,0},{4,2},{6,4},{8,14},{10,8},{12,10},{14,12},{16,22},{18,... | collective-permute-start | bytes 41480 | tf_op jit(solution)/shard_map/ppermute | solution.py:104
  27.3 4.8 %copy-start.7 = (u32[128]{0:T(128)S(1)}, u32[128]{0:T(128)}, u32[]{:S(2)}) copy-start(u32[128]{0:T(128)} %constant.58) | copy-start | bytes 1540
  27.4 6.9 %collective-permute-start.3 = (bf16[8,3456]{1,0:T(8,128)(2,1)S(1)}, bf16[8,3456]{1,0:T(8,128)(2,1)S(1)}, u32[]{:S(2)}, u32[]{:S(2)}) collective-permute-start(bf16[8,3456]{1,0:T(8,128)(2,1)S(1)} %pad_maximum_fusion), channel_id=1, source_target_pairs={{0,8},{2,10},{4,12},{6,14},{8,16},{10,18},{12,20},{14,22},{16,24},... | collective-permute-start | bytes 165896 | tf_op jit(solution)/shard_map/ppermute | solution.py:104
  27.4 6.8 %collective-permute-start.4 = (bf16[8,3456]{1,0:T(8,128)(2,1)S(1)}, bf16[8,3456]{1,0:T(8,128)(2,1)S(1)}, u32[]{:S(2)}, u32[]{:S(2)}) collective-permute-start(bf16[8,3456]{1,0:T(8,128)(2,1)S(1)} %pad_maximum_fusion), channel_id=1, source_target_pairs={{0,16},{2,18},{4,20},{6,22},{8,24},{10,26},{12,28},{14,30},{16,0},... | collective-permute-start | bytes 165896 | tf_op jit(solution)/shard_map/ppermute | solution.py:104
  29.5 4.8 %collective-permute-start.5 = (bf16[8,3456]{1,0:T(8,128)(2,1)S(1)}, bf16[8,3456]{1,0:T(8,128)(2,1)S(1)}, u32[]{:S(2)}, u32[]{:S(2)}) collective-permute-start(bf16[8,3456]{1,0:T(8,128)(2,1)S(1)} %pad_maximum_fusion), channel_id=1, source_target_pairs={{0,24},{2,26},{4,28},{6,30},{8,0},{10,2},{12,4},{14,6},{16,8},{18,... | collective-permute-start | bytes 165896 | tf_op jit(solution)/shard_map/ppermute | solution.py:104
  34.4 10.8 %copy-start = (bf16[32,3456]{1,0:T(8,128)(2,1)}, bf16[32,3456]{1,0:T(8,128)(2,1)S(1)}, u32[]{:S(2)}) copy-start(bf16[32,3456]{1,0:T(8,128)(2,1)S(1)} %concatenate.12.refs_1_) | copy-start | bytes 663556
  34.4 25.1 %collective-permute-start.6 = (bf16[32,3456]{1,0:T(8,128)(2,1)S(1)}, bf16[32,3456]{1,0:T(8,128)(2,1)S(1)}, u32[]{:S(2)}, u32[]{:S(2)}) collective-permute-start(bf16[32,3456]{1,0:T(8,128)(2,1)S(1)} %concatenate.12.refs_1_), channel_id=1, source_target_pairs={{0,32},{2,34},{4,36},{6,38},{8,40},{10,42},{12,44},{14,46},{16,48}... | collective-permute-start | bytes 663560 | tf_op jit(solution)/shard_map/ppermute | solution.py:104
  39.1 20.3 %collective-permute-start.7 = (bf16[32,3456]{1,0:T(8,128)(2,1)S(1)}, bf16[32,3456]{1,0:T(8,128)(2,1)S(1)}, u32[]{:S(2)}, u32[]{:S(2)}) collective-permute-start(bf16[32,3456]{1,0:T(8,128)(2,1)S(1)} %concatenate.12.refs_1_), channel_id=1, source_target_pairs={{0,64},{2,66},{4,68},{6,70},{8,72},{10,74},{12,76},{14,78},{16,80}... | collective-permute-start | bytes 663560 | tf_op jit(solution)/shard_map/ppermute | solution.py:104
  43.0 16.5 %collective-permute-start.8 = (bf16[32,3456]{1,0:T(8,128)(2,1)S(1)}, bf16[32,3456]{1,0:T(8,128)(2,1)S(1)}, u32[]{:S(2)}, u32[]{:S(2)}) collective-permute-start(bf16[32,3456]{1,0:T(8,128)(2,1)S(1)} %concatenate.12.refs_1_), channel_id=1, source_target_pairs={{0,96},{2,98},{4,100},{6,102},{8,104},{10,106},{12,108},{14,110},{... | collective-permute-start | bytes 663560 | tf_op jit(solution)/shard_map/ppermute | solution.py:104
  59.4 0.7 copy-start.1
  59.5 0.8 copy-start.2
  60.2 0.7 copy-start.3

commit v8 on v7

--- a/solution.py
+++ b/solution.py
@@ -75,10 +75,21 @@
 
 def average_kernel(w_ref, x_ref, o_ref, s_scr):
     block = o_ref.shape[0]
-    s_scr[...] = jnp.dot(w_ref[...], x_ref[...], preferred_element_type=jnp.float32)
-    total = s_scr[pl.ds(0, block), :]
-    for angle in range(1, ANGLES):
-        total = total + pltpu.roll(s_scr[pl.ds(angle * block, block), :], angle * RADII, 1)
+    flat_len = o_ref.shape[1]
+    s_scr[...] = jnp.dot(w_ref[...], x_ref[:, :flat_len], preferred_element_type=jnp.float32)
+    step = 8
+    total = None
+    for part in range(step):
+        partial = None
+        for whole in range(ANGLES // step):
+            angle = whole * step + part
+            rows = s_scr[pl.ds(angle * block, block), :]
+            if whole:
+                rows = pltpu.roll(rows, whole * step * RADII, 1)
+            partial = rows if partial is None else partial + rows
+        if part:
+            partial = pltpu.roll(partial, part * RADII, 1)
+        total = partial if total is None else total + partial
     o_ref[...] = total
 
 
@@ -139,7 +150,6 @@
     incoming = lax.all_to_all(outgoing, "loop", split_axis=0, concat_axis=0, tiled=True)
     incoming = incoming.reshape(slot_count, flat_len + label_lanes)
     labels_in = incoming[:, flat_len : flat_len + 3]
-    incoming = incoming[:, :flat_len]
     labels_in = labels_in.astype(jnp.float32)
     member_in = labels_in[:, 0]
     rotation = labels_in[:, 1]
@@ -161,14 +171,15 @@
     partial_sums = partial_sums.reshape(per_owner, flat_len)
     weighted = (member_grid[:per_owner, None] == member_in[None, :]).astype(jnp.float32) * weight_of[None, :]
     partial_weight = jnp.sum(weighted, axis=1)
-    class_sums, class_weight = (
-        lax.psum_scatter(partial_sums, "grp", scatter_dimension=0, tiled=True),
-        lax.psum_scatter(partial_weight, "grp", scatter_dimension=0, tiled=True),
-    )
+    partial_sums, partial_weight, pieces = lax.optimization_barrier((partial_sums, partial_weight, pieces))
+    highest, summed = score_all(particle_rows, pieces)
+    stats = jnp.stack([highest, summed], axis=0)
+    slots = jnp.arange(grp_size, dtype=jnp.int32)[:, None, None] == grp_index
+    stats = jnp.where(slots, stats[None], 0.0)
+    partial_sums, partial_weight, stats = lax.psum((partial_sums, partial_weight, stats), "grp")
+    class_sums = lax.dynamic_slice_in_dim(partial_sums, grp_index * references.shape[0], references.shape[0], 0)
+    class_weight = lax.dynamic_slice_in_dim(partial_weight, grp_index * references.shape[0], references.shape[0], 0)
     class_average = class_sums / class_weight[:, None]
-    class_average, pieces = lax.optimization_barrier((class_average, pieces))
-    highest, summed = score_all(particle_rows, pieces)
-    stats = lax.all_gather(jnp.stack([highest, summed], axis=0), "grp", axis=0, tiled=False)
     stats = lax.dynamic_slice_in_dim(stats, grp_index * half_rows, half_rows, 2)
     highest = jnp.max(stats[:, 0], axis=0)
     summed = jnp.sum(stats[:, 1] * jnp.exp(stats[:, 0] - highest[None, :]), axis=0)

time: 77.6 us -> 73.4 us (0.946)
  blocking collectives: 7.83 us -> 6.34 us
  local copies, waits for them, and re-layouts: 11 us -> 9.77 us
  waiting for transfers between devices: 4.91 us -> 6.08 us
  Pallas kernels: 17.2 us -> 16.4 us
    psum x0 -> x1, blocking collectives: none -> 6.34 us  [local(): lax.psum((partial_sums, partial_weight, stats), 'grp')]
    unnamed x1 -> x0, blocking collectives: 6.05 us -> none
    all_gather x1 -> x0, blocking collectives: 1.77 us -> none  [local(): lax.all_gather(jnp.stack([highest, summed], axis=0), 'grp', axis=0, tiled...]
    ppermute x9, waiting for transfers between devices: 4.91 us -> 6.08 us  [staged_gather(): parts.append(lax.ppermute(rows, axis, pairs))]
    slice x1 -> x0, local copies, waits for them, and re-layouts: 1.02 us -> none  [local(): incoming = incoming[:, :flat_len]]
  transfers between devices with their start and end apart: 10 -> 10, of which waited for: 4 -> 4; matrix products, arithmetic and copies ran while one was open for 9% -> 7% of each run, Pallas kernels for 5% -> 4%
where the time goes in v8:
time: 73.4 us; the launch traced here: 73.1 us
  starting transfers between devices  29.6 us (40%)
  Pallas kernels  16.4 us (22%)
  local copies, waits for them, and re-layouts  9.77 us (13%)
  blocking collectives  6.34 us (9%)
  waiting for transfers between devices  6.08 us (8%)
  other arithmetic  3.56 us (5%)
  between operations  0.86 us (1%)
    ppermute x9, starting transfers between devices, staged_gather(): parts.append(lax.ppermute(rows, axis, pairs))  17.5 us
    pallas_call x1, Pallas kernels, score_all(): pl.pallas_call(functools.partial(score_kernel, scale=scale), out_shape=(j...  13.1 us
    all_to_all x1, starting transfers between devices, local(): lax.all_to_all(outgoing, 'loop', split_axis=0, concat_axis=0, tiled=True)  12.1 us
    psum x1, blocking collectives, local(): lax.psum((partial_sums, partial_weight, stats), 'grp')  6.34 us
    ppermute x9, waiting for transfers between devices, staged_gather(): parts.append(lax.ppermute(rows, axis, pairs))  6.08 us
    unnamed x19, local copies, waits for them, and re-layouts  4.01 us
    pallas_call x1, Pallas kernels, local(): pl.pallas_call(average_kernel, out_shape=jax.ShapeDtypeStruct((block, fla...  3.27 us
    reshape x4, local copies, waits for them, and re-layouts, angle_major(): rows.reshape(count, RADII, ANGLES).transpose(0, 2, 1)  2.04 us
  transfers between devices with their start and end apart: 10, of which 4 were waited for; matrix products, arithmetic and copies ran while one was open for 7% of the time, Pallas kernels for 4%

profile of v8, /device:TPU:1, one launch (start us, length us, event | category | flops | bytes accessed | tf_op | source)
XLA Modules:
  0.0 73.1 jit_solution(6566146662646415568)
XLA Ops:
  0.6 1.9 %copy.22 = bf16[128,3456]{0,1:T(8,128)(2,1)S(1)} copy(bf16[128,3456]{1,0:T(8,128)(2,1)} %param.5) | data formatting | bytes 1769472 | tf_op args[0]
  2.7 0.5 copy-done.8
  3.4 0.2 select_reduce_fusion
  3.6 0.3 constant_dynamic-slice_fusion.1
  4.1 0.4 convolution_convert_fusion
  4.5 1.3 %reshape.100 = bf16[64,2,3584]{2,1,0:T(2,128)(2,1)} reshape(bf16[128,3584]{1,0:T(8,128)(2,1)S(1)} %convolution_convert_fusion) | data formatting | bytes 1835008 | tf_op jit(solution)/shard_map/reshape | solution.py:149
  5.8 12.1 %all-to-all-start = ((bf16[64,2,3584]{2,1,0:T(2,128)(2,1)}), bf16[64,2,3584]{2,1,0:T(2,128)(2,1)S(1)}, u32[]{:S(2)}, u32[]{:S(2)}) async-start(bf16[64,2,3584]{2,1,0:T(2,128)(2,1)} %reshape.100), calls=%async_computation | async-start | bytes 1835008 | tf_op jit(solution)/shard_map/all_to_all | solution.py:150
  18.2 1.1 %collective-permute-start = (bf16[2,3456]{1,0:T(2,128)(2,1)S(1)}, bf16[2,3456]{1,0:T(2,128)(2,1)S(1)}, u32[]{:S(2)}, u32[]{:S(2)}) collective-permute-start(bf16[2,3456]{1,0:T(2,128)(2,1)S(1)} %reshape.105), channel_id=1, source_target_pairs={{0,2},{2,4},{4,6},{6,0},{8,10},{10,12},{12,14},{14,8},{16,18},{18,... | collective-permute-start | bytes 41480 | tf_op jit(solution)/shard_map/ppermute | solution.py:115
  19.3 2.4 %collective-permute-start.1 = (bf16[2,3456]{1,0:T(2,128)(2,1)S(1)}, bf16[2,3456]{1,0:T(2,128)(2,1)S(1)}, u32[]{:S(2)}, u32[]{:S(2)}) collective-permute-start(bf16[2,3456]{1,0:T(2,128)(2,1)S(1)} %reshape.105), channel_id=1, source_target_pairs={{0,4},{2,6},{4,0},{6,2},{8,12},{10,14},{12,8},{14,10},{16,20},{18,... | collective-permute-start | bytes 41480 | tf_op jit(solution)/shard_map/ppermute | solution.py:115
  21.7 1.2 %collective-permute-start.2 = (bf16[2,3456]{1,0:T(2,128)(2,1)S(1)}, bf16[2,3456]{1,0:T(2,128)(2,1)S(1)}, u32[]{:S(2)}, u32[]{:S(2)}) collective-permute-start(bf16[2,3456]{1,0:T(2,128)(2,1)S(1)} %reshape.105), channel_id=1, source_target_pairs={{0,6},{2,0},{4,2},{6,4},{8,14},{10,8},{12,10},{14,12},{16,22},{18,... | collective-permute-start | bytes 41480 | tf_op jit(solution)/shard_map/ppermute | solution.py:115
  23.0 1.3 %collective-permute-done.1 = bf16[2,3456]{1,0:T(2,128)(2,1)S(1)} collective-permute-done((bf16[2,3456]{1,0:T(2,128)(2,1)S(1)}, bf16[2,3456]{1,0:T(2,128)(2,1)S(1)}, u32[]{:S(2)}, u32[]{:S(2)}) %collective-permute-start.1) | collective-permute-done | bytes 13856 | tf_op jit(solution)/shard_map/ppermute | solution.py:115
  24.3 2.6 %collective-permute-done.2 = bf16[2,3456]{1,0:T(2,128)(2,1)S(1)} collective-permute-done((bf16[2,3456]{1,0:T(2,128)(2,1)S(1)}, bf16[2,3456]{1,0:T(2,128)(2,1)S(1)}, u32[]{:S(2)}, u32[]{:S(2)}) %collective-permute-start.2) | collective-permute-done | bytes 13856 | tf_op jit(solution)/shard_map/ppermute | solution.py:115
  27.1 2.0 %collective-permute-start.4 = (bf16[8,3456]{1,0:T(8,128)(2,1)S(1)}, bf16[8,3456]{1,0:T(8,128)(2,1)S(1)}, u32[]{:S(2)}, u32[]{:S(2)}) collective-permute-start(bf16[8,3456]{1,0:T(8,128)(2,1)S(1)} %pad_maximum_fusion), channel_id=1, source_target_pairs={{0,16},{2,18},{4,20},{6,22},{8,24},{10,26},{12,28},{14,30},{16,0},... | collective-permute-start | bytes 165896 | tf_op jit(solution)/shard_map/ppermute | solution.py:115
  29.1 1.0 %collective-permute-start.5 = (bf16[8,3456]{1,0:T(8,128)(2,1)S(1)}, bf16[8,3456]{1,0:T(8,128)(2,1)S(1)}, u32[]{:S(2)}, u32[]{:S(2)}) collective-permute-start(bf16[8,3456]{1,0:T(8,128)(2,1)S(1)} %pad_maximum_fusion), channel_id=1, source_target_pairs={{0,24},{2,26},{4,28},{6,30},{8,0},{10,2},{12,4},{14,6},{16,8},{18,... | collective-permute-start | bytes 165896 | tf_op jit(solution)/shard_map/ppermute | solution.py:115
  30.1 1.7 %copy.26.refs_0_ = bf16[128,3456]{1,0:T(8,128)(2,1)} copy(bf16[128,3456]{0,1:T(8,128)(2,1)S(1)} %bitcast.28) | data formatting | bytes 1769472 | tf_op jit(solution)/shard_map/reshape | solution.py:20
  31.8 2.0 %collective-permute-done.3 = bf16[8,3456]{1,0:T(8,128)(2,1)S(1)} collective-permute-done((bf16[8,3456]{1,0:T(8,128)(2,1)S(1)}, bf16[8,3456]{1,0:T(8,128)(2,1)S(1)}, u32[]{:S(2)}, u32[]{:S(2)}) %collective-permute-start.3) | collective-permute-done | bytes 55328 | tf_op jit(solution)/shard_map/ppermute | solution.py:115
  34.0 3.8 %collective-permute-start.6 = (bf16[32,3456]{1,0:T(8,128)(2,1)S(1)}, bf16[32,3456]{1,0:T(8,128)(2,1)S(1)}, u32[]{:S(2)}, u32[]{:S(2)}) collective-permute-start(bf16[32,3456]{1,0:T(8,128)(2,1)S(1)} %concatenate.12.refs_1_), channel_id=1, source_target_pairs={{0,32},{2,34},{4,36},{6,38},{8,40},{10,42},{12,44},{14,46},{16,48}... | collective-permute-start | bytes 663560 | tf_op jit(solution)/shard_map/ppermute | solution.py:115
  37.9 3.9 %collective-permute-start.7 = (bf16[32,3456]{1,0:T(8,128)(2,1)S(1)}, bf16[32,3456]{1,0:T(8,128)(2,1)S(1)}, u32[]{:S(2)}, u32[]{:S(2)}) collective-permute-start(bf16[32,3456]{1,0:T(8,128)(2,1)S(1)} %concatenate.12.refs_1_), channel_id=1, source_target_pairs={{0,64},{2,66},{4,68},{6,70},{8,72},{10,74},{12,76},{14,78},{16,80}... | collective-permute-start | bytes 663560 | tf_op jit(solution)/shard_map/ppermute | solution.py:115
  41.8 2.0 %collective-permute-start.8 = (bf16[32,3456]{1,0:T(8,128)(2,1)S(1)}, bf16[32,3456]{1,0:T(8,128)(2,1)S(1)}, u32[]{:S(2)}, u32[]{:S(2)}) collective-permute-start(bf16[32,3456]{1,0:T(8,128)(2,1)S(1)} %concatenate.12.refs_1_), channel_id=1, source_target_pairs={{0,96},{2,98},{4,100},{6,102},{8,104},{10,106},{12,108},{14,110},{... | collective-permute-start | bytes 663560 | tf_op jit(solution)/shard_map/ppermute | solution.py:115
  43.8 0.3 reshape.101.x_ref
  44.2 0.2 slice_reduce_fusion.2
  44.4 0.7 select_convert_fusion.w_ref
  45.1 3.3 %shard_map.68 = f32[8,3456]{1,0:T(8,128)} custom-call(bf16[576,128]{1,0:T(8,128)(2,1)} %select_convert_fusion.w_ref, bf16[128,3584]{1,0:T(8,128)(2,1)} %copy-done), custom_call_target="tpu_custom_call" | custom-call | tf_op jit(solution)/shard_map/pallas_call | solution.py:165
  48.4 0.9 %slice.37 = f32[4,3456]{1,0:T(4,128)S(1)} slice(f32[8,3456]{1,0:T(8,128)} %shard_map.68), slice={[0:4], [0:3456]} | slice | bytes 110592 | tf_op jit(solution)/shard_map/slice | solution.py:170
  49.7 0.2 select_reduce_fusion.1
  49.9 0.6 copy-done.2
  50.6 0.7 copy-done.4
  51.3 13.1 %shard_map.69 = (f32[1,128]{1,0:T(1,128)}, f32[1,128]{1,0:T(1,128)}) custom-call(bf16[128,3456]{1,0:T(8,128)(2,1)} %copy.26.refs_0_, bf16[32,3456]{1,0:T(8,128)(2,1)} %copy-done.1, bf16[32,3456]{1,0:T(8,128)(2,1)} %copy-done.2, bf16[32,3456]{1,0:T(8,128)(2,1)} %copy-done.3, bf16[32,3456]{1,0:T(8,128)(2,1)} %copy-done.4), custom_call_target="tpu_custom_call" | custom-call | tf_op jit(solution)/shard_map/pallas_call | solution.py:62
  64.5 0.7 pad_maximum_fusion.1
  65.2 6.3 %all-reduce.1 = (f32[2,2,128]{2,0,1:T(2,128)S(1)}, f32[4,3456]{1,0:T(4,128)S(1)}, f32[4]{0:T(128)S(1)}) all-reduce(f32[2,2,128]{2,0,1:T(2,128)S(1)} %broadcast_select_fusion, f32[4,3456]{1,0:T(4,128)S(1)} %reshape.103, f32[4]{0:T(128)S(1)} %select_reduce_fusion.1), channel_id=1, replica_groups=mesh['loop'=64,'grp'=2] {'grp'}, use_global_device_ids=true, to_apply=%region_3.4 | all-reduce | flops 14340 | bytes 114720 | tf_op jit(solution)/shard_map/psum | solution.py:179
  71.8 0.5 log_add_fusion
  72.4 0.7 dynamic-slice_divide_fusion
  (47 shorter events, 2.1 us)
Async XLA Ops:
  2.5 0.7 copy-start.8
  3.4 0.7 copy-start.6
  3.4 0.7 copy-start.7
  5.8 12.1 %copy-start.5 = (bf16[2,3456]{1,0:T(2,128)(2,1)S(1)}, bf16[2,3456]{1,0:T(2,128)(2,1)}, u32[]{:S(2)}) copy-start(bf16[2,3456]{1,0:T(2,128)(2,1)} %param.6) | copy-start | bytes 41476
  5.8 38.0 %all-to-all-start = ((bf16[64,2,3584]{2,1,0:T(2,128)(2,1)}), bf16[64,2,3584]{2,1,0:T(2,128)(2,1)S(1)}, u32[]{:S(2)}, u32[]{:S(2)}) async-start(bf16[64,2,3584]{2,1,0:T(2,128)(2,1)} %reshape.100), calls=%async_computation | async-start | bytes 1835008 | tf_op jit(solution)/shard_map/all_to_all | solution.py:150
  18.2 4.8 %collective-permute-start = (bf16[2,3456]{1,0:T(2,128)(2,1)S(1)}, bf16[2,3456]{1,0:T(2,128)(2,1)S(1)}, u32[]{:S(2)}, u32[]{:S(2)}) collective-permute-start(bf16[2,3456]{1,0:T(2,128)(2,1)S(1)} %reshape.105), channel_id=1, source_target_pairs={{0,2},{2,4},{4,6},{6,0},{8,10},{10,12},{12,14},{14,8},{16,18},{18,... | collective-permute-start | bytes 41480 | tf_op jit(solution)/shard_map/ppermute | solution.py:115
  19.3 5.0 %collective-permute-start.1 = (bf16[2,3456]{1,0:T(2,128)(2,1)S(1)}, bf16[2,3456]{1,0:T(2,128)(2,1)S(1)}, u32[]{:S(2)}, u32[]{:S(2)}) collective-permute-start(bf16[2,3456]{1,0:T(2,128)(2,1)S(1)} %reshape.105), channel_id=1, source_target_pairs={{0,4},{2,6},{4,0},{6,2},{8,12},{10,14},{12,8},{14,10},{16,20},{18,... | collective-permute-start | bytes 41480 | tf_op jit(solution)/shard_map/ppermute | solution.py:115
  21.7 5.2 %collective-permute-start.2 = (bf16[2,3456]{1,0:T(2,128)(2,1)S(1)}, bf16[2,3456]{1,0:T(2,128)(2,1)S(1)}, u32[]{:S(2)}, u32[]{:S(2)}) collective-permute-start(bf16[2,3456]{1,0:T(2,128)(2,1)S(1)} %reshape.105), channel_id=1, source_target_pairs={{0,6},{2,0},{4,2},{6,4},{8,14},{10,8},{12,10},{14,12},{16,22},{18,... | collective-permute-start | bytes 41480 | tf_op jit(solution)/shard_map/ppermute | solution.py:115
  27.0 6.9 %collective-permute-start.3 = (bf16[8,3456]{1,0:T(8,128)(2,1)S(1)}, bf16[8,3456]{1,0:T(8,128)(2,1)S(1)}, u32[]{:S(2)}, u32[]{:S(2)}) collective-permute-start(bf16[8,3456]{1,0:T(8,128)(2,1)S(1)} %pad_maximum_fusion), channel_id=1, source_target_pairs={{0,8},{2,10},{4,12},{6,14},{8,16},{10,18},{12,20},{14,22},{16,24},... | collective-permute-start | bytes 165896 | tf_op jit(solution)/shard_map/ppermute | solution.py:115
  27.1 6.8 %collective-permute-start.4 = (bf16[8,3456]{1,0:T(8,128)(2,1)S(1)}, bf16[8,3456]{1,0:T(8,128)(2,1)S(1)}, u32[]{:S(2)}, u32[]{:S(2)}) collective-permute-start(bf16[8,3456]{1,0:T(8,128)(2,1)S(1)} %pad_maximum_fusion), channel_id=1, source_target_pairs={{0,16},{2,18},{4,20},{6,22},{8,24},{10,26},{12,28},{14,30},{16,0},... | collective-permute-start | bytes 165896 | tf_op jit(solution)/shard_map/ppermute | solution.py:115
  29.1 4.8 %collective-permute-start.5 = (bf16[8,3456]{1,0:T(8,128)(2,1)S(1)}, bf16[8,3456]{1,0:T(8,128)(2,1)S(1)}, u32[]{:S(2)}, u32[]{:S(2)}) collective-permute-start(bf16[8,3456]{1,0:T(8,128)(2,1)S(1)} %pad_maximum_fusion), channel_id=1, source_target_pairs={{0,24},{2,26},{4,28},{6,30},{8,0},{10,2},{12,4},{14,6},{16,8},{18,... | collective-permute-start | bytes 165896 | tf_op jit(solution)/shard_map/ppermute | solution.py:115
  34.0 10.1 %copy-start.1 = (bf16[32,3456]{1,0:T(8,128)(2,1)}, bf16[32,3456]{1,0:T(8,128)(2,1)S(1)}, u32[]{:S(2)}) copy-start(bf16[32,3456]{1,0:T(8,128)(2,1)S(1)} %concatenate.12.refs_1_) | copy-start | bytes 663556
  34.0 15.8 %collective-permute-start.6 = (bf16[32,3456]{1,0:T(8,128)(2,1)S(1)}, bf16[32,3456]{1,0:T(8,128)(2,1)S(1)}, u32[]{:S(2)}, u32[]{:S(2)}) collective-permute-start(bf16[32,3456]{1,0:T(8,128)(2,1)S(1)} %concatenate.12.refs_1_), channel_id=1, source_target_pairs={{0,32},{2,34},{4,36},{6,38},{8,40},{10,42},{12,44},{14,46},{16,48}... | collective-permute-start | bytes 663560 | tf_op jit(solution)/shard_map/ppermute | solution.py:115
  37.9 12.0 %collective-permute-start.7 = (bf16[32,3456]{1,0:T(8,128)(2,1)S(1)}, bf16[32,3456]{1,0:T(8,128)(2,1)S(1)}, u32[]{:S(2)}, u32[]{:S(2)}) collective-permute-start(bf16[32,3456]{1,0:T(8,128)(2,1)S(1)} %concatenate.12.refs_1_), channel_id=1, source_target_pairs={{0,64},{2,66},{4,68},{6,70},{8,72},{10,74},{12,76},{14,78},{16,80}... | collective-permute-start | bytes 663560 | tf_op jit(solution)/shard_map/ppermute | solution.py:115
  41.8 8.1 %collective-permute-start.8 = (bf16[32,3456]{1,0:T(8,128)(2,1)S(1)}, bf16[32,3456]{1,0:T(8,128)(2,1)S(1)}, u32[]{:S(2)}, u32[]{:S(2)}) collective-permute-start(bf16[32,3456]{1,0:T(8,128)(2,1)S(1)} %concatenate.12.refs_1_), channel_id=1, source_target_pairs={{0,96},{2,98},{4,100},{6,102},{8,104},{10,106},{12,108},{14,110},{... | collective-permute-start | bytes 663560 | tf_op jit(solution)/shard_map/ppermute | solution.py:115
  44.1 1.0 %copy-start = (bf16[128,3584]{1,0:T(8,128)(2,1)}, bf16[128,3584]{1,0:T(8,128)(2,1)S(1)}, u32[]{:S(2)}) copy-start(bf16[128,3584]{1,0:T(8,128)(2,1)S(1)} %reshape.101.x_ref) | copy-start | bytes 2752516
  49.9 0.7 copy-start.2
  49.9 0.8 %copy-start.3 = (bf16[32,3456]{1,0:T(8,128)(2,1)}, bf16[32,3456]{1,0:T(8,128)(2,1)S(1)}, u32[]{:S(2)}) copy-start(bf16[32,3456]{1,0:T(8,128)(2,1)S(1)} %collective-permute-done.7.refs_3_) | copy-start | bytes 663556
  50.6 0.7 copy-start.4

commit v9 on v8

--- a/solution.py
+++ b/solution.py
@@ -102,7 +102,7 @@
     return factors
 
 
-def staged_gather(rows, axis):
+def staged_gather(rows, axis, held):
     count = lax.axis_size(axis)
     stride = 1
     for factor in ring_factors(count):
@@ -114,8 +114,10 @@
                 pairs.append((source, source + ((digit + step) % factor - digit) * stride))
             parts.append(lax.ppermute(rows, axis, pairs))
         rows = jnp.concatenate(parts, axis=0)
+        if stride == 1:
+            rows, held = lax.optimization_barrier((rows, held))
         stride *= factor
-    return parts
+    return parts, held
 
 
 def local(particles, references, classes, angles, weights):
@@ -123,7 +125,6 @@
     grp_size = lax.axis_size("grp")
     half_rows = row_count // grp_size
     grp_index = lax.axis_index("grp")
-    pieces = staged_gather(angle_major(references), "loop")
     particle_rows = angle_major(particles)
     own_rows = lax.dynamic_slice_in_dim(particle_rows, grp_index * half_rows, half_rows, 0)
     owner_count = lax.axis_size("loop")
@@ -147,6 +148,7 @@
     own_rows = jnp.concatenate([own_rows, labels], axis=1)
     outgoing = jnp.dot(placement, own_rows, preferred_element_type=jnp.float32).astype(jnp.bfloat16)
     outgoing = outgoing.reshape(owner_count, capacity, flat_len + label_lanes)
+    pieces, outgoing = staged_gather(angle_major(references), "loop", outgoing)
     incoming = lax.all_to_all(outgoing, "loop", split_axis=0, concat_axis=0, tiled=True)
     incoming = incoming.reshape(slot_count, flat_len + label_lanes)
     labels_in = incoming[:, flat_len : flat_len + 3]

time: 73.4 us -> 73.3 us (level)
  starting transfers between devices: 29.6 us -> 22.4 us
  waiting for transfers between devices: 6.08 us -> 9.66 us
  blocking collectives: 6.34 us -> 9.4 us
    all_to_all x1, waiting for transfers between devices: 0.01 us -> 9.64 us  [local(): lax.all_to_all(outgoing, 'loop', split_axis=0, concat_axis=0, tiled=True)]
    ppermute x9, waiting for transfers between devices: 6.08 us -> 0.02 us  [staged_gather(): parts.append(lax.ppermute(rows, axis, pairs))]
    all_to_all x1, starting transfers between devices: 12.1 us -> 7.18 us  [local(): lax.all_to_all(outgoing, 'loop', split_axis=0, concat_axis=0, tiled=True)]
    psum x1, blocking collectives: 6.34 us -> 9.4 us  [local(): lax.psum((partial_sums, partial_weight, stats), 'grp')]
    ppermute x9, starting transfers between devices: 17.5 us -> 15.2 us  [staged_gather(): parts.append(lax.ppermute(rows, axis, pairs))]
    unnamed x19 -> x20, local copies, waits for them, and re-layouts: 4.01 us -> 3.86 us
  transfers between devices with their start and end apart: 10 -> 10, of which waited for: 4 -> 1; matrix products, arithmetic and copies ran while one was open for 7% -> 12% of each run, Pallas kernels for 4% -> 4%
where the time goes in v9:
time: 73.3 us; the launch traced here: 72.9 us
  starting transfers between devices  22.4 us (31%)
  Pallas kernels  16.4 us (22%)
  local copies, waits for them, and re-layouts  10.2 us (14%)
  waiting for transfers between devices  9.66 us (13%)
  blocking collectives  9.4 us (13%)
  other arithmetic  3.56 us (5%)
  between operations  0.92 us (1%)
    ppermute x9, starting transfers between devices, staged_gather(): parts.append(lax.ppermute(rows, axis, pairs))  15.2 us
    pallas_call x1, Pallas kernels, score_all(): pl.pallas_call(functools.partial(score_kernel, scale=scale), out_shape=(j...  13.1 us
    all_to_all x1, waiting for transfers between devices, local(): lax.all_to_all(outgoing, 'loop', split_axis=0, concat_axis=0, tiled=True)  9.64 us
    psum x1, blocking collectives, local(): lax.psum((partial_sums, partial_weight, stats), 'grp')  9.4 us
    all_to_all x1, starting transfers between devices, local(): lax.all_to_all(outgoing, 'loop', split_axis=0, concat_axis=0, tiled=True)  7.18 us
    unnamed x20, local copies, waits for them, and re-layouts  3.86 us
    pallas_call x1, Pallas kernels, local(): pl.pallas_call(average_kernel, out_shape=jax.ShapeDtypeStruct((block, fla...  3.27 us
    reshape x4, local copies, waits for them, and re-layouts, angle_major(): rows.reshape(count, RADII, ANGLES).transpose(0, 2, 1)  2.77 us
  transfers between devices with their start and end apart: 10, of which 1 were waited for; matrix products, arithmetic and copies ran while one was open for 12% of the time, Pallas kernels for 4%

profile of v9, /device:TPU:1, one launch (start us, length us, event | category | flops | bytes accessed | tf_op | source)
XLA Modules:
  0.0 72.9 jit_solution(7421964574368592354)
XLA Ops:
  0.6 0.8 %reshape.100 = bf16[2,48,72]{2,1,0:T(8,128)(2,1)S(1)} reshape(bf16[2,3456]{1,0:T(2,128)(2,1)} %param.6) | data formatting | bytes 27648 | tf_op jit(solution)/shard_map/reshape | solution.py:20
  1.7 3.6 %collective-permute-start.2 = (bf16[2,3456]{1,0:T(2,128)(2,1)S(1)}, bf16[2,3456]{1,0:T(2,128)(2,1)S(1)}, u32[]{:S(2)}, u32[]{:S(2)}) collective-permute-start(bf16[2,3456]{1,0:T(2,128)(2,1)S(1)} %reshape.101), channel_id=1, source_target_pairs={{0,6},{2,0},{4,2},{6,4},{8,14},{10,8},{12,10},{14,12},{16,22},{18,... | collective-permute-start | bytes 41480 | tf_op jit(solution)/shard_map/ppermute | solution.py:115
  5.3 0.3 collective-permute-start.1
  5.7 0.7 collective-permute-start
  6.4 1.9 %copy.22 = bf16[128,3456]{0,1:T(8,128)(2,1)S(1)} copy(bf16[128,3456]{1,0:T(8,128)(2,1)} %param.5) | data formatting | bytes 1769472 | tf_op args[0]
  8.4 0.5 copy-done.7
  9.1 0.2 select_reduce_fusion
  9.3 0.3 constant_dynamic-slice_fusion.1
  9.7 0.4 convolution_convert_fusion
  10.1 1.7 %copy.26.refs_0_ = bf16[128,3456]{1,0:T(8,128)(2,1)} copy(bf16[128,3456]{0,1:T(8,128)(2,1)S(1)} %bitcast.28) | data formatting | bytes 1769472 | tf_op jit(solution)/shard_map/reshape | solution.py:20
  11.8 1.3 %reshape.102 = bf16[64,2,3584]{2,1,0:T(2,128)(2,1)} reshape(bf16[128,3584]{1,0:T(8,128)(2,1)S(1)} %convolution_convert_fusion) | data formatting | bytes 1835008 | tf_op jit(solution)/shard_map/reshape | solution.py:150
  13.2 1.7 %collective-permute-start.3 = (bf16[8,3456]{1,0:T(8,128)(2,1)S(1)}, bf16[8,3456]{1,0:T(8,128)(2,1)S(1)}, u32[]{:S(2)}, u32[]{:S(2)}) collective-permute-start(bf16[8,3456]{1,0:T(8,128)(2,1)S(1)} %pad_maximum_fusion), channel_id=1, source_target_pairs={{0,8},{2,10},{4,12},{6,14},{8,16},{10,18},{12,20},{14,22},{16,24},... | collective-permute-start | bytes 165896 | tf_op jit(solution)/shard_map/ppermute | solution.py:115
  14.9 3.3 %collective-permute-start.4 = (bf16[8,3456]{1,0:T(8,128)(2,1)S(1)}, bf16[8,3456]{1,0:T(8,128)(2,1)S(1)}, u32[]{:S(2)}, u32[]{:S(2)}) collective-permute-start(bf16[8,3456]{1,0:T(8,128)(2,1)S(1)} %pad_maximum_fusion), channel_id=1, source_target_pairs={{0,16},{2,18},{4,20},{6,22},{8,24},{10,26},{12,28},{14,30},{16,0},... | collective-permute-start | bytes 165896 | tf_op jit(solution)/shard_map/ppermute | solution.py:115
  18.2 0.7 %collective-permute-start.5 = (bf16[8,3456]{1,0:T(8,128)(2,1)S(1)}, bf16[8,3456]{1,0:T(8,128)(2,1)S(1)}, u32[]{:S(2)}, u32[]{:S(2)}) collective-permute-start(bf16[8,3456]{1,0:T(8,128)(2,1)S(1)} %pad_maximum_fusion), channel_id=1, source_target_pairs={{0,24},{2,26},{4,28},{6,30},{8,0},{10,2},{12,4},{14,6},{16,8},{18,... | collective-permute-start | bytes 165896 | tf_op jit(solution)/shard_map/ppermute | solution.py:115
  18.9 7.2 %all-to-all-start = ((bf16[64,2,3584]{2,1,0:T(2,128)(2,1)}), bf16[64,2,3584]{2,1,0:T(2,128)(2,1)S(1)}, u32[]{:S(2)}, u32[]{:S(2)}) async-start(bf16[64,2,3584]{2,1,0:T(2,128)(2,1)} %reshape.102), calls=%async_computation | async-start | bytes 1835008 | tf_op jit(solution)/shard_map/all_to_all | solution.py:152
  26.2 1.1 %collective-permute-start.6 = (bf16[32,3456]{1,0:T(8,128)(2,1)S(1)}, bf16[32,3456]{1,0:T(8,128)(2,1)S(1)}, u32[]{:S(2)}, u32[]{:S(2)}) collective-permute-start(bf16[32,3456]{1,0:T(8,128)(2,1)S(1)} %constant_dynamic-update-slice_fusion.refs_1_), channel_id=1, source_target_pairs={{0,32},{2,34},{4,36},{6,38},{8,40},{10,42},{12,44},{14,46},{16,48}... | collective-permute-start | bytes 663560 | tf_op jit(solution)/shard_map/ppermute | solution.py:115
  27.3 2.6 %collective-permute-start.7 = (bf16[32,3456]{1,0:T(8,128)(2,1)S(1)}, bf16[32,3456]{1,0:T(8,128)(2,1)S(1)}, u32[]{:S(2)}, u32[]{:S(2)}) collective-permute-start(bf16[32,3456]{1,0:T(8,128)(2,1)S(1)} %constant_dynamic-update-slice_fusion.refs_1_), channel_id=1, source_target_pairs={{0,64},{2,66},{4,68},{6,70},{8,72},{10,74},{12,76},{14,78},{16,80}... | collective-permute-start | bytes 663560 | tf_op jit(solution)/shard_map/ppermute | solution.py:115
  29.9 1.1 %collective-permute-start.8 = (bf16[32,3456]{1,0:T(8,128)(2,1)S(1)}, bf16[32,3456]{1,0:T(8,128)(2,1)S(1)}, u32[]{:S(2)}, u32[]{:S(2)}) collective-permute-start(bf16[32,3456]{1,0:T(8,128)(2,1)S(1)} %constant_dynamic-update-slice_fusion.refs_1_), channel_id=1, source_target_pairs={{0,96},{2,98},{4,100},{6,102},{8,104},{10,106},{12,108},{14,110},{... | collective-permute-start | bytes 663560 | tf_op jit(solution)/shard_map/ppermute | solution.py:115
  31.0 9.6 %all-to-all-done = bf16[64,2,3584]{2,1,0:T(2,128)(2,1)S(1)} async-done(((bf16[64,2,3584]{2,1,0:T(2,128)(2,1)}), bf16[64,2,3584]{2,1,0:T(2,128)(2,1)S(1)}, u32[]{:S(2)}, u32[]{:S(2)}) %all-to-all-start) | async-done | bytes 917536 | tf_op jit(solution)/shard_map/all_to_all | solution.py:152
  40.6 0.3 reshape.103.x_ref
  41.0 0.2 slice_reduce_fusion.2
  41.2 0.7 select_convert_fusion.w_ref
  42.0 3.3 %shard_map.68 = f32[8,3456]{1,0:T(8,128)} custom-call(bf16[576,128]{1,0:T(8,128)(2,1)} %select_convert_fusion.w_ref, bf16[128,3584]{1,0:T(8,128)(2,1)} %copy-done), custom_call_target="tpu_custom_call" | custom-call | tf_op jit(solution)/shard_map/pallas_call | solution.py:167
  45.2 0.9 %slice.37 = f32[4,3456]{1,0:T(4,128)S(1)} slice(f32[8,3456]{1,0:T(8,128)} %shard_map.68), slice={[0:4], [0:3456]} | slice | bytes 110592 | tf_op jit(solution)/shard_map/slice | solution.py:172
  46.5 0.2 select_reduce_fusion.1
  46.7 0.6 copy-done.2
  47.5 0.7 copy-done.4
  48.2 13.1 %shard_map.69 = (f32[1,128]{1,0:T(1,128)}, f32[1,128]{1,0:T(1,128)}) custom-call(bf16[128,3456]{1,0:T(8,128)(2,1)} %copy.26.refs_0_, bf16[32,3456]{1,0:T(8,128)(2,1)} %copy-done.1, bf16[32,3456]{1,0:T(8,128)(2,1)} %copy-done.2, bf16[32,3456]{1,0:T(8,128)(2,1)} %copy-done.3, bf16[32,3456]{1,0:T(8,128)(2,1)} %copy-done.4), custom_call_target="tpu_custom_call" | custom-call | tf_op jit(solution)/shard_map/pallas_call | solution.py:62
  61.3 0.7 pad_maximum_fusion.1
  62.0 9.4 %all-reduce.1 = (f32[2,2,128]{2,0,1:T(2,128)S(1)}, f32[4,3456]{1,0:T(4,128)S(1)}, f32[4]{0:T(128)S(1)}) all-reduce(f32[2,2,128]{2,0,1:T(2,128)S(1)} %broadcast_select_fusion, f32[4,3456]{1,0:T(4,128)S(1)} %reshape.105, f32[4]{0:T(128)S(1)} %select_reduce_fusion.1), channel_id=1, replica_groups=mesh['loop'=64,'grp'=2] {'grp'}, use_global_device_ids=true, to_apply=%region_3.4 | all-reduce | flops 14340 | bytes 114720 | tf_op jit(solution)/shard_map/psum | solution.py:181
  71.6 0.5 log_add_fusion
  72.2 0.7 dynamic-slice_divide_fusion
  (48 shorter events, 1.5 us)
Async XLA Ops:
  1.7 11.4 %collective-permute-start.2 = (bf16[2,3456]{1,0:T(2,128)(2,1)S(1)}, bf16[2,3456]{1,0:T(2,128)(2,1)S(1)}, u32[]{:S(2)}, u32[]{:S(2)}) collective-permute-start(bf16[2,3456]{1,0:T(2,128)(2,1)S(1)} %reshape.101), channel_id=1, source_target_pairs={{0,6},{2,0},{4,2},{6,4},{8,14},{10,8},{12,10},{14,12},{16,22},{18,... | collective-permute-start | bytes 41480 | tf_op jit(solution)/shard_map/ppermute | solution.py:115
  5.3 7.8 %collective-permute-start.1 = (bf16[2,3456]{1,0:T(2,128)(2,1)S(1)}, bf16[2,3456]{1,0:T(2,128)(2,1)S(1)}, u32[]{:S(2)}, u32[]{:S(2)}) collective-permute-start(bf16[2,3456]{1,0:T(2,128)(2,1)S(1)} %reshape.101), channel_id=1, source_target_pairs={{0,4},{2,6},{4,0},{6,2},{8,12},{10,14},{12,8},{14,10},{16,20},{18,... | collective-permute-start | bytes 41480 | tf_op jit(solution)/shard_map/ppermute | solution.py:115
  5.7 7.4 %collective-permute-start = (bf16[2,3456]{1,0:T(2,128)(2,1)S(1)}, bf16[2,3456]{1,0:T(2,128)(2,1)S(1)}, u32[]{:S(2)}, u32[]{:S(2)}) collective-permute-start(bf16[2,3456]{1,0:T(2,128)(2,1)S(1)} %reshape.101), channel_id=1, source_target_pairs={{0,2},{2,4},{4,6},{6,0},{8,10},{10,12},{12,14},{14,8},{16,18},{18,... | collective-permute-start | bytes 41480 | tf_op jit(solution)/shard_map/ppermute | solution.py:115
  8.2 0.7 copy-start.7
  8.3 1.0 %copy-start.5 = (s32[64]{0:T(128)S(1)}, s32[64]{0:T(128)}, u32[]{:S(2)}) copy-start(s32[64]{0:T(128)} %param.9) | copy-start | bytes 772
  8.3 1.0 %copy-start.6 = (s32[64]{0:T(128)S(1)}, s32[64]{0:T(128)}, u32[]{:S(2)}) copy-start(s32[64]{0:T(128)} %param.8) | copy-start | bytes 772
  13.2 12.9 %collective-permute-start.3 = (bf16[8,3456]{1,0:T(8,128)(2,1)S(1)}, bf16[8,3456]{1,0:T(8,128)(2,1)S(1)}, u32[]{:S(2)}, u32[]{:S(2)}) collective-permute-start(bf16[8,3456]{1,0:T(8,128)(2,1)S(1)} %pad_maximum_fusion), channel_id=1, source_target_pairs={{0,8},{2,10},{4,12},{6,14},{8,16},{10,18},{12,20},{14,22},{16,24},... | collective-permute-start | bytes 165896 | tf_op jit(solution)/shard_map/ppermute | solution.py:115
  14.9 11.3 %collective-permute-start.4 = (bf16[8,3456]{1,0:T(8,128)(2,1)S(1)}, bf16[8,3456]{1,0:T(8,128)(2,1)S(1)}, u32[]{:S(2)}, u32[]{:S(2)}) collective-permute-start(bf16[8,3456]{1,0:T(8,128)(2,1)S(1)} %pad_maximum_fusion), channel_id=1, source_target_pairs={{0,16},{2,18},{4,20},{6,22},{8,24},{10,26},{12,28},{14,30},{16,0},... | collective-permute-start | bytes 165896 | tf_op jit(solution)/shard_map/ppermute | solution.py:115
  18.2 8.0 %collective-permute-start.5 = (bf16[8,3456]{1,0:T(8,128)(2,1)S(1)}, bf16[8,3456]{1,0:T(8,128)(2,1)S(1)}, u32[]{:S(2)}, u32[]{:S(2)}) collective-permute-start(bf16[8,3456]{1,0:T(8,128)(2,1)S(1)} %pad_maximum_fusion), channel_id=1, source_target_pairs={{0,24},{2,26},{4,28},{6,30},{8,0},{10,2},{12,4},{14,6},{16,8},{18,... | collective-permute-start | bytes 165896 | tf_op jit(solution)/shard_map/ppermute | solution.py:115
  18.9 21.7 %all-to-all-start = ((bf16[64,2,3584]{2,1,0:T(2,128)(2,1)}), bf16[64,2,3584]{2,1,0:T(2,128)(2,1)S(1)}, u32[]{:S(2)}, u32[]{:S(2)}) async-start(bf16[64,2,3584]{2,1,0:T(2,128)(2,1)} %reshape.102), calls=%async_computation | async-start | bytes 1835008 | tf_op jit(solution)/shard_map/all_to_all | solution.py:152
  26.2 14.8 %copy-start.1 = (bf16[32,3456]{1,0:T(8,128)(2,1)}, bf16[32,3456]{1,0:T(8,128)(2,1)S(1)}, u32[]{:S(2)}) copy-start(bf16[32,3456]{1,0:T(8,128)(2,1)S(1)} %constant_dynamic-update-slice_fusion.refs_1_) | copy-start | bytes 663556
  26.2 20.5 %collective-permute-start.6 = (bf16[32,3456]{1,0:T(8,128)(2,1)S(1)}, bf16[32,3456]{1,0:T(8,128)(2,1)S(1)}, u32[]{:S(2)}, u32[]{:S(2)}) collective-permute-start(bf16[32,3456]{1,0:T(8,128)(2,1)S(1)} %constant_dynamic-update-slice_fusion.refs_1_), channel_id=1, source_target_pairs={{0,32},{2,34},{4,36},{6,38},{8,40},{10,42},{12,44},{14,46},{16,48}... | collective-permute-start | bytes 663560 | tf_op jit(solution)/shard_map/ppermute | solution.py:115
  27.3 19.4 %collective-permute-start.7 = (bf16[32,3456]{1,0:T(8,128)(2,1)S(1)}, bf16[32,3456]{1,0:T(8,128)(2,1)S(1)}, u32[]{:S(2)}, u32[]{:S(2)}) collective-permute-start(bf16[32,3456]{1,0:T(8,128)(2,1)S(1)} %constant_dynamic-update-slice_fusion.refs_1_), channel_id=1, source_target_pairs={{0,64},{2,66},{4,68},{6,70},{8,72},{10,74},{12,76},{14,78},{16,80}... | collective-permute-start | bytes 663560 | tf_op jit(solution)/shard_map/ppermute | solution.py:115
  29.9 16.8 %collective-permute-start.8 = (bf16[32,3456]{1,0:T(8,128)(2,1)S(1)}, bf16[32,3456]{1,0:T(8,128)(2,1)S(1)}, u32[]{:S(2)}, u32[]{:S(2)}) collective-permute-start(bf16[32,3456]{1,0:T(8,128)(2,1)S(1)} %constant_dynamic-update-slice_fusion.refs_1_), channel_id=1, source_target_pairs={{0,96},{2,98},{4,100},{6,102},{8,104},{10,106},{12,108},{14,110},{... | collective-permute-start | bytes 663560 | tf_op jit(solution)/shard_map/ppermute | solution.py:115
  41.0 1.0 %copy-start = (bf16[128,3584]{1,0:T(8,128)(2,1)}, bf16[128,3584]{1,0:T(8,128)(2,1)S(1)}, u32[]{:S(2)}) copy-start(bf16[128,3584]{1,0:T(8,128)(2,1)S(1)} %reshape.103.x_ref) | copy-start | bytes 2752516
  46.7 0.7 copy-start.2
  46.7 0.8 %copy-start.3 = (bf16[32,3456]{1,0:T(8,128)(2,1)}, bf16[32,3456]{1,0:T(8,128)(2,1)S(1)}, u32[]{:S(2)}) copy-start(bf16[32,3456]{1,0:T(8,128)(2,1)S(1)} %collective-permute-done.7.refs_3_) | copy-start | bytes 663556
  47.5 0.7 copy-start.4

commit v10 on v9

--- a/solution.py
+++ b/solution.py
@@ -150,6 +150,8 @@
     outgoing = outgoing.reshape(owner_count, capacity, flat_len + label_lanes)
     pieces, outgoing = staged_gather(angle_major(references), "loop", outgoing)
     incoming = lax.all_to_all(outgoing, "loop", split_axis=0, concat_axis=0, tiled=True)
+    highest, summed = score_all(particle_rows, pieces)
+    incoming, highest, summed = lax.optimization_barrier((incoming, highest, summed))
     incoming = incoming.reshape(slot_count, flat_len + label_lanes)
     labels_in = incoming[:, flat_len : flat_len + 3]
     labels_in = labels_in.astype(jnp.float32)
@@ -173,8 +175,6 @@
     partial_sums = partial_sums.reshape(per_owner, flat_len)
     weighted = (member_grid[:per_owner, None] == member_in[None, :]).astype(jnp.float32) * weight_of[None, :]
     partial_weight = jnp.sum(weighted, axis=1)
-    partial_sums, partial_weight, pieces = lax.optimization_barrier((partial_sums, partial_weight, pieces))
-    highest, summed = score_all(particle_rows, pieces)
     stats = jnp.stack([highest, summed], axis=0)
     slots = jnp.arange(grp_size, dtype=jnp.int32)[:, None, None] == grp_index
     stats = jnp.where(slots, stats[None], 0.0)

time: 73.3 us -> 74 us (level)
  waiting for transfers between devices: 9.66 us -> 13.3 us
  blocking collectives: 9.4 us -> 6.93 us
    ppermute x9, waiting for transfers between devices: 0.02 us -> 13.3 us  [staged_gather(): parts.append(lax.ppermute(rows, axis, pairs))]
    all_to_all x1, waiting for transfers between devices: 9.64 us -> 0.01 us  [local(): lax.all_to_all(outgoing, 'loop', split_axis=0, concat_axis=0, tiled=True)]
    psum x1, blocking collectives: 9.4 us -> 6.93 us  [local(): lax.psum((partial_sums, partial_weight, stats), 'grp')]
    unnamed x20 -> x22, local copies, waits for them, and re-layouts: 3.86 us -> 3.44 us
  transfers between devices with their start and end apart: 10 -> 10, of which waited for: 1 -> 2; matrix products, arithmetic and copies ran while one was open for 12% -> 9% of each run, Pallas kernels for 4% -> 18%
where the time goes in v10:
time: 74 us; the launch traced here: 73.6 us
  starting transfers between devices  22.4 us (30%)
  Pallas kernels  16.4 us (22%)
  waiting for transfers between devices  13.3 us (18%)
  local copies, waits for them, and re-layouts  9.78 us (13%)
  blocking collectives  6.93 us (9%)
  other arithmetic  3.55 us (5%)
  between operations  0.87 us (1%)
    ppermute x9, starting transfers between devices, staged_gather(): parts.append(lax.ppermute(rows, axis, pairs))  15.2 us
    ppermute x9, waiting for transfers between devices, staged_gather(): parts.append(lax.ppermute(rows, axis, pairs))  13.3 us
    pallas_call x1, Pallas kernels, score_all(): pl.pallas_call(functools.partial(score_kernel, scale=scale), out_shape=(j...  13.1 us
    all_to_all x1, starting transfers between devices, local(): lax.all_to_all(outgoing, 'loop', split_axis=0, concat_axis=0, tiled=True)  7.19 us
    psum x1, blocking collectives, local(): lax.psum((partial_sums, partial_weight, stats), 'grp')  6.93 us
    unnamed x22, local copies, waits for them, and re-layouts  3.44 us
    pallas_call x1, Pallas kernels, local(): pl.pallas_call(average_kernel, out_shape=jax.ShapeDtypeStruct((block, fla...  3.3 us
    reshape x4, local copies, waits for them, and re-layouts, angle_major(): rows.reshape(count, RADII, ANGLES).transpose(0, 2, 1)  2.75 us
  transfers between devices with their start and end apart: 10, of which 2 were waited for; matrix products, arithmetic and copies ran while one was open for 9% of the time, Pallas kernels for 18%

profile of v10, /device:TPU:1, one launch (start us, length us, event | category | flops | bytes accessed | tf_op | source)
XLA Modules:
  0.0 73.6 jit_solution(16049833838894696334)
XLA Ops:
  0.6 0.8 %reshape.98 = bf16[2,48,72]{2,1,0:T(8,128)(2,1)S(1)} reshape(bf16[2,3456]{1,0:T(2,128)(2,1)} %param.6) | data formatting | bytes 27648 | tf_op jit(solution)/shard_map/reshape | solution.py:20
  1.7 3.6 %collective-permute-start.2 = (bf16[2,3456]{1,0:T(2,128)(2,1)S(1)}, bf16[2,3456]{1,0:T(2,128)(2,1)S(1)}, u32[]{:S(2)}, u32[]{:S(2)}) collective-permute-start(bf16[2,3456]{1,0:T(2,128)(2,1)S(1)} %reshape.99), channel_id=1, source_target_pairs={{0,6},{2,0},{4,2},{6,4},{8,14},{10,8},{12,10},{14,12},{16,22},{18,... | collective-permute-start | bytes 41480 | tf_op jit(solution)/shard_map/ppermute | solution.py:115
  5.3 0.3 collective-permute-start.1
  5.7 0.7 collective-permute-start
  6.4 0.7 and_select_fusion.1
  7.0 1.9 %copy.23 = bf16[128,3456]{0,1:T(8,128)(2,1)S(1)} copy(bf16[128,3456]{1,0:T(8,128)(2,1)} %param.5) | data formatting | bytes 1769472 | tf_op args[0]
  9.2 0.2 select_reduce_fusion
  9.6 0.3 constant_dynamic-slice_fusion.1
  9.9 0.4 convolution_convert_fusion
  10.3 1.3 %reshape.102 = bf16[64,2,3584]{2,1,0:T(2,128)(2,1)} reshape(bf16[128,3584]{1,0:T(8,128)(2,1)S(1)} %convolution_convert_fusion) | data formatting | bytes 1835008 | tf_op jit(solution)/shard_map/reshape | solution.py:150
  11.7 1.7 %collective-permute-start.3 = (bf16[8,3456]{1,0:T(8,128)(2,1)S(1)}, bf16[8,3456]{1,0:T(8,128)(2,1)S(1)}, u32[]{:S(2)}, u32[]{:S(2)}) collective-permute-start(bf16[8,3456]{1,0:T(8,128)(2,1)S(1)} %pad_maximum_fusion), channel_id=1, source_target_pairs={{0,8},{2,10},{4,12},{6,14},{8,16},{10,18},{12,20},{14,22},{16,24},... | collective-permute-start | bytes 165896 | tf_op jit(solution)/shard_map/ppermute | solution.py:115
  13.4 3.3 %collective-permute-start.4 = (bf16[8,3456]{1,0:T(8,128)(2,1)S(1)}, bf16[8,3456]{1,0:T(8,128)(2,1)S(1)}, u32[]{:S(2)}, u32[]{:S(2)}) collective-permute-start(bf16[8,3456]{1,0:T(8,128)(2,1)S(1)} %pad_maximum_fusion), channel_id=1, source_target_pairs={{0,16},{2,18},{4,20},{6,22},{8,24},{10,26},{12,28},{14,30},{16,0},... | collective-permute-start | bytes 165896 | tf_op jit(solution)/shard_map/ppermute | solution.py:115
  16.7 0.7 collective-permute-start.5
  17.5 7.2 %all-to-all-start = ((bf16[64,2,3584]{2,1,0:T(2,128)(2,1)}), bf16[64,2,3584]{2,1,0:T(2,128)(2,1)S(1)}, u32[]{:S(2)}, u32[]{:S(2)}) async-start(bf16[64,2,3584]{2,1,0:T(2,128)(2,1)} %reshape.102), calls=%async_computation | async-start | bytes 1835008 | tf_op jit(solution)/shard_map/all_to_all | solution.py:152
  24.7 1.1 %collective-permute-start.6 = (bf16[32,3456]{1,0:T(8,128)(2,1)S(1)}, bf16[32,3456]{1,0:T(8,128)(2,1)S(1)}, u32[]{:S(2)}, u32[]{:S(2)}) collective-permute-start(bf16[32,3456]{1,0:T(8,128)(2,1)S(1)} %constant_dynamic-update-slice_fusion.refs_1_), channel_id=1, source_target_pairs={{0,32},{2,34},{4,36},{6,38},{8,40},{10,42},{12,44},{14,46},{16,48}... | collective-permute-start | bytes 663560 | tf_op jit(solution)/shard_map/ppermute | solution.py:115
  25.8 2.6 %collective-permute-start.7 = (bf16[32,3456]{1,0:T(8,128)(2,1)S(1)}, bf16[32,3456]{1,0:T(8,128)(2,1)S(1)}, u32[]{:S(2)}, u32[]{:S(2)}) collective-permute-start(bf16[32,3456]{1,0:T(8,128)(2,1)S(1)} %constant_dynamic-update-slice_fusion.refs_1_), channel_id=1, source_target_pairs={{0,64},{2,66},{4,68},{6,70},{8,72},{10,74},{12,76},{14,78},{16,80}... | collective-permute-start | bytes 663560 | tf_op jit(solution)/shard_map/ppermute | solution.py:115
  28.4 1.1 %collective-permute-start.8 = (bf16[32,3456]{1,0:T(8,128)(2,1)S(1)}, bf16[32,3456]{1,0:T(8,128)(2,1)S(1)}, u32[]{:S(2)}, u32[]{:S(2)}) collective-permute-start(bf16[32,3456]{1,0:T(8,128)(2,1)S(1)} %constant_dynamic-update-slice_fusion.refs_1_), channel_id=1, source_target_pairs={{0,96},{2,98},{4,100},{6,102},{8,104},{10,106},{12,108},{14,110},{... | collective-permute-start | bytes 663560 | tf_op jit(solution)/shard_map/ppermute | solution.py:115
  29.5 1.7 %copy.25.refs_0_ = bf16[128,3456]{1,0:T(8,128)(2,1)} copy(bf16[128,3456]{0,1:T(8,128)(2,1)S(1)} %bitcast.32) | data formatting | bytes 1769472 | tf_op jit(solution)/shard_map/reshape | solution.py:20
  31.2 11.5 %collective-permute-done.6.refs_2_ = bf16[32,3456]{1,0:T(8,128)(2,1)S(1)} collective-permute-done((bf16[32,3456]{1,0:T(8,128)(2,1)S(1)}, bf16[32,3456]{1,0:T(8,128)(2,1)S(1)}, u32[]{:S(2)}, u32[]{:S(2)}) %collective-permute-start.6) | collective-permute-done | bytes 221216 | tf_op jit(solution)/shard_map/ppermute | solution.py:115
  42.7 1.8 %collective-permute-done.7.refs_3_ = bf16[32,3456]{1,0:T(8,128)(2,1)S(1)} collective-permute-done((bf16[32,3456]{1,0:T(8,128)(2,1)S(1)}, bf16[32,3456]{1,0:T(8,128)(2,1)S(1)}, u32[]{:S(2)}, u32[]{:S(2)}) %collective-permute-start.7) | collective-permute-done | bytes 221216 | tf_op jit(solution)/shard_map/ppermute | solution.py:115
  44.5 0.7 copy-done.3
  45.2 0.7 copy-done.4
  45.9 13.1 %shard_map.68 = (f32[1,128]{1,0:T(1,128)}, f32[1,128]{1,0:T(1,128)}) custom-call(bf16[128,3456]{1,0:T(8,128)(2,1)} %copy.25.refs_0_, bf16[32,3456]{1,0:T(8,128)(2,1)} %copy-done.1, bf16[32,3456]{1,0:T(8,128)(2,1)} %copy-done.2, bf16[32,3456]{1,0:T(8,128)(2,1)} %copy-done.3, bf16[32,3456]{1,0:T(8,128)(2,1)} %copy-done.4), custom_call_target="tpu_custom_call" | custom-call | tf_op jit(solution)/shard_map/pallas_call | solution.py:62
  59.0 0.3 reshape.103.x_ref
  59.4 0.2 slice_reduce_fusion.2
  59.6 0.7 select_convert_fusion.w_ref
  60.4 3.3 %shard_map.69 = f32[8,3456]{1,0:T(8,128)} custom-call(bf16[576,128]{1,0:T(8,128)(2,1)} %select_convert_fusion.w_ref, bf16[128,3584]{1,0:T(8,128)(2,1)} %copy-done), custom_call_target="tpu_custom_call" | custom-call | tf_op jit(solution)/shard_map/pallas_call | solution.py:169
  63.7 0.9 %slice.37 = f32[4,3456]{1,0:T(4,128)S(1)} slice(f32[8,3456]{1,0:T(8,128)} %shard_map.69), slice={[0:4], [0:3456]} | slice | bytes 110592 | tf_op jit(solution)/shard_map/slice | solution.py:174
  64.9 0.2 select_reduce_fusion.1
  65.2 6.9 %all-reduce.1 = (f32[2,2,128]{2,0,1:T(2,128)S(1)}, f32[4,3456]{1,0:T(4,128)S(1)}, f32[4]{0:T(128)S(1)}) all-reduce(f32[2,2,128]{2,0,1:T(2,128)S(1)} %broadcast_select_fusion, f32[4,3456]{1,0:T(4,128)S(1)} %reshape.105, f32[4]{0:T(128)S(1)} %select_reduce_fusion.1), channel_id=1, replica_groups=mesh['loop'=64,'grp'=2] {'grp'}, use_global_device_ids=true, to_apply=%region_2.3 | all-reduce | flops 14340 | bytes 114720 | tf_op jit(solution)/shard_map/psum | solution.py:181
  72.3 0.5 log_add_fusion
  72.9 0.7 dynamic-slice_divide_fusion
  (50 shorter events, 1.6 us)
Async XLA Ops:
  1.7 9.9 %collective-permute-start.2 = (bf16[2,3456]{1,0:T(2,128)(2,1)S(1)}, bf16[2,3456]{1,0:T(2,128)(2,1)S(1)}, u32[]{:S(2)}, u32[]{:S(2)}) collective-permute-start(bf16[2,3456]{1,0:T(2,128)(2,1)S(1)} %reshape.99), channel_id=1, source_target_pairs={{0,6},{2,0},{4,2},{6,4},{8,14},{10,8},{12,10},{14,12},{16,22},{18,... | collective-permute-start | bytes 41480 | tf_op jit(solution)/shard_map/ppermute | solution.py:115
  5.3 6.3 %collective-permute-start.1 = (bf16[2,3456]{1,0:T(2,128)(2,1)S(1)}, bf16[2,3456]{1,0:T(2,128)(2,1)S(1)}, u32[]{:S(2)}, u32[]{:S(2)}) collective-permute-start(bf16[2,3456]{1,0:T(2,128)(2,1)S(1)} %reshape.99), channel_id=1, source_target_pairs={{0,4},{2,6},{4,0},{6,2},{8,12},{10,14},{12,8},{14,10},{16,20},{18,... | collective-permute-start | bytes 41480 | tf_op jit(solution)/shard_map/ppermute | solution.py:115
  5.7 6.0 %collective-permute-start = (bf16[2,3456]{1,0:T(2,128)(2,1)S(1)}, bf16[2,3456]{1,0:T(2,128)(2,1)S(1)}, u32[]{:S(2)}, u32[]{:S(2)}) collective-permute-start(bf16[2,3456]{1,0:T(2,128)(2,1)S(1)} %reshape.99), channel_id=1, source_target_pairs={{0,2},{2,4},{4,6},{6,0},{8,10},{10,12},{12,14},{14,8},{16,18},{18,... | collective-permute-start | bytes 41480 | tf_op jit(solution)/shard_map/ppermute | solution.py:115
  8.9 0.7 copy-start.5
  8.9 0.7 copy-start.6
  11.7 12.9 %collective-permute-start.3 = (bf16[8,3456]{1,0:T(8,128)(2,1)S(1)}, bf16[8,3456]{1,0:T(8,128)(2,1)S(1)}, u32[]{:S(2)}, u32[]{:S(2)}) collective-permute-start(bf16[8,3456]{1,0:T(8,128)(2,1)S(1)} %pad_maximum_fusion), channel_id=1, source_target_pairs={{0,8},{2,10},{4,12},{6,14},{8,16},{10,18},{12,20},{14,22},{16,24},... | collective-permute-start | bytes 165896 | tf_op jit(solution)/shard_map/ppermute | solution.py:115
  13.4 11.3 %collective-permute-start.4 = (bf16[8,3456]{1,0:T(8,128)(2,1)S(1)}, bf16[8,3456]{1,0:T(8,128)(2,1)S(1)}, u32[]{:S(2)}, u32[]{:S(2)}) collective-permute-start(bf16[8,3456]{1,0:T(8,128)(2,1)S(1)} %pad_maximum_fusion), channel_id=1, source_target_pairs={{0,16},{2,18},{4,20},{6,22},{8,24},{10,26},{12,28},{14,30},{16,0},... | collective-permute-start | bytes 165896 | tf_op jit(solution)/shard_map/ppermute | solution.py:115
  16.7 8.0 %collective-permute-start.5 = (bf16[8,3456]{1,0:T(8,128)(2,1)S(1)}, bf16[8,3456]{1,0:T(8,128)(2,1)S(1)}, u32[]{:S(2)}, u32[]{:S(2)}) collective-permute-start(bf16[8,3456]{1,0:T(8,128)(2,1)S(1)} %pad_maximum_fusion), channel_id=1, source_target_pairs={{0,24},{2,26},{4,28},{6,30},{8,0},{10,2},{12,4},{14,6},{16,8},{18,... | collective-permute-start | bytes 165896 | tf_op jit(solution)/shard_map/ppermute | solution.py:115
  17.5 41.5 %all-to-all-start = ((bf16[64,2,3584]{2,1,0:T(2,128)(2,1)}), bf16[64,2,3584]{2,1,0:T(2,128)(2,1)S(1)}, u32[]{:S(2)}, u32[]{:S(2)}) async-start(bf16[64,2,3584]{2,1,0:T(2,128)(2,1)} %reshape.102), calls=%async_computation | async-start | bytes 1835008 | tf_op jit(solution)/shard_map/all_to_all | solution.py:152
  24.7 19.8 %copy-start.1 = (bf16[32,3456]{1,0:T(8,128)(2,1)}, bf16[32,3456]{1,0:T(8,128)(2,1)S(1)}, u32[]{:S(2)}) copy-start(bf16[32,3456]{1,0:T(8,128)(2,1)S(1)} %constant_dynamic-update-slice_fusion.refs_1_) | copy-start | bytes 663556
  24.7 18.0 %collective-permute-start.6 = (bf16[32,3456]{1,0:T(8,128)(2,1)S(1)}, bf16[32,3456]{1,0:T(8,128)(2,1)S(1)}, u32[]{:S(2)}, u32[]{:S(2)}) collective-permute-start(bf16[32,3456]{1,0:T(8,128)(2,1)S(1)} %constant_dynamic-update-slice_fusion.refs_1_), channel_id=1, source_target_pairs={{0,32},{2,34},{4,36},{6,38},{8,40},{10,42},{12,44},{14,46},{16,48}... | collective-permute-start | bytes 663560 | tf_op jit(solution)/shard_map/ppermute | solution.py:115
  25.8 18.7 %collective-permute-start.7 = (bf16[32,3456]{1,0:T(8,128)(2,1)S(1)}, bf16[32,3456]{1,0:T(8,128)(2,1)S(1)}, u32[]{:S(2)}, u32[]{:S(2)}) collective-permute-start(bf16[32,3456]{1,0:T(8,128)(2,1)S(1)} %constant_dynamic-update-slice_fusion.refs_1_), channel_id=1, source_target_pairs={{0,64},{2,66},{4,68},{6,70},{8,72},{10,74},{12,76},{14,78},{16,80}... | collective-permute-start | bytes 663560 | tf_op jit(solution)/shard_map/ppermute | solution.py:115
  28.4 16.1 %collective-permute-start.8 = (bf16[32,3456]{1,0:T(8,128)(2,1)S(1)}, bf16[32,3456]{1,0:T(8,128)(2,1)S(1)}, u32[]{:S(2)}, u32[]{:S(2)}) collective-permute-start(bf16[32,3456]{1,0:T(8,128)(2,1)S(1)} %constant_dynamic-update-slice_fusion.refs_1_), channel_id=1, source_target_pairs={{0,96},{2,98},{4,100},{6,102},{8,104},{10,106},{12,108},{14,110},{... | collective-permute-start | bytes 663560 | tf_op jit(solution)/shard_map/ppermute | solution.py:115
  42.7 1.8 %copy-start.2 = (bf16[32,3456]{1,0:T(8,128)(2,1)}, bf16[32,3456]{1,0:T(8,128)(2,1)S(1)}, u32[]{:S(2)}) copy-start(bf16[32,3456]{1,0:T(8,128)(2,1)S(1)} %collective-permute-done.6.refs_2_) | copy-start | bytes 663556
  44.5 0.7 copy-start.3
  45.2 0.7 copy-start.4
  59.4 1.0 %copy-start = (bf16[128,3584]{1,0:T(8,128)(2,1)}, bf16[128,3584]{1,0:T(8,128)(2,1)S(1)}, u32[]{:S(2)}) copy-start(bf16[128,3584]{1,0:T(8,128)(2,1)S(1)} %reshape.103.x_ref) | copy-start | bytes 2752516
  60.4 4.8 %copy-start.7 = (f32[1,128]{1,0:T(1,128)S(1)}, f32[1,128]{1,0:T(1,128)}, u32[]{:S(2)}) copy-start(f32[1,128]{1,0:T(1,128)} %get-tuple-element.11) | copy-start | bytes 1540
  60.4 4.8 %copy-start.8 = (f32[1,128]{1,0:T(1,128)S(1)}, f32[1,128]{1,0:T(1,128)}, u32[]{:S(2)}) copy-start(f32[1,128]{1,0:T(1,128)} %get-tuple-element.12) | copy-start | bytes 1540

commit v11 on v10

--- a/solution.py
+++ b/solution.py
@@ -105,7 +105,8 @@
 def staged_gather(rows, axis, held):
     count = lax.axis_size(axis)
     stride = 1
-    for factor in ring_factors(count):
+    factors = ring_factors(count)
+    for round_index, factor in enumerate(factors):
         parts = [rows]
         for step in range(1, factor):
             pairs = []
@@ -114,8 +115,8 @@
                 pairs.append((source, source + ((digit + step) % factor - digit) * stride))
             parts.append(lax.ppermute(rows, axis, pairs))
         rows = jnp.concatenate(parts, axis=0)
-        if stride == 1:
-            rows, held = lax.optimization_barrier((rows, held))
+        if round_index == len(factors) - 1:
+            parts, held = lax.optimization_barrier((parts, held))
         stride *= factor
     return parts, held
 

time: 74 us -> 67.7 us (0.915)
  waiting for transfers between devices: 13.3 us -> 7.85 us
    ppermute x9, waiting for transfers between devices: 13.3 us -> 7.85 us  [staged_gather(): parts.append(lax.ppermute(rows, axis, pairs))]
    ppermute x9, starting transfers between devices: 15.2 us -> 16.5 us  [staged_gather(): parts.append(lax.ppermute(rows, axis, pairs))]
    all_to_all x1, starting transfers between devices: 7.19 us -> 6 us  [local(): lax.all_to_all(outgoing, 'loop', split_axis=0, concat_axis=0, tiled=True)]
    unnamed x22 -> x19, local copies, waits for them, and re-layouts: 3.44 us -> 3.27 us
  transfers between devices with their start and end apart: 10 -> 10, of which waited for: 2 -> 3; matrix products, arithmetic and copies ran while one was open for 9% -> 9% of each run, Pallas kernels for 18% -> 19%
where the time goes in v11:
time: 67.7 us; the launch traced here: 67.4 us
  starting transfers between devices  22.5 us (33%)
  Pallas kernels  16.4 us (24%)
  local copies, waits for them, and re-layouts  9.76 us (14%)
  waiting for transfers between devices  7.85 us (12%)
  blocking collectives  6.66 us (10%)
  other arithmetic  2.88 us (4%)
  between operations  0.87 us (1%)
    ppermute x9, starting transfers between devices, staged_gather(): parts.append(lax.ppermute(rows, axis, pairs))  16.5 us
    pallas_call x1, Pallas kernels, score_all(): pl.pallas_call(functools.partial(score_kernel, scale=scale), out_shape=(j...  13.1 us
    ppermute x9, waiting for transfers between devices, staged_gather(): parts.append(lax.ppermute(rows, axis, pairs))  7.85 us
    psum x1, blocking collectives, local(): lax.psum((partial_sums, partial_weight, stats), 'grp')  6.66 us
    all_to_all x1, starting transfers between devices, local(): lax.all_to_all(outgoing, 'loop', split_axis=0, concat_axis=0, tiled=True)  6 us
    pallas_call x1, Pallas kernels, local(): pl.pallas_call(average_kernel, out_shape=jax.ShapeDtypeStruct((block, fla...  3.29 us
    unnamed x19, local copies, waits for them, and re-layouts  3.27 us
    reshape x4, local copies, waits for them, and re-layouts, angle_major(): rows.reshape(count, RADII, ANGLES).transpose(0, 2, 1)  2.77 us
  transfers between devices with their start and end apart: 10, of which 3 were waited for; matrix products, arithmetic and copies ran while one was open for 9% of the time, Pallas kernels for 19%

profile of v11, /device:TPU:1, one launch (start us, length us, event | category | flops | bytes accessed | tf_op | source)
XLA Modules:
  0.0 67.4 jit_solution(9484979517742896009)
XLA Ops:
  0.6 0.8 %reshape.98 = bf16[2,48,72]{2,1,0:T(8,128)(2,1)S(1)} reshape(bf16[2,3456]{1,0:T(2,128)(2,1)} %param.6) | data formatting | bytes 27648 | tf_op jit(solution)/shard_map/reshape | solution.py:20
  1.7 2.2 %collective-permute-start = (bf16[2,3456]{1,0:T(2,128)(2,1)S(1)}, bf16[2,3456]{1,0:T(2,128)(2,1)S(1)}, u32[]{:S(2)}, u32[]{:S(2)}) collective-permute-start(bf16[2,3456]{1,0:T(2,128)(2,1)S(1)} %reshape.99), channel_id=1, source_target_pairs={{0,2},{2,4},{4,6},{6,0},{8,10},{10,12},{12,14},{14,8},{16,18},{18,... | collective-permute-start | bytes 41480 | tf_op jit(solution)/shard_map/ppermute | solution.py:116
  3.9 2.6 %collective-permute-start.1 = (bf16[2,3456]{1,0:T(2,128)(2,1)S(1)}, bf16[2,3456]{1,0:T(2,128)(2,1)S(1)}, u32[]{:S(2)}, u32[]{:S(2)}) collective-permute-start(bf16[2,3456]{1,0:T(2,128)(2,1)S(1)} %reshape.99), channel_id=1, source_target_pairs={{0,4},{2,6},{4,0},{6,2},{8,12},{10,14},{12,8},{14,10},{16,20},{18,... | collective-permute-start | bytes 41480 | tf_op jit(solution)/shard_map/ppermute | solution.py:116
  6.5 1.1 %collective-permute-start.2 = (bf16[2,3456]{1,0:T(2,128)(2,1)S(1)}, bf16[2,3456]{1,0:T(2,128)(2,1)S(1)}, u32[]{:S(2)}, u32[]{:S(2)}) collective-permute-start(bf16[2,3456]{1,0:T(2,128)(2,1)S(1)} %reshape.99), channel_id=1, source_target_pairs={{0,6},{2,0},{4,2},{6,4},{8,14},{10,8},{12,10},{14,12},{16,22},{18,... | collective-permute-start | bytes 41480 | tf_op jit(solution)/shard_map/ppermute | solution.py:116
  7.6 1.9 %copy.23 = bf16[128,3456]{0,1:T(8,128)(2,1)S(1)} copy(bf16[128,3456]{1,0:T(8,128)(2,1)} %param.5) | data formatting | bytes 1769472 | tf_op args[0]
  9.6 0.5 copy-done.8
  10.3 0.2 select_reduce_fusion
  10.5 0.3 constant_dynamic-slice_fusion.1
  11.1 1.7 %collective-permute-start.3 = (bf16[8,3456]{1,0:T(8,128)(2,1)S(1)}, bf16[8,3456]{1,0:T(8,128)(2,1)S(1)}, u32[]{:S(2)}, u32[]{:S(2)}) collective-permute-start(bf16[8,3456]{1,0:T(8,128)(2,1)S(1)} %pad_maximum_fusion), channel_id=1, source_target_pairs={{0,8},{2,10},{4,12},{6,14},{8,16},{10,18},{12,20},{14,22},{16,24},... | collective-permute-start | bytes 165896 | tf_op jit(solution)/shard_map/ppermute | solution.py:116
  12.8 3.3 %collective-permute-start.4 = (bf16[8,3456]{1,0:T(8,128)(2,1)S(1)}, bf16[8,3456]{1,0:T(8,128)(2,1)S(1)}, u32[]{:S(2)}, u32[]{:S(2)}) collective-permute-start(bf16[8,3456]{1,0:T(8,128)(2,1)S(1)} %pad_maximum_fusion), channel_id=1, source_target_pairs={{0,16},{2,18},{4,20},{6,22},{8,24},{10,26},{12,28},{14,30},{16,0},... | collective-permute-start | bytes 165896 | tf_op jit(solution)/shard_map/ppermute | solution.py:116
  16.1 0.7 %collective-permute-start.5 = (bf16[8,3456]{1,0:T(8,128)(2,1)S(1)}, bf16[8,3456]{1,0:T(8,128)(2,1)S(1)}, u32[]{:S(2)}, u32[]{:S(2)}) collective-permute-start(bf16[8,3456]{1,0:T(8,128)(2,1)S(1)} %pad_maximum_fusion), channel_id=1, source_target_pairs={{0,24},{2,26},{4,28},{6,30},{8,0},{10,2},{12,4},{14,6},{16,8},{18,... | collective-permute-start | bytes 165896 | tf_op jit(solution)/shard_map/ppermute | solution.py:116
  16.9 1.5 %collective-permute-done.4 = bf16[8,3456]{1,0:T(8,128)(2,1)S(1)} collective-permute-done((bf16[8,3456]{1,0:T(8,128)(2,1)S(1)}, bf16[8,3456]{1,0:T(8,128)(2,1)S(1)}, u32[]{:S(2)}, u32[]{:S(2)}) %collective-permute-start.4) | collective-permute-done | bytes 55328 | tf_op jit(solution)/shard_map/ppermute | solution.py:116
  18.3 1.7 %collective-permute-done.5 = bf16[8,3456]{1,0:T(8,128)(2,1)S(1)} collective-permute-done((bf16[8,3456]{1,0:T(8,128)(2,1)S(1)}, bf16[8,3456]{1,0:T(8,128)(2,1)S(1)}, u32[]{:S(2)}, u32[]{:S(2)}) %collective-permute-start.5) | collective-permute-done | bytes 55328 | tf_op jit(solution)/shard_map/ppermute | solution.py:116
  20.1 1.3 %collective-permute-start.6 = (bf16[32,3456]{1,0:T(8,128)(2,1)S(1)}, bf16[32,3456]{1,0:T(8,128)(2,1)S(1)}, u32[]{:S(2)}, u32[]{:S(2)}) collective-permute-start(bf16[32,3456]{1,0:T(8,128)(2,1)S(1)} %concatenate.11.refs_1_), channel_id=1, source_target_pairs={{0,32},{2,34},{4,36},{6,38},{8,40},{10,42},{12,44},{14,46},{16,48}... | collective-permute-start | bytes 663560 | tf_op jit(solution)/shard_map/ppermute | solution.py:116
  21.4 2.5 %collective-permute-start.7 = (bf16[32,3456]{1,0:T(8,128)(2,1)S(1)}, bf16[32,3456]{1,0:T(8,128)(2,1)S(1)}, u32[]{:S(2)}, u32[]{:S(2)}) collective-permute-start(bf16[32,3456]{1,0:T(8,128)(2,1)S(1)} %concatenate.11.refs_1_), channel_id=1, source_target_pairs={{0,64},{2,66},{4,68},{6,70},{8,72},{10,74},{12,76},{14,78},{16,80}... | collective-permute-start | bytes 663560 | tf_op jit(solution)/shard_map/ppermute | solution.py:116
  23.9 1.2 %collective-permute-start.8 = (bf16[32,3456]{1,0:T(8,128)(2,1)S(1)}, bf16[32,3456]{1,0:T(8,128)(2,1)}, u32[]{:S(2)}, u32[]{:S(2)}) collective-permute-start(bf16[32,3456]{1,0:T(8,128)(2,1)S(1)} %concatenate.11.refs_1_), channel_id=1, source_target_pairs={{0,96},{2,98},{4,100},{6,102},{8,104},{10,106},{12,108},{14,110},{... | collective-permute-start | bytes 663560 | tf_op jit(solution)/shard_map/ppermute | solution.py:116
  25.0 0.4 convolution_convert_fusion
  25.4 1.3 %reshape.102 = bf16[64,2,3584]{2,1,0:T(2,128)(2,1)} reshape(bf16[128,3584]{1,0:T(8,128)(2,1)S(1)} %convolution_convert_fusion) | data formatting | bytes 1835008 | tf_op jit(solution)/shard_map/reshape | solution.py:151
  26.7 4.7 %collective-permute-done.7.refs_3_ = bf16[32,3456]{1,0:T(8,128)(2,1)S(1)} collective-permute-done((bf16[32,3456]{1,0:T(8,128)(2,1)S(1)}, bf16[32,3456]{1,0:T(8,128)(2,1)S(1)}, u32[]{:S(2)}, u32[]{:S(2)}) %collective-permute-start.7) | collective-permute-done | bytes 221216 | tf_op jit(solution)/shard_map/ppermute | solution.py:116
  31.4 0.7 %copy-done.3 = bf16[32,3456]{1,0:T(8,128)(2,1)} copy-done((bf16[32,3456]{1,0:T(8,128)(2,1)}, bf16[32,3456]{1,0:T(8,128)(2,1)S(1)}, u32[]{:S(2)}) %copy-start.3) | copy-done | bytes 221208
  32.1 6.0 %all-to-all-start = ((bf16[64,2,3584]{2,1,0:T(2,128)(2,1)}), bf16[64,2,3584]{2,1,0:T(2,128)(2,1)S(1)}, u32[]{:S(2)}, u32[]{:S(2)}) async-start(bf16[64,2,3584]{2,1,0:T(2,128)(2,1)} %reshape.102), calls=%async_computation | async-start | bytes 1835008 | tf_op jit(solution)/shard_map/all_to_all | solution.py:153
  38.1 1.7 %copy.25.refs_0_ = bf16[128,3456]{1,0:T(8,128)(2,1)} copy(bf16[128,3456]{0,1:T(8,128)(2,1)S(1)} %bitcast.32) | data formatting | bytes 1769472 | tf_op jit(solution)/shard_map/reshape | solution.py:20
  39.9 13.1 %shard_map.68 = (f32[1,128]{1,0:T(1,128)}, f32[1,128]{1,0:T(1,128)}) custom-call(bf16[128,3456]{1,0:T(8,128)(2,1)} %copy.25.refs_0_, bf16[32,3456]{1,0:T(8,128)(2,1)} %copy-done.1, bf16[32,3456]{1,0:T(8,128)(2,1)} %copy-done.2, bf16[32,3456]{1,0:T(8,128)(2,1)} %copy-done.3, bf16[32,3456]{1,0:T(8,128)(2,1)} %collective-permute-done.8.refs_4_), custom_call_target="tpu_custom_call" | custom-call | tf_op jit(solution)/shard_map/pallas_call | solution.py:62
  53.0 0.3 reshape.103.x_ref
  53.4 0.2 slice_reduce_fusion.2
  53.6 0.2 select_reduce_fusion.1
  53.8 0.7 %select_convert_fusion.w_ref = bf16[576,128]{1,0:T(8,128)(2,1)} fusion(f32[128]{0:T(128)S(1)} %get-tuple-element.23, pred[8,128]{1,0:T(8,128)(4,1)S(1)} %iota_compare_fusion.5, pred[72,128]{1,0:T(8,128)(4,1)S(1)} %iota_compare_fusion.3), kind=kLoop, calls=%fused_computation.4 | loop fusion | flops 147456 | bytes 158208 | tf_op jit(solution)/shard_map/convert_element_type | solution.py:168
  54.5 3.3 %shard_map.69 = f32[8,3456]{1,0:T(8,128)} custom-call(bf16[576,128]{1,0:T(8,128)(2,1)} %select_convert_fusion.w_ref, bf16[128,3584]{1,0:T(8,128)(2,1)} %copy-done), custom_call_target="tpu_custom_call" | custom-call | tf_op jit(solution)/shard_map/pallas_call | solution.py:170
  57.8 0.9 %slice.37 = f32[4,3456]{1,0:T(4,128)S(1)} slice(f32[8,3456]{1,0:T(8,128)} %shard_map.69), slice={[0:4], [0:3456]} | slice | bytes 110592 | tf_op jit(solution)/shard_map/slice | solution.py:175
  59.2 6.7 %all-reduce.1 = (f32[2,2,128]{2,0,1:T(2,128)S(1)}, f32[4,3456]{1,0:T(4,128)S(1)}, f32[4]{0:T(128)S(1)}) all-reduce(f32[2,2,128]{2,0,1:T(2,128)S(1)} %broadcast_select_fusion, f32[4,3456]{1,0:T(4,128)S(1)} %reshape.105, f32[4]{0:T(128)S(1)} %select_reduce_fusion.1), channel_id=1, replica_groups=mesh['loop'=64,'grp'=2] {'grp'}, use_global_device_ids=true, to_apply=%region_2.3 | all-reduce | flops 14340 | bytes 114720 | tf_op jit(solution)/shard_map/psum | solution.py:182
  66.1 0.5 log_add_fusion
  66.7 0.7 %dynamic-slice_divide_fusion = f32[2,3456]{1,0:T(2,128)} fusion(f32[4,3456]{1,0:T(4,128)S(1)} %get-tuple-element.26, s32[]{:T(128)S(6)} %select_n.34, f32[2]{0:T(128)S(1)} %dynamic_slice.15), kind=kLoop, calls=%fused_computation.22 | loop fusion | flops 6912 | bytes 55308 | tf_op jit(solution)/shard_map/div | solution.py:185
  (47 shorter events, 1.7 us)
Async XLA Ops:
  1.7 9.3 %collective-permute-start = (bf16[2,3456]{1,0:T(2,128)(2,1)S(1)}, bf16[2,3456]{1,0:T(2,128)(2,1)S(1)}, u32[]{:S(2)}, u32[]{:S(2)}) collective-permute-start(bf16[2,3456]{1,0:T(2,128)(2,1)S(1)} %reshape.99), channel_id=1, source_target_pairs={{0,2},{2,4},{4,6},{6,0},{8,10},{10,12},{12,14},{14,8},{16,18},{18,... | collective-permute-start | bytes 41480 | tf_op jit(solution)/shard_map/ppermute | solution.py:116
  3.9 7.1 %collective-permute-start.1 = (bf16[2,3456]{1,0:T(2,128)(2,1)S(1)}, bf16[2,3456]{1,0:T(2,128)(2,1)S(1)}, u32[]{:S(2)}, u32[]{:S(2)}) collective-permute-start(bf16[2,3456]{1,0:T(2,128)(2,1)S(1)} %reshape.99), channel_id=1, source_target_pairs={{0,4},{2,6},{4,0},{6,2},{8,12},{10,14},{12,8},{14,10},{16,20},{18,... | collective-permute-start | bytes 41480 | tf_op jit(solution)/shard_map/ppermute | solution.py:116
  6.5 4.5 %collective-permute-start.2 = (bf16[2,3456]{1,0:T(2,128)(2,1)S(1)}, bf16[2,3456]{1,0:T(2,128)(2,1)S(1)}, u32[]{:S(2)}, u32[]{:S(2)}) collective-permute-start(bf16[2,3456]{1,0:T(2,128)(2,1)S(1)} %reshape.99), channel_id=1, source_target_pairs={{0,6},{2,0},{4,2},{6,4},{8,14},{10,8},{12,10},{14,12},{16,22},{18,... | collective-permute-start | bytes 41480 | tf_op jit(solution)/shard_map/ppermute | solution.py:116
  9.5 0.7 copy-start.8
  10.3 0.7 copy-start.4
  10.3 0.7 copy-start.5
  11.1 5.8 %collective-permute-start.3 = (bf16[8,3456]{1,0:T(8,128)(2,1)S(1)}, bf16[8,3456]{1,0:T(8,128)(2,1)S(1)}, u32[]{:S(2)}, u32[]{:S(2)}) collective-permute-start(bf16[8,3456]{1,0:T(8,128)(2,1)S(1)} %pad_maximum_fusion), channel_id=1, source_target_pairs={{0,8},{2,10},{4,12},{6,14},{8,16},{10,18},{12,20},{14,22},{16,24},... | collective-permute-start | bytes 165896 | tf_op jit(solution)/shard_map/ppermute | solution.py:116
  12.8 5.5 %collective-permute-start.4 = (bf16[8,3456]{1,0:T(8,128)(2,1)S(1)}, bf16[8,3456]{1,0:T(8,128)(2,1)S(1)}, u32[]{:S(2)}, u32[]{:S(2)}) collective-permute-start(bf16[8,3456]{1,0:T(8,128)(2,1)S(1)} %pad_maximum_fusion), channel_id=1, source_target_pairs={{0,16},{2,18},{4,20},{6,22},{8,24},{10,26},{12,28},{14,30},{16,0},... | collective-permute-start | bytes 165896 | tf_op jit(solution)/shard_map/ppermute | solution.py:116
  16.1 3.9 %collective-permute-start.5 = (bf16[8,3456]{1,0:T(8,128)(2,1)S(1)}, bf16[8,3456]{1,0:T(8,128)(2,1)S(1)}, u32[]{:S(2)}, u32[]{:S(2)}) collective-permute-start(bf16[8,3456]{1,0:T(8,128)(2,1)S(1)} %pad_maximum_fusion), channel_id=1, source_target_pairs={{0,24},{2,26},{4,28},{6,30},{8,0},{10,2},{12,4},{14,6},{16,8},{18,... | collective-permute-start | bytes 165896 | tf_op jit(solution)/shard_map/ppermute | solution.py:116
  20.1 5.3 %copy-start.1 = (bf16[32,3456]{1,0:T(8,128)(2,1)}, bf16[32,3456]{1,0:T(8,128)(2,1)S(1)}, u32[]{:S(2)}) copy-start(bf16[32,3456]{1,0:T(8,128)(2,1)S(1)} %concatenate.11.refs_1_) | copy-start | bytes 663556
  20.1 6.6 %collective-permute-start.6 = (bf16[32,3456]{1,0:T(8,128)(2,1)S(1)}, bf16[32,3456]{1,0:T(8,128)(2,1)S(1)}, u32[]{:S(2)}, u32[]{:S(2)}) collective-permute-start(bf16[32,3456]{1,0:T(8,128)(2,1)S(1)} %concatenate.11.refs_1_), channel_id=1, source_target_pairs={{0,32},{2,34},{4,36},{6,38},{8,40},{10,42},{12,44},{14,46},{16,48}... | collective-permute-start | bytes 663560 | tf_op jit(solution)/shard_map/ppermute | solution.py:116
  21.4 10.0 %collective-permute-start.7 = (bf16[32,3456]{1,0:T(8,128)(2,1)S(1)}, bf16[32,3456]{1,0:T(8,128)(2,1)S(1)}, u32[]{:S(2)}, u32[]{:S(2)}) collective-permute-start(bf16[32,3456]{1,0:T(8,128)(2,1)S(1)} %concatenate.11.refs_1_), channel_id=1, source_target_pairs={{0,64},{2,66},{4,68},{6,70},{8,72},{10,74},{12,76},{14,78},{16,80}... | collective-permute-start | bytes 663560 | tf_op jit(solution)/shard_map/ppermute | solution.py:116
  23.9 7.6 %collective-permute-start.8 = (bf16[32,3456]{1,0:T(8,128)(2,1)S(1)}, bf16[32,3456]{1,0:T(8,128)(2,1)}, u32[]{:S(2)}, u32[]{:S(2)}) collective-permute-start(bf16[32,3456]{1,0:T(8,128)(2,1)S(1)} %concatenate.11.refs_1_), channel_id=1, source_target_pairs={{0,96},{2,98},{4,100},{6,102},{8,104},{10,106},{12,108},{14,110},{... | collective-permute-start | bytes 663560 | tf_op jit(solution)/shard_map/ppermute | solution.py:116
  26.7 4.7 %copy-start.2 = (bf16[32,3456]{1,0:T(8,128)(2,1)}, bf16[32,3456]{1,0:T(8,128)(2,1)S(1)}, u32[]{:S(2)}) copy-start(bf16[32,3456]{1,0:T(8,128)(2,1)S(1)} %collective-permute-done.6.refs_2_) | copy-start | bytes 663556
  31.4 0.7 %copy-start.3 = (bf16[32,3456]{1,0:T(8,128)(2,1)}, bf16[32,3456]{1,0:T(8,128)(2,1)S(1)}, u32[]{:S(2)}) copy-start(bf16[32,3456]{1,0:T(8,128)(2,1)S(1)} %collective-permute-done.7.refs_3_) | copy-start | bytes 663556
  32.1 20.9 %all-to-all-start = ((bf16[64,2,3584]{2,1,0:T(2,128)(2,1)}), bf16[64,2,3584]{2,1,0:T(2,128)(2,1)S(1)}, u32[]{:S(2)}, u32[]{:S(2)}) async-start(bf16[64,2,3584]{2,1,0:T(2,128)(2,1)} %reshape.102), calls=%async_computation | async-start | bytes 1835008 | tf_op jit(solution)/shard_map/all_to_all | solution.py:153
  53.3 1.2 %copy-start = (bf16[128,3584]{1,0:T(8,128)(2,1)}, bf16[128,3584]{1,0:T(8,128)(2,1)S(1)}, u32[]{:S(2)}) copy-start(bf16[128,3584]{1,0:T(8,128)(2,1)S(1)} %reshape.103.x_ref) | copy-start | bytes 2752516
  54.5 4.6 %copy-start.6 = (f32[1,128]{1,0:T(1,128)S(1)}, f32[1,128]{1,0:T(1,128)}, u32[]{:S(2)}) copy-start(f32[1,128]{1,0:T(1,128)} %get-tuple-element.17) | copy-start | bytes 1540
  54.5 4.6 %copy-start.7 = (f32[1,128]{1,0:T(1,128)S(1)}, f32[1,128]{1,0:T(1,128)}, u32[]{:S(2)}) copy-start(f32[1,128]{1,0:T(1,128)} %get-tuple-element.18) | copy-start | bytes 1540

commit v12 on v11

--- a/solution.py
+++ b/solution.py
@@ -149,7 +149,7 @@
     own_rows = jnp.concatenate([own_rows, labels], axis=1)
     outgoing = jnp.dot(placement, own_rows, preferred_element_type=jnp.float32).astype(jnp.bfloat16)
     outgoing = outgoing.reshape(owner_count, capacity, flat_len + label_lanes)
-    pieces, outgoing = staged_gather(angle_major(references), "loop", outgoing)
+    pieces, (outgoing, particle_rows) = staged_gather(angle_major(references), "loop", (outgoing, particle_rows))
     incoming = lax.all_to_all(outgoing, "loop", split_axis=0, concat_axis=0, tiled=True)
     highest, summed = score_all(particle_rows, pieces)
     incoming, highest, summed = lax.optimization_barrier((incoming, highest, summed))
@@ -172,8 +172,7 @@
         out_shape=jax.ShapeDtypeStruct((block, flat_len), jnp.float32),
         scratch_shapes=[pltpu.VMEM((ANGLES * block, flat_len), jnp.float32)],
     )(by_angle, incoming)
-    partial_sums = partial_sums[:per_owner].reshape(per_owner, ANGLES, RADII).transpose(0, 2, 1)
-    partial_sums = partial_sums.reshape(per_owner, flat_len)
+    partial_sums = partial_sums[:per_owner]
     weighted = (member_grid[:per_owner, None] == member_in[None, :]).astype(jnp.float32) * weight_of[None, :]
     partial_weight = jnp.sum(weighted, axis=1)
     stats = jnp.stack([highest, summed], axis=0)
@@ -183,6 +182,7 @@
     class_sums = lax.dynamic_slice_in_dim(partial_sums, grp_index * references.shape[0], references.shape[0], 0)
     class_weight = lax.dynamic_slice_in_dim(partial_weight, grp_index * references.shape[0], references.shape[0], 0)
     class_average = class_sums / class_weight[:, None]
+    class_average = class_average.reshape(-1, ANGLES, RADII).transpose(0, 2, 1).reshape(-1, flat_len)
     stats = lax.dynamic_slice_in_dim(stats, grp_index * half_rows, half_rows, 2)
     highest = jnp.max(stats[:, 0], axis=0)
     summed = jnp.sum(stats[:, 1] * jnp.exp(stats[:, 0] - highest[None, :]), axis=0)

time: 67.7 us -> 67.7 us (level)
    reshape x4 -> x3, local copies, waits for them, and re-layouts: 2.77 us -> 1.04 us  [angle_major(): rows.reshape(count, RADII, ANGLES).transpose(0, 2, 1)]
    optimization_barrier x0 -> x1, local copies, waits for them, and re-layouts: none -> 1.73 us  [staged_gather(): parts, held = lax.optimization_barrier((parts, held))]
  transfers between devices with their start and end apart: 10 -> 10, of which waited for: 3 -> 3; matrix products, arithmetic and copies ran while one was open for 9% -> 9% of each run, Pallas kernels for 19% -> 20%
where the time goes in v12:
time: 67.7 us; the launch traced here: 67.3 us
  starting transfers between devices  22.5 us (33%)
  Pallas kernels  16.4 us (24%)
  local copies, waits for them, and re-layouts  10.3 us (15%)
  waiting for transfers between devices  7.85 us (12%)
  blocking collectives  6.67 us (10%)
  other arithmetic  2.27 us (3%)
  between operations  0.87 us (1%)
    ppermute x9, starting transfers between devices, staged_gather(): parts.append(lax.ppermute(rows, axis, pairs))  16.5 us
    pallas_call x1, Pallas kernels, score_all(): pl.pallas_call(functools.partial(score_kernel, scale=scale), out_shape=(j...  13.1 us
    ppermute x9, waiting for transfers between devices, staged_gather(): parts.append(lax.ppermute(rows, axis, pairs))  7.85 us
    psum x1, blocking collectives, local(): lax.psum((partial_sums, partial_weight, stats), 'grp')  6.67 us
    all_to_all x1, starting transfers between devices, local(): lax.all_to_all(outgoing, 'loop', split_axis=0, concat_axis=0, tiled=True)  6 us
    unnamed x19, local copies, waits for them, and re-layouts  3.27 us
    pallas_call x1, Pallas kernels, local(): pl.pallas_call(average_kernel, out_shape=jax.ShapeDtypeStruct((block, fla...  3.27 us
    optimization_barrier x1, local copies, waits for them, and re-layouts, staged_gather(): parts, held = lax.optimization_barrier((parts, held))  1.73 us
  transfers between devices with their start and end apart: 10, of which 3 were waited for; matrix products, arithmetic and copies ran while one was open for 9% of the time, Pallas kernels for 20%

profile of v12, /device:TPU:1, one launch (start us, length us, event | category | flops | bytes accessed | tf_op | source)
XLA Modules:
  0.0 67.3 jit_solution(9188753425717140917)
XLA Ops:
  0.6 0.8 %reshape.98 = bf16[2,48,72]{2,1,0:T(8,128)(2,1)S(1)} reshape(bf16[2,3456]{1,0:T(2,128)(2,1)} %param.6) | data formatting | bytes 27648 | tf_op jit(solution)/shard_map/reshape | solution.py:20
  1.7 2.2 %collective-permute-start = (bf16[2,3456]{1,0:T(2,128)(2,1)S(1)}, bf16[2,3456]{1,0:T(2,128)(2,1)S(1)}, u32[]{:S(2)}, u32[]{:S(2)}) collective-permute-start(bf16[2,3456]{1,0:T(2,128)(2,1)S(1)} %reshape.99), channel_id=1, source_target_pairs={{0,2},{2,4},{4,6},{6,0},{8,10},{10,12},{12,14},{14,8},{16,18},{18,... | collective-permute-start | bytes 41480 | tf_op jit(solution)/shard_map/ppermute | solution.py:116
  3.9 2.6 %collective-permute-start.1 = (bf16[2,3456]{1,0:T(2,128)(2,1)S(1)}, bf16[2,3456]{1,0:T(2,128)(2,1)S(1)}, u32[]{:S(2)}, u32[]{:S(2)}) collective-permute-start(bf16[2,3456]{1,0:T(2,128)(2,1)S(1)} %reshape.99), channel_id=1, source_target_pairs={{0,4},{2,6},{4,0},{6,2},{8,12},{10,14},{12,8},{14,10},{16,20},{18,... | collective-permute-start | bytes 41480 | tf_op jit(solution)/shard_map/ppermute | solution.py:116
  6.5 1.1 %collective-permute-start.2 = (bf16[2,3456]{1,0:T(2,128)(2,1)S(1)}, bf16[2,3456]{1,0:T(2,128)(2,1)S(1)}, u32[]{:S(2)}, u32[]{:S(2)}) collective-permute-start(bf16[2,3456]{1,0:T(2,128)(2,1)S(1)} %reshape.99), channel_id=1, source_target_pairs={{0,6},{2,0},{4,2},{6,4},{8,14},{10,8},{12,10},{14,12},{16,22},{18,... | collective-permute-start | bytes 41480 | tf_op jit(solution)/shard_map/ppermute | solution.py:116
  7.6 1.9 %copy.23 = bf16[128,3456]{0,1:T(8,128)(2,1)S(1)} copy(bf16[128,3456]{1,0:T(8,128)(2,1)} %param.5) | data formatting | bytes 1769472 | tf_op args[0]
  9.6 0.5 copy-done.8
  10.3 0.2 select_reduce_fusion
  10.5 0.3 constant_dynamic-slice_fusion.1
  11.1 1.7 %collective-permute-start.3 = (bf16[8,3456]{1,0:T(8,128)(2,1)S(1)}, bf16[8,3456]{1,0:T(8,128)(2,1)S(1)}, u32[]{:S(2)}, u32[]{:S(2)}) collective-permute-start(bf16[8,3456]{1,0:T(8,128)(2,1)S(1)} %pad_maximum_fusion), channel_id=1, source_target_pairs={{0,8},{2,10},{4,12},{6,14},{8,16},{10,18},{12,20},{14,22},{16,24},... | collective-permute-start | bytes 165896 | tf_op jit(solution)/shard_map/ppermute | solution.py:116
  12.8 3.3 %collective-permute-start.4 = (bf16[8,3456]{1,0:T(8,128)(2,1)S(1)}, bf16[8,3456]{1,0:T(8,128)(2,1)S(1)}, u32[]{:S(2)}, u32[]{:S(2)}) collective-permute-start(bf16[8,3456]{1,0:T(8,128)(2,1)S(1)} %pad_maximum_fusion), channel_id=1, source_target_pairs={{0,16},{2,18},{4,20},{6,22},{8,24},{10,26},{12,28},{14,30},{16,0},... | collective-permute-start | bytes 165896 | tf_op jit(solution)/shard_map/ppermute | solution.py:116
  16.1 0.7 %collective-permute-start.5 = (bf16[8,3456]{1,0:T(8,128)(2,1)S(1)}, bf16[8,3456]{1,0:T(8,128)(2,1)S(1)}, u32[]{:S(2)}, u32[]{:S(2)}) collective-permute-start(bf16[8,3456]{1,0:T(8,128)(2,1)S(1)} %pad_maximum_fusion), channel_id=1, source_target_pairs={{0,24},{2,26},{4,28},{6,30},{8,0},{10,2},{12,4},{14,6},{16,8},{18,... | collective-permute-start | bytes 165896 | tf_op jit(solution)/shard_map/ppermute | solution.py:116
  16.9 1.5 %collective-permute-done.4 = bf16[8,3456]{1,0:T(8,128)(2,1)S(1)} collective-permute-done((bf16[8,3456]{1,0:T(8,128)(2,1)S(1)}, bf16[8,3456]{1,0:T(8,128)(2,1)S(1)}, u32[]{:S(2)}, u32[]{:S(2)}) %collective-permute-start.4) | collective-permute-done | bytes 55328 | tf_op jit(solution)/shard_map/ppermute | solution.py:116
  18.3 1.7 %collective-permute-done.5 = bf16[8,3456]{1,0:T(8,128)(2,1)S(1)} collective-permute-done((bf16[8,3456]{1,0:T(8,128)(2,1)S(1)}, bf16[8,3456]{1,0:T(8,128)(2,1)S(1)}, u32[]{:S(2)}, u32[]{:S(2)}) %collective-permute-start.5) | collective-permute-done | bytes 55328 | tf_op jit(solution)/shard_map/ppermute | solution.py:116
  20.1 1.3 %collective-permute-start.6 = (bf16[32,3456]{1,0:T(8,128)(2,1)S(1)}, bf16[32,3456]{1,0:T(8,128)(2,1)S(1)}, u32[]{:S(2)}, u32[]{:S(2)}) collective-permute-start(bf16[32,3456]{1,0:T(8,128)(2,1)S(1)} %concatenate.11.refs_1_), channel_id=1, source_target_pairs={{0,32},{2,34},{4,36},{6,38},{8,40},{10,42},{12,44},{14,46},{16,48}... | collective-permute-start | bytes 663560 | tf_op jit(solution)/shard_map/ppermute | solution.py:116
  21.4 2.5 %collective-permute-start.7 = (bf16[32,3456]{1,0:T(8,128)(2,1)S(1)}, bf16[32,3456]{1,0:T(8,128)(2,1)S(1)}, u32[]{:S(2)}, u32[]{:S(2)}) collective-permute-start(bf16[32,3456]{1,0:T(8,128)(2,1)S(1)} %concatenate.11.refs_1_), channel_id=1, source_target_pairs={{0,64},{2,66},{4,68},{6,70},{8,72},{10,74},{12,76},{14,78},{16,80}... | collective-permute-start | bytes 663560 | tf_op jit(solution)/shard_map/ppermute | solution.py:116
  23.9 1.2 %collective-permute-start.8 = (bf16[32,3456]{1,0:T(8,128)(2,1)S(1)}, bf16[32,3456]{1,0:T(8,128)(2,1)}, u32[]{:S(2)}, u32[]{:S(2)}) collective-permute-start(bf16[32,3456]{1,0:T(8,128)(2,1)S(1)} %concatenate.11.refs_1_), channel_id=1, source_target_pairs={{0,96},{2,98},{4,100},{6,102},{8,104},{10,106},{12,108},{14,110},{... | collective-permute-start | bytes 663560 | tf_op jit(solution)/shard_map/ppermute | solution.py:116
  25.0 0.4 convolution_convert_fusion
  25.4 1.3 %reshape.102 = bf16[64,2,3584]{2,1,0:T(2,128)(2,1)} reshape(bf16[128,3584]{1,0:T(8,128)(2,1)S(1)} %convolution_convert_fusion) | data formatting | bytes 1835008 | tf_op jit(solution)/shard_map/reshape | solution.py:151
  26.7 4.7 %collective-permute-done.7.refs_3_ = bf16[32,3456]{1,0:T(8,128)(2,1)S(1)} collective-permute-done((bf16[32,3456]{1,0:T(8,128)(2,1)S(1)}, bf16[32,3456]{1,0:T(8,128)(2,1)S(1)}, u32[]{:S(2)}, u32[]{:S(2)}) %collective-permute-start.7) | collective-permute-done | bytes 221216 | tf_op jit(solution)/shard_map/ppermute | solution.py:116
  31.4 0.7 %copy-done.3 = bf16[32,3456]{1,0:T(8,128)(2,1)} copy-done((bf16[32,3456]{1,0:T(8,128)(2,1)}, bf16[32,3456]{1,0:T(8,128)(2,1)S(1)}, u32[]{:S(2)}) %copy-start.3) | copy-done | bytes 221208
  32.1 6.0 %all-to-all-start = ((bf16[64,2,3584]{2,1,0:T(2,128)(2,1)}), bf16[64,2,3584]{2,1,0:T(2,128)(2,1)S(1)}, u32[]{:S(2)}, u32[]{:S(2)}) async-start(bf16[64,2,3584]{2,1,0:T(2,128)(2,1)} %reshape.102), calls=%async_computation | async-start | bytes 1835008 | tf_op jit(solution)/shard_map/all_to_all | solution.py:153
  38.1 1.7 %copy.25.refs_0_ = bf16[128,3456]{1,0:T(8,128)(2,1)} copy(bf16[128,3456]{0,1:T(8,128)(2,1)S(1)} %bitcast.32) | data formatting | bytes 1769472 | tf_op jit(solution)/shard_map/optimization_barrier | solution.py:119
  39.9 13.1 %shard_map.68 = (f32[1,128]{1,0:T(1,128)}, f32[1,128]{1,0:T(1,128)}) custom-call(bf16[128,3456]{1,0:T(8,128)(2,1)} %copy.25.refs_0_, bf16[32,3456]{1,0:T(8,128)(2,1)} %copy-done.1, bf16[32,3456]{1,0:T(8,128)(2,1)} %copy-done.2, bf16[32,3456]{1,0:T(8,128)(2,1)} %copy-done.3, bf16[32,3456]{1,0:T(8,128)(2,1)} %collective-permute-done.8.refs_4_), custom_call_target="tpu_custom_call" | custom-call | tf_op jit(solution)/shard_map/pallas_call | solution.py:62
  53.0 0.3 reshape.103.x_ref
  53.4 0.2 slice_reduce_fusion.2
  53.7 0.2 select_reduce_fusion.1
  53.8 0.7 %select_convert_fusion.w_ref = bf16[576,128]{1,0:T(8,128)(2,1)} fusion(f32[128]{0:T(128)S(1)} %get-tuple-element.25, pred[8,128]{1,0:T(8,128)(4,1)S(1)} %iota_compare_fusion.5, pred[72,128]{1,0:T(8,128)(4,1)S(1)} %iota_compare_fusion.3), kind=kLoop, calls=%fused_computation.4 | loop fusion | flops 147456 | bytes 158208 | tf_op jit(solution)/shard_map/convert_element_type | solution.py:168
  54.6 3.3 %shard_map.69 = f32[8,3456]{1,0:T(8,128)} custom-call(bf16[576,128]{1,0:T(8,128)(2,1)} %select_convert_fusion.w_ref, bf16[128,3584]{1,0:T(8,128)(2,1)} %copy-done), custom_call_target="tpu_custom_call" | custom-call | tf_op jit(solution)/shard_map/pallas_call | solution.py:170
  57.8 0.9 %slice.37 = f32[4,3456]{1,0:T(4,128)S(1)} slice(f32[8,3456]{1,0:T(8,128)} %shard_map.69), slice={[0:4], [0:3456]} | slice | bytes 110592 | tf_op jit(solution)/shard_map/slice | solution.py:175
  58.8 6.7 %all-reduce.1 = (f32[2,2,128]{2,0,1:T(2,128)S(1)}, f32[4,3456]{1,0:T(4,128)S(1)}, f32[4]{0:T(128)S(1)}) all-reduce(f32[2,2,128]{2,0,1:T(2,128)S(1)} %broadcast_select_fusion, f32[4,3456]{1,0:T(4,128)S(1)} %slice.37, f32[4]{0:T(128)S(1)} %select_reduce_fusion.1), channel_id=1, replica_groups=mesh['loop'=64,'grp'=2] {'grp'}, use_global_device_ids=true, to_apply=%region_2.3 | all-reduce | flops 14340 | bytes 114720 | tf_op jit(solution)/shard_map/psum | solution.py:181
  65.9 0.7 %reshape.105 = f32[2,3456]{1,0:T(2,128)} reshape(f32[2,48,72]{2,1,0:T(8,128)S(1)} %copy.26) | data formatting | bytes 55296 | tf_op jit(solution)/shard_map/reshape | solution.py:185
  66.8 0.5 log_add_fusion
  (47 shorter events, 1.6 us)
Async XLA Ops:
  1.7 9.3 %collective-permute-start = (bf16[2,3456]{1,0:T(2,128)(2,1)S(1)}, bf16[2,3456]{1,0:T(2,128)(2,1)S(1)}, u32[]{:S(2)}, u32[]{:S(2)}) collective-permute-start(bf16[2,3456]{1,0:T(2,128)(2,1)S(1)} %reshape.99), channel_id=1, source_target_pairs={{0,2},{2,4},{4,6},{6,0},{8,10},{10,12},{12,14},{14,8},{16,18},{18,... | collective-permute-start | bytes 41480 | tf_op jit(solution)/shard_map/ppermute | solution.py:116
  3.9 7.1 %collective-permute-start.1 = (bf16[2,3456]{1,0:T(2,128)(2,1)S(1)}, bf16[2,3456]{1,0:T(2,128)(2,1)S(1)}, u32[]{:S(2)}, u32[]{:S(2)}) collective-permute-start(bf16[2,3456]{1,0:T(2,128)(2,1)S(1)} %reshape.99), channel_id=1, source_target_pairs={{0,4},{2,6},{4,0},{6,2},{8,12},{10,14},{12,8},{14,10},{16,20},{18,... | collective-permute-start | bytes 41480 | tf_op jit(solution)/shard_map/ppermute | solution.py:116
  6.5 4.5 %collective-permute-start.2 = (bf16[2,3456]{1,0:T(2,128)(2,1)S(1)}, bf16[2,3456]{1,0:T(2,128)(2,1)S(1)}, u32[]{:S(2)}, u32[]{:S(2)}) collective-permute-start(bf16[2,3456]{1,0:T(2,128)(2,1)S(1)} %reshape.99), channel_id=1, source_target_pairs={{0,6},{2,0},{4,2},{6,4},{8,14},{10,8},{12,10},{14,12},{16,22},{18,... | collective-permute-start | bytes 41480 | tf_op jit(solution)/shard_map/ppermute | solution.py:116
  9.5 0.7 copy-start.8
  10.3 0.7 copy-start.4
  10.3 0.7 copy-start.5
  11.1 5.8 %collective-permute-start.3 = (bf16[8,3456]{1,0:T(8,128)(2,1)S(1)}, bf16[8,3456]{1,0:T(8,128)(2,1)S(1)}, u32[]{:S(2)}, u32[]{:S(2)}) collective-permute-start(bf16[8,3456]{1,0:T(8,128)(2,1)S(1)} %pad_maximum_fusion), channel_id=1, source_target_pairs={{0,8},{2,10},{4,12},{6,14},{8,16},{10,18},{12,20},{14,22},{16,24},... | collective-permute-start | bytes 165896 | tf_op jit(solution)/shard_map/ppermute | solution.py:116
  12.8 5.5 %collective-permute-start.4 = (bf16[8,3456]{1,0:T(8,128)(2,1)S(1)}, bf16[8,3456]{1,0:T(8,128)(2,1)S(1)}, u32[]{:S(2)}, u32[]{:S(2)}) collective-permute-start(bf16[8,3456]{1,0:T(8,128)(2,1)S(1)} %pad_maximum_fusion), channel_id=1, source_target_pairs={{0,16},{2,18},{4,20},{6,22},{8,24},{10,26},{12,28},{14,30},{16,0},... | collective-permute-start | bytes 165896 | tf_op jit(solution)/shard_map/ppermute | solution.py:116
  16.1 3.9 %collective-permute-start.5 = (bf16[8,3456]{1,0:T(8,128)(2,1)S(1)}, bf16[8,3456]{1,0:T(8,128)(2,1)S(1)}, u32[]{:S(2)}, u32[]{:S(2)}) collective-permute-start(bf16[8,3456]{1,0:T(8,128)(2,1)S(1)} %pad_maximum_fusion), channel_id=1, source_target_pairs={{0,24},{2,26},{4,28},{6,30},{8,0},{10,2},{12,4},{14,6},{16,8},{18,... | collective-permute-start | bytes 165896 | tf_op jit(solution)/shard_map/ppermute | solution.py:116
  20.1 5.3 %copy-start.1 = (bf16[32,3456]{1,0:T(8,128)(2,1)}, bf16[32,3456]{1,0:T(8,128)(2,1)S(1)}, u32[]{:S(2)}) copy-start(bf16[32,3456]{1,0:T(8,128)(2,1)S(1)} %concatenate.11.refs_1_) | copy-start | bytes 663556
  20.1 6.6 %collective-permute-start.6 = (bf16[32,3456]{1,0:T(8,128)(2,1)S(1)}, bf16[32,3456]{1,0:T(8,128)(2,1)S(1)}, u32[]{:S(2)}, u32[]{:S(2)}) collective-permute-start(bf16[32,3456]{1,0:T(8,128)(2,1)S(1)} %concatenate.11.refs_1_), channel_id=1, source_target_pairs={{0,32},{2,34},{4,36},{6,38},{8,40},{10,42},{12,44},{14,46},{16,48}... | collective-permute-start | bytes 663560 | tf_op jit(solution)/shard_map/ppermute | solution.py:116
  21.4 10.0 %collective-permute-start.7 = (bf16[32,3456]{1,0:T(8,128)(2,1)S(1)}, bf16[32,3456]{1,0:T(8,128)(2,1)S(1)}, u32[]{:S(2)}, u32[]{:S(2)}) collective-permute-start(bf16[32,3456]{1,0:T(8,128)(2,1)S(1)} %concatenate.11.refs_1_), channel_id=1, source_target_pairs={{0,64},{2,66},{4,68},{6,70},{8,72},{10,74},{12,76},{14,78},{16,80}... | collective-permute-start | bytes 663560 | tf_op jit(solution)/shard_map/ppermute | solution.py:116
  23.9 7.6 %collective-permute-start.8 = (bf16[32,3456]{1,0:T(8,128)(2,1)S(1)}, bf16[32,3456]{1,0:T(8,128)(2,1)}, u32[]{:S(2)}, u32[]{:S(2)}) collective-permute-start(bf16[32,3456]{1,0:T(8,128)(2,1)S(1)} %concatenate.11.refs_1_), channel_id=1, source_target_pairs={{0,96},{2,98},{4,100},{6,102},{8,104},{10,106},{12,108},{14,110},{... | collective-permute-start | bytes 663560 | tf_op jit(solution)/shard_map/ppermute | solution.py:116
  26.7 4.7 %copy-start.2 = (bf16[32,3456]{1,0:T(8,128)(2,1)}, bf16[32,3456]{1,0:T(8,128)(2,1)S(1)}, u32[]{:S(2)}) copy-start(bf16[32,3456]{1,0:T(8,128)(2,1)S(1)} %collective-permute-done.6.refs_2_) | copy-start | bytes 663556
  31.4 0.7 %copy-start.3 = (bf16[32,3456]{1,0:T(8,128)(2,1)}, bf16[32,3456]{1,0:T(8,128)(2,1)S(1)}, u32[]{:S(2)}) copy-start(bf16[32,3456]{1,0:T(8,128)(2,1)S(1)} %collective-permute-done.7.refs_3_) | copy-start | bytes 663556
  32.1 20.9 %all-to-all-start = ((bf16[64,2,3584]{2,1,0:T(2,128)(2,1)}), bf16[64,2,3584]{2,1,0:T(2,128)(2,1)S(1)}, u32[]{:S(2)}, u32[]{:S(2)}) async-start(bf16[64,2,3584]{2,1,0:T(2,128)(2,1)} %reshape.102), calls=%async_computation | async-start | bytes 1835008 | tf_op jit(solution)/shard_map/all_to_all | solution.py:153
  53.3 1.2 %copy-start = (bf16[128,3584]{1,0:T(8,128)(2,1)}, bf16[128,3584]{1,0:T(8,128)(2,1)S(1)}, u32[]{:S(2)}) copy-start(bf16[128,3584]{1,0:T(8,128)(2,1)S(1)} %reshape.103.x_ref) | copy-start | bytes 2752516
  53.4 5.4 %copy-start.6 = (f32[1,128]{1,0:T(1,128)S(1)}, f32[1,128]{1,0:T(1,128)}, u32[]{:S(2)}) copy-start(f32[1,128]{1,0:T(1,128)} %get-tuple-element.19) | copy-start | bytes 1540
  53.4 5.4 %copy-start.7 = (f32[1,128]{1,0:T(1,128)S(1)}, f32[1,128]{1,0:T(1,128)}, u32[]{:S(2)}) copy-start(f32[1,128]{1,0:T(1,128)} %get-tuple-element.20) | copy-start | bytes 1540

commit v13 on v11

--- a/solution.py
+++ b/solution.py
@@ -18,6 +18,25 @@
 def angle_major(rows):
     count = rows.shape[0]
     return rows.reshape(count, RADII, ANGLES).transpose(0, 2, 1).reshape(count, RADII * ANGLES)
+
+
+def angle_major_kernel(x_ref, o_ref, t_scr, a_scr):
+    t_scr[...] = x_ref[...].astype(jnp.float32).T
+    for angle in range(ANGLES):
+        a_scr[pl.ds(angle * RADII, RADII), :] = t_scr[pl.ds(angle, RADII, stride=ANGLES), :]
+    o_ref[...] = a_scr[...].T.astype(o_ref.dtype)
+
+
+def angle_major_rows(rows):
+    count, flat_len = rows.shape
+    return pl.pallas_call(
+        angle_major_kernel,
+        out_shape=jax.ShapeDtypeStruct((count, flat_len), rows.dtype),
+        scratch_shapes=[
+            pltpu.VMEM((flat_len, count), jnp.float32),
+            pltpu.VMEM((flat_len, count), jnp.float32),
+        ],
+    )(rows)
 
 
 def score_kernel(*refs, scale):
@@ -126,7 +145,7 @@
     grp_size = lax.axis_size("grp")
     half_rows = row_count // grp_size
     grp_index = lax.axis_index("grp")
-    particle_rows = angle_major(particles)
+    particle_rows = angle_major_rows(particles)
     own_rows = lax.dynamic_slice_in_dim(particle_rows, grp_index * half_rows, half_rows, 0)
     owner_count = lax.axis_size("loop")
     per_owner = references.shape[0] * grp_size

time: 67.7 us -> 68.9 us (1.018)
  local copies, waits for them, and re-layouts: 9.76 us -> 5.53 us
  Pallas kernels: 16.4 us -> 19.2 us
  waiting for transfers between devices: 7.85 us -> 8.98 us
  starting transfers between devices: 22.5 us -> 23.5 us
    unnamed x19 -> x20, local copies, waits for them, and re-layouts: 3.27 us -> 0.04 us
    pallas_call x0 -> x1, Pallas kernels: none -> 2.76 us  [angle_major_rows(): pl.pallas_call(angle_major_kernel, out_shape=jax.ShapeDtypeStruct((count,...]
    reshape x4 -> x3, local copies, waits for them, and re-layouts: 2.77 us -> 1.04 us  [angle_major(): rows.reshape(count, RADII, ANGLES).transpose(0, 2, 1)]
    all_to_all x1, waiting for transfers between devices: 0.01 us -> 1.19 us  [local(): lax.all_to_all(outgoing, 'loop', split_axis=0, concat_axis=0, tiled=True)]
    all_to_all x1, starting transfers between devices: 6 us -> 7 us  [local(): lax.all_to_all(outgoing, 'loop', split_axis=0, concat_axis=0, tiled=True)]
    dynamic_slice x1, local copies, waits for them, and re-layouts: 0.32 us -> 1.05 us  [local(): lax.dynamic_slice_in_dim(particle_rows, grp_index * half_rows, half_rows, 0)]
  transfers between devices with their start and end apart: 10 -> 10, of which waited for: 3 -> 4; matrix products, arithmetic and copies ran while one was open for 9% -> 5% of each run, Pallas kernels for 19% -> 23%
where the time goes in v13:
time: 68.9 us; the launch traced here: 68.5 us
  starting transfers between devices  23.5 us (34%)
  Pallas kernels  19.2 us (28%)
  waiting for transfers between devices  8.98 us (13%)
  blocking collectives  7.17 us (10%)
  local copies, waits for them, and re-layouts  5.53 us (8%)
  other arithmetic  2.89 us (4%)
  between operations  0.88 us (1%)
    ppermute x9, starting transfers between devices, staged_gather(): parts.append(lax.ppermute(rows, axis, pairs))  16.5 us
    pallas_call x1, Pallas kernels, score_all(): pl.pallas_call(functools.partial(score_kernel, scale=scale), out_shape=(j...  13.1 us
    ppermute x9, waiting for transfers between devices, staged_gather(): parts.append(lax.ppermute(rows, axis, pairs))  7.79 us
    psum x1, blocking collectives, local(): lax.psum((partial_sums, partial_weight, stats), 'grp')  7.17 us
    all_to_all x1, starting transfers between devices, local(): lax.all_to_all(outgoing, 'loop', split_axis=0, concat_axis=0, tiled=True)  7 us
    pallas_call x1, Pallas kernels, local(): pl.pallas_call(average_kernel, out_shape=jax.ShapeDtypeStruct((block, fla...  3.29 us
    pallas_call x1, Pallas kernels, angle_major_rows(): pl.pallas_call(angle_major_kernel, out_shape=jax.ShapeDtypeStruct((count,...  2.76 us
  transfers between devices with their start and end apart: 10, of which 4 were waited for; matrix products, arithmetic and copies ran while one was open for 5% of the time, Pallas kernels for 23%

profile of v13, /device:TPU:1, one launch (start us, length us, event | category | flops | bytes accessed | tf_op | source)
XLA Modules:
  0.0 68.5 jit_solution(14747744297843346369)
XLA Ops:
  0.6 0.8 %reshape.92 = bf16[2,48,72]{2,1,0:T(8,128)(2,1)S(1)} reshape(bf16[2,3456]{1,0:T(2,128)(2,1)} %param.6) | data formatting | bytes 27648 | tf_op jit(solution)/shard_map/reshape | solution.py:20
  1.7 2.2 %collective-permute-start = (bf16[2,3456]{1,0:T(2,128)(2,1)S(1)}, bf16[2,3456]{1,0:T(2,128)(2,1)S(1)}, u32[]{:S(2)}, u32[]{:S(2)}) collective-permute-start(bf16[2,3456]{1,0:T(2,128)(2,1)S(1)} %reshape.93), channel_id=1, source_target_pairs={{0,2},{2,4},{4,6},{6,0},{8,10},{10,12},{12,14},{14,8},{16,18},{18,... | collective-permute-start | bytes 41480 | tf_op jit(solution)/shard_map/ppermute | solution.py:135
  3.9 2.6 %collective-permute-start.1 = (bf16[2,3456]{1,0:T(2,128)(2,1)S(1)}, bf16[2,3456]{1,0:T(2,128)(2,1)S(1)}, u32[]{:S(2)}, u32[]{:S(2)}) collective-permute-start(bf16[2,3456]{1,0:T(2,128)(2,1)S(1)} %reshape.93), channel_id=1, source_target_pairs={{0,4},{2,6},{4,0},{6,2},{8,12},{10,14},{12,8},{14,10},{16,20},{18,... | collective-permute-start | bytes 41480 | tf_op jit(solution)/shard_map/ppermute | solution.py:135
  6.5 1.1 %collective-permute-start.2 = (bf16[2,3456]{1,0:T(2,128)(2,1)S(1)}, bf16[2,3456]{1,0:T(2,128)(2,1)S(1)}, u32[]{:S(2)}, u32[]{:S(2)}) collective-permute-start(bf16[2,3456]{1,0:T(2,128)(2,1)S(1)} %reshape.93), channel_id=1, source_target_pairs={{0,6},{2,0},{4,2},{6,4},{8,14},{10,8},{12,10},{14,12},{16,22},{18,... | collective-permute-start | bytes 41480 | tf_op jit(solution)/shard_map/ppermute | solution.py:135
  7.6 2.8 %shard_map.68.refs_0_ = bf16[128,3456]{1,0:T(8,128)(2,1)} custom-call(bf16[128,3456]{1,0:T(8,128)(2,1)} %x_ref.1), custom_call_target="tpu_custom_call" | custom-call | tf_op jit(solution)/shard_map/pallas_call | solution.py:32
  10.5 0.2 select_reduce_fusion
  10.7 1.1 %constant_dynamic-slice_fusion.1 = bf16[64,3456]{1,0:T(8,128)(2,1)S(1)} fusion(bf16[128,3456]{1,0:T(8,128)(2,1)} %shard_map.68.refs_0_, s32[]{:T(128)S(6)} %select_n.30), kind=kLoop, calls=%fused_computation.37 | loop fusion | bytes 884740 | tf_op jit(solution)/shard_map/dynamic_slice | solution.py:149
  11.9 1.7 %collective-permute-start.3 = (bf16[8,3456]{1,0:T(8,128)(2,1)S(1)}, bf16[8,3456]{1,0:T(8,128)(2,1)S(1)}, u32[]{:S(2)}, u32[]{:S(2)}) collective-permute-start(bf16[8,3456]{1,0:T(8,128)(2,1)S(1)} %pad_maximum_fusion), channel_id=1, source_target_pairs={{0,8},{2,10},{4,12},{6,14},{8,16},{10,18},{12,20},{14,22},{16,24},... | collective-permute-start | bytes 165896 | tf_op jit(solution)/shard_map/ppermute | solution.py:135
  13.6 3.3 %collective-permute-start.4 = (bf16[8,3456]{1,0:T(8,128)(2,1)S(1)}, bf16[8,3456]{1,0:T(8,128)(2,1)S(1)}, u32[]{:S(2)}, u32[]{:S(2)}) collective-permute-start(bf16[8,3456]{1,0:T(8,128)(2,1)S(1)} %pad_maximum_fusion), channel_id=1, source_target_pairs={{0,16},{2,18},{4,20},{6,22},{8,24},{10,26},{12,28},{14,30},{16,0},... | collective-permute-start | bytes 165896 | tf_op jit(solution)/shard_map/ppermute | solution.py:135
  16.9 0.7 %collective-permute-start.5 = (bf16[8,3456]{1,0:T(8,128)(2,1)S(1)}, bf16[8,3456]{1,0:T(8,128)(2,1)S(1)}, u32[]{:S(2)}, u32[]{:S(2)}) collective-permute-start(bf16[8,3456]{1,0:T(8,128)(2,1)S(1)} %pad_maximum_fusion), channel_id=1, source_target_pairs={{0,24},{2,26},{4,28},{6,30},{8,0},{10,2},{12,4},{14,6},{16,8},{18,... | collective-permute-start | bytes 165896 | tf_op jit(solution)/shard_map/ppermute | solution.py:135
  17.8 1.4 %collective-permute-done.4 = bf16[8,3456]{1,0:T(8,128)(2,1)S(1)} collective-permute-done((bf16[8,3456]{1,0:T(8,128)(2,1)S(1)}, bf16[8,3456]{1,0:T(8,128)(2,1)S(1)}, u32[]{:S(2)}, u32[]{:S(2)}) %collective-permute-start.4) | collective-permute-done | bytes 55328 | tf_op jit(solution)/shard_map/ppermute | solution.py:135
  19.2 1.7 %collective-permute-done.5 = bf16[8,3456]{1,0:T(8,128)(2,1)S(1)} collective-permute-done((bf16[8,3456]{1,0:T(8,128)(2,1)S(1)}, bf16[8,3456]{1,0:T(8,128)(2,1)S(1)}, u32[]{:S(2)}, u32[]{:S(2)}) %collective-permute-start.5) | collective-permute-done | bytes 55328 | tf_op jit(solution)/shard_map/ppermute | solution.py:135
  20.8 0.1 concatenate.11.refs_1_
  21.0 1.3 %collective-permute-start.6 = (bf16[32,3456]{1,0:T(8,128)(2,1)S(1)}, bf16[32,3456]{1,0:T(8,128)(2,1)S(1)}, u32[]{:S(2)}, u32[]{:S(2)}) collective-permute-start(bf16[32,3456]{1,0:T(8,128)(2,1)S(1)} %concatenate.11.refs_1_), channel_id=1, source_target_pairs={{0,32},{2,34},{4,36},{6,38},{8,40},{10,42},{12,44},{14,46},{16,48}... | collective-permute-start | bytes 663560 | tf_op jit(solution)/shard_map/ppermute | solution.py:135
  22.2 2.5 %collective-permute-start.7 = (bf16[32,3456]{1,0:T(8,128)(2,1)S(1)}, bf16[32,3456]{1,0:T(8,128)(2,1)S(1)}, u32[]{:S(2)}, u32[]{:S(2)}) collective-permute-start(bf16[32,3456]{1,0:T(8,128)(2,1)S(1)} %concatenate.11.refs_1_), channel_id=1, source_target_pairs={{0,64},{2,66},{4,68},{6,70},{8,72},{10,74},{12,76},{14,78},{16,80}... | collective-permute-start | bytes 663560 | tf_op jit(solution)/shard_map/ppermute | solution.py:135
  24.7 1.2 %collective-permute-start.8 = (bf16[32,3456]{1,0:T(8,128)(2,1)S(1)}, bf16[32,3456]{1,0:T(8,128)(2,1)S(1)}, u32[]{:S(2)}, u32[]{:S(2)}) collective-permute-start(bf16[32,3456]{1,0:T(8,128)(2,1)S(1)} %concatenate.11.refs_1_), channel_id=1, source_target_pairs={{0,96},{2,98},{4,100},{6,102},{8,104},{10,106},{12,108},{14,110},{... | collective-permute-start | bytes 663560 | tf_op jit(solution)/shard_map/ppermute | solution.py:135
  25.8 0.4 convolution_convert_fusion
  26.2 1.3 %reshape.94 = bf16[64,2,3584]{2,1,0:T(2,128)(2,1)} reshape(bf16[128,3584]{1,0:T(8,128)(2,1)S(1)} %convolution_convert_fusion) | data formatting | bytes 1835008 | tf_op jit(solution)/shard_map/reshape | solution.py:170
  27.5 4.7 %collective-permute-done.7.refs_3_ = bf16[32,3456]{1,0:T(8,128)(2,1)S(1)} collective-permute-done((bf16[32,3456]{1,0:T(8,128)(2,1)S(1)}, bf16[32,3456]{1,0:T(8,128)(2,1)S(1)}, u32[]{:S(2)}, u32[]{:S(2)}) %collective-permute-start.7) | collective-permute-done | bytes 221216 | tf_op jit(solution)/shard_map/ppermute | solution.py:135
  32.3 7.0 %all-to-all-start = ((bf16[64,2,3584]{2,1,0:T(2,128)(2,1)}), bf16[64,2,3584]{2,1,0:T(2,128)(2,1)S(1)}, u32[]{:S(2)}, u32[]{:S(2)}) async-start(bf16[64,2,3584]{2,1,0:T(2,128)(2,1)} %reshape.94), calls=%async_computation | async-start | bytes 1835008 | tf_op jit(solution)/shard_map/all_to_all | solution.py:172
  39.3 13.1 %shard_map.69 = (f32[1,128]{1,0:T(1,128)}, f32[1,128]{1,0:T(1,128)}) custom-call(bf16[128,3456]{1,0:T(8,128)(2,1)} %shard_map.68.refs_0_, bf16[32,3456]{1,0:T(8,128)(2,1)} %copy-done.1, bf16[32,3456]{1,0:T(8,128)(2,1)} %copy-done.2, bf16[32,3456]{1,0:T(8,128)(2,1)} %copy-done.3, bf16[32,3456]{1,0:T(8,128)(2,1)} %copy-done.4), custom_call_target="tpu_custom_call" | custom-call | tf_op jit(solution)/shard_map/pallas_call | solution.py:81
  52.4 1.2 %all-to-all-done = bf16[64,2,3584]{2,1,0:T(2,128)(2,1)S(1)} async-done(((bf16[64,2,3584]{2,1,0:T(2,128)(2,1)}), bf16[64,2,3584]{2,1,0:T(2,128)(2,1)S(1)}, u32[]{:S(2)}, u32[]{:S(2)}) %all-to-all-start) | async-done | bytes 917536 | tf_op jit(solution)/shard_map/all_to_all | solution.py:172
  53.6 0.3 reshape.95.x_ref
  54.0 0.2 slice_reduce_fusion.2
  54.3 0.2 select_reduce_fusion.1
  54.5 0.7 %select_convert_fusion.w_ref = bf16[576,128]{1,0:T(8,128)(2,1)} fusion(f32[128]{0:T(128)S(1)} %get-tuple-element.23, pred[8,128]{1,0:T(8,128)(4,1)S(1)} %iota_compare_fusion.5, pred[72,128]{1,0:T(8,128)(4,1)S(1)} %iota_compare_fusion.3), kind=kLoop, calls=%fused_computation.7 | loop fusion | flops 147456 | bytes 158208 | tf_op jit(solution)/shard_map/convert_element_type | solution.py:187
  55.2 3.3 %shard_map.70 = f32[8,3456]{1,0:T(8,128)} custom-call(bf16[576,128]{1,0:T(8,128)(2,1)} %select_convert_fusion.w_ref, bf16[128,3584]{1,0:T(8,128)(2,1)} %copy-done), custom_call_target="tpu_custom_call" | custom-call | tf_op jit(solution)/shard_map/pallas_call | solution.py:189
  58.5 0.9 %slice.37 = f32[4,3456]{1,0:T(4,128)S(1)} slice(f32[8,3456]{1,0:T(8,128)} %shard_map.70), slice={[0:4], [0:3456]} | slice | bytes 110592 | tf_op jit(solution)/shard_map/slice | solution.py:194
  59.6 0.1 reshape.97
  59.8 7.2 %all-reduce.1 = (f32[2,2,128]{2,0,1:T(2,128)S(1)}, f32[4,3456]{1,0:T(4,128)S(1)}, f32[4]{0:T(128)S(1)}) all-reduce(f32[2,2,128]{2,0,1:T(2,128)S(1)} %broadcast_select_fusion, f32[4,3456]{1,0:T(4,128)S(1)} %reshape.97, f32[4]{0:T(128)S(1)} %select_reduce_fusion.1), channel_id=1, replica_groups=mesh['loop'=64,'grp'=2] {'grp'}, use_global_device_ids=true, to_apply=%region_2.3 | all-reduce | flops 14340 | bytes 114720 | tf_op jit(solution)/shard_map/psum | solution.py:201
  67.2 0.5 log_add_fusion
  67.8 0.7 %dynamic-slice_divide_fusion = f32[2,3456]{1,0:T(2,128)} fusion(f32[4,3456]{1,0:T(4,128)S(1)} %get-tuple-element.26, s32[]{:T(128)S(6)} %select_n.34, f32[2]{0:T(128)S(1)} %dynamic_slice.15), kind=kLoop, calls=%fused_computation.20 | loop fusion | flops 6912 | bytes 55308 | tf_op jit(solution)/shard_map/div | solution.py:204
  (48 shorter events, 1.2 us)
Async XLA Ops:
  1.6 8.8 %copy-start.9 = (s32[64]{0:T(128)S(1)}, s32[64]{0:T(128)}, u32[]{:S(2)}) copy-start(s32[64]{0:T(128)} %param.7) | copy-start | bytes 772
  1.7 10.1 %collective-permute-start = (bf16[2,3456]{1,0:T(2,128)(2,1)S(1)}, bf16[2,3456]{1,0:T(2,128)(2,1)S(1)}, u32[]{:S(2)}, u32[]{:S(2)}) collective-permute-start(bf16[2,3456]{1,0:T(2,128)(2,1)S(1)} %reshape.93), channel_id=1, source_target_pairs={{0,2},{2,4},{4,6},{6,0},{8,10},{10,12},{12,14},{14,8},{16,18},{18,... | collective-permute-start | bytes 41480 | tf_op jit(solution)/shard_map/ppermute | solution.py:135
  3.9 7.9 %collective-permute-start.1 = (bf16[2,3456]{1,0:T(2,128)(2,1)S(1)}, bf16[2,3456]{1,0:T(2,128)(2,1)S(1)}, u32[]{:S(2)}, u32[]{:S(2)}) collective-permute-start(bf16[2,3456]{1,0:T(2,128)(2,1)S(1)} %reshape.93), channel_id=1, source_target_pairs={{0,4},{2,6},{4,0},{6,2},{8,12},{10,14},{12,8},{14,10},{16,20},{18,... | collective-permute-start | bytes 41480 | tf_op jit(solution)/shard_map/ppermute | solution.py:135
  6.5 5.3 %collective-permute-start.2 = (bf16[2,3456]{1,0:T(2,128)(2,1)S(1)}, bf16[2,3456]{1,0:T(2,128)(2,1)S(1)}, u32[]{:S(2)}, u32[]{:S(2)}) collective-permute-start(bf16[2,3456]{1,0:T(2,128)(2,1)S(1)} %reshape.93), channel_id=1, source_target_pairs={{0,6},{2,0},{4,2},{6,4},{8,14},{10,8},{12,10},{14,12},{16,22},{18,... | collective-permute-start | bytes 41480 | tf_op jit(solution)/shard_map/ppermute | solution.py:135
  10.3 1.4 %copy-start.5 = (s32[64]{0:T(128)S(1)}, s32[64]{0:T(128)}, u32[]{:S(2)}) copy-start(s32[64]{0:T(128)} %param.9) | copy-start | bytes 772
  10.3 1.4 %copy-start.6 = (s32[64]{0:T(128)S(1)}, s32[64]{0:T(128)}, u32[]{:S(2)}) copy-start(s32[64]{0:T(128)} %param.8) | copy-start | bytes 772
  11.9 5.9 %collective-permute-start.3 = (bf16[8,3456]{1,0:T(8,128)(2,1)S(1)}, bf16[8,3456]{1,0:T(8,128)(2,1)S(1)}, u32[]{:S(2)}, u32[]{:S(2)}) collective-permute-start(bf16[8,3456]{1,0:T(8,128)(2,1)S(1)} %pad_maximum_fusion), channel_id=1, source_target_pairs={{0,8},{2,10},{4,12},{6,14},{8,16},{10,18},{12,20},{14,22},{16,24},... | collective-permute-start | bytes 165896 | tf_op jit(solution)/shard_map/ppermute | solution.py:135
  13.6 5.5 %collective-permute-start.4 = (bf16[8,3456]{1,0:T(8,128)(2,1)S(1)}, bf16[8,3456]{1,0:T(8,128)(2,1)S(1)}, u32[]{:S(2)}, u32[]{:S(2)}) collective-permute-start(bf16[8,3456]{1,0:T(8,128)(2,1)S(1)} %pad_maximum_fusion), channel_id=1, source_target_pairs={{0,16},{2,18},{4,20},{6,22},{8,24},{10,26},{12,28},{14,30},{16,0},... | collective-permute-start | bytes 165896 | tf_op jit(solution)/shard_map/ppermute | solution.py:135
  16.9 3.9 %collective-permute-start.5 = (bf16[8,3456]{1,0:T(8,128)(2,1)S(1)}, bf16[8,3456]{1,0:T(8,128)(2,1)S(1)}, u32[]{:S(2)}, u32[]{:S(2)}) collective-permute-start(bf16[8,3456]{1,0:T(8,128)(2,1)S(1)} %pad_maximum_fusion), channel_id=1, source_target_pairs={{0,24},{2,26},{4,28},{6,30},{8,0},{10,2},{12,4},{14,6},{16,8},{18,... | collective-permute-start | bytes 165896 | tf_op jit(solution)/shard_map/ppermute | solution.py:135
  21.0 6.5 %copy-start.1 = (bf16[32,3456]{1,0:T(8,128)(2,1)}, bf16[32,3456]{1,0:T(8,128)(2,1)S(1)}, u32[]{:S(2)}) copy-start(bf16[32,3456]{1,0:T(8,128)(2,1)S(1)} %concatenate.11.refs_1_) | copy-start | bytes 663556
  21.0 6.5 %collective-permute-start.6 = (bf16[32,3456]{1,0:T(8,128)(2,1)S(1)}, bf16[32,3456]{1,0:T(8,128)(2,1)S(1)}, u32[]{:S(2)}, u32[]{:S(2)}) collective-permute-start(bf16[32,3456]{1,0:T(8,128)(2,1)S(1)} %concatenate.11.refs_1_), channel_id=1, source_target_pairs={{0,32},{2,34},{4,36},{6,38},{8,40},{10,42},{12,44},{14,46},{16,48}... | collective-permute-start | bytes 663560 | tf_op jit(solution)/shard_map/ppermute | solution.py:135
  22.2 10.0 %collective-permute-start.7 = (bf16[32,3456]{1,0:T(8,128)(2,1)S(1)}, bf16[32,3456]{1,0:T(8,128)(2,1)S(1)}, u32[]{:S(2)}, u32[]{:S(2)}) collective-permute-start(bf16[32,3456]{1,0:T(8,128)(2,1)S(1)} %concatenate.11.refs_1_), channel_id=1, source_target_pairs={{0,64},{2,66},{4,68},{6,70},{8,72},{10,74},{12,76},{14,78},{16,80}... | collective-permute-start | bytes 663560 | tf_op jit(solution)/shard_map/ppermute | solution.py:135
  24.7 7.6 %collective-permute-start.8 = (bf16[32,3456]{1,0:T(8,128)(2,1)S(1)}, bf16[32,3456]{1,0:T(8,128)(2,1)S(1)}, u32[]{:S(2)}, u32[]{:S(2)}) collective-permute-start(bf16[32,3456]{1,0:T(8,128)(2,1)S(1)} %concatenate.11.refs_1_), channel_id=1, source_target_pairs={{0,96},{2,98},{4,100},{6,102},{8,104},{10,106},{12,108},{14,110},{... | collective-permute-start | bytes 663560 | tf_op jit(solution)/shard_map/ppermute | solution.py:135
  27.5 11.8 %copy-start.2 = (bf16[32,3456]{1,0:T(8,128)(2,1)}, bf16[32,3456]{1,0:T(8,128)(2,1)S(1)}, u32[]{:S(2)}) copy-start(bf16[32,3456]{1,0:T(8,128)(2,1)S(1)} %collective-permute-done.6.refs_2_) | copy-start | bytes 663556
  32.2 7.0 %copy-start.3 = (bf16[32,3456]{1,0:T(8,128)(2,1)}, bf16[32,3456]{1,0:T(8,128)(2,1)S(1)}, u32[]{:S(2)}) copy-start(bf16[32,3456]{1,0:T(8,128)(2,1)S(1)} %collective-permute-done.7.refs_3_) | copy-start | bytes 663556
  32.2 7.0 %copy-start.4 = (bf16[32,3456]{1,0:T(8,128)(2,1)}, bf16[32,3456]{1,0:T(8,128)(2,1)S(1)}, u32[]{:S(2)}) copy-start(bf16[32,3456]{1,0:T(8,128)(2,1)S(1)} %collective-permute-done.8.refs_4_) | copy-start | bytes 663556
  32.3 21.4 %all-to-all-start = ((bf16[64,2,3584]{2,1,0:T(2,128)(2,1)}), bf16[64,2,3584]{2,1,0:T(2,128)(2,1)S(1)}, u32[]{:S(2)}, u32[]{:S(2)}) async-start(bf16[64,2,3584]{2,1,0:T(2,128)(2,1)} %reshape.94), calls=%async_computation | async-start | bytes 1835008 | tf_op jit(solution)/shard_map/all_to_all | solution.py:172
  54.0 1.2 %copy-start = (bf16[128,3584]{1,0:T(8,128)(2,1)}, bf16[128,3584]{1,0:T(8,128)(2,1)S(1)}, u32[]{:S(2)}) copy-start(bf16[128,3584]{1,0:T(8,128)(2,1)S(1)} %reshape.95.x_ref) | copy-start | bytes 2752516
  55.2 4.6 %copy-start.7 = (f32[1,128]{1,0:T(1,128)S(1)}, f32[1,128]{1,0:T(1,128)}, u32[]{:S(2)}) copy-start(f32[1,128]{1,0:T(1,128)} %get-tuple-element.17) | copy-start | bytes 1540
  55.2 4.6 %copy-start.8 = (f32[1,128]{1,0:T(1,128)S(1)}, f32[1,128]{1,0:T(1,128)}, u32[]{:S(2)}) copy-start(f32[1,128]{1,0:T(1,128)} %get-tuple-element.18) | copy-start | bytes 1540

commit v14 on v13

--- a/solution.py
+++ b/solution.py
@@ -171,7 +171,12 @@
     pieces, outgoing = staged_gather(angle_major(references), "loop", outgoing)
     incoming = lax.all_to_all(outgoing, "loop", split_axis=0, concat_axis=0, tiled=True)
     highest, summed = score_all(particle_rows, pieces)
-    incoming, highest, summed = lax.optimization_barrier((incoming, highest, summed))
+    stats = lax.all_gather(jnp.stack([highest, summed], axis=0), "grp", axis=0, tiled=False)
+    stats = lax.dynamic_slice_in_dim(stats, grp_index * half_rows, half_rows, 2)
+    highest = jnp.max(stats[:, 0], axis=0)
+    summed = jnp.sum(stats[:, 1] * jnp.exp(stats[:, 0] - highest[None, :]), axis=0)
+    log_evidence = highest + jnp.log(summed)
+    incoming, log_evidence = lax.optimization_barrier((incoming, log_evidence))
     incoming = incoming.reshape(slot_count, flat_len + label_lanes)
     labels_in = incoming[:, flat_len : flat_len + 3]
     labels_in = labels_in.astype(jnp.float32)
@@ -195,17 +200,10 @@
     partial_sums = partial_sums.reshape(per_owner, flat_len)
     weighted = (member_grid[:per_owner, None] == member_in[None, :]).astype(jnp.float32) * weight_of[None, :]
     partial_weight = jnp.sum(weighted, axis=1)
-    stats = jnp.stack([highest, summed], axis=0)
-    slots = jnp.arange(grp_size, dtype=jnp.int32)[:, None, None] == grp_index
-    stats = jnp.where(slots, stats[None], 0.0)
-    partial_sums, partial_weight, stats = lax.psum((partial_sums, partial_weight, stats), "grp")
-    class_sums = lax.dynamic_slice_in_dim(partial_sums, grp_index * references.shape[0], references.shape[0], 0)
-    class_weight = lax.dynamic_slice_in_dim(partial_weight, grp_index * references.shape[0], references.shape[0], 0)
+    class_sums, class_weight = lax.psum((partial_sums, partial_weight), "grp")
+    class_sums = lax.dynamic_slice_in_dim(class_sums, grp_index * references.shape[0], references.shape[0], 0)
+    class_weight = lax.dynamic_slice_in_dim(class_weight, grp_index * references.shape[0], references.shape[0], 0)
     class_average = class_sums / class_weight[:, None]
-    stats = lax.dynamic_slice_in_dim(stats, grp_index * half_rows, half_rows, 2)
-    highest = jnp.max(stats[:, 0], axis=0)
-    summed = jnp.sum(stats[:, 1] * jnp.exp(stats[:, 0] - highest[None, :]), axis=0)
-    log_evidence = highest + jnp.log(summed)
     return (log_evidence, class_average)
 
 

time: 68.9 us -> 69.2 us (level)
  waiting for transfers between devices: 8.98 us -> 7.79 us
  blocking collectives: 7.17 us -> 8.11 us
    all_gather x0 -> x1, blocking collectives: none -> 4.4 us  [local(): lax.all_gather(jnp.stack([highest, summed], axis=0), 'grp', axis=0, tiled...]
    psum x1, blocking collectives: 7.17 us -> 3.72 us  [local(): class_sums, class_weight = lax.psum((partial_sums, partial_weight), 'grp')]
    all_to_all x1, waiting for transfers between devices: 1.19 us -> 0.01 us  [local(): lax.all_to_all(outgoing, 'loop', split_axis=0, concat_axis=0, tiled=True)]
  transfers between devices with their start and end apart: 10 -> 10, of which waited for: 4 -> 3; matrix products, arithmetic and copies ran while one was open for 5% -> 7% of each run, Pallas kernels for 23% -> 23%
where the time goes in v14:
time: 69.2 us; the launch traced here: 68.7 us
  starting transfers between devices  23.5 us (34%)
  Pallas kernels  19.2 us (28%)
  blocking collectives  8.11 us (12%)
  waiting for transfers between devices  7.79 us (11%)
  local copies, waits for them, and re-layouts  5.53 us (8%)
  other arithmetic  3.41 us (5%)
  between operations  0.85 us (1%)
    ppermute x9, starting transfers between devices, staged_gather(): parts.append(lax.ppermute(rows, axis, pairs))  16.5 us
    pallas_call x1, Pallas kernels, score_all(): pl.pallas_call(functools.partial(score_kernel, scale=scale), out_shape=(j...  13.1 us
    ppermute x9, waiting for transfers between devices, staged_gather(): parts.append(lax.ppermute(rows, axis, pairs))  7.79 us
    all_to_all x1, starting transfers between devices, local(): lax.all_to_all(outgoing, 'loop', split_axis=0, concat_axis=0, tiled=True)  7 us
    all_gather x1, blocking collectives, local(): lax.all_gather(jnp.stack([highest, summed], axis=0), 'grp', axis=0, tiled...  4.4 us
    psum x1, blocking collectives, local(): class_sums, class_weight = lax.psum((partial_sums, partial_weight), 'grp')  3.72 us
    pallas_call x1, Pallas kernels, local(): pl.pallas_call(average_kernel, out_shape=jax.ShapeDtypeStruct((block, fla...  3.28 us
    pallas_call x1, Pallas kernels, angle_major_rows(): pl.pallas_call(angle_major_kernel, out_shape=jax.ShapeDtypeStruct((count,...  2.76 us
  transfers between devices with their start and end apart: 10, of which 3 were waited for; matrix products, arithmetic and copies ran while one was open for 7% of the time, Pallas kernels for 23%

profile of v14, /device:TPU:1, one launch (start us, length us, event | category | flops | bytes accessed | tf_op | source)
XLA Modules:
  0.0 68.7 jit_solution(4928244824087315235)
XLA Ops:
  0.6 0.8 %reshape.86 = bf16[2,48,72]{2,1,0:T(8,128)(2,1)S(1)} reshape(bf16[2,3456]{1,0:T(2,128)(2,1)} %param.6) | data formatting | bytes 27648 | tf_op jit(solution)/shard_map/reshape | solution.py:20
  1.7 2.2 %collective-permute-start = (bf16[2,3456]{1,0:T(2,128)(2,1)S(1)}, bf16[2,3456]{1,0:T(2,128)(2,1)S(1)}, u32[]{:S(2)}, u32[]{:S(2)}) collective-permute-start(bf16[2,3456]{1,0:T(2,128)(2,1)S(1)} %reshape.87), channel_id=1, source_target_pairs={{0,2},{2,4},{4,6},{6,0},{8,10},{10,12},{12,14},{14,8},{16,18},{18,... | collective-permute-start | bytes 41480 | tf_op jit(solution)/shard_map/ppermute | solution.py:135
  3.9 2.6 %collective-permute-start.1 = (bf16[2,3456]{1,0:T(2,128)(2,1)S(1)}, bf16[2,3456]{1,0:T(2,128)(2,1)S(1)}, u32[]{:S(2)}, u32[]{:S(2)}) collective-permute-start(bf16[2,3456]{1,0:T(2,128)(2,1)S(1)} %reshape.87), channel_id=1, source_target_pairs={{0,4},{2,6},{4,0},{6,2},{8,12},{10,14},{12,8},{14,10},{16,20},{18,... | collective-permute-start | bytes 41480 | tf_op jit(solution)/shard_map/ppermute | solution.py:135
  6.5 1.1 %collective-permute-start.2 = (bf16[2,3456]{1,0:T(2,128)(2,1)S(1)}, bf16[2,3456]{1,0:T(2,128)(2,1)S(1)}, u32[]{:S(2)}, u32[]{:S(2)}) collective-permute-start(bf16[2,3456]{1,0:T(2,128)(2,1)S(1)} %reshape.87), channel_id=1, source_target_pairs={{0,6},{2,0},{4,2},{6,4},{8,14},{10,8},{12,10},{14,12},{16,22},{18,... | collective-permute-start | bytes 41480 | tf_op jit(solution)/shard_map/ppermute | solution.py:135
  7.6 2.8 %shard_map.68.refs_0_ = bf16[128,3456]{1,0:T(8,128)(2,1)} custom-call(bf16[128,3456]{1,0:T(8,128)(2,1)} %x_ref.1), custom_call_target="tpu_custom_call" | custom-call | tf_op jit(solution)/shard_map/pallas_call | solution.py:32
  10.5 0.2 select_reduce_fusion
  10.7 1.1 %constant_dynamic-slice_fusion.2 = bf16[64,3456]{1,0:T(8,128)(2,1)S(1)} fusion(bf16[128,3456]{1,0:T(8,128)(2,1)} %shard_map.68.refs_0_, s32[]{:T(128)S(6)} %select_n.26), kind=kLoop, calls=%fused_computation.33 | loop fusion | bytes 884740 | tf_op jit(solution)/shard_map/dynamic_slice | solution.py:149
  11.9 1.7 %collective-permute-start.3 = (bf16[8,3456]{1,0:T(8,128)(2,1)S(1)}, bf16[8,3456]{1,0:T(8,128)(2,1)S(1)}, u32[]{:S(2)}, u32[]{:S(2)}) collective-permute-start(bf16[8,3456]{1,0:T(8,128)(2,1)S(1)} %pad_maximum_fusion), channel_id=1, source_target_pairs={{0,8},{2,10},{4,12},{6,14},{8,16},{10,18},{12,20},{14,22},{16,24},... | collective-permute-start | bytes 165896 | tf_op jit(solution)/shard_map/ppermute | solution.py:135
  13.6 3.3 %collective-permute-start.4 = (bf16[8,3456]{1,0:T(8,128)(2,1)S(1)}, bf16[8,3456]{1,0:T(8,128)(2,1)S(1)}, u32[]{:S(2)}, u32[]{:S(2)}) collective-permute-start(bf16[8,3456]{1,0:T(8,128)(2,1)S(1)} %pad_maximum_fusion), channel_id=1, source_target_pairs={{0,16},{2,18},{4,20},{6,22},{8,24},{10,26},{12,28},{14,30},{16,0},... | collective-permute-start | bytes 165896 | tf_op jit(solution)/shard_map/ppermute | solution.py:135
  16.9 0.7 %collective-permute-start.5 = (bf16[8,3456]{1,0:T(8,128)(2,1)S(1)}, bf16[8,3456]{1,0:T(8,128)(2,1)S(1)}, u32[]{:S(2)}, u32[]{:S(2)}) collective-permute-start(bf16[8,3456]{1,0:T(8,128)(2,1)S(1)} %pad_maximum_fusion), channel_id=1, source_target_pairs={{0,24},{2,26},{4,28},{6,30},{8,0},{10,2},{12,4},{14,6},{16,8},{18,... | collective-permute-start | bytes 165896 | tf_op jit(solution)/shard_map/ppermute | solution.py:135
  17.8 1.4 %collective-permute-done.4 = bf16[8,3456]{1,0:T(8,128)(2,1)S(1)} collective-permute-done((bf16[8,3456]{1,0:T(8,128)(2,1)S(1)}, bf16[8,3456]{1,0:T(8,128)(2,1)S(1)}, u32[]{:S(2)}, u32[]{:S(2)}) %collective-permute-start.4) | collective-permute-done | bytes 55328 | tf_op jit(solution)/shard_map/ppermute | solution.py:135
  19.2 1.7 %collective-permute-done.5 = bf16[8,3456]{1,0:T(8,128)(2,1)S(1)} collective-permute-done((bf16[8,3456]{1,0:T(8,128)(2,1)S(1)}, bf16[8,3456]{1,0:T(8,128)(2,1)S(1)}, u32[]{:S(2)}, u32[]{:S(2)}) %collective-permute-start.5) | collective-permute-done | bytes 55328 | tf_op jit(solution)/shard_map/ppermute | solution.py:135
  20.8 0.1 concatenate.11.refs_1_
  21.0 1.3 %collective-permute-start.6 = (bf16[32,3456]{1,0:T(8,128)(2,1)S(1)}, bf16[32,3456]{1,0:T(8,128)(2,1)S(1)}, u32[]{:S(2)}, u32[]{:S(2)}) collective-permute-start(bf16[32,3456]{1,0:T(8,128)(2,1)S(1)} %concatenate.11.refs_1_), channel_id=1, source_target_pairs={{0,32},{2,34},{4,36},{6,38},{8,40},{10,42},{12,44},{14,46},{16,48}... | collective-permute-start | bytes 663560 | tf_op jit(solution)/shard_map/ppermute | solution.py:135
  22.2 2.5 %collective-permute-start.7 = (bf16[32,3456]{1,0:T(8,128)(2,1)S(1)}, bf16[32,3456]{1,0:T(8,128)(2,1)S(1)}, u32[]{:S(2)}, u32[]{:S(2)}) collective-permute-start(bf16[32,3456]{1,0:T(8,128)(2,1)S(1)} %concatenate.11.refs_1_), channel_id=1, source_target_pairs={{0,64},{2,66},{4,68},{6,70},{8,72},{10,74},{12,76},{14,78},{16,80}... | collective-permute-start | bytes 663560 | tf_op jit(solution)/shard_map/ppermute | solution.py:135
  24.7 1.2 %collective-permute-start.8 = (bf16[32,3456]{1,0:T(8,128)(2,1)S(1)}, bf16[32,3456]{1,0:T(8,128)(2,1)S(1)}, u32[]{:S(2)}, u32[]{:S(2)}) collective-permute-start(bf16[32,3456]{1,0:T(8,128)(2,1)S(1)} %concatenate.11.refs_1_), channel_id=1, source_target_pairs={{0,96},{2,98},{4,100},{6,102},{8,104},{10,106},{12,108},{14,110},{... | collective-permute-start | bytes 663560 | tf_op jit(solution)/shard_map/ppermute | solution.py:135
  25.8 0.4 convolution_convert_fusion
  26.2 1.3 %reshape.88 = bf16[64,2,3584]{2,1,0:T(2,128)(2,1)} reshape(bf16[128,3584]{1,0:T(8,128)(2,1)S(1)} %convolution_convert_fusion) | data formatting | bytes 1835008 | tf_op jit(solution)/shard_map/reshape | solution.py:170
  27.5 4.7 %collective-permute-done.7.refs_3_ = bf16[32,3456]{1,0:T(8,128)(2,1)S(1)} collective-permute-done((bf16[32,3456]{1,0:T(8,128)(2,1)S(1)}, bf16[32,3456]{1,0:T(8,128)(2,1)S(1)}, u32[]{:S(2)}, u32[]{:S(2)}) %collective-permute-start.7) | collective-permute-done | bytes 221216 | tf_op jit(solution)/shard_map/ppermute | solution.py:135
  32.3 7.0 %all-to-all-start = ((bf16[64,2,3584]{2,1,0:T(2,128)(2,1)}), bf16[64,2,3584]{2,1,0:T(2,128)(2,1)S(1)}, u32[]{:S(2)}, u32[]{:S(2)}) async-start(bf16[64,2,3584]{2,1,0:T(2,128)(2,1)} %reshape.88), calls=%async_computation | async-start | bytes 1835008 | tf_op jit(solution)/shard_map/all_to_all | solution.py:172
  39.3 13.1 %shard_map.69 = (f32[1,128]{1,0:T(1,128)}, f32[1,128]{1,0:T(1,128)}) custom-call(bf16[128,3456]{1,0:T(8,128)(2,1)} %shard_map.68.refs_0_, bf16[32,3456]{1,0:T(8,128)(2,1)} %copy-done.1, bf16[32,3456]{1,0:T(8,128)(2,1)} %copy-done.2, bf16[32,3456]{1,0:T(8,128)(2,1)} %copy-done.3, bf16[32,3456]{1,0:T(8,128)(2,1)} %copy-done.4), custom_call_target="tpu_custom_call" | custom-call | tf_op jit(solution)/shard_map/pallas_call | solution.py:81
  52.4 0.7 maximum_bitcast_fusion
  53.1 4.4 %all-gather.1 = f32[2,2,128]{2,1,0:T(2,128)S(1)} all-gather(f32[1,2,128]{2,1,0:T(2,128)S(1)} %maximum_bitcast_fusion), channel_id=2, replica_groups=mesh['loop'=64,'grp'=2] {'grp'}, dimensions={0}, use_global_device_ids=true | all-gather | bytes 3072 | tf_op jit(solution)/shard_map/all_gather | solution.py:174
  57.6 0.5 log_add_fusion
  58.1 0.3 reshape.89.x_ref
  58.5 0.2 slice_reduce_fusion.2
  58.8 0.2 select_reduce_fusion.1
  59.0 0.7 %select_convert_fusion.w_ref = bf16[576,128]{1,0:T(8,128)(2,1)} fusion(f32[128]{0:T(128)S(1)} %get-tuple-element.21, pred[8,128]{1,0:T(8,128)(4,1)S(1)} %iota_compare_fusion.5, pred[72,128]{1,0:T(8,128)(4,1)S(1)} %iota_compare_fusion.3), kind=kLoop, calls=%fused_computation.7 | loop fusion | flops 147456 | bytes 158208 | tf_op jit(solution)/shard_map/convert_element_type | solution.py:192
  59.7 3.3 %shard_map.70 = f32[8,3456]{1,0:T(8,128)} custom-call(bf16[576,128]{1,0:T(8,128)(2,1)} %select_convert_fusion.w_ref, bf16[128,3584]{1,0:T(8,128)(2,1)} %copy-done), custom_call_target="tpu_custom_call" | custom-call | tf_op jit(solution)/shard_map/pallas_call | solution.py:194
  63.0 0.9 %slice.37 = f32[4,3456]{1,0:T(4,128)S(1)} slice(f32[8,3456]{1,0:T(8,128)} %shard_map.70), slice={[0:4], [0:3456]} | slice | bytes 110592 | tf_op jit(solution)/shard_map/slice | solution.py:199
  64.2 3.7 %all-reduce.1 = (f32[4,3456]{1,0:T(4,128)S(1)}, f32[4]{0:T(128)S(1)}) all-reduce(f32[4,3456]{1,0:T(4,128)S(1)} %reshape.91, f32[4]{0:T(128)S(1)} %select_reduce_fusion.1), channel_id=1, replica_groups=mesh['loop'=64,'grp'=2] {'grp'}, use_global_device_ids=true, to_apply=%region_4.5 | all-reduce | flops 13828 | bytes 110624 | tf_op jit(solution)/shard_map/psum | solution.py:203
  68.0 0.7 %dynamic-slice_divide_fusion = f32[2,3456]{1,0:T(2,128)} fusion(f32[4,3456]{1,0:T(4,128)S(1)} %get-tuple-element.23, s32[]{:T(128)S(6)} %select_n.29, f32[2]{0:T(128)S(1)} %dynamic_slice.15), kind=kLoop, calls=%fused_computation.20 | loop fusion | flops 6912 | bytes 55308 | tf_op jit(solution)/shard_map/div | solution.py:206
  (43 shorter events, 1.2 us)
Async XLA Ops:
  1.6 8.8 %copy-start.7 = (s32[64]{0:T(128)S(1)}, s32[64]{0:T(128)}, u32[]{:S(2)}) copy-start(s32[64]{0:T(128)} %param.7) | copy-start | bytes 772
  1.7 10.1 %collective-permute-start = (bf16[2,3456]{1,0:T(2,128)(2,1)S(1)}, bf16[2,3456]{1,0:T(2,128)(2,1)S(1)}, u32[]{:S(2)}, u32[]{:S(2)}) collective-permute-start(bf16[2,3456]{1,0:T(2,128)(2,1)S(1)} %reshape.87), channel_id=1, source_target_pairs={{0,2},{2,4},{4,6},{6,0},{8,10},{10,12},{12,14},{14,8},{16,18},{18,... | collective-permute-start | bytes 41480 | tf_op jit(solution)/shard_map/ppermute | solution.py:135
  3.9 7.9 %collective-permute-start.1 = (bf16[2,3456]{1,0:T(2,128)(2,1)S(1)}, bf16[2,3456]{1,0:T(2,128)(2,1)S(1)}, u32[]{:S(2)}, u32[]{:S(2)}) collective-permute-start(bf16[2,3456]{1,0:T(2,128)(2,1)S(1)} %reshape.87), channel_id=1, source_target_pairs={{0,4},{2,6},{4,0},{6,2},{8,12},{10,14},{12,8},{14,10},{16,20},{18,... | collective-permute-start | bytes 41480 | tf_op jit(solution)/shard_map/ppermute | solution.py:135
  6.5 5.3 %collective-permute-start.2 = (bf16[2,3456]{1,0:T(2,128)(2,1)S(1)}, bf16[2,3456]{1,0:T(2,128)(2,1)S(1)}, u32[]{:S(2)}, u32[]{:S(2)}) collective-permute-start(bf16[2,3456]{1,0:T(2,128)(2,1)S(1)} %reshape.87), channel_id=1, source_target_pairs={{0,6},{2,0},{4,2},{6,4},{8,14},{10,8},{12,10},{14,12},{16,22},{18,... | collective-permute-start | bytes 41480 | tf_op jit(solution)/shard_map/ppermute | solution.py:135
  10.3 1.4 %copy-start.5 = (s32[64]{0:T(128)S(1)}, s32[64]{0:T(128)}, u32[]{:S(2)}) copy-start(s32[64]{0:T(128)} %param.9) | copy-start | bytes 772
  10.3 1.4 %copy-start.6 = (s32[64]{0:T(128)S(1)}, s32[64]{0:T(128)}, u32[]{:S(2)}) copy-start(s32[64]{0:T(128)} %param.8) | copy-start | bytes 772
  11.9 5.9 %collective-permute-start.3 = (bf16[8,3456]{1,0:T(8,128)(2,1)S(1)}, bf16[8,3456]{1,0:T(8,128)(2,1)S(1)}, u32[]{:S(2)}, u32[]{:S(2)}) collective-permute-start(bf16[8,3456]{1,0:T(8,128)(2,1)S(1)} %pad_maximum_fusion), channel_id=1, source_target_pairs={{0,8},{2,10},{4,12},{6,14},{8,16},{10,18},{12,20},{14,22},{16,24},... | collective-permute-start | bytes 165896 | tf_op jit(solution)/shard_map/ppermute | solution.py:135
  13.6 5.5 %collective-permute-start.4 = (bf16[8,3456]{1,0:T(8,128)(2,1)S(1)}, bf16[8,3456]{1,0:T(8,128)(2,1)S(1)}, u32[]{:S(2)}, u32[]{:S(2)}) collective-permute-start(bf16[8,3456]{1,0:T(8,128)(2,1)S(1)} %pad_maximum_fusion), channel_id=1, source_target_pairs={{0,16},{2,18},{4,20},{6,22},{8,24},{10,26},{12,28},{14,30},{16,0},... | collective-permute-start | bytes 165896 | tf_op jit(solution)/shard_map/ppermute | solution.py:135
  16.9 3.9 %collective-permute-start.5 = (bf16[8,3456]{1,0:T(8,128)(2,1)S(1)}, bf16[8,3456]{1,0:T(8,128)(2,1)S(1)}, u32[]{:S(2)}, u32[]{:S(2)}) collective-permute-start(bf16[8,3456]{1,0:T(8,128)(2,1)S(1)} %pad_maximum_fusion), channel_id=1, source_target_pairs={{0,24},{2,26},{4,28},{6,30},{8,0},{10,2},{12,4},{14,6},{16,8},{18,... | collective-permute-start | bytes 165896 | tf_op jit(solution)/shard_map/ppermute | solution.py:135
  21.0 6.5 %copy-start.1 = (bf16[32,3456]{1,0:T(8,128)(2,1)}, bf16[32,3456]{1,0:T(8,128)(2,1)S(1)}, u32[]{:S(2)}) copy-start(bf16[32,3456]{1,0:T(8,128)(2,1)S(1)} %concatenate.11.refs_1_) | copy-start | bytes 663556
  21.0 6.5 %collective-permute-start.6 = (bf16[32,3456]{1,0:T(8,128)(2,1)S(1)}, bf16[32,3456]{1,0:T(8,128)(2,1)S(1)}, u32[]{:S(2)}, u32[]{:S(2)}) collective-permute-start(bf16[32,3456]{1,0:T(8,128)(2,1)S(1)} %concatenate.11.refs_1_), channel_id=1, source_target_pairs={{0,32},{2,34},{4,36},{6,38},{8,40},{10,42},{12,44},{14,46},{16,48}... | collective-permute-start | bytes 663560 | tf_op jit(solution)/shard_map/ppermute | solution.py:135
  22.2 10.0 %collective-permute-start.7 = (bf16[32,3456]{1,0:T(8,128)(2,1)S(1)}, bf16[32,3456]{1,0:T(8,128)(2,1)S(1)}, u32[]{:S(2)}, u32[]{:S(2)}) collective-permute-start(bf16[32,3456]{1,0:T(8,128)(2,1)S(1)} %concatenate.11.refs_1_), channel_id=1, source_target_pairs={{0,64},{2,66},{4,68},{6,70},{8,72},{10,74},{12,76},{14,78},{16,80}... | collective-permute-start | bytes 663560 | tf_op jit(solution)/shard_map/ppermute | solution.py:135
  24.7 7.6 %collective-permute-start.8 = (bf16[32,3456]{1,0:T(8,128)(2,1)S(1)}, bf16[32,3456]{1,0:T(8,128)(2,1)S(1)}, u32[]{:S(2)}, u32[]{:S(2)}) collective-permute-start(bf16[32,3456]{1,0:T(8,128)(2,1)S(1)} %concatenate.11.refs_1_), channel_id=1, source_target_pairs={{0,96},{2,98},{4,100},{6,102},{8,104},{10,106},{12,108},{14,110},{... | collective-permute-start | bytes 663560 | tf_op jit(solution)/shard_map/ppermute | solution.py:135
  27.5 11.8 %copy-start.2 = (bf16[32,3456]{1,0:T(8,128)(2,1)}, bf16[32,3456]{1,0:T(8,128)(2,1)S(1)}, u32[]{:S(2)}) copy-start(bf16[32,3456]{1,0:T(8,128)(2,1)S(1)} %collective-permute-done.6.refs_2_) | copy-start | bytes 663556
  32.2 7.0 %copy-start.3 = (bf16[32,3456]{1,0:T(8,128)(2,1)}, bf16[32,3456]{1,0:T(8,128)(2,1)S(1)}, u32[]{:S(2)}) copy-start(bf16[32,3456]{1,0:T(8,128)(2,1)S(1)} %collective-permute-done.7.refs_3_) | copy-start | bytes 663556
  32.2 7.0 %copy-start.4 = (bf16[32,3456]{1,0:T(8,128)(2,1)}, bf16[32,3456]{1,0:T(8,128)(2,1)S(1)}, u32[]{:S(2)}) copy-start(bf16[32,3456]{1,0:T(8,128)(2,1)S(1)} %collective-permute-done.8.refs_4_) | copy-start | bytes 663556
  32.3 25.9 %all-to-all-start = ((bf16[64,2,3584]{2,1,0:T(2,128)(2,1)}), bf16[64,2,3584]{2,1,0:T(2,128)(2,1)S(1)}, u32[]{:S(2)}, u32[]{:S(2)}) async-start(bf16[64,2,3584]{2,1,0:T(2,128)(2,1)} %reshape.88), calls=%async_computation | async-start | bytes 1835008 | tf_op jit(solution)/shard_map/all_to_all | solution.py:172
  58.5 1.2 %copy-start = (bf16[128,3584]{1,0:T(8,128)(2,1)}, bf16[128,3584]{1,0:T(8,128)(2,1)S(1)}, u32[]{:S(2)}) copy-start(bf16[128,3584]{1,0:T(8,128)(2,1)S(1)} %reshape.89.x_ref) | copy-start | bytes 2752516

commit v15 on v11

--- a/solution.py
+++ b/solution.py
@@ -73,10 +73,17 @@
     return highest[0], summed[0]
 
 
-def average_kernel(w_ref, x_ref, o_ref, s_scr):
+def average_kernel(x_ref, o_ref, w_out_ref, w_scr, s_scr):
     block = o_ref.shape[0]
     flat_len = o_ref.shape[1]
-    s_scr[...] = jnp.dot(w_ref[...], x_ref[:, :flat_len], preferred_element_type=jnp.float32)
+    labels = x_ref[:, flat_len:].astype(jnp.float32).T
+    member, rotation, weight = labels[0:1, :], labels[1:2, :], labels[2:3, :]
+    row = lax.broadcasted_iota(jnp.int32, w_scr.shape, 0)
+    chosen = ((row // block).astype(jnp.float32) == rotation) & ((row % block).astype(jnp.float32) == member)
+    w_scr[...] = jnp.where(chosen, weight, 0.0).astype(w_scr.dtype)
+    class_row = lax.broadcasted_iota(jnp.int32, (block, x_ref.shape[0]), 0).astype(jnp.float32)
+    w_out_ref[...] = jnp.sum(jnp.where(class_row == member, weight, 0.0), axis=1, keepdims=True)
+    s_scr[...] = jnp.dot(w_scr[...], x_ref[:, :flat_len], preferred_element_type=jnp.float32)
     step = 8
     total = None
     for part in range(step):
@@ -154,28 +161,21 @@
     highest, summed = score_all(particle_rows, pieces)
     incoming, highest, summed = lax.optimization_barrier((incoming, highest, summed))
     incoming = incoming.reshape(slot_count, flat_len + label_lanes)
-    labels_in = incoming[:, flat_len : flat_len + 3]
-    labels_in = labels_in.astype(jnp.float32)
-    member_in = labels_in[:, 0]
-    rotation = labels_in[:, 1]
-    weight_of = labels_in[:, 2]
     block = -(-per_owner // 8) * 8
-    angle_grid = jnp.arange(ANGLES, dtype=jnp.float32)
-    member_grid = jnp.arange(block, dtype=jnp.float32)
-    chosen = (angle_grid[:, None, None] == rotation[None, None, :]) & (
-        member_grid[None, :, None] == member_in[None, None, :]
-    )
-    by_angle = jnp.where(chosen, weight_of[None, None, :], 0.0).astype(jnp.bfloat16)
-    by_angle = by_angle.reshape(ANGLES * block, slot_count)
-    partial_sums = pl.pallas_call(
+    partial_sums, partial_weight = pl.pallas_call(
         average_kernel,
-        out_shape=jax.ShapeDtypeStruct((block, flat_len), jnp.float32),
-        scratch_shapes=[pltpu.VMEM((ANGLES * block, flat_len), jnp.float32)],
-    )(by_angle, incoming)
+        out_shape=(
+            jax.ShapeDtypeStruct((block, flat_len), jnp.float32),
+            jax.ShapeDtypeStruct((block, 1), jnp.float32),
+        ),
+        scratch_shapes=[
+            pltpu.VMEM((ANGLES * block, slot_count), jnp.bfloat16),
+            pltpu.VMEM((ANGLES * block, flat_len), jnp.float32),
+        ],
+    )(incoming)
     partial_sums = partial_sums[:per_owner].reshape(per_owner, ANGLES, RADII).transpose(0, 2, 1)
     partial_sums = partial_sums.reshape(per_owner, flat_len)
-    weighted = (member_grid[:per_owner, None] == member_in[None, :]).astype(jnp.float32) * weight_of[None, :]
-    partial_weight = jnp.sum(weighted, axis=1)
+    partial_weight = partial_weight[:per_owner, 0]
     stats = jnp.stack([highest, summed], axis=0)
     slots = jnp.arange(grp_size, dtype=jnp.int32)[:, None, None] == grp_index
     stats = jnp.where(slots, stats[None], 0.0)

time: 67.7 us -> 68.3 us (level)
  local copies, waits for them, and re-layouts: 9.76 us -> 11.3 us
  other arithmetic: 2.88 us -> 1.94 us
    reshape x1, local copies, waits for them, and re-layouts: 0.34 us -> 1.3 us  [local(): incoming = incoming.reshape(slot_count, flat_len + label_lanes)]
    convert_element_type x2 -> x0, other arithmetic: 0.73 us -> none  [the longest x1 0.72 us: local(): jnp.where(chosen, weight_of[None, None, :], 0.0).astype(jnp.bfloat16)]
    unnamed x19 -> x17, local copies, waits for them, and re-layouts: 3.27 us -> 3.26 us
where the time goes in v15:
time: 68.3 us; the launch traced here: 67.9 us
  starting transfers between devices  22.5 us (33%)
  Pallas kernels  16.4 us (24%)
  local copies, waits for them, and re-layouts  11.3 us (17%)
  waiting for transfers between devices  7.82 us (11%)
  blocking collectives  6.69 us (10%)
  other arithmetic  1.94 us (3%)
  between operations  0.82 us (1%)
    ppermute x9, starting transfers between devices, staged_gather(): parts.append(lax.ppermute(rows, axis, pairs))  16.5 us
    pallas_call x1, Pallas kernels, score_all(): pl.pallas_call(functools.partial(score_kernel, scale=scale), out_shape=(j...  13.1 us
    ppermute x9, waiting for transfers between devices, staged_gather(): parts.append(lax.ppermute(rows, axis, pairs))  7.82 us
    psum x1, blocking collectives, local(): lax.psum((partial_sums, partial_weight, stats), 'grp')  6.69 us
    all_to_all x1, starting transfers between devices, local(): lax.all_to_all(outgoing, 'loop', split_axis=0, concat_axis=0, tiled=True)  6 us
    pallas_call x1, Pallas kernels, local(): pl.pallas_call(average_kernel, out_shape=(jax.ShapeDtypeStruct((block, fl...  3.31 us
    unnamed x17, local copies, waits for them, and re-layouts  3.26 us
    reshape x4, local copies, waits for them, and re-layouts, angle_major(): rows.reshape(count, RADII, ANGLES).transpose(0, 2, 1)  2.76 us
  transfers between devices with their start and end apart: 10, of which 3 were waited for; matrix products, arithmetic and copies ran while one was open for 9% of the time, Pallas kernels for 19%

profile of v15, /device:TPU:1, one launch (start us, length us, event | category | flops | bytes accessed | tf_op | source)
XLA Modules:
  0.0 67.9 jit_solution(2054472327651885845)
XLA Ops:
  0.6 0.8 %reshape.38 = bf16[2,48,72]{2,1,0:T(8,128)(2,1)S(1)} reshape(bf16[2,3456]{1,0:T(2,128)(2,1)} %param.6) | data formatting | bytes 27648 | tf_op jit(solution)/shard_map/reshape | solution.py:20
  1.7 2.2 %collective-permute-start = (bf16[2,3456]{1,0:T(2,128)(2,1)S(1)}, bf16[2,3456]{1,0:T(2,128)(2,1)S(1)}, u32[]{:S(2)}, u32[]{:S(2)}) collective-permute-start(bf16[2,3456]{1,0:T(2,128)(2,1)S(1)} %reshape.39), channel_id=1, source_target_pairs={{0,2},{2,4},{4,6},{6,0},{8,10},{10,12},{12,14},{14,8},{16,18},{18,... | collective-permute-start | bytes 41480 | tf_op jit(solution)/shard_map/ppermute | solution.py:123
  3.9 2.6 %collective-permute-start.1 = (bf16[2,3456]{1,0:T(2,128)(2,1)S(1)}, bf16[2,3456]{1,0:T(2,128)(2,1)S(1)}, u32[]{:S(2)}, u32[]{:S(2)}) collective-permute-start(bf16[2,3456]{1,0:T(2,128)(2,1)S(1)} %reshape.39), channel_id=1, source_target_pairs={{0,4},{2,6},{4,0},{6,2},{8,12},{10,14},{12,8},{14,10},{16,20},{18,... | collective-permute-start | bytes 41480 | tf_op jit(solution)/shard_map/ppermute | solution.py:123
  6.5 1.1 %collective-permute-start.2 = (bf16[2,3456]{1,0:T(2,128)(2,1)S(1)}, bf16[2,3456]{1,0:T(2,128)(2,1)S(1)}, u32[]{:S(2)}, u32[]{:S(2)}) collective-permute-start(bf16[2,3456]{1,0:T(2,128)(2,1)S(1)} %reshape.39), channel_id=1, source_target_pairs={{0,6},{2,0},{4,2},{6,4},{8,14},{10,8},{12,10},{14,12},{16,22},{18,... | collective-permute-start | bytes 41480 | tf_op jit(solution)/shard_map/ppermute | solution.py:123
  7.6 1.9 %copy.18 = bf16[128,3456]{0,1:T(8,128)(2,1)S(1)} copy(bf16[128,3456]{1,0:T(8,128)(2,1)} %param.5) | data formatting | bytes 1769472 | tf_op args[0]
  9.6 0.5 copy-done.7
  10.3 0.2 select_reduce_fusion
  10.5 0.3 constant_dynamic-slice_fusion.1
  10.8 0.1 copy-done.3
  11.1 1.7 %collective-permute-start.3 = (bf16[8,3456]{1,0:T(8,128)(2,1)S(1)}, bf16[8,3456]{1,0:T(8,128)(2,1)S(1)}, u32[]{:S(2)}, u32[]{:S(2)}) collective-permute-start(bf16[8,3456]{1,0:T(8,128)(2,1)S(1)} %pad_maximum_fusion), channel_id=1, source_target_pairs={{0,8},{2,10},{4,12},{6,14},{8,16},{10,18},{12,20},{14,22},{16,24},... | collective-permute-start | bytes 165896 | tf_op jit(solution)/shard_map/ppermute | solution.py:123
  12.8 3.3 %collective-permute-start.4 = (bf16[8,3456]{1,0:T(8,128)(2,1)S(1)}, bf16[8,3456]{1,0:T(8,128)(2,1)S(1)}, u32[]{:S(2)}, u32[]{:S(2)}) collective-permute-start(bf16[8,3456]{1,0:T(8,128)(2,1)S(1)} %pad_maximum_fusion), channel_id=1, source_target_pairs={{0,16},{2,18},{4,20},{6,22},{8,24},{10,26},{12,28},{14,30},{16,0},... | collective-permute-start | bytes 165896 | tf_op jit(solution)/shard_map/ppermute | solution.py:123
  16.1 0.7 %collective-permute-start.5 = (bf16[8,3456]{1,0:T(8,128)(2,1)S(1)}, bf16[8,3456]{1,0:T(8,128)(2,1)S(1)}, u32[]{:S(2)}, u32[]{:S(2)}) collective-permute-start(bf16[8,3456]{1,0:T(8,128)(2,1)S(1)} %pad_maximum_fusion), channel_id=1, source_target_pairs={{0,24},{2,26},{4,28},{6,30},{8,0},{10,2},{12,4},{14,6},{16,8},{18,... | collective-permute-start | bytes 165896 | tf_op jit(solution)/shard_map/ppermute | solution.py:123
  16.9 1.5 %collective-permute-done.4 = bf16[8,3456]{1,0:T(8,128)(2,1)S(1)} collective-permute-done((bf16[8,3456]{1,0:T(8,128)(2,1)S(1)}, bf16[8,3456]{1,0:T(8,128)(2,1)S(1)}, u32[]{:S(2)}, u32[]{:S(2)}) %collective-permute-start.4) | collective-permute-done | bytes 55328 | tf_op jit(solution)/shard_map/ppermute | solution.py:123
  18.3 1.7 %collective-permute-done.5 = bf16[8,3456]{1,0:T(8,128)(2,1)S(1)} collective-permute-done((bf16[8,3456]{1,0:T(8,128)(2,1)S(1)}, bf16[8,3456]{1,0:T(8,128)(2,1)S(1)}, u32[]{:S(2)}, u32[]{:S(2)}) %collective-permute-start.5) | collective-permute-done | bytes 55328 | tf_op jit(solution)/shard_map/ppermute | solution.py:123
  20.0 0.1 concatenate.11.refs_1_
  20.1 1.3 %collective-permute-start.6 = (bf16[32,3456]{1,0:T(8,128)(2,1)S(1)}, bf16[32,3456]{1,0:T(8,128)(2,1)S(1)}, u32[]{:S(2)}, u32[]{:S(2)}) collective-permute-start(bf16[32,3456]{1,0:T(8,128)(2,1)S(1)} %concatenate.11.refs_1_), channel_id=1, source_target_pairs={{0,32},{2,34},{4,36},{6,38},{8,40},{10,42},{12,44},{14,46},{16,48}... | collective-permute-start | bytes 663560 | tf_op jit(solution)/shard_map/ppermute | solution.py:123
  21.4 2.5 %collective-permute-start.7 = (bf16[32,3456]{1,0:T(8,128)(2,1)S(1)}, bf16[32,3456]{1,0:T(8,128)(2,1)S(1)}, u32[]{:S(2)}, u32[]{:S(2)}) collective-permute-start(bf16[32,3456]{1,0:T(8,128)(2,1)S(1)} %concatenate.11.refs_1_), channel_id=1, source_target_pairs={{0,64},{2,66},{4,68},{6,70},{8,72},{10,74},{12,76},{14,78},{16,80}... | collective-permute-start | bytes 663560 | tf_op jit(solution)/shard_map/ppermute | solution.py:123
  23.9 1.2 %collective-permute-start.8 = (bf16[32,3456]{1,0:T(8,128)(2,1)S(1)}, bf16[32,3456]{1,0:T(8,128)(2,1)}, u32[]{:S(2)}, u32[]{:S(2)}) collective-permute-start(bf16[32,3456]{1,0:T(8,128)(2,1)S(1)} %concatenate.11.refs_1_), channel_id=1, source_target_pairs={{0,96},{2,98},{4,100},{6,102},{8,104},{10,106},{12,108},{14,110},{... | collective-permute-start | bytes 663560 | tf_op jit(solution)/shard_map/ppermute | solution.py:123
  25.0 0.4 convolution_convert_fusion
  25.4 1.3 %reshape.42 = bf16[64,2,3584]{2,1,0:T(2,128)(2,1)} reshape(bf16[128,3584]{1,0:T(8,128)(2,1)S(1)} %convolution_convert_fusion) | data formatting | bytes 1835008 | tf_op jit(solution)/shard_map/reshape | solution.py:158
  26.8 4.7 %collective-permute-done.7.refs_3_ = bf16[32,3456]{1,0:T(8,128)(2,1)S(1)} collective-permute-done((bf16[32,3456]{1,0:T(8,128)(2,1)S(1)}, bf16[32,3456]{1,0:T(8,128)(2,1)S(1)}, u32[]{:S(2)}, u32[]{:S(2)}) %collective-permute-start.7) | collective-permute-done | bytes 221216 | tf_op jit(solution)/shard_map/ppermute | solution.py:123
  31.4 0.7 copy-done.2
  32.1 6.0 %all-to-all-start = ((bf16[64,2,3584]{2,1,0:T(2,128)(2,1)}), bf16[64,2,3584]{2,1,0:T(2,128)(2,1)S(1)}, u32[]{:S(2)}, u32[]{:S(2)}) async-start(bf16[64,2,3584]{2,1,0:T(2,128)(2,1)} %reshape.42), calls=%async_computation | async-start | bytes 1835008 | tf_op jit(solution)/shard_map/all_to_all | solution.py:160
  38.1 1.7 %copy.20.refs_0_ = bf16[128,3456]{1,0:T(8,128)(2,1)} copy(bf16[128,3456]{0,1:T(8,128)(2,1)S(1)} %bitcast.29) | data formatting | bytes 1769472 | tf_op jit(solution)/shard_map/reshape | solution.py:20
  39.8 13.1 %shard_map.68 = (f32[1,128]{1,0:T(1,128)}, f32[1,128]{1,0:T(1,128)}) custom-call(bf16[128,3456]{1,0:T(8,128)(2,1)} %copy.20.refs_0_, bf16[32,3456]{1,0:T(8,128)(2,1)} %copy-done, bf16[32,3456]{1,0:T(8,128)(2,1)} %copy-done.1, bf16[32,3456]{1,0:T(8,128)(2,1)} %copy-done.2, bf16[32,3456]{1,0:T(8,128)(2,1)} %collective-permute-done.8.refs_4_), custom_call_target="tpu_custom_call" | custom-call | tf_op jit(solution)/shard_map/pallas_call | solution.py:62
  53.0 1.3 %reshape.43.x_ref = bf16[128,3584]{1,0:T(8,128)(2,1)} reshape(bf16[64,2,3584]{2,1,0:T(2,128)(2,1)S(1)} %all-to-all-done) | data formatting | bytes 1835008 | tf_op jit(solution)/shard_map/reshape | solution.py:163
  54.3 3.3 %shard_map.69 = (f32[8,3456]{1,0:T(8,128)}, f32[8,1]{1,0:T(8,128)}) custom-call(bf16[128,3584]{1,0:T(8,128)(2,1)} %reshape.43.x_ref), custom_call_target="tpu_custom_call" | custom-call | tf_op jit(solution)/shard_map/pallas_call | solution.py:165
  57.6 0.9 %slice.15 = f32[4,3456]{1,0:T(4,128)S(1)} slice(f32[8,3456]{1,0:T(8,128)} %get-tuple-element.24), slice={[0:4], [0:3456]} | slice | bytes 110592 | tf_op jit(solution)/shard_map/slice | solution.py:176
  58.8 0.8 %slice_reduce_fusion = f32[4]{0:T(128)S(1)} fusion(f32[8,1]{1,0:T(8,128)} %get-tuple-element.25), kind=kLoop, calls=%fused_computation.17 | loop fusion | bytes 32 | tf_op jit(solution)/shard_map/slice | solution.py:178
  59.7 6.7 %all-reduce.1 = (f32[2,2,128]{2,0,1:T(2,128)S(1)}, f32[4,3456]{1,0:T(4,128)S(1)}, f32[4]{0:T(128)S(1)}) all-reduce(f32[2,2,128]{2,0,1:T(2,128)S(1)} %broadcast_select_fusion, f32[4,3456]{1,0:T(4,128)S(1)} %reshape.45, f32[4]{0:T(128)S(1)} %slice_reduce_fusion), channel_id=1, replica_groups=mesh['loop'=64,'grp'=2] {'grp'}, use_global_device_ids=true, to_apply=%region_2.3 | all-reduce | flops 14340 | bytes 114720 | tf_op jit(solution)/shard_map/psum | solution.py:182
  66.6 0.5 log_add_fusion
  67.2 0.7 %dynamic-slice_divide_fusion = f32[2,3456]{1,0:T(2,128)} fusion(f32[4,3456]{1,0:T(4,128)S(1)} %get-tuple-element.27, s32[]{:T(128)S(6)} %select_n.28, f32[2]{0:T(128)S(1)} %dynamic_slice.15), kind=kLoop, calls=%fused_computation.16 | loop fusion | flops 6912 | bytes 55308 | tf_op jit(solution)/shard_map/div | solution.py:185
  (39 shorter events, 1.3 us)
Async XLA Ops:
  1.7 9.3 %collective-permute-start = (bf16[2,3456]{1,0:T(2,128)(2,1)S(1)}, bf16[2,3456]{1,0:T(2,128)(2,1)S(1)}, u32[]{:S(2)}, u32[]{:S(2)}) collective-permute-start(bf16[2,3456]{1,0:T(2,128)(2,1)S(1)} %reshape.39), channel_id=1, source_target_pairs={{0,2},{2,4},{4,6},{6,0},{8,10},{10,12},{12,14},{14,8},{16,18},{18,... | collective-permute-start | bytes 41480 | tf_op jit(solution)/shard_map/ppermute | solution.py:123
  3.9 7.1 %collective-permute-start.1 = (bf16[2,3456]{1,0:T(2,128)(2,1)S(1)}, bf16[2,3456]{1,0:T(2,128)(2,1)S(1)}, u32[]{:S(2)}, u32[]{:S(2)}) collective-permute-start(bf16[2,3456]{1,0:T(2,128)(2,1)S(1)} %reshape.39), channel_id=1, source_target_pairs={{0,4},{2,6},{4,0},{6,2},{8,12},{10,14},{12,8},{14,10},{16,20},{18,... | collective-permute-start | bytes 41480 | tf_op jit(solution)/shard_map/ppermute | solution.py:123
  6.5 4.5 %collective-permute-start.2 = (bf16[2,3456]{1,0:T(2,128)(2,1)S(1)}, bf16[2,3456]{1,0:T(2,128)(2,1)S(1)}, u32[]{:S(2)}, u32[]{:S(2)}) collective-permute-start(bf16[2,3456]{1,0:T(2,128)(2,1)S(1)} %reshape.39), channel_id=1, source_target_pairs={{0,6},{2,0},{4,2},{6,4},{8,14},{10,8},{12,10},{14,12},{16,22},{18,... | collective-permute-start | bytes 41480 | tf_op jit(solution)/shard_map/ppermute | solution.py:123
  9.5 0.7 copy-start.7
  10.3 0.7 copy-start.3
  10.3 0.7 copy-start.4
  11.1 5.8 %collective-permute-start.3 = (bf16[8,3456]{1,0:T(8,128)(2,1)S(1)}, bf16[8,3456]{1,0:T(8,128)(2,1)S(1)}, u32[]{:S(2)}, u32[]{:S(2)}) collective-permute-start(bf16[8,3456]{1,0:T(8,128)(2,1)S(1)} %pad_maximum_fusion), channel_id=1, source_target_pairs={{0,8},{2,10},{4,12},{6,14},{8,16},{10,18},{12,20},{14,22},{16,24},... | collective-permute-start | bytes 165896 | tf_op jit(solution)/shard_map/ppermute | solution.py:123
  12.8 5.5 %collective-permute-start.4 = (bf16[8,3456]{1,0:T(8,128)(2,1)S(1)}, bf16[8,3456]{1,0:T(8,128)(2,1)S(1)}, u32[]{:S(2)}, u32[]{:S(2)}) collective-permute-start(bf16[8,3456]{1,0:T(8,128)(2,1)S(1)} %pad_maximum_fusion), channel_id=1, source_target_pairs={{0,16},{2,18},{4,20},{6,22},{8,24},{10,26},{12,28},{14,30},{16,0},... | collective-permute-start | bytes 165896 | tf_op jit(solution)/shard_map/ppermute | solution.py:123
  16.1 3.9 %collective-permute-start.5 = (bf16[8,3456]{1,0:T(8,128)(2,1)S(1)}, bf16[8,3456]{1,0:T(8,128)(2,1)S(1)}, u32[]{:S(2)}, u32[]{:S(2)}) collective-permute-start(bf16[8,3456]{1,0:T(8,128)(2,1)S(1)} %pad_maximum_fusion), channel_id=1, source_target_pairs={{0,24},{2,26},{4,28},{6,30},{8,0},{10,2},{12,4},{14,6},{16,8},{18,... | collective-permute-start | bytes 165896 | tf_op jit(solution)/shard_map/ppermute | solution.py:123
  20.1 5.3 %copy-start = (bf16[32,3456]{1,0:T(8,128)(2,1)}, bf16[32,3456]{1,0:T(8,128)(2,1)S(1)}, u32[]{:S(2)}) copy-start(bf16[32,3456]{1,0:T(8,128)(2,1)S(1)} %concatenate.11.refs_1_) | copy-start | bytes 663556
  20.1 6.6 %collective-permute-start.6 = (bf16[32,3456]{1,0:T(8,128)(2,1)S(1)}, bf16[32,3456]{1,0:T(8,128)(2,1)S(1)}, u32[]{:S(2)}, u32[]{:S(2)}) collective-permute-start(bf16[32,3456]{1,0:T(8,128)(2,1)S(1)} %concatenate.11.refs_1_), channel_id=1, source_target_pairs={{0,32},{2,34},{4,36},{6,38},{8,40},{10,42},{12,44},{14,46},{16,48}... | collective-permute-start | bytes 663560 | tf_op jit(solution)/shard_map/ppermute | solution.py:123
  21.4 10.0 %collective-permute-start.7 = (bf16[32,3456]{1,0:T(8,128)(2,1)S(1)}, bf16[32,3456]{1,0:T(8,128)(2,1)S(1)}, u32[]{:S(2)}, u32[]{:S(2)}) collective-permute-start(bf16[32,3456]{1,0:T(8,128)(2,1)S(1)} %concatenate.11.refs_1_), channel_id=1, source_target_pairs={{0,64},{2,66},{4,68},{6,70},{8,72},{10,74},{12,76},{14,78},{16,80}... | collective-permute-start | bytes 663560 | tf_op jit(solution)/shard_map/ppermute | solution.py:123
  23.9 7.6 %collective-permute-start.8 = (bf16[32,3456]{1,0:T(8,128)(2,1)S(1)}, bf16[32,3456]{1,0:T(8,128)(2,1)}, u32[]{:S(2)}, u32[]{:S(2)}) collective-permute-start(bf16[32,3456]{1,0:T(8,128)(2,1)S(1)} %concatenate.11.refs_1_), channel_id=1, source_target_pairs={{0,96},{2,98},{4,100},{6,102},{8,104},{10,106},{12,108},{14,110},{... | collective-permute-start | bytes 663560 | tf_op jit(solution)/shard_map/ppermute | solution.py:123
  26.8 4.7 %copy-start.1 = (bf16[32,3456]{1,0:T(8,128)(2,1)}, bf16[32,3456]{1,0:T(8,128)(2,1)S(1)}, u32[]{:S(2)}) copy-start(bf16[32,3456]{1,0:T(8,128)(2,1)S(1)} %collective-permute-done.6.refs_2_) | copy-start | bytes 663556
  31.4 0.7 %copy-start.2 = (bf16[32,3456]{1,0:T(8,128)(2,1)}, bf16[32,3456]{1,0:T(8,128)(2,1)S(1)}, u32[]{:S(2)}) copy-start(bf16[32,3456]{1,0:T(8,128)(2,1)S(1)} %collective-permute-done.7.refs_3_) | copy-start | bytes 663556
  32.1 20.9 %all-to-all-start = ((bf16[64,2,3584]{2,1,0:T(2,128)(2,1)}), bf16[64,2,3584]{2,1,0:T(2,128)(2,1)S(1)}, u32[]{:S(2)}, u32[]{:S(2)}) async-start(bf16[64,2,3584]{2,1,0:T(2,128)(2,1)} %reshape.42), calls=%async_computation | async-start | bytes 1835008 | tf_op jit(solution)/shard_map/all_to_all | solution.py:160
  54.3 5.4 %copy-start.5 = (f32[1,128]{1,0:T(1,128)S(1)}, f32[1,128]{1,0:T(1,128)}, u32[]{:S(2)}) copy-start(f32[1,128]{1,0:T(1,128)} %get-tuple-element.19) | copy-start | bytes 1540
  54.3 5.4 %copy-start.6 = (f32[1,128]{1,0:T(1,128)S(1)}, f32[1,128]{1,0:T(1,128)}, u32[]{:S(2)}) copy-start(f32[1,128]{1,0:T(1,128)} %get-tuple-element.20) | copy-start | bytes 1540

commit v16 on v11

--- a/solution.py
+++ b/solution.py
@@ -176,14 +176,38 @@
     partial_sums = partial_sums.reshape(per_owner, flat_len)
     weighted = (member_grid[:per_owner, None] == member_in[None, :]).astype(jnp.float32) * weight_of[None, :]
     partial_weight = jnp.sum(weighted, axis=1)
+    own_classes = references.shape[0]
     stats = jnp.stack([highest, summed], axis=0)
-    slots = jnp.arange(grp_size, dtype=jnp.int32)[:, None, None] == grp_index
-    stats = jnp.where(slots, stats[None], 0.0)
-    partial_sums, partial_weight, stats = lax.psum((partial_sums, partial_weight, stats), "grp")
-    class_sums = lax.dynamic_slice_in_dim(partial_sums, grp_index * references.shape[0], references.shape[0], 0)
-    class_weight = lax.dynamic_slice_in_dim(partial_weight, grp_index * references.shape[0], references.shape[0], 0)
+    if grp_size == 2:
+        partner = 1 - grp_index
+        weight_row = jnp.zeros((1, flat_len), jnp.float32)
+        weight_row = lax.dynamic_update_slice_in_dim(
+            weight_row, lax.dynamic_slice_in_dim(partial_weight, partner * own_classes, own_classes, 0)[None], 0, 1
+        )
+        stat_rows = jnp.pad(
+            lax.dynamic_slice_in_dim(stats, partner * half_rows, half_rows, 1), ((0, 0), (0, flat_len - half_rows))
+        )
+        sent = jnp.concatenate(
+            [lax.dynamic_slice_in_dim(partial_sums, partner * own_classes, own_classes, 0), weight_row, stat_rows], axis=0
+        )
+        got = lax.ppermute(sent, "grp", [(0, 1), (1, 0)])
+        class_sums = lax.dynamic_slice_in_dim(partial_sums, grp_index * own_classes, own_classes, 0) + got[:own_classes]
+        class_weight = (
+            lax.dynamic_slice_in_dim(partial_weight, grp_index * own_classes, own_classes, 0)
+            + got[own_classes, :own_classes]
+        )
+        stats = jnp.stack(
+            [lax.dynamic_slice_in_dim(stats, grp_index * half_rows, half_rows, 1), got[own_classes + 1 :, :half_rows]],
+            axis=0,
+        )
+    else:
+        slots = jnp.arange(grp_size, dtype=jnp.int32)[:, None, None] == grp_index
+        stats = jnp.where(slots, stats[None], 0.0)
+        partial_sums, partial_weight, stats = lax.psum((partial_sums, partial_weight, stats), "grp")
+        class_sums = lax.dynamic_slice_in_dim(partial_sums, grp_index * own_classes, own_classes, 0)
+        class_weight = lax.dynamic_slice_in_dim(partial_weight, grp_index * own_classes, own_classes, 0)
+        stats = lax.dynamic_slice_in_dim(stats, grp_index * half_rows, half_rows, 2)
     class_average = class_sums / class_weight[:, None]
-    stats = lax.dynamic_slice_in_dim(stats, grp_index * half_rows, half_rows, 2)
     highest = jnp.max(stats[:, 0], axis=0)
     summed = jnp.sum(stats[:, 1] * jnp.exp(stats[:, 0] - highest[None, :]), axis=0)
     log_evidence = highest + jnp.log(summed)

time: 67.7 us -> 65.4 us (0.966)
  blocking collectives: 6.66 us -> 0 us
  starting transfers between devices: 22.5 us -> 25.9 us
  waiting for transfers between devices: 7.85 us -> 8.81 us
    psum x1 -> x0, blocking collectives: 6.66 us -> none  [local(): lax.psum((partial_sums, partial_weight, stats), 'grp')]
    ppermute x0 -> x1, starting transfers between devices: none -> 3.37 us  [local(): got = lax.ppermute(sent, 'grp', [(0, 1), (1, 0)])]
    ppermute x0 -> x1, waiting for transfers between devices: none -> 0.96 us  [local(): got = lax.ppermute(sent, 'grp', [(0, 1), (1, 0)])]
  transfers between devices with their start and end apart: 10 -> 11, of which waited for: 3 -> 4; matrix products, arithmetic and copies ran while one was open for 9% -> 9% of each run, Pallas kernels for 19% -> 20%
where the time goes in v16:
time: 65.4 us; the launch traced here: 65 us
  starting transfers between devices  25.9 us (40%)
  Pallas kernels  16.4 us (25%)
  local copies, waits for them, and re-layouts  9.85 us (15%)
  waiting for transfers between devices  8.81 us (13%)
  other arithmetic  2.76 us (4%)
  between operations  0.85 us (1%)
    ppermute x9, starting transfers between devices, staged_gather(): parts.append(lax.ppermute(rows, axis, pairs))  16.5 us
    pallas_call x1, Pallas kernels, score_all(): pl.pallas_call(functools.partial(score_kernel, scale=scale), out_shape=(j...  13.1 us
    ppermute x9, waiting for transfers between devices, staged_gather(): parts.append(lax.ppermute(rows, axis, pairs))  7.84 us
    all_to_all x1, starting transfers between devices, local(): lax.all_to_all(outgoing, 'loop', split_axis=0, concat_axis=0, tiled=True)  6.01 us
    ppermute x1, starting transfers between devices, local(): got = lax.ppermute(sent, 'grp', [(0, 1), (1, 0)])  3.37 us
    pallas_call x1, Pallas kernels, local(): pl.pallas_call(average_kernel, out_shape=jax.ShapeDtypeStruct((block, fla...  3.29 us
    unnamed x19, local copies, waits for them, and re-layouts  3.25 us
    reshape x4, local copies, waits for them, and re-layouts, angle_major(): rows.reshape(count, RADII, ANGLES).transpose(0, 2, 1)  2.77 us
  transfers between devices with their start and end apart: 11, of which 4 were waited for; matrix products, arithmetic and copies ran while one was open for 9% of the time, Pallas kernels for 20%

profile of v16, /device:TPU:1, one launch (start us, length us, event | category | flops | bytes accessed | tf_op | source)
XLA Modules:
  0.0 65.0 jit_solution(3858442208624809563)
XLA Ops:
  0.6 0.8 %reshape.92 = bf16[2,48,72]{2,1,0:T(8,128)(2,1)S(1)} reshape(bf16[2,3456]{1,0:T(2,128)(2,1)} %param.6) | data formatting | bytes 27648 | tf_op jit(solution)/shard_map/reshape | solution.py:20
  1.7 2.2 %collective-permute-start = (bf16[2,3456]{1,0:T(2,128)(2,1)S(1)}, bf16[2,3456]{1,0:T(2,128)(2,1)S(1)}, u32[]{:S(2)}, u32[]{:S(2)}) collective-permute-start(bf16[2,3456]{1,0:T(2,128)(2,1)S(1)} %reshape.93), channel_id=1, source_target_pairs={{0,2},{2,4},{4,6},{6,0},{8,10},{10,12},{12,14},{14,8},{16,18},{18,... | collective-permute-start | bytes 41480 | tf_op jit(solution)/shard_map/ppermute | solution.py:116
  3.9 2.6 %collective-permute-start.1 = (bf16[2,3456]{1,0:T(2,128)(2,1)S(1)}, bf16[2,3456]{1,0:T(2,128)(2,1)S(1)}, u32[]{:S(2)}, u32[]{:S(2)}) collective-permute-start(bf16[2,3456]{1,0:T(2,128)(2,1)S(1)} %reshape.93), channel_id=1, source_target_pairs={{0,4},{2,6},{4,0},{6,2},{8,12},{10,14},{12,8},{14,10},{16,20},{18,... | collective-permute-start | bytes 41480 | tf_op jit(solution)/shard_map/ppermute | solution.py:116
  6.5 1.1 %collective-permute-start.2 = (bf16[2,3456]{1,0:T(2,128)(2,1)S(1)}, bf16[2,3456]{1,0:T(2,128)(2,1)S(1)}, u32[]{:S(2)}, u32[]{:S(2)}) collective-permute-start(bf16[2,3456]{1,0:T(2,128)(2,1)S(1)} %reshape.93), channel_id=1, source_target_pairs={{0,6},{2,0},{4,2},{6,4},{8,14},{10,8},{12,10},{14,12},{16,22},{18,... | collective-permute-start | bytes 41480 | tf_op jit(solution)/shard_map/ppermute | solution.py:116
  7.6 1.9 %copy.19 = bf16[128,3456]{0,1:T(8,128)(2,1)S(1)} copy(bf16[128,3456]{1,0:T(8,128)(2,1)} %param.5) | data formatting | bytes 1769472 | tf_op args[0]
  9.6 0.5 copy-done.8
  10.5 0.3 constant_dynamic-slice_fusion.3
  11.1 1.7 %collective-permute-start.3 = (bf16[8,3456]{1,0:T(8,128)(2,1)S(1)}, bf16[8,3456]{1,0:T(8,128)(2,1)S(1)}, u32[]{:S(2)}, u32[]{:S(2)}) collective-permute-start(bf16[8,3456]{1,0:T(8,128)(2,1)S(1)} %pad_maximum_fusion), channel_id=1, source_target_pairs={{0,8},{2,10},{4,12},{6,14},{8,16},{10,18},{12,20},{14,22},{16,24},... | collective-permute-start | bytes 165896 | tf_op jit(solution)/shard_map/ppermute | solution.py:116
  12.8 3.3 %collective-permute-start.4 = (bf16[8,3456]{1,0:T(8,128)(2,1)S(1)}, bf16[8,3456]{1,0:T(8,128)(2,1)S(1)}, u32[]{:S(2)}, u32[]{:S(2)}) collective-permute-start(bf16[8,3456]{1,0:T(8,128)(2,1)S(1)} %pad_maximum_fusion), channel_id=1, source_target_pairs={{0,16},{2,18},{4,20},{6,22},{8,24},{10,26},{12,28},{14,30},{16,0},... | collective-permute-start | bytes 165896 | tf_op jit(solution)/shard_map/ppermute | solution.py:116
  16.1 0.7 %collective-permute-start.5 = (bf16[8,3456]{1,0:T(8,128)(2,1)S(1)}, bf16[8,3456]{1,0:T(8,128)(2,1)S(1)}, u32[]{:S(2)}, u32[]{:S(2)}) collective-permute-start(bf16[8,3456]{1,0:T(8,128)(2,1)S(1)} %pad_maximum_fusion), channel_id=1, source_target_pairs={{0,24},{2,26},{4,28},{6,30},{8,0},{10,2},{12,4},{14,6},{16,8},{18,... | collective-permute-start | bytes 165896 | tf_op jit(solution)/shard_map/ppermute | solution.py:116
  16.9 1.5 %collective-permute-done.4 = bf16[8,3456]{1,0:T(8,128)(2,1)S(1)} collective-permute-done((bf16[8,3456]{1,0:T(8,128)(2,1)S(1)}, bf16[8,3456]{1,0:T(8,128)(2,1)S(1)}, u32[]{:S(2)}, u32[]{:S(2)}) %collective-permute-start.4) | collective-permute-done | bytes 55328 | tf_op jit(solution)/shard_map/ppermute | solution.py:116
  18.3 1.7 %collective-permute-done.5 = bf16[8,3456]{1,0:T(8,128)(2,1)S(1)} collective-permute-done((bf16[8,3456]{1,0:T(8,128)(2,1)S(1)}, bf16[8,3456]{1,0:T(8,128)(2,1)S(1)}, u32[]{:S(2)}, u32[]{:S(2)}) %collective-permute-start.5) | collective-permute-done | bytes 55328 | tf_op jit(solution)/shard_map/ppermute | solution.py:116
  20.1 1.3 %collective-permute-start.6 = (bf16[32,3456]{1,0:T(8,128)(2,1)S(1)}, bf16[32,3456]{1,0:T(8,128)(2,1)S(1)}, u32[]{:S(2)}, u32[]{:S(2)}) collective-permute-start(bf16[32,3456]{1,0:T(8,128)(2,1)S(1)} %concatenate.14.refs_1_), channel_id=1, source_target_pairs={{0,32},{2,34},{4,36},{6,38},{8,40},{10,42},{12,44},{14,46},{16,48}... | collective-permute-start | bytes 663560 | tf_op jit(solution)/shard_map/ppermute | solution.py:116
  21.4 2.5 %collective-permute-start.7 = (bf16[32,3456]{1,0:T(8,128)(2,1)S(1)}, bf16[32,3456]{1,0:T(8,128)(2,1)S(1)}, u32[]{:S(2)}, u32[]{:S(2)}) collective-permute-start(bf16[32,3456]{1,0:T(8,128)(2,1)S(1)} %concatenate.14.refs_1_), channel_id=1, source_target_pairs={{0,64},{2,66},{4,68},{6,70},{8,72},{10,74},{12,76},{14,78},{16,80}... | collective-permute-start | bytes 663560 | tf_op jit(solution)/shard_map/ppermute | solution.py:116
  23.9 1.2 %collective-permute-start.8 = (bf16[32,3456]{1,0:T(8,128)(2,1)S(1)}, bf16[32,3456]{1,0:T(8,128)(2,1)}, u32[]{:S(2)}, u32[]{:S(2)}) collective-permute-start(bf16[32,3456]{1,0:T(8,128)(2,1)S(1)} %concatenate.14.refs_1_), channel_id=1, source_target_pairs={{0,96},{2,98},{4,100},{6,102},{8,104},{10,106},{12,108},{14,110},{... | collective-permute-start | bytes 663560 | tf_op jit(solution)/shard_map/ppermute | solution.py:116
  25.0 0.4 convolution_convert_fusion
  25.4 1.3 %reshape.96 = bf16[64,2,3584]{2,1,0:T(2,128)(2,1)} reshape(bf16[128,3584]{1,0:T(8,128)(2,1)S(1)} %convolution_convert_fusion) | data formatting | bytes 1835008 | tf_op jit(solution)/shard_map/reshape | solution.py:151
  26.7 4.7 %collective-permute-done.7.refs_3_ = bf16[32,3456]{1,0:T(8,128)(2,1)S(1)} collective-permute-done((bf16[32,3456]{1,0:T(8,128)(2,1)S(1)}, bf16[32,3456]{1,0:T(8,128)(2,1)S(1)}, u32[]{:S(2)}, u32[]{:S(2)}) %collective-permute-start.7) | collective-permute-done | bytes 221216 | tf_op jit(solution)/shard_map/ppermute | solution.py:116
  31.4 0.7 %copy-done.3 = bf16[32,3456]{1,0:T(8,128)(2,1)} copy-done((bf16[32,3456]{1,0:T(8,128)(2,1)}, bf16[32,3456]{1,0:T(8,128)(2,1)S(1)}, u32[]{:S(2)}) %copy-start.3) | copy-done | bytes 221208
  32.1 6.0 %all-to-all-start = ((bf16[64,2,3584]{2,1,0:T(2,128)(2,1)}), bf16[64,2,3584]{2,1,0:T(2,128)(2,1)S(1)}, u32[]{:S(2)}, u32[]{:S(2)}) async-start(bf16[64,2,3584]{2,1,0:T(2,128)(2,1)} %reshape.96), calls=%async_computation | async-start | bytes 1835008 | tf_op jit(solution)/shard_map/all_to_all | solution.py:153
  38.1 1.7 %copy.21.refs_0_ = bf16[128,3456]{1,0:T(8,128)(2,1)} copy(bf16[128,3456]{0,1:T(8,128)(2,1)S(1)} %bitcast.32) | data formatting | bytes 1769472 | tf_op jit(solution)/shard_map/reshape | solution.py:20
  39.8 13.1 %shard_map.68 = (f32[1,128]{1,0:T(1,128)}, f32[1,128]{1,0:T(1,128)}) custom-call(bf16[128,3456]{1,0:T(8,128)(2,1)} %copy.21.refs_0_, bf16[32,3456]{1,0:T(8,128)(2,1)} %copy-done.1, bf16[32,3456]{1,0:T(8,128)(2,1)} %copy-done.2, bf16[32,3456]{1,0:T(8,128)(2,1)} %copy-done.3, bf16[32,3456]{1,0:T(8,128)(2,1)} %collective-permute-done.8.refs_4_), custom_call_target="tpu_custom_call" | custom-call | tf_op jit(solution)/shard_map/pallas_call | solution.py:62
  53.0 0.3 reshape.97.x_ref
  53.4 0.2 slice_reduce_fusion.2
  53.6 0.7 %select_convert_fusion.w_ref = bf16[576,128]{1,0:T(8,128)(2,1)} fusion(f32[128]{0:T(128)S(1)} %get-tuple-element.23, pred[8,128]{1,0:T(8,128)(4,1)S(1)} %iota_compare_fusion.8, pred[72,128]{1,0:T(8,128)(4,1)S(1)} %iota_compare_fusion.6), kind=kLoop, calls=%fused_computation.4 | loop fusion | flops 147456 | bytes 158208 | tf_op jit(solution)/shard_map/convert_element_type | solution.py:168
  54.4 3.3 %shard_map.69 = f32[8,3456]{1,0:T(8,128)} custom-call(bf16[576,128]{1,0:T(8,128)(2,1)} %select_convert_fusion.w_ref, bf16[128,3584]{1,0:T(8,128)(2,1)} %copy-done), custom_call_target="tpu_custom_call" | custom-call | tf_op jit(solution)/shard_map/pallas_call | solution.py:170
  57.6 0.9 %slice.49 = f32[4,3456]{1,0:T(4,128)S(1)} slice(f32[8,3456]{1,0:T(8,128)} %shard_map.69), slice={[0:4], [0:3456]} | slice | bytes 110592 | tf_op jit(solution)/shard_map/slice | solution.py:175
  58.9 0.2 select_reduce_fusion.1
  59.3 3.4 %collective-permute-start.9 = (f32[5,3456]{1,0:T(8,128)S(1)}, f32[5,3456]{1,0:T(8,128)S(1)}, u32[]{:S(2)}, u32[]{:S(2)}) collective-permute-start(f32[5,3456]{1,0:T(8,128)S(1)} %select_maximum_fusion), channel_id=1, source_target_pairs={{0,1},{1,0},{2,3},{3,2},{4,5},{5,4},{6,7},{7,6},{8,9},{9,8},{10,11... | collective-permute-start | bytes 207368 | tf_op jit(solution)/shard_map/ppermute | solution.py:193
  62.7 1.0 %collective-permute-done.9 = f32[5,3456]{1,0:T(8,128)S(1)} collective-permute-done((f32[5,3456]{1,0:T(8,128)S(1)}, f32[5,3456]{1,0:T(8,128)S(1)}, u32[]{:S(2)}, u32[]{:S(2)}) %collective-permute-start.9) | collective-permute-done | bytes 69152 | tf_op jit(solution)/shard_map/ppermute | solution.py:193
  63.7 0.5 log_add_fusion
  64.3 0.7 %fusion.11 = f32[2,3456]{1,0:T(2,128)} fusion(f32[5,3456]{1,0:T(8,128)S(1)} %collective-permute-done.9, f32[4,3456]{1,0:T(4,128)S(1)} %reshape.99, s32[]{:T(128)S(6)} %select_n.38, f32[2]{0:T(128)S(1)} %fusion.16), kind=kLoop, calls=%fused_computation.29 | loop fusion | flops 13824 | bytes 82956 | tf_op jit(solution)/shard_map/div | solution.py:210
  (51 shorter events, 1.8 us)
Async XLA Ops:
  1.7 9.3 %collective-permute-start = (bf16[2,3456]{1,0:T(2,128)(2,1)S(1)}, bf16[2,3456]{1,0:T(2,128)(2,1)S(1)}, u32[]{:S(2)}, u32[]{:S(2)}) collective-permute-start(bf16[2,3456]{1,0:T(2,128)(2,1)S(1)} %reshape.93), channel_id=1, source_target_pairs={{0,2},{2,4},{4,6},{6,0},{8,10},{10,12},{12,14},{14,8},{16,18},{18,... | collective-permute-start | bytes 41480 | tf_op jit(solution)/shard_map/ppermute | solution.py:116
  3.9 7.1 %collective-permute-start.1 = (bf16[2,3456]{1,0:T(2,128)(2,1)S(1)}, bf16[2,3456]{1,0:T(2,128)(2,1)S(1)}, u32[]{:S(2)}, u32[]{:S(2)}) collective-permute-start(bf16[2,3456]{1,0:T(2,128)(2,1)S(1)} %reshape.93), channel_id=1, source_target_pairs={{0,4},{2,6},{4,0},{6,2},{8,12},{10,14},{12,8},{14,10},{16,20},{18,... | collective-permute-start | bytes 41480 | tf_op jit(solution)/shard_map/ppermute | solution.py:116
  6.5 4.5 %collective-permute-start.2 = (bf16[2,3456]{1,0:T(2,128)(2,1)S(1)}, bf16[2,3456]{1,0:T(2,128)(2,1)S(1)}, u32[]{:S(2)}, u32[]{:S(2)}) collective-permute-start(bf16[2,3456]{1,0:T(2,128)(2,1)S(1)} %reshape.93), channel_id=1, source_target_pairs={{0,6},{2,0},{4,2},{6,4},{8,14},{10,8},{12,10},{14,12},{16,22},{18,... | collective-permute-start | bytes 41480 | tf_op jit(solution)/shard_map/ppermute | solution.py:116
  9.5 0.7 %copy-start.8 = (s32[64]{0:T(128)S(1)}, s32[64]{0:T(128)}, u32[]{:S(2)}) copy-start(s32[64]{0:T(128)} %param.7) | copy-start | bytes 772
  10.3 0.7 %copy-start.4 = (s32[64]{0:T(128)S(1)}, s32[64]{0:T(128)}, u32[]{:S(2)}) copy-start(s32[64]{0:T(128)} %param.9) | copy-start | bytes 772
  10.3 0.7 %copy-start.5 = (s32[64]{0:T(128)S(1)}, s32[64]{0:T(128)}, u32[]{:S(2)}) copy-start(s32[64]{0:T(128)} %param.8) | copy-start | bytes 772
  11.1 5.8 %collective-permute-start.3 = (bf16[8,3456]{1,0:T(8,128)(2,1)S(1)}, bf16[8,3456]{1,0:T(8,128)(2,1)S(1)}, u32[]{:S(2)}, u32[]{:S(2)}) collective-permute-start(bf16[8,3456]{1,0:T(8,128)(2,1)S(1)} %pad_maximum_fusion), channel_id=1, source_target_pairs={{0,8},{2,10},{4,12},{6,14},{8,16},{10,18},{12,20},{14,22},{16,24},... | collective-permute-start | bytes 165896 | tf_op jit(solution)/shard_map/ppermute | solution.py:116
  12.8 5.5 %collective-permute-start.4 = (bf16[8,3456]{1,0:T(8,128)(2,1)S(1)}, bf16[8,3456]{1,0:T(8,128)(2,1)S(1)}, u32[]{:S(2)}, u32[]{:S(2)}) collective-permute-start(bf16[8,3456]{1,0:T(8,128)(2,1)S(1)} %pad_maximum_fusion), channel_id=1, source_target_pairs={{0,16},{2,18},{4,20},{6,22},{8,24},{10,26},{12,28},{14,30},{16,0},... | collective-permute-start | bytes 165896 | tf_op jit(solution)/shard_map/ppermute | solution.py:116
  16.1 3.9 %collective-permute-start.5 = (bf16[8,3456]{1,0:T(8,128)(2,1)S(1)}, bf16[8,3456]{1,0:T(8,128)(2,1)S(1)}, u32[]{:S(2)}, u32[]{:S(2)}) collective-permute-start(bf16[8,3456]{1,0:T(8,128)(2,1)S(1)} %pad_maximum_fusion), channel_id=1, source_target_pairs={{0,24},{2,26},{4,28},{6,30},{8,0},{10,2},{12,4},{14,6},{16,8},{18,... | collective-permute-start | bytes 165896 | tf_op jit(solution)/shard_map/ppermute | solution.py:116
  20.1 5.3 %copy-start.1 = (bf16[32,3456]{1,0:T(8,128)(2,1)}, bf16[32,3456]{1,0:T(8,128)(2,1)S(1)}, u32[]{:S(2)}) copy-start(bf16[32,3456]{1,0:T(8,128)(2,1)S(1)} %concatenate.14.refs_1_) | copy-start | bytes 663556
  20.1 6.6 %collective-permute-start.6 = (bf16[32,3456]{1,0:T(8,128)(2,1)S(1)}, bf16[32,3456]{1,0:T(8,128)(2,1)S(1)}, u32[]{:S(2)}, u32[]{:S(2)}) collective-permute-start(bf16[32,3456]{1,0:T(8,128)(2,1)S(1)} %concatenate.14.refs_1_), channel_id=1, source_target_pairs={{0,32},{2,34},{4,36},{6,38},{8,40},{10,42},{12,44},{14,46},{16,48}... | collective-permute-start | bytes 663560 | tf_op jit(solution)/shard_map/ppermute | solution.py:116
  21.4 10.0 %collective-permute-start.7 = (bf16[32,3456]{1,0:T(8,128)(2,1)S(1)}, bf16[32,3456]{1,0:T(8,128)(2,1)S(1)}, u32[]{:S(2)}, u32[]{:S(2)}) collective-permute-start(bf16[32,3456]{1,0:T(8,128)(2,1)S(1)} %concatenate.14.refs_1_), channel_id=1, source_target_pairs={{0,64},{2,66},{4,68},{6,70},{8,72},{10,74},{12,76},{14,78},{16,80}... | collective-permute-start | bytes 663560 | tf_op jit(solution)/shard_map/ppermute | solution.py:116
  23.9 7.6 %collective-permute-start.8 = (bf16[32,3456]{1,0:T(8,128)(2,1)S(1)}, bf16[32,3456]{1,0:T(8,128)(2,1)}, u32[]{:S(2)}, u32[]{:S(2)}) collective-permute-start(bf16[32,3456]{1,0:T(8,128)(2,1)S(1)} %concatenate.14.refs_1_), channel_id=1, source_target_pairs={{0,96},{2,98},{4,100},{6,102},{8,104},{10,106},{12,108},{14,110},{... | collective-permute-start | bytes 663560 | tf_op jit(solution)/shard_map/ppermute | solution.py:116
  26.7 4.7 %copy-start.2 = (bf16[32,3456]{1,0:T(8,128)(2,1)}, bf16[32,3456]{1,0:T(8,128)(2,1)S(1)}, u32[]{:S(2)}) copy-start(bf16[32,3456]{1,0:T(8,128)(2,1)S(1)} %collective-permute-done.6.refs_2_) | copy-start | bytes 663556
  31.4 0.7 %copy-start.3 = (bf16[32,3456]{1,0:T(8,128)(2,1)}, bf16[32,3456]{1,0:T(8,128)(2,1)S(1)}, u32[]{:S(2)}) copy-start(bf16[32,3456]{1,0:T(8,128)(2,1)S(1)} %collective-permute-done.7.refs_3_) | copy-start | bytes 663556
  32.1 20.9 %all-to-all-start = ((bf16[64,2,3584]{2,1,0:T(2,128)(2,1)}), bf16[64,2,3584]{2,1,0:T(2,128)(2,1)S(1)}, u32[]{:S(2)}, u32[]{:S(2)}) async-start(bf16[64,2,3584]{2,1,0:T(2,128)(2,1)} %reshape.96), calls=%async_computation | async-start | bytes 1835008 | tf_op jit(solution)/shard_map/all_to_all | solution.py:153
  53.3 1.0 %copy-start = (bf16[128,3584]{1,0:T(8,128)(2,1)}, bf16[128,3584]{1,0:T(8,128)(2,1)S(1)}, u32[]{:S(2)}) copy-start(bf16[128,3584]{1,0:T(8,128)(2,1)S(1)} %reshape.97.x_ref) | copy-start | bytes 2752516
  54.4 4.8 %copy-start.6 = (f32[1,128]{1,0:T(1,128)S(1)}, f32[1,128]{1,0:T(1,128)}, u32[]{:S(2)}) copy-start(f32[1,128]{1,0:T(1,128)} %get-tuple-element.17) | copy-start | bytes 1540
  54.4 4.8 %copy-start.7 = (f32[1,128]{1,0:T(1,128)S(1)}, f32[1,128]{1,0:T(1,128)}, u32[]{:S(2)}) copy-start(f32[1,128]{1,0:T(1,128)} %get-tuple-element.18) | copy-start | bytes 1540
  59.3 4.3 %collective-permute-start.9 = (f32[5,3456]{1,0:T(8,128)S(1)}, f32[5,3456]{1,0:T(8,128)S(1)}, u32[]{:S(2)}, u32[]{:S(2)}) collective-permute-start(f32[5,3456]{1,0:T(8,128)S(1)} %select_maximum_fusion), channel_id=1, source_target_pairs={{0,1},{1,0},{2,3},{3,2},{4,5},{5,4},{6,7},{7,6},{8,9},{9,8},{10,11... | collective-permute-start | bytes 207368 | tf_op jit(solution)/shard_map/ppermute | solution.py:193

commit v17 on v16

--- a/solution.py
+++ b/solution.py
@@ -18,6 +18,25 @@
 def angle_major(rows):
     count = rows.shape[0]
     return rows.reshape(count, RADII, ANGLES).transpose(0, 2, 1).reshape(count, RADII * ANGLES)
+
+
+def angle_major_kernel(x_ref, o_ref, t_scr, a_scr):
+    t_scr[...] = x_ref[...].astype(jnp.float32).T
+    for angle in range(ANGLES):
+        a_scr[pl.ds(angle * RADII, RADII), :] = t_scr[pl.ds(angle, RADII, stride=ANGLES), :]
+    o_ref[...] = a_scr[...].T.astype(o_ref.dtype)
+
+
+def angle_major_rows(rows):
+    count, flat_len = rows.shape
+    return pl.pallas_call(
+        angle_major_kernel,
+        out_shape=jax.ShapeDtypeStruct((count, flat_len), rows.dtype),
+        scratch_shapes=[
+            pltpu.VMEM((flat_len, count), jnp.float32),
+            pltpu.VMEM((flat_len, count), jnp.float32),
+        ],
+    )(rows)
 
 
 def score_kernel(*refs, scale):
@@ -126,7 +145,7 @@
     grp_size = lax.axis_size("grp")
     half_rows = row_count // grp_size
     grp_index = lax.axis_index("grp")
-    particle_rows = angle_major(particles)
+    particle_rows = angle_major_rows(particles)
     own_rows = lax.dynamic_slice_in_dim(particle_rows, grp_index * half_rows, half_rows, 0)
     owner_count = lax.axis_size("loop")
     per_owner = references.shape[0] * grp_size

time: 65.4 us -> 66.5 us (1.017)
  local copies, waits for them, and re-layouts: 9.85 us -> 5.63 us
  Pallas kernels: 16.4 us -> 19.2 us
  starting transfers between devices: 25.9 us -> 27.4 us
  waiting for transfers between devices: 8.81 us -> 9.93 us
    unnamed x19 -> x20, local copies, waits for them, and re-layouts: 3.25 us -> 0.04 us
    pallas_call x0 -> x1, Pallas kernels: none -> 2.75 us  [angle_major_rows(): pl.pallas_call(angle_major_kernel, out_shape=jax.ShapeDtypeStruct((count,...]
    reshape x4 -> x3, local copies, waits for them, and re-layouts: 2.77 us -> 1.04 us  [angle_major(): rows.reshape(count, RADII, ANGLES).transpose(0, 2, 1)]
    all_to_all x1, waiting for transfers between devices: 0.01 us -> 1.19 us  [local(): lax.all_to_all(outgoing, 'loop', split_axis=0, concat_axis=0, tiled=True)]
    all_to_all x1, starting transfers between devices: 6.01 us -> 7 us  [local(): lax.all_to_all(outgoing, 'loop', split_axis=0, concat_axis=0, tiled=True)]
    dynamic_slice x1, local copies, waits for them, and re-layouts: 0.32 us -> 1.05 us  [local(): lax.dynamic_slice_in_dim(particle_rows, grp_index * half_rows, half_rows, 0)]
  transfers between devices with their start and end apart: 11 -> 11, of which waited for: 4 -> 5; matrix products, arithmetic and copies ran while one was open for 9% -> 5% of each run, Pallas kernels for 20% -> 24%
where the time goes in v17:
time: 66.5 us; the launch traced here: 66.1 us
  starting transfers between devices  27.4 us (41%)
  Pallas kernels  19.2 us (29%)
  waiting for transfers between devices  9.93 us (15%)
  local copies, waits for them, and re-layouts  5.63 us (8%)
  other arithmetic  2.76 us (4%)
  between operations  0.86 us (1%)
    ppermute x9, starting transfers between devices, staged_gather(): parts.append(lax.ppermute(rows, axis, pairs))  16.5 us
    pallas_call x1, Pallas kernels, score_all(): pl.pallas_call(functools.partial(score_kernel, scale=scale), out_shape=(j...  13.1 us
    ppermute x9, waiting for transfers between devices, staged_gather(): parts.append(lax.ppermute(rows, axis, pairs))  7.78 us
    all_to_all x1, starting transfers between devices, local(): lax.all_to_all(outgoing, 'loop', split_axis=0, concat_axis=0, tiled=True)  7 us
    ppermute x1, starting transfers between devices, local(): got = lax.ppermute(sent, 'grp', [(0, 1), (1, 0)])  3.87 us
    pallas_call x1, Pallas kernels, local(): pl.pallas_call(average_kernel, out_shape=jax.ShapeDtypeStruct((block, fla...  3.3 us
    pallas_call x1, Pallas kernels, angle_major_rows(): pl.pallas_call(angle_major_kernel, out_shape=jax.ShapeDtypeStruct((count,...  2.75 us
  transfers between devices with their start and end apart: 11, of which 5 were waited for; matrix products, arithmetic and copies ran while one was open for 5% of the time, Pallas kernels for 24%

profile of v17, /device:TPU:1, one launch (start us, length us, event | category | flops | bytes accessed | tf_op | source)
XLA Modules:
  0.0 66.1 jit_solution(4740007722097285906)
XLA Ops:
  0.6 0.8 %reshape.86 = bf16[2,48,72]{2,1,0:T(8,128)(2,1)S(1)} reshape(bf16[2,3456]{1,0:T(2,128)(2,1)} %param.6) | data formatting | bytes 27648 | tf_op jit(solution)/shard_map/reshape | solution.py:20
  1.7 2.2 %collective-permute-start = (bf16[2,3456]{1,0:T(2,128)(2,1)S(1)}, bf16[2,3456]{1,0:T(2,128)(2,1)S(1)}, u32[]{:S(2)}, u32[]{:S(2)}) collective-permute-start(bf16[2,3456]{1,0:T(2,128)(2,1)S(1)} %reshape.87), channel_id=1, source_target_pairs={{0,2},{2,4},{4,6},{6,0},{8,10},{10,12},{12,14},{14,8},{16,18},{18,... | collective-permute-start | bytes 41480 | tf_op jit(solution)/shard_map/ppermute | solution.py:135
  3.9 2.6 %collective-permute-start.1 = (bf16[2,3456]{1,0:T(2,128)(2,1)S(1)}, bf16[2,3456]{1,0:T(2,128)(2,1)S(1)}, u32[]{:S(2)}, u32[]{:S(2)}) collective-permute-start(bf16[2,3456]{1,0:T(2,128)(2,1)S(1)} %reshape.87), channel_id=1, source_target_pairs={{0,4},{2,6},{4,0},{6,2},{8,12},{10,14},{12,8},{14,10},{16,20},{18,... | collective-permute-start | bytes 41480 | tf_op jit(solution)/shard_map/ppermute | solution.py:135
  6.5 1.1 %collective-permute-start.2 = (bf16[2,3456]{1,0:T(2,128)(2,1)S(1)}, bf16[2,3456]{1,0:T(2,128)(2,1)S(1)}, u32[]{:S(2)}, u32[]{:S(2)}) collective-permute-start(bf16[2,3456]{1,0:T(2,128)(2,1)S(1)} %reshape.87), channel_id=1, source_target_pairs={{0,6},{2,0},{4,2},{6,4},{8,14},{10,8},{12,10},{14,12},{16,22},{18,... | collective-permute-start | bytes 41480 | tf_op jit(solution)/shard_map/ppermute | solution.py:135
  7.6 2.7 %shard_map.68.refs_0_ = bf16[128,3456]{1,0:T(8,128)(2,1)} custom-call(bf16[128,3456]{1,0:T(8,128)(2,1)} %x_ref.1), custom_call_target="tpu_custom_call" | custom-call | tf_op jit(solution)/shard_map/pallas_call | solution.py:32
  10.5 0.2 select_reduce_fusion
  10.7 1.1 %constant_dynamic-slice_fusion.3 = bf16[64,3456]{1,0:T(8,128)(2,1)S(1)} fusion(bf16[128,3456]{1,0:T(8,128)(2,1)} %shard_map.68.refs_0_, s32[]{:T(128)S(6)} %select_n.33), kind=kLoop, calls=%fused_computation.37 | loop fusion | bytes 884740 | tf_op jit(solution)/shard_map/dynamic_slice | solution.py:149
  11.9 1.7 %collective-permute-start.3 = (bf16[8,3456]{1,0:T(8,128)(2,1)S(1)}, bf16[8,3456]{1,0:T(8,128)(2,1)S(1)}, u32[]{:S(2)}, u32[]{:S(2)}) collective-permute-start(bf16[8,3456]{1,0:T(8,128)(2,1)S(1)} %pad_maximum_fusion), channel_id=1, source_target_pairs={{0,8},{2,10},{4,12},{6,14},{8,16},{10,18},{12,20},{14,22},{16,24},... | collective-permute-start | bytes 165896 | tf_op jit(solution)/shard_map/ppermute | solution.py:135
  13.6 3.3 %collective-permute-start.4 = (bf16[8,3456]{1,0:T(8,128)(2,1)S(1)}, bf16[8,3456]{1,0:T(8,128)(2,1)S(1)}, u32[]{:S(2)}, u32[]{:S(2)}) collective-permute-start(bf16[8,3456]{1,0:T(8,128)(2,1)S(1)} %pad_maximum_fusion), channel_id=1, source_target_pairs={{0,16},{2,18},{4,20},{6,22},{8,24},{10,26},{12,28},{14,30},{16,0},... | collective-permute-start | bytes 165896 | tf_op jit(solution)/shard_map/ppermute | solution.py:135
  16.9 0.7 %collective-permute-start.5 = (bf16[8,3456]{1,0:T(8,128)(2,1)S(1)}, bf16[8,3456]{1,0:T(8,128)(2,1)S(1)}, u32[]{:S(2)}, u32[]{:S(2)}) collective-permute-start(bf16[8,3456]{1,0:T(8,128)(2,1)S(1)} %pad_maximum_fusion), channel_id=1, source_target_pairs={{0,24},{2,26},{4,28},{6,30},{8,0},{10,2},{12,4},{14,6},{16,8},{18,... | collective-permute-start | bytes 165896 | tf_op jit(solution)/shard_map/ppermute | solution.py:135
  17.8 1.4 %collective-permute-done.4 = bf16[8,3456]{1,0:T(8,128)(2,1)S(1)} collective-permute-done((bf16[8,3456]{1,0:T(8,128)(2,1)S(1)}, bf16[8,3456]{1,0:T(8,128)(2,1)S(1)}, u32[]{:S(2)}, u32[]{:S(2)}) %collective-permute-start.4) | collective-permute-done | bytes 55328 | tf_op jit(solution)/shard_map/ppermute | solution.py:135
  19.2 1.7 %collective-permute-done.5 = bf16[8,3456]{1,0:T(8,128)(2,1)S(1)} collective-permute-done((bf16[8,3456]{1,0:T(8,128)(2,1)S(1)}, bf16[8,3456]{1,0:T(8,128)(2,1)S(1)}, u32[]{:S(2)}, u32[]{:S(2)}) %collective-permute-start.5) | collective-permute-done | bytes 55328 | tf_op jit(solution)/shard_map/ppermute | solution.py:135
  20.8 0.1 concatenate.14.refs_1_
  20.9 1.3 %collective-permute-start.6 = (bf16[32,3456]{1,0:T(8,128)(2,1)S(1)}, bf16[32,3456]{1,0:T(8,128)(2,1)S(1)}, u32[]{:S(2)}, u32[]{:S(2)}) collective-permute-start(bf16[32,3456]{1,0:T(8,128)(2,1)S(1)} %concatenate.14.refs_1_), channel_id=1, source_target_pairs={{0,32},{2,34},{4,36},{6,38},{8,40},{10,42},{12,44},{14,46},{16,48}... | collective-permute-start | bytes 663560 | tf_op jit(solution)/shard_map/ppermute | solution.py:135
  22.2 2.5 %collective-permute-start.7 = (bf16[32,3456]{1,0:T(8,128)(2,1)S(1)}, bf16[32,3456]{1,0:T(8,128)(2,1)S(1)}, u32[]{:S(2)}, u32[]{:S(2)}) collective-permute-start(bf16[32,3456]{1,0:T(8,128)(2,1)S(1)} %concatenate.14.refs_1_), channel_id=1, source_target_pairs={{0,64},{2,66},{4,68},{6,70},{8,72},{10,74},{12,76},{14,78},{16,80}... | collective-permute-start | bytes 663560 | tf_op jit(solution)/shard_map/ppermute | solution.py:135
  24.7 1.2 %collective-permute-start.8 = (bf16[32,3456]{1,0:T(8,128)(2,1)S(1)}, bf16[32,3456]{1,0:T(8,128)(2,1)S(1)}, u32[]{:S(2)}, u32[]{:S(2)}) collective-permute-start(bf16[32,3456]{1,0:T(8,128)(2,1)S(1)} %concatenate.14.refs_1_), channel_id=1, source_target_pairs={{0,96},{2,98},{4,100},{6,102},{8,104},{10,106},{12,108},{14,110},{... | collective-permute-start | bytes 663560 | tf_op jit(solution)/shard_map/ppermute | solution.py:135
  25.8 0.4 convolution_convert_fusion
  26.2 1.3 %reshape.88 = bf16[64,2,3584]{2,1,0:T(2,128)(2,1)} reshape(bf16[128,3584]{1,0:T(8,128)(2,1)S(1)} %convolution_convert_fusion) | data formatting | bytes 1835008 | tf_op jit(solution)/shard_map/reshape | solution.py:170
  27.5 4.7 %collective-permute-done.7.refs_3_ = bf16[32,3456]{1,0:T(8,128)(2,1)S(1)} collective-permute-done((bf16[32,3456]{1,0:T(8,128)(2,1)S(1)}, bf16[32,3456]{1,0:T(8,128)(2,1)S(1)}, u32[]{:S(2)}, u32[]{:S(2)}) %collective-permute-start.7) | collective-permute-done | bytes 221216 | tf_op jit(solution)/shard_map/ppermute | solution.py:135
  32.2 7.0 %all-to-all-start = ((bf16[64,2,3584]{2,1,0:T(2,128)(2,1)}), bf16[64,2,3584]{2,1,0:T(2,128)(2,1)S(1)}, u32[]{:S(2)}, u32[]{:S(2)}) async-start(bf16[64,2,3584]{2,1,0:T(2,128)(2,1)} %reshape.88), calls=%async_computation | async-start | bytes 1835008 | tf_op jit(solution)/shard_map/all_to_all | solution.py:172
  39.3 13.1 %shard_map.69 = (f32[1,128]{1,0:T(1,128)}, f32[1,128]{1,0:T(1,128)}) custom-call(bf16[128,3456]{1,0:T(8,128)(2,1)} %shard_map.68.refs_0_, bf16[32,3456]{1,0:T(8,128)(2,1)} %copy-done.1, bf16[32,3456]{1,0:T(8,128)(2,1)} %copy-done.2, bf16[32,3456]{1,0:T(8,128)(2,1)} %copy-done.3, bf16[32,3456]{1,0:T(8,128)(2,1)} %copy-done.4), custom_call_target="tpu_custom_call" | custom-call | tf_op jit(solution)/shard_map/pallas_call | solution.py:81
  52.4 1.2 %all-to-all-done = bf16[64,2,3584]{2,1,0:T(2,128)(2,1)S(1)} async-done(((bf16[64,2,3584]{2,1,0:T(2,128)(2,1)}), bf16[64,2,3584]{2,1,0:T(2,128)(2,1)S(1)}, u32[]{:S(2)}, u32[]{:S(2)}) %all-to-all-start) | async-done | bytes 917536 | tf_op jit(solution)/shard_map/all_to_all | solution.py:172
  53.6 0.3 reshape.89.x_ref
  54.0 0.2 slice_reduce_fusion.2
  54.2 0.7 %select_convert_fusion.w_ref = bf16[576,128]{1,0:T(8,128)(2,1)} fusion(f32[128]{0:T(128)S(1)} %get-tuple-element.23, pred[8,128]{1,0:T(8,128)(4,1)S(1)} %iota_compare_fusion.8, pred[72,128]{1,0:T(8,128)(4,1)S(1)} %iota_compare_fusion.6), kind=kLoop, calls=%fused_computation.7 | loop fusion | flops 147456 | bytes 158208 | tf_op jit(solution)/shard_map/convert_element_type | solution.py:187
  55.0 3.3 %shard_map.70 = f32[8,3456]{1,0:T(8,128)} custom-call(bf16[576,128]{1,0:T(8,128)(2,1)} %select_convert_fusion.w_ref, bf16[128,3584]{1,0:T(8,128)(2,1)} %copy-done), custom_call_target="tpu_custom_call" | custom-call | tf_op jit(solution)/shard_map/pallas_call | solution.py:189
  58.3 0.9 %slice.49 = f32[4,3456]{1,0:T(4,128)S(1)} slice(f32[8,3456]{1,0:T(8,128)} %shard_map.70), slice={[0:4], [0:3456]} | slice | bytes 110592 | tf_op jit(solution)/shard_map/slice | solution.py:194
  59.5 0.2 select_reduce_fusion.1
  59.9 3.9 %collective-permute-start.9 = (f32[5,3456]{1,0:T(8,128)S(1)}, f32[5,3456]{1,0:T(8,128)S(1)}, u32[]{:S(2)}, u32[]{:S(2)}) collective-permute-start(f32[5,3456]{1,0:T(8,128)S(1)} %select_maximum_fusion), channel_id=1, source_target_pairs={{0,1},{1,0},{2,3},{3,2},{4,5},{5,4},{6,7},{7,6},{8,9},{9,8},{10,11... | collective-permute-start | bytes 207368 | tf_op jit(solution)/shard_map/ppermute | solution.py:212
  63.8 1.0 %collective-permute-done.9 = f32[5,3456]{1,0:T(8,128)S(1)} collective-permute-done((f32[5,3456]{1,0:T(8,128)S(1)}, f32[5,3456]{1,0:T(8,128)S(1)}, u32[]{:S(2)}, u32[]{:S(2)}) %collective-permute-start.9) | collective-permute-done | bytes 69152 | tf_op jit(solution)/shard_map/ppermute | solution.py:212
  64.8 0.5 log_add_fusion
  65.4 0.7 %fusion.10 = f32[2,3456]{1,0:T(2,128)} fusion(f32[5,3456]{1,0:T(8,128)S(1)} %collective-permute-done.9, f32[4,3456]{1,0:T(4,128)S(1)} %reshape.91, s32[]{:T(128)S(6)} %select_n.38, f32[2]{0:T(128)S(1)} %fusion.15), kind=kLoop, calls=%fused_computation.27 | loop fusion | flops 13824 | bytes 82956 | tf_op jit(solution)/shard_map/div | solution.py:229
  (52 shorter events, 1.4 us)
Async XLA Ops:
  1.6 8.8 %copy-start.9 = (s32[64]{0:T(128)S(1)}, s32[64]{0:T(128)}, u32[]{:S(2)}) copy-start(s32[64]{0:T(128)} %param.7) | copy-start | bytes 772
  1.7 10.1 %collective-permute-start = (bf16[2,3456]{1,0:T(2,128)(2,1)S(1)}, bf16[2,3456]{1,0:T(2,128)(2,1)S(1)}, u32[]{:S(2)}, u32[]{:S(2)}) collective-permute-start(bf16[2,3456]{1,0:T(2,128)(2,1)S(1)} %reshape.87), channel_id=1, source_target_pairs={{0,2},{2,4},{4,6},{6,0},{8,10},{10,12},{12,14},{14,8},{16,18},{18,... | collective-permute-start | bytes 41480 | tf_op jit(solution)/shard_map/ppermute | solution.py:135
  3.9 7.9 %collective-permute-start.1 = (bf16[2,3456]{1,0:T(2,128)(2,1)S(1)}, bf16[2,3456]{1,0:T(2,128)(2,1)S(1)}, u32[]{:S(2)}, u32[]{:S(2)}) collective-permute-start(bf16[2,3456]{1,0:T(2,128)(2,1)S(1)} %reshape.87), channel_id=1, source_target_pairs={{0,4},{2,6},{4,0},{6,2},{8,12},{10,14},{12,8},{14,10},{16,20},{18,... | collective-permute-start | bytes 41480 | tf_op jit(solution)/shard_map/ppermute | solution.py:135
  6.5 5.3 %collective-permute-start.2 = (bf16[2,3456]{1,0:T(2,128)(2,1)S(1)}, bf16[2,3456]{1,0:T(2,128)(2,1)S(1)}, u32[]{:S(2)}, u32[]{:S(2)}) collective-permute-start(bf16[2,3456]{1,0:T(2,128)(2,1)S(1)} %reshape.87), channel_id=1, source_target_pairs={{0,6},{2,0},{4,2},{6,4},{8,14},{10,8},{12,10},{14,12},{16,22},{18,... | collective-permute-start | bytes 41480 | tf_op jit(solution)/shard_map/ppermute | solution.py:135
  10.3 1.4 %copy-start.5 = (s32[64]{0:T(128)S(1)}, s32[64]{0:T(128)}, u32[]{:S(2)}) copy-start(s32[64]{0:T(128)} %param.9) | copy-start | bytes 772
  10.3 1.4 %copy-start.6 = (s32[64]{0:T(128)S(1)}, s32[64]{0:T(128)}, u32[]{:S(2)}) copy-start(s32[64]{0:T(128)} %param.8) | copy-start | bytes 772
  11.9 5.9 %collective-permute-start.3 = (bf16[8,3456]{1,0:T(8,128)(2,1)S(1)}, bf16[8,3456]{1,0:T(8,128)(2,1)S(1)}, u32[]{:S(2)}, u32[]{:S(2)}) collective-permute-start(bf16[8,3456]{1,0:T(8,128)(2,1)S(1)} %pad_maximum_fusion), channel_id=1, source_target_pairs={{0,8},{2,10},{4,12},{6,14},{8,16},{10,18},{12,20},{14,22},{16,24},... | collective-permute-start | bytes 165896 | tf_op jit(solution)/shard_map/ppermute | solution.py:135
  13.6 5.5 %collective-permute-start.4 = (bf16[8,3456]{1,0:T(8,128)(2,1)S(1)}, bf16[8,3456]{1,0:T(8,128)(2,1)S(1)}, u32[]{:S(2)}, u32[]{:S(2)}) collective-permute-start(bf16[8,3456]{1,0:T(8,128)(2,1)S(1)} %pad_maximum_fusion), channel_id=1, source_target_pairs={{0,16},{2,18},{4,20},{6,22},{8,24},{10,26},{12,28},{14,30},{16,0},... | collective-permute-start | bytes 165896 | tf_op jit(solution)/shard_map/ppermute | solution.py:135
  16.9 3.9 %collective-permute-start.5 = (bf16[8,3456]{1,0:T(8,128)(2,1)S(1)}, bf16[8,3456]{1,0:T(8,128)(2,1)S(1)}, u32[]{:S(2)}, u32[]{:S(2)}) collective-permute-start(bf16[8,3456]{1,0:T(8,128)(2,1)S(1)} %pad_maximum_fusion), channel_id=1, source_target_pairs={{0,24},{2,26},{4,28},{6,30},{8,0},{10,2},{12,4},{14,6},{16,8},{18,... | collective-permute-start | bytes 165896 | tf_op jit(solution)/shard_map/ppermute | solution.py:135
  20.9 6.5 %copy-start.1 = (bf16[32,3456]{1,0:T(8,128)(2,1)}, bf16[32,3456]{1,0:T(8,128)(2,1)S(1)}, u32[]{:S(2)}) copy-start(bf16[32,3456]{1,0:T(8,128)(2,1)S(1)} %concatenate.14.refs_1_) | copy-start | bytes 663556
  20.9 6.5 %collective-permute-start.6 = (bf16[32,3456]{1,0:T(8,128)(2,1)S(1)}, bf16[32,3456]{1,0:T(8,128)(2,1)S(1)}, u32[]{:S(2)}, u32[]{:S(2)}) collective-permute-start(bf16[32,3456]{1,0:T(8,128)(2,1)S(1)} %concatenate.14.refs_1_), channel_id=1, source_target_pairs={{0,32},{2,34},{4,36},{6,38},{8,40},{10,42},{12,44},{14,46},{16,48}... | collective-permute-start | bytes 663560 | tf_op jit(solution)/shard_map/ppermute | solution.py:135
  22.2 10.0 %collective-permute-start.7 = (bf16[32,3456]{1,0:T(8,128)(2,1)S(1)}, bf16[32,3456]{1,0:T(8,128)(2,1)S(1)}, u32[]{:S(2)}, u32[]{:S(2)}) collective-permute-start(bf16[32,3456]{1,0:T(8,128)(2,1)S(1)} %concatenate.14.refs_1_), channel_id=1, source_target_pairs={{0,64},{2,66},{4,68},{6,70},{8,72},{10,74},{12,76},{14,78},{16,80}... | collective-permute-start | bytes 663560 | tf_op jit(solution)/shard_map/ppermute | solution.py:135
  24.7 7.6 %collective-permute-start.8 = (bf16[32,3456]{1,0:T(8,128)(2,1)S(1)}, bf16[32,3456]{1,0:T(8,128)(2,1)S(1)}, u32[]{:S(2)}, u32[]{:S(2)}) collective-permute-start(bf16[32,3456]{1,0:T(8,128)(2,1)S(1)} %concatenate.14.refs_1_), channel_id=1, source_target_pairs={{0,96},{2,98},{4,100},{6,102},{8,104},{10,106},{12,108},{14,110},{... | collective-permute-start | bytes 663560 | tf_op jit(solution)/shard_map/ppermute | solution.py:135
  27.5 11.8 %copy-start.2 = (bf16[32,3456]{1,0:T(8,128)(2,1)}, bf16[32,3456]{1,0:T(8,128)(2,1)S(1)}, u32[]{:S(2)}) copy-start(bf16[32,3456]{1,0:T(8,128)(2,1)S(1)} %collective-permute-done.6.refs_2_) | copy-start | bytes 663556
  32.2 7.0 %copy-start.3 = (bf16[32,3456]{1,0:T(8,128)(2,1)}, bf16[32,3456]{1,0:T(8,128)(2,1)S(1)}, u32[]{:S(2)}) copy-start(bf16[32,3456]{1,0:T(8,128)(2,1)S(1)} %collective-permute-done.7.refs_3_) | copy-start | bytes 663556
  32.2 7.0 %copy-start.4 = (bf16[32,3456]{1,0:T(8,128)(2,1)}, bf16[32,3456]{1,0:T(8,128)(2,1)S(1)}, u32[]{:S(2)}) copy-start(bf16[32,3456]{1,0:T(8,128)(2,1)S(1)} %collective-permute-done.8.refs_4_) | copy-start | bytes 663556
  32.2 21.4 %all-to-all-start = ((bf16[64,2,3584]{2,1,0:T(2,128)(2,1)}), bf16[64,2,3584]{2,1,0:T(2,128)(2,1)S(1)}, u32[]{:S(2)}, u32[]{:S(2)}) async-start(bf16[64,2,3584]{2,1,0:T(2,128)(2,1)} %reshape.88), calls=%async_computation | async-start | bytes 1835008 | tf_op jit(solution)/shard_map/all_to_all | solution.py:172
  54.0 1.0 %copy-start = (bf16[128,3584]{1,0:T(8,128)(2,1)}, bf16[128,3584]{1,0:T(8,128)(2,1)S(1)}, u32[]{:S(2)}) copy-start(bf16[128,3584]{1,0:T(8,128)(2,1)S(1)} %reshape.89.x_ref) | copy-start | bytes 2752516
  55.0 4.9 %copy-start.7 = (f32[1,128]{1,0:T(1,128)S(1)}, f32[1,128]{1,0:T(1,128)}, u32[]{:S(2)}) copy-start(f32[1,128]{1,0:T(1,128)} %get-tuple-element.17) | copy-start | bytes 1540
  55.0 4.9 %copy-start.8 = (f32[1,128]{1,0:T(1,128)S(1)}, f32[1,128]{1,0:T(1,128)}, u32[]{:S(2)}) copy-start(f32[1,128]{1,0:T(1,128)} %get-tuple-element.18) | copy-start | bytes 1540
  59.9 4.8 %collective-permute-start.9 = (f32[5,3456]{1,0:T(8,128)S(1)}, f32[5,3456]{1,0:T(8,128)S(1)}, u32[]{:S(2)}, u32[]{:S(2)}) collective-permute-start(f32[5,3456]{1,0:T(8,128)S(1)} %select_maximum_fusion), channel_id=1, source_target_pairs={{0,1},{1,0},{2,3},{3,2},{4,5},{5,4},{6,7},{7,6},{8,9},{9,8},{10,11... | collective-permute-start | bytes 207368 | tf_op jit(solution)/shard_map/ppermute | solution.py:212

commit v18 on v16

--- a/solution.py
+++ b/solution.py
@@ -102,18 +102,28 @@
     return factors
 
 
+def ring_pairs(count, stride, factor, step):
+    pairs = []
+    for source in range(count):
+        digit = (source // stride) % factor
+        pairs.append((source, source + ((digit + step) % factor - digit) * stride))
+    return pairs
+
+
 def staged_gather(rows, axis, held):
     count = lax.axis_size(axis)
     stride = 1
     factors = ring_factors(count)
     for round_index, factor in enumerate(factors):
-        parts = [rows]
-        for step in range(1, factor):
-            pairs = []
-            for source in range(count):
-                digit = (source // stride) % factor
-                pairs.append((source, source + ((digit + step) % factor - digit) * stride))
-            parts.append(lax.ppermute(rows, axis, pairs))
+        if factor == 4 and round_index < len(factors) - 1:
+            from_below = lax.ppermute(rows, axis, ring_pairs(count, stride, factor, 1))
+            from_above = lax.ppermute(rows, axis, ring_pairs(count, stride, factor, factor - 1))
+            two_below = lax.ppermute(from_below, axis, ring_pairs(count, stride, factor, 1))
+            parts = [rows, from_below, two_below, from_above]
+        else:
+            parts = [rows]
+            for step in range(1, factor):
+                parts.append(lax.ppermute(rows, axis, ring_pairs(count, stride, factor, step)))
         rows = jnp.concatenate(parts, axis=0)
         if round_index == len(factors) - 1:
             parts, held = lax.optimization_barrier((parts, held))

time: 65.4 us -> 67.4 us (1.031)
  waiting for transfers between devices: 8.81 us -> 13.1 us
  starting transfers between devices: 25.9 us -> 23.5 us
    ppermute x9, waiting for transfers between devices: 7.84 us -> 12.1 us  [the longest x2 7.76 us: staged_gather(): lax.ppermute(from_below, axis, ring_pairs(count, stride, factor, 1))]
    ppermute x9, starting transfers between devices: 16.5 us -> 12.6 us  [the longest x3 4.88 us: staged_gather(): lax.ppermute(rows, axis, ring_pairs(count, stride, factor, step))]
    ppermute x1, starting transfers between devices: 3.37 us -> 6.15 us  [local(): got = lax.ppermute(sent, 'grp', [(0, 1), (1, 0)])]
    all_to_all x1, starting transfers between devices: 6.01 us -> 4.79 us  [local(): lax.all_to_all(outgoing, 'loop', split_axis=0, concat_axis=0, tiled=True)]
  transfers between devices with their start and end apart: 11 -> 11, of which waited for: 4 -> 5; matrix products, arithmetic and copies ran while one was open for 9% -> 9% of each run, Pallas kernels for 20% -> 20%
where the time goes in v18:
time: 67.4 us; the launch traced here: 67 us
  starting transfers between devices  23.5 us (35%)
  Pallas kernels  16.4 us (24%)
  waiting for transfers between devices  13.1 us (19%)
  local copies, waits for them, and re-layouts  9.94 us (15%)
  other arithmetic  2.76 us (4%)
  between operations  0.83 us (1%)
    pallas_call x1, Pallas kernels, score_all(): pl.pallas_call(functools.partial(score_kernel, scale=scale), out_shape=(j...  13.1 us
    ppermute x2, waiting for transfers between devices, staged_gather(): lax.ppermute(from_below, axis, ring_pairs(count, stride, factor, 1))  7.76 us
    ppermute x1, starting transfers between devices, local(): got = lax.ppermute(sent, 'grp', [(0, 1), (1, 0)])  6.15 us
    ppermute x3, starting transfers between devices, staged_gather(): lax.ppermute(rows, axis, ring_pairs(count, stride, factor, step))  4.88 us
    all_to_all x1, starting transfers between devices, local(): lax.all_to_all(outgoing, 'loop', split_axis=0, concat_axis=0, tiled=True)  4.79 us
    ppermute x2, starting transfers between devices, staged_gather(): from_below = lax.ppermute(rows, axis, ring_pairs(count, stride, factor, 1))  3.9 us
    ppermute x2, starting transfers between devices, staged_gather(): lax.ppermute(rows, axis, ring_pairs(count, stride, factor, factor - 1))  3.73 us
    unnamed x19, local copies, waits for them, and re-layouts  3.35 us
  transfers between devices with their start and end apart: 11, of which 5 were waited for; matrix products, arithmetic and copies ran while one was open for 9% of the time, Pallas kernels for 20%

profile of v18, /device:TPU:1, one launch (start us, length us, event | category | flops | bytes accessed | tf_op | source)
XLA Modules:
  0.0 67.0 jit_solution(3792648015272793544)
XLA Ops:
  0.6 0.8 %reshape.92 = bf16[2,48,72]{2,1,0:T(8,128)(2,1)S(1)} reshape(bf16[2,3456]{1,0:T(2,128)(2,1)} %param.6) | data formatting | bytes 27648 | tf_op jit(solution)/shard_map/reshape | solution.py:20
  1.7 2.2 %collective-permute-start = (bf16[2,3456]{1,0:T(2,128)(2,1)S(1)}, bf16[2,3456]{1,0:T(2,128)(2,1)S(1)}, u32[]{:S(2)}, u32[]{:S(2)}) collective-permute-start(bf16[2,3456]{1,0:T(2,128)(2,1)S(1)} %reshape.93), channel_id=1, source_target_pairs={{0,2},{2,4},{4,6},{6,0},{8,10},{10,12},{12,14},{14,8},{16,18},{18,... | collective-permute-start | bytes 41480 | tf_op jit(solution)/shard_map/ppermute | solution.py:119
  3.9 1.5 %collective-permute-start.2 = (bf16[2,3456]{1,0:T(2,128)(2,1)S(1)}, bf16[2,3456]{1,0:T(2,128)(2,1)S(1)}, u32[]{:S(2)}, u32[]{:S(2)}) collective-permute-start(bf16[2,3456]{1,0:T(2,128)(2,1)S(1)} %reshape.93), channel_id=1, source_target_pairs={{0,6},{2,0},{4,2},{6,4},{8,14},{10,8},{12,10},{14,12},{16,22},{18,... | collective-permute-start | bytes 41480 | tf_op jit(solution)/shard_map/ppermute | solution.py:120
  5.4 1.9 %copy.19 = bf16[128,3456]{0,1:T(8,128)(2,1)S(1)} copy(bf16[128,3456]{1,0:T(8,128)(2,1)} %param.5) | data formatting | bytes 1769472 | tf_op args[0]
  7.4 0.5 copy-done.8
  8.0 0.3 constant_dynamic-slice_fusion.3
  8.4 0.2 copy-done.4
  9.0 3.6 %collective-permute-done.1 = bf16[2,3456]{1,0:T(2,128)(2,1)S(1)} collective-permute-done((bf16[2,3456]{1,0:T(2,128)(2,1)S(1)}, bf16[2,3456]{1,0:T(2,128)(2,1)S(1)}, u32[]{:S(2)}, u32[]{:S(2)}) %collective-permute-start.1) | collective-permute-done | bytes 13856 | tf_op jit(solution)/shard_map/ppermute | solution.py:121
  12.6 1.7 %collective-permute-start.3 = (bf16[8,3456]{1,0:T(8,128)(2,1)S(1)}, bf16[8,3456]{1,0:T(8,128)(2,1)S(1)}, u32[]{:S(2)}, u32[]{:S(2)}) collective-permute-start(bf16[8,3456]{1,0:T(8,128)(2,1)S(1)} %pad_maximum_fusion), channel_id=1, source_target_pairs={{0,8},{2,10},{4,12},{6,14},{8,16},{10,18},{12,20},{14,22},{16,24},... | collective-permute-start | bytes 165896 | tf_op jit(solution)/shard_map/ppermute | solution.py:119
  14.3 2.2 %collective-permute-start.5 = (bf16[8,3456]{1,0:T(8,128)(2,1)S(1)}, bf16[8,3456]{1,0:T(8,128)(2,1)S(1)}, u32[]{:S(2)}, u32[]{:S(2)}) collective-permute-start(bf16[8,3456]{1,0:T(8,128)(2,1)S(1)} %pad_maximum_fusion), channel_id=1, source_target_pairs={{0,24},{2,26},{4,28},{6,30},{8,0},{10,2},{12,4},{14,6},{16,8},{18,... | collective-permute-start | bytes 165896 | tf_op jit(solution)/shard_map/ppermute | solution.py:120
  16.6 1.5 %collective-permute-done.3 = bf16[8,3456]{1,0:T(8,128)(2,1)S(1)} collective-permute-done((bf16[8,3456]{1,0:T(8,128)(2,1)S(1)}, bf16[8,3456]{1,0:T(8,128)(2,1)S(1)}, u32[]{:S(2)}, u32[]{:S(2)}) %collective-permute-start.3) | collective-permute-done | bytes 55328 | tf_op jit(solution)/shard_map/ppermute | solution.py:119
  18.0 4.2 %collective-permute-done.4 = bf16[8,3456]{1,0:T(8,128)(2,1)S(1)} collective-permute-done((bf16[8,3456]{1,0:T(8,128)(2,1)S(1)}, bf16[8,3456]{1,0:T(8,128)(2,1)S(1)}, u32[]{:S(2)}, u32[]{:S(2)}) %collective-permute-start.4) | collective-permute-done | bytes 55328 | tf_op jit(solution)/shard_map/ppermute | solution.py:121
  22.4 1.3 %collective-permute-start.6 = (bf16[32,3456]{1,0:T(8,128)(2,1)S(1)}, bf16[32,3456]{1,0:T(8,128)(2,1)S(1)}, u32[]{:S(2)}, u32[]{:S(2)}) collective-permute-start(bf16[32,3456]{1,0:T(8,128)(2,1)S(1)} %concatenate.14.refs_1_), channel_id=1, source_target_pairs={{0,32},{2,34},{4,36},{6,38},{8,40},{10,42},{12,44},{14,46},{16,48}... | collective-permute-start | bytes 663560 | tf_op jit(solution)/shard_map/ppermute | solution.py:126
  23.6 2.5 %collective-permute-start.7 = (bf16[32,3456]{1,0:T(8,128)(2,1)S(1)}, bf16[32,3456]{1,0:T(8,128)(2,1)S(1)}, u32[]{:S(2)}, u32[]{:S(2)}) collective-permute-start(bf16[32,3456]{1,0:T(8,128)(2,1)S(1)} %concatenate.14.refs_1_), channel_id=1, source_target_pairs={{0,64},{2,66},{4,68},{6,70},{8,72},{10,74},{12,76},{14,78},{16,80}... | collective-permute-start | bytes 663560 | tf_op jit(solution)/shard_map/ppermute | solution.py:126
  26.1 1.2 %collective-permute-start.8 = (bf16[32,3456]{1,0:T(8,128)(2,1)S(1)}, bf16[32,3456]{1,0:T(8,128)(2,1)}, u32[]{:S(2)}, u32[]{:S(2)}) collective-permute-start(bf16[32,3456]{1,0:T(8,128)(2,1)S(1)} %concatenate.14.refs_1_), channel_id=1, source_target_pairs={{0,96},{2,98},{4,100},{6,102},{8,104},{10,106},{12,108},{14,110},{... | collective-permute-start | bytes 663560 | tf_op jit(solution)/shard_map/ppermute | solution.py:126
  27.2 0.4 convolution_convert_fusion
  27.7 1.3 %reshape.96 = bf16[64,2,3584]{2,1,0:T(2,128)(2,1)} reshape(bf16[128,3584]{1,0:T(8,128)(2,1)S(1)} %convolution_convert_fusion) | data formatting | bytes 1835008 | tf_op jit(solution)/shard_map/reshape | solution.py:161
  29.0 2.9 %collective-permute-done.7.refs_3_ = bf16[32,3456]{1,0:T(8,128)(2,1)S(1)} collective-permute-done((bf16[32,3456]{1,0:T(8,128)(2,1)S(1)}, bf16[32,3456]{1,0:T(8,128)(2,1)S(1)}, u32[]{:S(2)}, u32[]{:S(2)}) %collective-permute-start.7) | collective-permute-done | bytes 221216 | tf_op jit(solution)/shard_map/ppermute | solution.py:126
  31.9 0.7 copy-done.3
  32.6 4.8 %all-to-all-start = ((bf16[64,2,3584]{2,1,0:T(2,128)(2,1)}), bf16[64,2,3584]{2,1,0:T(2,128)(2,1)S(1)}, u32[]{:S(2)}, u32[]{:S(2)}) async-start(bf16[64,2,3584]{2,1,0:T(2,128)(2,1)} %reshape.96), calls=%async_computation | async-start | bytes 1835008 | tf_op jit(solution)/shard_map/all_to_all | solution.py:163
  37.4 1.7 %copy.21.refs_0_ = bf16[128,3456]{1,0:T(8,128)(2,1)} copy(bf16[128,3456]{0,1:T(8,128)(2,1)S(1)} %bitcast.32) | data formatting | bytes 1769472 | tf_op jit(solution)/shard_map/reshape | solution.py:20
  39.1 13.1 %shard_map.68 = (f32[1,128]{1,0:T(1,128)}, f32[1,128]{1,0:T(1,128)}) custom-call(bf16[128,3456]{1,0:T(8,128)(2,1)} %copy.21.refs_0_, bf16[32,3456]{1,0:T(8,128)(2,1)} %copy-done.1, bf16[32,3456]{1,0:T(8,128)(2,1)} %copy-done.2, bf16[32,3456]{1,0:T(8,128)(2,1)} %copy-done.3, bf16[32,3456]{1,0:T(8,128)(2,1)} %collective-permute-done.8.refs_4_), custom_call_target="tpu_custom_call" | custom-call | tf_op jit(solution)/shard_map/pallas_call | solution.py:62
  52.2 0.3 reshape.97.x_ref
  52.6 0.2 slice_reduce_fusion.2
  52.9 0.7 %select_convert_fusion.w_ref = bf16[576,128]{1,0:T(8,128)(2,1)} fusion(f32[128]{0:T(128)S(1)} %get-tuple-element.23, pred[8,128]{1,0:T(8,128)(4,1)S(1)} %iota_compare_fusion.8, pred[72,128]{1,0:T(8,128)(4,1)S(1)} %iota_compare_fusion.6), kind=kLoop, calls=%fused_computation.4 | loop fusion | flops 147456 | bytes 158208 | tf_op jit(solution)/shard_map/convert_element_type | solution.py:178
  53.6 3.3 %shard_map.69 = f32[8,3456]{1,0:T(8,128)} custom-call(bf16[576,128]{1,0:T(8,128)(2,1)} %select_convert_fusion.w_ref, bf16[128,3584]{1,0:T(8,128)(2,1)} %copy-done), custom_call_target="tpu_custom_call" | custom-call | tf_op jit(solution)/shard_map/pallas_call | solution.py:180
  56.9 0.9 %slice.49 = f32[4,3456]{1,0:T(4,128)S(1)} slice(f32[8,3456]{1,0:T(8,128)} %shard_map.69), slice={[0:4], [0:3456]} | slice | bytes 110592 | tf_op jit(solution)/shard_map/slice | solution.py:185
  58.1 0.2 select_reduce_fusion.1
  58.6 6.2 %collective-permute-start.9 = (f32[5,3456]{1,0:T(8,128)S(1)}, f32[5,3456]{1,0:T(8,128)S(1)}, u32[]{:S(2)}, u32[]{:S(2)}) collective-permute-start(f32[5,3456]{1,0:T(8,128)S(1)} %select_maximum_fusion), channel_id=1, source_target_pairs={{0,1},{1,0},{2,3},{3,2},{4,5},{5,4},{6,7},{7,6},{8,9},{9,8},{10,11... | collective-permute-start | bytes 207368 | tf_op jit(solution)/shard_map/ppermute | solution.py:203
  64.7 1.0 %collective-permute-done.9 = f32[5,3456]{1,0:T(8,128)S(1)} collective-permute-done((f32[5,3456]{1,0:T(8,128)S(1)}, f32[5,3456]{1,0:T(8,128)S(1)}, u32[]{:S(2)}, u32[]{:S(2)}) %collective-permute-start.9) | collective-permute-done | bytes 69152 | tf_op jit(solution)/shard_map/ppermute | solution.py:203
  65.7 0.5 log_add_fusion
  66.3 0.7 %fusion.11 = f32[2,3456]{1,0:T(2,128)} fusion(f32[5,3456]{1,0:T(8,128)S(1)} %collective-permute-done.9, f32[4,3456]{1,0:T(4,128)S(1)} %reshape.99, s32[]{:T(128)S(6)} %select_n.38, f32[2]{0:T(128)S(1)} %fusion.16), kind=kLoop, calls=%fused_computation.29 | loop fusion | flops 13824 | bytes 82956 | tf_op jit(solution)/shard_map/div | solution.py:220
  (51 shorter events, 1.8 us)
Async XLA Ops:
  1.7 7.0 %collective-permute-start = (bf16[2,3456]{1,0:T(2,128)(2,1)S(1)}, bf16[2,3456]{1,0:T(2,128)(2,1)S(1)}, u32[]{:S(2)}, u32[]{:S(2)}) collective-permute-start(bf16[2,3456]{1,0:T(2,128)(2,1)S(1)} %reshape.93), channel_id=1, source_target_pairs={{0,2},{2,4},{4,6},{6,0},{8,10},{10,12},{12,14},{14,8},{16,18},{18,... | collective-permute-start | bytes 41480 | tf_op jit(solution)/shard_map/ppermute | solution.py:119
  3.9 5.1 %collective-permute-start.2 = (bf16[2,3456]{1,0:T(2,128)(2,1)S(1)}, bf16[2,3456]{1,0:T(2,128)(2,1)S(1)}, u32[]{:S(2)}, u32[]{:S(2)}) collective-permute-start(bf16[2,3456]{1,0:T(2,128)(2,1)S(1)} %reshape.93), channel_id=1, source_target_pairs={{0,6},{2,0},{4,2},{6,4},{8,14},{10,8},{12,10},{14,12},{16,22},{18,... | collective-permute-start | bytes 41480 | tf_op jit(solution)/shard_map/ppermute | solution.py:120
  7.3 0.7 copy-start.8
  7.9 0.7 copy-start.4
  7.9 0.7 copy-start.5
  8.7 3.8 %collective-permute-start.1 = (bf16[2,3456]{1,0:T(2,128)(2,1)S(1)}, bf16[2,3456]{1,0:T(2,128)(2,1)S(1)}, u32[]{:S(2)}, u32[]{:S(2)}) collective-permute-start(bf16[2,3456]{1,0:T(2,128)(2,1)S(1)} %collective-permute-done), channel_id=1, source_target_pairs={{0,2},{2,4},{4,6},{6,0},{8,10},{10,12},{12,14},{14,8},{16,18},{18,... | collective-permute-start | bytes 41480 | tf_op jit(solution)/shard_map/ppermute | solution.py:121
  12.6 5.4 %collective-permute-start.3 = (bf16[8,3456]{1,0:T(8,128)(2,1)S(1)}, bf16[8,3456]{1,0:T(8,128)(2,1)S(1)}, u32[]{:S(2)}, u32[]{:S(2)}) collective-permute-start(bf16[8,3456]{1,0:T(8,128)(2,1)S(1)} %pad_maximum_fusion), channel_id=1, source_target_pairs={{0,8},{2,10},{4,12},{6,14},{8,16},{10,18},{12,20},{14,22},{16,24},... | collective-permute-start | bytes 165896 | tf_op jit(solution)/shard_map/ppermute | solution.py:119
  14.3 3.7 %collective-permute-start.5 = (bf16[8,3456]{1,0:T(8,128)(2,1)S(1)}, bf16[8,3456]{1,0:T(8,128)(2,1)S(1)}, u32[]{:S(2)}, u32[]{:S(2)}) collective-permute-start(bf16[8,3456]{1,0:T(8,128)(2,1)S(1)} %pad_maximum_fusion), channel_id=1, source_target_pairs={{0,24},{2,26},{4,28},{6,30},{8,0},{10,2},{12,4},{14,6},{16,8},{18,... | collective-permute-start | bytes 165896 | tf_op jit(solution)/shard_map/ppermute | solution.py:120
  18.0 4.2 %collective-permute-start.4 = (bf16[8,3456]{1,0:T(8,128)(2,1)S(1)}, bf16[8,3456]{1,0:T(8,128)(2,1)S(1)}, u32[]{:S(2)}, u32[]{:S(2)}) collective-permute-start(bf16[8,3456]{1,0:T(8,128)(2,1)S(1)} %collective-permute-done.3), channel_id=1, source_target_pairs={{0,8},{2,10},{4,12},{6,14},{8,16},{10,18},{12,20},{14,22},{16,24},... | collective-permute-start | bytes 165896 | tf_op jit(solution)/shard_map/ppermute | solution.py:121
  22.4 5.3 %copy-start.1 = (bf16[32,3456]{1,0:T(8,128)(2,1)}, bf16[32,3456]{1,0:T(8,128)(2,1)S(1)}, u32[]{:S(2)}) copy-start(bf16[32,3456]{1,0:T(8,128)(2,1)S(1)} %concatenate.14.refs_1_) | copy-start | bytes 663556
  22.4 6.6 %collective-permute-start.6 = (bf16[32,3456]{1,0:T(8,128)(2,1)S(1)}, bf16[32,3456]{1,0:T(8,128)(2,1)S(1)}, u32[]{:S(2)}, u32[]{:S(2)}) collective-permute-start(bf16[32,3456]{1,0:T(8,128)(2,1)S(1)} %concatenate.14.refs_1_), channel_id=1, source_target_pairs={{0,32},{2,34},{4,36},{6,38},{8,40},{10,42},{12,44},{14,46},{16,48}... | collective-permute-start | bytes 663560 | tf_op jit(solution)/shard_map/ppermute | solution.py:126
  23.6 8.2 %collective-permute-start.7 = (bf16[32,3456]{1,0:T(8,128)(2,1)S(1)}, bf16[32,3456]{1,0:T(8,128)(2,1)S(1)}, u32[]{:S(2)}, u32[]{:S(2)}) collective-permute-start(bf16[32,3456]{1,0:T(8,128)(2,1)S(1)} %concatenate.14.refs_1_), channel_id=1, source_target_pairs={{0,64},{2,66},{4,68},{6,70},{8,72},{10,74},{12,76},{14,78},{16,80}... | collective-permute-start | bytes 663560 | tf_op jit(solution)/shard_map/ppermute | solution.py:126
  26.1 5.8 %collective-permute-start.8 = (bf16[32,3456]{1,0:T(8,128)(2,1)S(1)}, bf16[32,3456]{1,0:T(8,128)(2,1)}, u32[]{:S(2)}, u32[]{:S(2)}) collective-permute-start(bf16[32,3456]{1,0:T(8,128)(2,1)S(1)} %concatenate.14.refs_1_), channel_id=1, source_target_pairs={{0,96},{2,98},{4,100},{6,102},{8,104},{10,106},{12,108},{14,110},{... | collective-permute-start | bytes 663560 | tf_op jit(solution)/shard_map/ppermute | solution.py:126
  29.0 2.9 %copy-start.2 = (bf16[32,3456]{1,0:T(8,128)(2,1)}, bf16[32,3456]{1,0:T(8,128)(2,1)S(1)}, u32[]{:S(2)}) copy-start(bf16[32,3456]{1,0:T(8,128)(2,1)S(1)} %collective-permute-done.6.refs_2_) | copy-start | bytes 663556
  31.9 0.7 %copy-start.3 = (bf16[32,3456]{1,0:T(8,128)(2,1)}, bf16[32,3456]{1,0:T(8,128)(2,1)S(1)}, u32[]{:S(2)}) copy-start(bf16[32,3456]{1,0:T(8,128)(2,1)S(1)} %collective-permute-done.7.refs_3_) | copy-start | bytes 663556
  32.6 19.7 %all-to-all-start = ((bf16[64,2,3584]{2,1,0:T(2,128)(2,1)}), bf16[64,2,3584]{2,1,0:T(2,128)(2,1)S(1)}, u32[]{:S(2)}, u32[]{:S(2)}) async-start(bf16[64,2,3584]{2,1,0:T(2,128)(2,1)} %reshape.96), calls=%async_computation | async-start | bytes 1835008 | tf_op jit(solution)/shard_map/all_to_all | solution.py:163
  52.6 1.0 %copy-start = (bf16[128,3584]{1,0:T(8,128)(2,1)}, bf16[128,3584]{1,0:T(8,128)(2,1)S(1)}, u32[]{:S(2)}) copy-start(bf16[128,3584]{1,0:T(8,128)(2,1)S(1)} %reshape.97.x_ref) | copy-start | bytes 2752516
  53.6 4.9 %copy-start.6 = (f32[1,128]{1,0:T(1,128)S(1)}, f32[1,128]{1,0:T(1,128)}, u32[]{:S(2)}) copy-start(f32[1,128]{1,0:T(1,128)} %get-tuple-element.17) | copy-start | bytes 1540
  53.6 4.9 %copy-start.7 = (f32[1,128]{1,0:T(1,128)S(1)}, f32[1,128]{1,0:T(1,128)}, u32[]{:S(2)}) copy-start(f32[1,128]{1,0:T(1,128)} %get-tuple-element.18) | copy-start | bytes 1540
  58.6 7.1 %collective-permute-start.9 = (f32[5,3456]{1,0:T(8,128)S(1)}, f32[5,3456]{1,0:T(8,128)S(1)}, u32[]{:S(2)}, u32[]{:S(2)}) collective-permute-start(f32[5,3456]{1,0:T(8,128)S(1)} %select_maximum_fusion), channel_id=1, source_target_pairs={{0,1},{1,0},{2,3},{3,2},{4,5},{5,4},{6,7},{7,6},{8,9},{9,8},{10,11... | collective-permute-start | bytes 207368 | tf_op jit(solution)/shard_map/ppermute | solution.py:203

commit v19 on v16

--- a/solution.py
+++ b/solution.py
@@ -21,12 +21,14 @@
 
 
 def score_kernel(*refs, scale):
-    p_ref, piece_refs = refs[0], refs[1:-4]
-    max_ref, sum_ref, r_scr, s_scr = refs[-4:]
+    p_ref, piece_refs = refs[0], refs[1:-5]
+    max_ref, sum_ref, r_scr, t_scr, s_scr = refs[-5:]
     flat_len = p_ref.shape[1]
-    columns = jnp.concatenate([piece[...] for piece in piece_refs], axis=0).T
-    r_scr[pl.ds(0, flat_len), :] = columns
-    r_scr[pl.ds(flat_len, flat_len), :] = columns
+    t_scr[...] = jnp.concatenate([piece[...] for piece in piece_refs], axis=0).astype(jnp.float32).T
+    for angle in range(ANGLES):
+        picked = t_scr[pl.ds(angle, RADII, stride=ANGLES), :].astype(r_scr.dtype)
+        r_scr[pl.ds(angle * RADII, RADII), :] = picked
+        r_scr[pl.ds(flat_len + angle * RADII, RADII), :] = picked
     images = p_ref[...]
     half = ANGLES // 2
 
@@ -67,6 +69,7 @@
         ),
         scratch_shapes=[
             pltpu.VMEM((2 * flat_len, ref_count), jnp.bfloat16),
+            pltpu.VMEM((flat_len, ref_count), jnp.float32),
             pltpu.VMEM((ANGLES // 2, row_count, 2 * ref_count), jnp.float32),
         ],
     )(lhs, *pieces)
@@ -149,7 +152,7 @@
     own_rows = jnp.concatenate([own_rows, labels], axis=1)
     outgoing = jnp.dot(placement, own_rows, preferred_element_type=jnp.float32).astype(jnp.bfloat16)
     outgoing = outgoing.reshape(owner_count, capacity, flat_len + label_lanes)
-    pieces, outgoing = staged_gather(angle_major(references), "loop", outgoing)
+    pieces, outgoing = staged_gather(references, "loop", outgoing)
     incoming = lax.all_to_all(outgoing, "loop", split_axis=0, concat_axis=0, tiled=True)
     highest, summed = score_all(particle_rows, pieces)
     incoming, highest, summed = lax.optimization_barrier((incoming, highest, summed))

time: 65.4 us -> 64.6 us (0.988)
  local copies, waits for them, and re-layouts: 9.85 us -> 8.77 us
    reshape x4 -> x1, local copies, waits for them, and re-layouts: 2.77 us -> 1.68 us  [angle_major(): rows.reshape(count, RADII, ANGLES).transpose(0, 2, 1)]
    unnamed x19 -> x21, local copies, waits for them, and re-layouts: 3.25 us -> 3.27 us
  transfers between devices with their start and end apart: 11 -> 11, of which waited for: 4 -> 4; matrix products, arithmetic and copies ran while one was open for 9% -> 9% of each run, Pallas kernels for 20% -> 21%
where the time goes in v19:
time: 64.6 us; the launch traced here: 64.3 us
  starting transfers between devices  25.9 us (40%)
  Pallas kernels  16.8 us (26%)
  waiting for transfers between devices  8.81 us (14%)
  local copies, waits for them, and re-layouts  8.77 us (14%)
  other arithmetic  2.76 us (4%)
  between operations  0.84 us (1%)
    ppermute x9, starting transfers between devices, staged_gather(): parts.append(lax.ppermute(rows, axis, pairs))  16.5 us
    pallas_call x1, Pallas kernels, score_all(): pl.pallas_call(functools.partial(score_kernel, scale=scale), out_shape=(j...  13.5 us
    ppermute x9, waiting for transfers between devices, staged_gather(): parts.append(lax.ppermute(rows, axis, pairs))  7.85 us
    all_to_all x1, starting transfers between devices, local(): lax.all_to_all(outgoing, 'loop', split_axis=0, concat_axis=0, tiled=True)  5.76 us
    ppermute x1, starting transfers between devices, local(): got = lax.ppermute(sent, 'grp', [(0, 1), (1, 0)])  3.63 us
    pallas_call x1, Pallas kernels, local(): pl.pallas_call(average_kernel, out_shape=jax.ShapeDtypeStruct((block, fla...  3.3 us
    unnamed x21, local copies, waits for them, and re-layouts  3.27 us
    reshape x1, local copies, waits for them, and re-layouts, angle_major(): rows.reshape(count, RADII, ANGLES).transpose(0, 2, 1)  1.68 us
  transfers between devices with their start and end apart: 11, of which 4 were waited for; matrix products, arithmetic and copies ran while one was open for 9% of the time, Pallas kernels for 21%

profile of v19, /device:TPU:1, one launch (start us, length us, event | category | flops | bytes accessed | tf_op | source)
XLA Modules:
  0.0 64.3 jit_solution(5978161673302313506)
XLA Ops:
  0.6 2.2 %collective-permute-start = (bf16[2,3456]{1,0:T(2,128)(2,1)}, bf16[2,3456]{1,0:T(2,128)(2,1)S(1)}, u32[]{:S(2)}, u32[]{:S(2)}) collective-permute-start(bf16[2,3456]{1,0:T(2,128)(2,1)} %param.6), channel_id=1, source_target_pairs={{0,2},{2,4},{4,6},{6,0},{8,10},{10,12},{12,14},{14,8},{16,18},{18,... | collective-permute-start | bytes 41480 | tf_op jit(solution)/shard_map/ppermute | solution.py:119
  2.8 2.6 %collective-permute-start.1 = (bf16[2,3456]{1,0:T(2,128)(2,1)}, bf16[2,3456]{1,0:T(2,128)(2,1)S(1)}, u32[]{:S(2)}, u32[]{:S(2)}) collective-permute-start(bf16[2,3456]{1,0:T(2,128)(2,1)} %param.6), channel_id=1, source_target_pairs={{0,4},{2,6},{4,0},{6,2},{8,12},{10,14},{12,8},{14,10},{16,20},{18,... | collective-permute-start | bytes 41480 | tf_op jit(solution)/shard_map/ppermute | solution.py:119
  5.4 1.1 %collective-permute-start.2 = (bf16[2,3456]{1,0:T(2,128)(2,1)}, bf16[2,3456]{1,0:T(2,128)(2,1)S(1)}, u32[]{:S(2)}, u32[]{:S(2)}) collective-permute-start(bf16[2,3456]{1,0:T(2,128)(2,1)} %param.6), channel_id=1, source_target_pairs={{0,6},{2,0},{4,2},{6,4},{8,14},{10,8},{12,10},{14,12},{16,22},{18,... | collective-permute-start | bytes 41480 | tf_op jit(solution)/shard_map/ppermute | solution.py:119
  6.5 1.9 %copy.16 = bf16[128,3456]{0,1:T(8,128)(2,1)S(1)} copy(bf16[128,3456]{1,0:T(8,128)(2,1)} %param.5) | data formatting | bytes 1769472 | tf_op args[0]
  8.5 0.5 copy-done.9
  9.3 0.2 select_reduce_fusion
  9.4 0.3 constant_dynamic-slice_fusion.3
  10.1 1.7 %collective-permute-start.3 = (bf16[8,3456]{1,0:T(8,128)(2,1)S(1)}, bf16[8,3456]{1,0:T(8,128)(2,1)S(1)}, u32[]{:S(2)}, u32[]{:S(2)}) collective-permute-start(bf16[8,3456]{1,0:T(8,128)(2,1)S(1)} %pad_maximum_fusion), channel_id=1, source_target_pairs={{0,8},{2,10},{4,12},{6,14},{8,16},{10,18},{12,20},{14,22},{16,24},... | collective-permute-start | bytes 165896 | tf_op jit(solution)/shard_map/ppermute | solution.py:119
  11.8 3.3 %collective-permute-start.4 = (bf16[8,3456]{1,0:T(8,128)(2,1)S(1)}, bf16[8,3456]{1,0:T(8,128)(2,1)S(1)}, u32[]{:S(2)}, u32[]{:S(2)}) collective-permute-start(bf16[8,3456]{1,0:T(8,128)(2,1)S(1)} %pad_maximum_fusion), channel_id=1, source_target_pairs={{0,16},{2,18},{4,20},{6,22},{8,24},{10,26},{12,28},{14,30},{16,0},... | collective-permute-start | bytes 165896 | tf_op jit(solution)/shard_map/ppermute | solution.py:119
  15.1 0.7 %collective-permute-start.5 = (bf16[8,3456]{1,0:T(8,128)(2,1)S(1)}, bf16[8,3456]{1,0:T(8,128)(2,1)S(1)}, u32[]{:S(2)}, u32[]{:S(2)}) collective-permute-start(bf16[8,3456]{1,0:T(8,128)(2,1)S(1)} %pad_maximum_fusion), channel_id=1, source_target_pairs={{0,24},{2,26},{4,28},{6,30},{8,0},{10,2},{12,4},{14,6},{16,8},{18,... | collective-permute-start | bytes 165896 | tf_op jit(solution)/shard_map/ppermute | solution.py:119
  15.8 1.5 %collective-permute-done.4 = bf16[8,3456]{1,0:T(8,128)(2,1)S(1)} collective-permute-done((bf16[8,3456]{1,0:T(8,128)(2,1)S(1)}, bf16[8,3456]{1,0:T(8,128)(2,1)S(1)}, u32[]{:S(2)}, u32[]{:S(2)}) %collective-permute-start.4) | collective-permute-done | bytes 55328 | tf_op jit(solution)/shard_map/ppermute | solution.py:119
  17.3 1.7 %collective-permute-done.5 = bf16[8,3456]{1,0:T(8,128)(2,1)S(1)} collective-permute-done((bf16[8,3456]{1,0:T(8,128)(2,1)S(1)}, bf16[8,3456]{1,0:T(8,128)(2,1)S(1)}, u32[]{:S(2)}, u32[]{:S(2)}) %collective-permute-start.5) | collective-permute-done | bytes 55328 | tf_op jit(solution)/shard_map/ppermute | solution.py:119
  19.1 1.3 %collective-permute-start.6 = (bf16[32,3456]{1,0:T(8,128)(2,1)S(1)}, bf16[32,3456]{1,0:T(8,128)(2,1)S(1)}, u32[]{:S(2)}, u32[]{:S(2)}) collective-permute-start(bf16[32,3456]{1,0:T(8,128)(2,1)S(1)} %concatenate.14.refs_1_), channel_id=1, source_target_pairs={{0,32},{2,34},{4,36},{6,38},{8,40},{10,42},{12,44},{14,46},{16,48}... | collective-permute-start | bytes 663560 | tf_op jit(solution)/shard_map/ppermute | solution.py:119
  20.4 2.5 %collective-permute-start.7 = (bf16[32,3456]{1,0:T(8,128)(2,1)S(1)}, bf16[32,3456]{1,0:T(8,128)(2,1)S(1)}, u32[]{:S(2)}, u32[]{:S(2)}) collective-permute-start(bf16[32,3456]{1,0:T(8,128)(2,1)S(1)} %concatenate.14.refs_1_), channel_id=1, source_target_pairs={{0,64},{2,66},{4,68},{6,70},{8,72},{10,74},{12,76},{14,78},{16,80}... | collective-permute-start | bytes 663560 | tf_op jit(solution)/shard_map/ppermute | solution.py:119
  22.8 1.2 %collective-permute-start.8 = (bf16[32,3456]{1,0:T(8,128)(2,1)S(1)}, bf16[32,3456]{1,0:T(8,128)(2,1)}, u32[]{:S(2)}, u32[]{:S(2)}) collective-permute-start(bf16[32,3456]{1,0:T(8,128)(2,1)S(1)} %concatenate.14.refs_1_), channel_id=1, source_target_pairs={{0,96},{2,98},{4,100},{6,102},{8,104},{10,106},{12,108},{14,110},{... | collective-permute-start | bytes 663560 | tf_op jit(solution)/shard_map/ppermute | solution.py:119
  24.0 0.4 convolution_convert_fusion
  24.4 1.3 %reshape.88 = bf16[64,2,3584]{2,1,0:T(2,128)(2,1)} reshape(bf16[128,3584]{1,0:T(8,128)(2,1)S(1)} %convolution_convert_fusion) | data formatting | bytes 1835008 | tf_op jit(solution)/shard_map/reshape | solution.py:154
  25.7 4.7 %collective-permute-done.7.refs_3_ = bf16[32,3456]{1,0:T(8,128)(2,1)S(1)} collective-permute-done((bf16[32,3456]{1,0:T(8,128)(2,1)S(1)}, bf16[32,3456]{1,0:T(8,128)(2,1)S(1)}, u32[]{:S(2)}, u32[]{:S(2)}) %collective-permute-start.7) | collective-permute-done | bytes 221216 | tf_op jit(solution)/shard_map/ppermute | solution.py:119
  30.4 0.7 %copy-done.3 = bf16[32,3456]{1,0:T(8,128)(2,1)} copy-done((bf16[32,3456]{1,0:T(8,128)(2,1)}, bf16[32,3456]{1,0:T(8,128)(2,1)S(1)}, u32[]{:S(2)}) %copy-start.3) | copy-done | bytes 221208
  31.1 5.8 %all-to-all-start = ((bf16[64,2,3584]{2,1,0:T(2,128)(2,1)}), bf16[64,2,3584]{2,1,0:T(2,128)(2,1)S(1)}, u32[]{:S(2)}, u32[]{:S(2)}) async-start(bf16[64,2,3584]{2,1,0:T(2,128)(2,1)} %reshape.88), calls=%async_computation | async-start | bytes 1835008 | tf_op jit(solution)/shard_map/all_to_all | solution.py:156
  36.8 1.7 %copy.18.refs_0_ = bf16[128,3456]{1,0:T(8,128)(2,1)} copy(bf16[128,3456]{0,1:T(8,128)(2,1)S(1)} %bitcast.31) | data formatting | bytes 1769472 | tf_op jit(solution)/shard_map/reshape | solution.py:20
  38.5 13.5 %shard_map.68 = (f32[1,128]{1,0:T(1,128)}, f32[1,128]{1,0:T(1,128)}) custom-call(bf16[128,3456]{1,0:T(8,128)(2,1)} %copy.18.refs_0_, bf16[32,3456]{1,0:T(8,128)(2,1)} %copy-done.1, bf16[32,3456]{1,0:T(8,128)(2,1)} %copy-done.2, bf16[32,3456]{1,0:T(8,128)(2,1)} %copy-done.3, bf16[32,3456]{1,0:T(8,128)(2,1)} %collective-permute-done.8.refs_4_), custom_call_target="tpu_custom_call" | custom-call | tf_op jit(solution)/shard_map/pallas_call | solution.py:64
  52.0 0.3 reshape.89.x_ref
  52.4 0.2 slice_reduce_fusion.2
  52.6 0.7 %select_convert_fusion.w_ref = bf16[576,128]{1,0:T(8,128)(2,1)} fusion(f32[128]{0:T(128)S(1)} %get-tuple-element.23, pred[8,128]{1,0:T(8,128)(4,1)S(1)} %iota_compare_fusion.8, pred[72,128]{1,0:T(8,128)(4,1)S(1)} %iota_compare_fusion.6), kind=kLoop, calls=%fused_computation.4 | loop fusion | flops 147456 | bytes 158208 | tf_op jit(solution)/shard_map/convert_element_type | solution.py:171
  53.4 3.3 %shard_map.69 = f32[8,3456]{1,0:T(8,128)} custom-call(bf16[576,128]{1,0:T(8,128)(2,1)} %select_convert_fusion.w_ref, bf16[128,3584]{1,0:T(8,128)(2,1)} %copy-done), custom_call_target="tpu_custom_call" | custom-call | tf_op jit(solution)/shard_map/pallas_call | solution.py:173
  56.7 0.9 %slice.49 = f32[4,3456]{1,0:T(4,128)S(1)} slice(f32[8,3456]{1,0:T(8,128)} %shard_map.69), slice={[0:4], [0:3456]} | slice | bytes 110592 | tf_op jit(solution)/shard_map/slice | solution.py:178
  57.9 0.2 select_reduce_fusion.1
  58.3 3.6 %collective-permute-start.9 = (f32[5,3456]{1,0:T(8,128)S(1)}, f32[5,3456]{1,0:T(8,128)S(1)}, u32[]{:S(2)}, u32[]{:S(2)}) collective-permute-start(f32[5,3456]{1,0:T(8,128)S(1)} %select_maximum_fusion), channel_id=1, source_target_pairs={{0,1},{1,0},{2,3},{3,2},{4,5},{5,4},{6,7},{7,6},{8,9},{9,8},{10,11... | collective-permute-start | bytes 207368 | tf_op jit(solution)/shard_map/ppermute | solution.py:196
  62.0 1.0 %collective-permute-done.9 = f32[5,3456]{1,0:T(8,128)S(1)} collective-permute-done((f32[5,3456]{1,0:T(8,128)S(1)}, f32[5,3456]{1,0:T(8,128)S(1)}, u32[]{:S(2)}, u32[]{:S(2)}) %collective-permute-start.9) | collective-permute-done | bytes 69152 | tf_op jit(solution)/shard_map/ppermute | solution.py:196
  63.0 0.5 log_add_fusion
  63.6 0.7 %fusion.11 = f32[2,3456]{1,0:T(2,128)} fusion(f32[5,3456]{1,0:T(8,128)S(1)} %collective-permute-done.9, f32[4,3456]{1,0:T(4,128)S(1)} %reshape.91, s32[]{:T(128)S(6)} %select_n.38, f32[2]{0:T(128)S(1)} %fusion.16), kind=kLoop, calls=%fused_computation.29 | loop fusion | flops 13824 | bytes 82956 | tf_op jit(solution)/shard_map/div | solution.py:213
  (50 shorter events, 1.5 us)
Async XLA Ops:
  0.6 9.3 %collective-permute-start = (bf16[2,3456]{1,0:T(2,128)(2,1)}, bf16[2,3456]{1,0:T(2,128)(2,1)S(1)}, u32[]{:S(2)}, u32[]{:S(2)}) collective-permute-start(bf16[2,3456]{1,0:T(2,128)(2,1)} %param.6), channel_id=1, source_target_pairs={{0,2},{2,4},{4,6},{6,0},{8,10},{10,12},{12,14},{14,8},{16,18},{18,... | collective-permute-start | bytes 41480 | tf_op jit(solution)/shard_map/ppermute | solution.py:119
  2.8 7.1 %collective-permute-start.1 = (bf16[2,3456]{1,0:T(2,128)(2,1)}, bf16[2,3456]{1,0:T(2,128)(2,1)S(1)}, u32[]{:S(2)}, u32[]{:S(2)}) collective-permute-start(bf16[2,3456]{1,0:T(2,128)(2,1)} %param.6), channel_id=1, source_target_pairs={{0,4},{2,6},{4,0},{6,2},{8,12},{10,14},{12,8},{14,10},{16,20},{18,... | collective-permute-start | bytes 41480 | tf_op jit(solution)/shard_map/ppermute | solution.py:119
  5.4 4.5 %collective-permute-start.2 = (bf16[2,3456]{1,0:T(2,128)(2,1)}, bf16[2,3456]{1,0:T(2,128)(2,1)S(1)}, u32[]{:S(2)}, u32[]{:S(2)}) collective-permute-start(bf16[2,3456]{1,0:T(2,128)(2,1)} %param.6), channel_id=1, source_target_pairs={{0,6},{2,0},{4,2},{6,4},{8,14},{10,8},{12,10},{14,12},{16,22},{18,... | collective-permute-start | bytes 41480 | tf_op jit(solution)/shard_map/ppermute | solution.py:119
  8.4 0.7 %copy-start.9 = (s32[64]{0:T(128)S(1)}, s32[64]{0:T(128)}, u32[]{:S(2)}) copy-start(s32[64]{0:T(128)} %param.7) | copy-start | bytes 772
  9.2 0.7 %copy-start.5 = (s32[64]{0:T(128)S(1)}, s32[64]{0:T(128)}, u32[]{:S(2)}) copy-start(s32[64]{0:T(128)} %param.9) | copy-start | bytes 772
  9.2 0.7 %copy-start.6 = (s32[64]{0:T(128)S(1)}, s32[64]{0:T(128)}, u32[]{:S(2)}) copy-start(s32[64]{0:T(128)} %param.8) | copy-start | bytes 772
  9.3 0.7 %copy-start.4 = (bf16[2,3456]{1,0:T(2,128)(2,1)S(1)}, bf16[2,3456]{1,0:T(2,128)(2,1)}, u32[]{:S(2)}) copy-start(bf16[2,3456]{1,0:T(2,128)(2,1)} %param.6) | copy-start | bytes 41476
  10.1 5.8 %collective-permute-start.3 = (bf16[8,3456]{1,0:T(8,128)(2,1)S(1)}, bf16[8,3456]{1,0:T(8,128)(2,1)S(1)}, u32[]{:S(2)}, u32[]{:S(2)}) collective-permute-start(bf16[8,3456]{1,0:T(8,128)(2,1)S(1)} %pad_maximum_fusion), channel_id=1, source_target_pairs={{0,8},{2,10},{4,12},{6,14},{8,16},{10,18},{12,20},{14,22},{16,24},... | collective-permute-start | bytes 165896 | tf_op jit(solution)/shard_map/ppermute | solution.py:119
  11.8 5.5 %collective-permute-start.4 = (bf16[8,3456]{1,0:T(8,128)(2,1)S(1)}, bf16[8,3456]{1,0:T(8,128)(2,1)S(1)}, u32[]{:S(2)}, u32[]{:S(2)}) collective-permute-start(bf16[8,3456]{1,0:T(8,128)(2,1)S(1)} %pad_maximum_fusion), channel_id=1, source_target_pairs={{0,16},{2,18},{4,20},{6,22},{8,24},{10,26},{12,28},{14,30},{16,0},... | collective-permute-start | bytes 165896 | tf_op jit(solution)/shard_map/ppermute | solution.py:119
  15.1 3.9 %collective-permute-start.5 = (bf16[8,3456]{1,0:T(8,128)(2,1)S(1)}, bf16[8,3456]{1,0:T(8,128)(2,1)S(1)}, u32[]{:S(2)}, u32[]{:S(2)}) collective-permute-start(bf16[8,3456]{1,0:T(8,128)(2,1)S(1)} %pad_maximum_fusion), channel_id=1, source_target_pairs={{0,24},{2,26},{4,28},{6,30},{8,0},{10,2},{12,4},{14,6},{16,8},{18,... | collective-permute-start | bytes 165896 | tf_op jit(solution)/shard_map/ppermute | solution.py:119
  19.1 5.3 %copy-start.1 = (bf16[32,3456]{1,0:T(8,128)(2,1)}, bf16[32,3456]{1,0:T(8,128)(2,1)S(1)}, u32[]{:S(2)}) copy-start(bf16[32,3456]{1,0:T(8,128)(2,1)S(1)} %concatenate.14.refs_1_) | copy-start | bytes 663556
  19.1 6.6 %collective-permute-start.6 = (bf16[32,3456]{1,0:T(8,128)(2,1)S(1)}, bf16[32,3456]{1,0:T(8,128)(2,1)S(1)}, u32[]{:S(2)}, u32[]{:S(2)}) collective-permute-start(bf16[32,3456]{1,0:T(8,128)(2,1)S(1)} %concatenate.14.refs_1_), channel_id=1, source_target_pairs={{0,32},{2,34},{4,36},{6,38},{8,40},{10,42},{12,44},{14,46},{16,48}... | collective-permute-start | bytes 663560 | tf_op jit(solution)/shard_map/ppermute | solution.py:119
  20.4 10.0 %collective-permute-start.7 = (bf16[32,3456]{1,0:T(8,128)(2,1)S(1)}, bf16[32,3456]{1,0:T(8,128)(2,1)S(1)}, u32[]{:S(2)}, u32[]{:S(2)}) collective-permute-start(bf16[32,3456]{1,0:T(8,128)(2,1)S(1)} %concatenate.14.refs_1_), channel_id=1, source_target_pairs={{0,64},{2,66},{4,68},{6,70},{8,72},{10,74},{12,76},{14,78},{16,80}... | collective-permute-start | bytes 663560 | tf_op jit(solution)/shard_map/ppermute | solution.py:119
  22.8 7.6 %collective-permute-start.8 = (bf16[32,3456]{1,0:T(8,128)(2,1)S(1)}, bf16[32,3456]{1,0:T(8,128)(2,1)}, u32[]{:S(2)}, u32[]{:S(2)}) collective-permute-start(bf16[32,3456]{1,0:T(8,128)(2,1)S(1)} %concatenate.14.refs_1_), channel_id=1, source_target_pairs={{0,96},{2,98},{4,100},{6,102},{8,104},{10,106},{12,108},{14,110},{... | collective-permute-start | bytes 663560 | tf_op jit(solution)/shard_map/ppermute | solution.py:119
  25.7 4.7 %copy-start.2 = (bf16[32,3456]{1,0:T(8,128)(2,1)}, bf16[32,3456]{1,0:T(8,128)(2,1)S(1)}, u32[]{:S(2)}) copy-start(bf16[32,3456]{1,0:T(8,128)(2,1)S(1)} %collective-permute-done.6.refs_2_) | copy-start | bytes 663556
  30.4 0.7 %copy-start.3 = (bf16[32,3456]{1,0:T(8,128)(2,1)}, bf16[32,3456]{1,0:T(8,128)(2,1)S(1)}, u32[]{:S(2)}) copy-start(bf16[32,3456]{1,0:T(8,128)(2,1)S(1)} %collective-permute-done.7.refs_3_) | copy-start | bytes 663556
  31.1 20.9 %all-to-all-start = ((bf16[64,2,3584]{2,1,0:T(2,128)(2,1)}), bf16[64,2,3584]{2,1,0:T(2,128)(2,1)S(1)}, u32[]{:S(2)}, u32[]{:S(2)}) async-start(bf16[64,2,3584]{2,1,0:T(2,128)(2,1)} %reshape.88), calls=%async_computation | async-start | bytes 1835008 | tf_op jit(solution)/shard_map/all_to_all | solution.py:156
  52.3 1.0 %copy-start = (bf16[128,3584]{1,0:T(8,128)(2,1)}, bf16[128,3584]{1,0:T(8,128)(2,1)S(1)}, u32[]{:S(2)}) copy-start(bf16[128,3584]{1,0:T(8,128)(2,1)S(1)} %reshape.89.x_ref) | copy-start | bytes 2752516
  53.4 4.9 %copy-start.7 = (f32[1,128]{1,0:T(1,128)S(1)}, f32[1,128]{1,0:T(1,128)}, u32[]{:S(2)}) copy-start(f32[1,128]{1,0:T(1,128)} %get-tuple-element.17) | copy-start | bytes 1540
  53.4 4.9 %copy-start.8 = (f32[1,128]{1,0:T(1,128)S(1)}, f32[1,128]{1,0:T(1,128)}, u32[]{:S(2)}) copy-start(f32[1,128]{1,0:T(1,128)} %get-tuple-element.18) | copy-start | bytes 1540
  58.3 4.6 %collective-permute-start.9 = (f32[5,3456]{1,0:T(8,128)S(1)}, f32[5,3456]{1,0:T(8,128)S(1)}, u32[]{:S(2)}, u32[]{:S(2)}) collective-permute-start(f32[5,3456]{1,0:T(8,128)S(1)} %select_maximum_fusion), channel_id=1, source_target_pairs={{0,1},{1,0},{2,3},{3,2},{4,5},{5,4},{6,7},{7,6},{8,9},{9,8},{10,11... | collective-permute-start | bytes 207368 | tf_op jit(solution)/shard_map/ppermute | solution.py:196

commit v20 on v19

--- a/solution.py
+++ b/solution.py
@@ -76,10 +76,17 @@
     return highest[0], summed[0]
 
 
-def average_kernel(w_ref, x_ref, o_ref, s_scr):
+def average_kernel(x_ref, o_ref, w_out_ref, w_scr, s_scr):
     block = o_ref.shape[0]
     flat_len = o_ref.shape[1]
-    s_scr[...] = jnp.dot(w_ref[...], x_ref[:, :flat_len], preferred_element_type=jnp.float32)
+    labels = x_ref[:, flat_len:].astype(jnp.float32).T
+    member, rotation, weight = labels[0:1, :], labels[1:2, :], labels[2:3, :]
+    row = lax.broadcasted_iota(jnp.int32, w_scr.shape, 0)
+    chosen = ((row // block).astype(jnp.float32) == rotation) & ((row % block).astype(jnp.float32) == member)
+    w_scr[...] = jnp.where(chosen, weight, 0.0).astype(w_scr.dtype)
+    class_row = lax.broadcasted_iota(jnp.int32, (block, x_ref.shape[0]), 0).astype(jnp.float32)
+    w_out_ref[...] = jnp.sum(jnp.where(class_row == member, weight, 0.0), axis=1, keepdims=True)
+    s_scr[...] = jnp.dot(w_scr[...], x_ref[:, :flat_len], preferred_element_type=jnp.float32)
     step = 8
     total = None
     for part in range(step):
@@ -157,28 +164,21 @@
     highest, summed = score_all(particle_rows, pieces)
     incoming, highest, summed = lax.optimization_barrier((incoming, highest, summed))
     incoming = incoming.reshape(slot_count, flat_len + label_lanes)
-    labels_in = incoming[:, flat_len : flat_len + 3]
-    labels_in = labels_in.astype(jnp.float32)
-    member_in = labels_in[:, 0]
-    rotation = labels_in[:, 1]
-    weight_of = labels_in[:, 2]
     block = -(-per_owner // 8) * 8
-    angle_grid = jnp.arange(ANGLES, dtype=jnp.float32)
-    member_grid = jnp.arange(block, dtype=jnp.float32)
-    chosen = (angle_grid[:, None, None] == rotation[None, None, :]) & (
-        member_grid[None, :, None] == member_in[None, None, :]
-    )
-    by_angle = jnp.where(chosen, weight_of[None, None, :], 0.0).astype(jnp.bfloat16)
-    by_angle = by_angle.reshape(ANGLES * block, slot_count)
-    partial_sums = pl.pallas_call(
+    partial_sums, partial_weight = pl.pallas_call(
         average_kernel,
-        out_shape=jax.ShapeDtypeStruct((block, flat_len), jnp.float32),
-        scratch_shapes=[pltpu.VMEM((ANGLES * block, flat_len), jnp.float32)],
-    )(by_angle, incoming)
+        out_shape=(
+            jax.ShapeDtypeStruct((block, flat_len), jnp.float32),
+            jax.ShapeDtypeStruct((block, 1), jnp.float32),
+        ),
+        scratch_shapes=[
+            pltpu.VMEM((ANGLES * block, slot_count), jnp.bfloat16),
+            pltpu.VMEM((ANGLES * block, flat_len), jnp.float32),
+        ],
+    )(incoming)
     partial_sums = partial_sums[:per_owner].reshape(per_owner, ANGLES, RADII).transpose(0, 2, 1)
     partial_sums = partial_sums.reshape(per_owner, flat_len)
-    weighted = (member_grid[:per_owner, None] == member_in[None, :]).astype(jnp.float32) * weight_of[None, :]
-    partial_weight = jnp.sum(weighted, axis=1)
+    partial_weight = partial_weight[:per_owner, 0]
     own_classes = references.shape[0]
     stats = jnp.stack([highest, summed], axis=0)
     if grp_size == 2:

time: 64.6 us -> 65.4 us (1.012)
  local copies, waits for them, and re-layouts: 8.77 us -> 10.4 us
  other arithmetic: 2.76 us -> 1.86 us
    reshape x1, local copies, waits for them, and re-layouts: 0.34 us -> 1.28 us  [local(): incoming = incoming.reshape(slot_count, flat_len + label_lanes)]
    convert_element_type x2 -> x0, other arithmetic: 0.72 us -> none  [the longest x1 0.72 us: local(): jnp.where(chosen, weight_of[None, None, :], 0.0).astype(jnp.bfloat16)]
    unnamed x21 -> x19, local copies, waits for them, and re-layouts: 3.27 us -> 3.29 us
where the time goes in v20:
time: 65.4 us; the launch traced here: 65 us
  starting transfers between devices  25.9 us (40%)
  Pallas kernels  16.9 us (26%)
  local copies, waits for them, and re-layouts  10.4 us (16%)
  waiting for transfers between devices  8.8 us (13%)
  other arithmetic  1.86 us (3%)
  between operations  0.81 us (1%)
    ppermute x9, starting transfers between devices, staged_gather(): parts.append(lax.ppermute(rows, axis, pairs))  16.5 us
    pallas_call x1, Pallas kernels, score_all(): pl.pallas_call(functools.partial(score_kernel, scale=scale), out_shape=(j...  13.5 us
    ppermute x9, waiting for transfers between devices, staged_gather(): parts.append(lax.ppermute(rows, axis, pairs))  7.84 us
    all_to_all x1, starting transfers between devices, local(): lax.all_to_all(outgoing, 'loop', split_axis=0, concat_axis=0, tiled=True)  5.74 us
    ppermute x1, starting transfers between devices, local(): got = lax.ppermute(sent, 'grp', [(0, 1), (1, 0)])  3.63 us
    pallas_call x1, Pallas kernels, local(): pl.pallas_call(average_kernel, out_shape=(jax.ShapeDtypeStruct((block, fl...  3.31 us
    unnamed x19, local copies, waits for them, and re-layouts  3.29 us
    reshape x1, local copies, waits for them, and re-layouts, angle_major(): rows.reshape(count, RADII, ANGLES).transpose(0, 2, 1)  1.71 us
  transfers between devices with their start and end apart: 11, of which 4 were waited for; matrix products, arithmetic and copies ran while one was open for 9% of the time, Pallas kernels for 21%

profile of v20, /device:TPU:1, one launch (start us, length us, event | category | flops | bytes accessed | tf_op | source)
XLA Modules:
  0.0 65.0 jit_solution(14422061297909123258)
XLA Ops:
  0.6 2.2 %collective-permute-start = (bf16[2,3456]{1,0:T(2,128)(2,1)}, bf16[2,3456]{1,0:T(2,128)(2,1)S(1)}, u32[]{:S(2)}, u32[]{:S(2)}) collective-permute-start(bf16[2,3456]{1,0:T(2,128)(2,1)} %param.6), channel_id=1, source_target_pairs={{0,2},{2,4},{4,6},{6,0},{8,10},{10,12},{12,14},{14,8},{16,18},{18,... | collective-permute-start | bytes 41480 | tf_op jit(solution)/shard_map/ppermute | solution.py:126
  2.8 2.6 %collective-permute-start.1 = (bf16[2,3456]{1,0:T(2,128)(2,1)}, bf16[2,3456]{1,0:T(2,128)(2,1)S(1)}, u32[]{:S(2)}, u32[]{:S(2)}) collective-permute-start(bf16[2,3456]{1,0:T(2,128)(2,1)} %param.6), channel_id=1, source_target_pairs={{0,4},{2,6},{4,0},{6,2},{8,12},{10,14},{12,8},{14,10},{16,20},{18,... | collective-permute-start | bytes 41480 | tf_op jit(solution)/shard_map/ppermute | solution.py:126
  5.4 1.1 %collective-permute-start.2 = (bf16[2,3456]{1,0:T(2,128)(2,1)}, bf16[2,3456]{1,0:T(2,128)(2,1)S(1)}, u32[]{:S(2)}, u32[]{:S(2)}) collective-permute-start(bf16[2,3456]{1,0:T(2,128)(2,1)} %param.6), channel_id=1, source_target_pairs={{0,6},{2,0},{4,2},{6,4},{8,14},{10,8},{12,10},{14,12},{16,22},{18,... | collective-permute-start | bytes 41480 | tf_op jit(solution)/shard_map/ppermute | solution.py:126
  6.5 1.9 %copy.13 = bf16[128,3456]{0,1:T(8,128)(2,1)S(1)} copy(bf16[128,3456]{1,0:T(8,128)(2,1)} %param.5) | data formatting | bytes 1769472 | tf_op args[0]
  8.5 0.5 copy-done.8
  9.3 0.2 select_reduce_fusion
  9.4 0.3 constant_dynamic-slice_fusion.4
  10.1 1.7 %collective-permute-start.3 = (bf16[8,3456]{1,0:T(8,128)(2,1)S(1)}, bf16[8,3456]{1,0:T(8,128)(2,1)S(1)}, u32[]{:S(2)}, u32[]{:S(2)}) collective-permute-start(bf16[8,3456]{1,0:T(8,128)(2,1)S(1)} %pad_maximum_fusion), channel_id=1, source_target_pairs={{0,8},{2,10},{4,12},{6,14},{8,16},{10,18},{12,20},{14,22},{16,24},... | collective-permute-start | bytes 165896 | tf_op jit(solution)/shard_map/ppermute | solution.py:126
  11.8 3.3 %collective-permute-start.4 = (bf16[8,3456]{1,0:T(8,128)(2,1)S(1)}, bf16[8,3456]{1,0:T(8,128)(2,1)S(1)}, u32[]{:S(2)}, u32[]{:S(2)}) collective-permute-start(bf16[8,3456]{1,0:T(8,128)(2,1)S(1)} %pad_maximum_fusion), channel_id=1, source_target_pairs={{0,16},{2,18},{4,20},{6,22},{8,24},{10,26},{12,28},{14,30},{16,0},... | collective-permute-start | bytes 165896 | tf_op jit(solution)/shard_map/ppermute | solution.py:126
  15.1 0.7 %collective-permute-start.5 = (bf16[8,3456]{1,0:T(8,128)(2,1)S(1)}, bf16[8,3456]{1,0:T(8,128)(2,1)S(1)}, u32[]{:S(2)}, u32[]{:S(2)}) collective-permute-start(bf16[8,3456]{1,0:T(8,128)(2,1)S(1)} %pad_maximum_fusion), channel_id=1, source_target_pairs={{0,24},{2,26},{4,28},{6,30},{8,0},{10,2},{12,4},{14,6},{16,8},{18,... | collective-permute-start | bytes 165896 | tf_op jit(solution)/shard_map/ppermute | solution.py:126
  15.8 1.5 %collective-permute-done.4 = bf16[8,3456]{1,0:T(8,128)(2,1)S(1)} collective-permute-done((bf16[8,3456]{1,0:T(8,128)(2,1)S(1)}, bf16[8,3456]{1,0:T(8,128)(2,1)S(1)}, u32[]{:S(2)}, u32[]{:S(2)}) %collective-permute-start.4) | collective-permute-done | bytes 55328 | tf_op jit(solution)/shard_map/ppermute | solution.py:126
  17.3 1.7 %collective-permute-done.5 = bf16[8,3456]{1,0:T(8,128)(2,1)S(1)} collective-permute-done((bf16[8,3456]{1,0:T(8,128)(2,1)S(1)}, bf16[8,3456]{1,0:T(8,128)(2,1)S(1)}, u32[]{:S(2)}, u32[]{:S(2)}) %collective-permute-start.5) | collective-permute-done | bytes 55328 | tf_op jit(solution)/shard_map/ppermute | solution.py:126
  19.0 0.1 concatenate.14.refs_1_
  19.1 1.3 %collective-permute-start.6 = (bf16[32,3456]{1,0:T(8,128)(2,1)S(1)}, bf16[32,3456]{1,0:T(8,128)(2,1)S(1)}, u32[]{:S(2)}, u32[]{:S(2)}) collective-permute-start(bf16[32,3456]{1,0:T(8,128)(2,1)S(1)} %concatenate.14.refs_1_), channel_id=1, source_target_pairs={{0,32},{2,34},{4,36},{6,38},{8,40},{10,42},{12,44},{14,46},{16,48}... | collective-permute-start | bytes 663560 | tf_op jit(solution)/shard_map/ppermute | solution.py:126
  20.4 2.5 %collective-permute-start.7 = (bf16[32,3456]{1,0:T(8,128)(2,1)S(1)}, bf16[32,3456]{1,0:T(8,128)(2,1)S(1)}, u32[]{:S(2)}, u32[]{:S(2)}) collective-permute-start(bf16[32,3456]{1,0:T(8,128)(2,1)S(1)} %concatenate.14.refs_1_), channel_id=1, source_target_pairs={{0,64},{2,66},{4,68},{6,70},{8,72},{10,74},{12,76},{14,78},{16,80}... | collective-permute-start | bytes 663560 | tf_op jit(solution)/shard_map/ppermute | solution.py:126
  22.8 1.2 %collective-permute-start.8 = (bf16[32,3456]{1,0:T(8,128)(2,1)S(1)}, bf16[32,3456]{1,0:T(8,128)(2,1)}, u32[]{:S(2)}, u32[]{:S(2)}) collective-permute-start(bf16[32,3456]{1,0:T(8,128)(2,1)S(1)} %concatenate.14.refs_1_), channel_id=1, source_target_pairs={{0,96},{2,98},{4,100},{6,102},{8,104},{10,106},{12,108},{14,110},{... | collective-permute-start | bytes 663560 | tf_op jit(solution)/shard_map/ppermute | solution.py:126
  24.0 0.4 convolution_convert_fusion
  24.4 1.3 %reshape.31 = bf16[64,2,3584]{2,1,0:T(2,128)(2,1)} reshape(bf16[128,3584]{1,0:T(8,128)(2,1)S(1)} %convolution_convert_fusion) | data formatting | bytes 1835008 | tf_op jit(solution)/shard_map/reshape | solution.py:161
  25.7 4.7 %collective-permute-done.7.refs_3_ = bf16[32,3456]{1,0:T(8,128)(2,1)S(1)} collective-permute-done((bf16[32,3456]{1,0:T(8,128)(2,1)S(1)}, bf16[32,3456]{1,0:T(8,128)(2,1)S(1)}, u32[]{:S(2)}, u32[]{:S(2)}) %collective-permute-start.7) | collective-permute-done | bytes 221216 | tf_op jit(solution)/shard_map/ppermute | solution.py:126
  30.4 0.7 %copy-done.2 = bf16[32,3456]{1,0:T(8,128)(2,1)} copy-done((bf16[32,3456]{1,0:T(8,128)(2,1)}, bf16[32,3456]{1,0:T(8,128)(2,1)S(1)}, u32[]{:S(2)}) %copy-start.2) | copy-done | bytes 221208
  31.1 5.7 %all-to-all-start = ((bf16[64,2,3584]{2,1,0:T(2,128)(2,1)}), bf16[64,2,3584]{2,1,0:T(2,128)(2,1)S(1)}, u32[]{:S(2)}, u32[]{:S(2)}) async-start(bf16[64,2,3584]{2,1,0:T(2,128)(2,1)} %reshape.31), calls=%async_computation | async-start | bytes 1835008 | tf_op jit(solution)/shard_map/all_to_all | solution.py:163
  36.8 1.7 %copy.15.refs_0_ = bf16[128,3456]{1,0:T(8,128)(2,1)} copy(bf16[128,3456]{0,1:T(8,128)(2,1)S(1)} %bitcast.25) | data formatting | bytes 1769472 | tf_op jit(solution)/shard_map/reshape | solution.py:20
  38.5 13.5 %shard_map.68 = (f32[1,128]{1,0:T(1,128)}, f32[1,128]{1,0:T(1,128)}) custom-call(bf16[128,3456]{1,0:T(8,128)(2,1)} %copy.15.refs_0_, bf16[32,3456]{1,0:T(8,128)(2,1)} %copy-done, bf16[32,3456]{1,0:T(8,128)(2,1)} %copy-done.1, bf16[32,3456]{1,0:T(8,128)(2,1)} %copy-done.2, bf16[32,3456]{1,0:T(8,128)(2,1)} %collective-permute-done.8.refs_4_), custom_call_target="tpu_custom_call" | custom-call | tf_op jit(solution)/shard_map/pallas_call | solution.py:64
  52.1 1.3 %reshape.32.x_ref = bf16[128,3584]{1,0:T(8,128)(2,1)} reshape(bf16[64,2,3584]{2,1,0:T(2,128)(2,1)S(1)} %all-to-all-done) | data formatting | bytes 1835008 | tf_op jit(solution)/shard_map/reshape | solution.py:166
  53.4 3.3 %shard_map.69 = (f32[8,3456]{1,0:T(8,128)}, f32[8,1]{1,0:T(8,128)}) custom-call(bf16[128,3584]{1,0:T(8,128)(2,1)} %reshape.32.x_ref), custom_call_target="tpu_custom_call" | custom-call | tf_op jit(solution)/shard_map/pallas_call | solution.py:168
  56.7 0.9 %slice.22 = f32[4,3456]{1,0:T(4,128)S(1)} slice(f32[8,3456]{1,0:T(8,128)} %get-tuple-element.24), slice={[0:4], [0:3456]} | slice | bytes 110592 | tf_op jit(solution)/shard_map/slice | solution.py:179
  57.8 0.1 reshape.34
  57.9 0.7 %slice.23 = f32[4,1]{1,0:T(4,128)S(1)} slice(f32[8,1]{1,0:T(8,128)} %get-tuple-element.25), slice={[0:4], [0:1]} | slice | bytes 32 | tf_op jit(solution)/shard_map/slice | solution.py:181
  58.9 3.6 %collective-permute-start.9 = (f32[5,3456]{1,0:T(8,128)S(1)}, f32[5,3456]{1,0:T(8,128)S(1)}, u32[]{:S(2)}, u32[]{:S(2)}) collective-permute-start(f32[5,3456]{1,0:T(8,128)S(1)} %select_maximum_fusion), channel_id=1, source_target_pairs={{0,1},{1,0},{2,3},{3,2},{4,5},{5,4},{6,7},{7,6},{8,9},{9,8},{10,11... | collective-permute-start | bytes 207368 | tf_op jit(solution)/shard_map/ppermute | solution.py:196
  62.5 1.0 %collective-permute-done.9 = f32[5,3456]{1,0:T(8,128)S(1)} collective-permute-done((f32[5,3456]{1,0:T(8,128)S(1)}, f32[5,3456]{1,0:T(8,128)S(1)}, u32[]{:S(2)}, u32[]{:S(2)}) %collective-permute-start.9) | collective-permute-done | bytes 69152 | tf_op jit(solution)/shard_map/ppermute | solution.py:196
  63.6 0.5 log_add_fusion
  64.3 0.7 %fusion.11 = f32[2,3456]{1,0:T(2,128)} fusion(f32[5,3456]{1,0:T(8,128)S(1)} %collective-permute-done.9, f32[4,3456]{1,0:T(4,128)S(1)} %reshape.34, s32[]{:T(128)S(6)} %select_n.32, f32[2]{0:T(128)S(1)} %fusion.13), kind=kLoop, calls=%fused_computation.23 | loop fusion | flops 13824 | bytes 82956 | tf_op jit(solution)/shard_map/div | solution.py:213
  (44 shorter events, 1.3 us)
Async XLA Ops:
  0.6 9.3 %collective-permute-start = (bf16[2,3456]{1,0:T(2,128)(2,1)}, bf16[2,3456]{1,0:T(2,128)(2,1)S(1)}, u32[]{:S(2)}, u32[]{:S(2)}) collective-permute-start(bf16[2,3456]{1,0:T(2,128)(2,1)} %param.6), channel_id=1, source_target_pairs={{0,2},{2,4},{4,6},{6,0},{8,10},{10,12},{12,14},{14,8},{16,18},{18,... | collective-permute-start | bytes 41480 | tf_op jit(solution)/shard_map/ppermute | solution.py:126
  2.8 7.1 %collective-permute-start.1 = (bf16[2,3456]{1,0:T(2,128)(2,1)}, bf16[2,3456]{1,0:T(2,128)(2,1)S(1)}, u32[]{:S(2)}, u32[]{:S(2)}) collective-permute-start(bf16[2,3456]{1,0:T(2,128)(2,1)} %param.6), channel_id=1, source_target_pairs={{0,4},{2,6},{4,0},{6,2},{8,12},{10,14},{12,8},{14,10},{16,20},{18,... | collective-permute-start | bytes 41480 | tf_op jit(solution)/shard_map/ppermute | solution.py:126
  5.4 4.5 %collective-permute-start.2 = (bf16[2,3456]{1,0:T(2,128)(2,1)}, bf16[2,3456]{1,0:T(2,128)(2,1)S(1)}, u32[]{:S(2)}, u32[]{:S(2)}) collective-permute-start(bf16[2,3456]{1,0:T(2,128)(2,1)} %param.6), channel_id=1, source_target_pairs={{0,6},{2,0},{4,2},{6,4},{8,14},{10,8},{12,10},{14,12},{16,22},{18,... | collective-permute-start | bytes 41480 | tf_op jit(solution)/shard_map/ppermute | solution.py:126
  8.4 0.7 %copy-start.8 = (s32[64]{0:T(128)S(1)}, s32[64]{0:T(128)}, u32[]{:S(2)}) copy-start(s32[64]{0:T(128)} %param.7) | copy-start | bytes 772
  9.2 0.7 %copy-start.4 = (s32[64]{0:T(128)S(1)}, s32[64]{0:T(128)}, u32[]{:S(2)}) copy-start(s32[64]{0:T(128)} %param.9) | copy-start | bytes 772
  9.2 0.7 %copy-start.5 = (s32[64]{0:T(128)S(1)}, s32[64]{0:T(128)}, u32[]{:S(2)}) copy-start(s32[64]{0:T(128)} %param.8) | copy-start | bytes 772
  9.3 0.7 %copy-start.3 = (bf16[2,3456]{1,0:T(2,128)(2,1)S(1)}, bf16[2,3456]{1,0:T(2,128)(2,1)}, u32[]{:S(2)}) copy-start(bf16[2,3456]{1,0:T(2,128)(2,1)} %param.6) | copy-start | bytes 41476
  10.1 5.8 %collective-permute-start.3 = (bf16[8,3456]{1,0:T(8,128)(2,1)S(1)}, bf16[8,3456]{1,0:T(8,128)(2,1)S(1)}, u32[]{:S(2)}, u32[]{:S(2)}) collective-permute-start(bf16[8,3456]{1,0:T(8,128)(2,1)S(1)} %pad_maximum_fusion), channel_id=1, source_target_pairs={{0,8},{2,10},{4,12},{6,14},{8,16},{10,18},{12,20},{14,22},{16,24},... | collective-permute-start | bytes 165896 | tf_op jit(solution)/shard_map/ppermute | solution.py:126
  11.8 5.5 %collective-permute-start.4 = (bf16[8,3456]{1,0:T(8,128)(2,1)S(1)}, bf16[8,3456]{1,0:T(8,128)(2,1)S(1)}, u32[]{:S(2)}, u32[]{:S(2)}) collective-permute-start(bf16[8,3456]{1,0:T(8,128)(2,1)S(1)} %pad_maximum_fusion), channel_id=1, source_target_pairs={{0,16},{2,18},{4,20},{6,22},{8,24},{10,26},{12,28},{14,30},{16,0},... | collective-permute-start | bytes 165896 | tf_op jit(solution)/shard_map/ppermute | solution.py:126
  15.1 3.9 %collective-permute-start.5 = (bf16[8,3456]{1,0:T(8,128)(2,1)S(1)}, bf16[8,3456]{1,0:T(8,128)(2,1)S(1)}, u32[]{:S(2)}, u32[]{:S(2)}) collective-permute-start(bf16[8,3456]{1,0:T(8,128)(2,1)S(1)} %pad_maximum_fusion), channel_id=1, source_target_pairs={{0,24},{2,26},{4,28},{6,30},{8,0},{10,2},{12,4},{14,6},{16,8},{18,... | collective-permute-start | bytes 165896 | tf_op jit(solution)/shard_map/ppermute | solution.py:126
  19.1 5.3 %copy-start = (bf16[32,3456]{1,0:T(8,128)(2,1)}, bf16[32,3456]{1,0:T(8,128)(2,1)S(1)}, u32[]{:S(2)}) copy-start(bf16[32,3456]{1,0:T(8,128)(2,1)S(1)} %concatenate.14.refs_1_) | copy-start | bytes 663556
  19.1 6.6 %collective-permute-start.6 = (bf16[32,3456]{1,0:T(8,128)(2,1)S(1)}, bf16[32,3456]{1,0:T(8,128)(2,1)S(1)}, u32[]{:S(2)}, u32[]{:S(2)}) collective-permute-start(bf16[32,3456]{1,0:T(8,128)(2,1)S(1)} %concatenate.14.refs_1_), channel_id=1, source_target_pairs={{0,32},{2,34},{4,36},{6,38},{8,40},{10,42},{12,44},{14,46},{16,48}... | collective-permute-start | bytes 663560 | tf_op jit(solution)/shard_map/ppermute | solution.py:126
  20.4 10.0 %collective-permute-start.7 = (bf16[32,3456]{1,0:T(8,128)(2,1)S(1)}, bf16[32,3456]{1,0:T(8,128)(2,1)S(1)}, u32[]{:S(2)}, u32[]{:S(2)}) collective-permute-start(bf16[32,3456]{1,0:T(8,128)(2,1)S(1)} %concatenate.14.refs_1_), channel_id=1, source_target_pairs={{0,64},{2,66},{4,68},{6,70},{8,72},{10,74},{12,76},{14,78},{16,80}... | collective-permute-start | bytes 663560 | tf_op jit(solution)/shard_map/ppermute | solution.py:126
  22.8 7.6 %collective-permute-start.8 = (bf16[32,3456]{1,0:T(8,128)(2,1)S(1)}, bf16[32,3456]{1,0:T(8,128)(2,1)}, u32[]{:S(2)}, u32[]{:S(2)}) collective-permute-start(bf16[32,3456]{1,0:T(8,128)(2,1)S(1)} %concatenate.14.refs_1_), channel_id=1, source_target_pairs={{0,96},{2,98},{4,100},{6,102},{8,104},{10,106},{12,108},{14,110},{... | collective-permute-start | bytes 663560 | tf_op jit(solution)/shard_map/ppermute | solution.py:126
  25.7 4.7 %copy-start.1 = (bf16[32,3456]{1,0:T(8,128)(2,1)}, bf16[32,3456]{1,0:T(8,128)(2,1)S(1)}, u32[]{:S(2)}) copy-start(bf16[32,3456]{1,0:T(8,128)(2,1)S(1)} %collective-permute-done.6.refs_2_) | copy-start | bytes 663556
  30.4 0.7 %copy-start.2 = (bf16[32,3456]{1,0:T(8,128)(2,1)}, bf16[32,3456]{1,0:T(8,128)(2,1)S(1)}, u32[]{:S(2)}) copy-start(bf16[32,3456]{1,0:T(8,128)(2,1)S(1)} %collective-permute-done.7.refs_3_) | copy-start | bytes 663556
  31.1 21.0 %all-to-all-start = ((bf16[64,2,3584]{2,1,0:T(2,128)(2,1)}), bf16[64,2,3584]{2,1,0:T(2,128)(2,1)S(1)}, u32[]{:S(2)}, u32[]{:S(2)}) async-start(bf16[64,2,3584]{2,1,0:T(2,128)(2,1)} %reshape.31), calls=%async_computation | async-start | bytes 1835008 | tf_op jit(solution)/shard_map/all_to_all | solution.py:163
  53.4 5.4 %copy-start.6 = (f32[1,128]{1,0:T(1,128)S(1)}, f32[1,128]{1,0:T(1,128)}, u32[]{:S(2)}) copy-start(f32[1,128]{1,0:T(1,128)} %get-tuple-element.19) | copy-start | bytes 1540
  53.4 5.4 %copy-start.7 = (f32[1,128]{1,0:T(1,128)S(1)}, f32[1,128]{1,0:T(1,128)}, u32[]{:S(2)}) copy-start(f32[1,128]{1,0:T(1,128)} %get-tuple-element.20) | copy-start | bytes 1540
  58.9 4.6 %collective-permute-start.9 = (f32[5,3456]{1,0:T(8,128)S(1)}, f32[5,3456]{1,0:T(8,128)S(1)}, u32[]{:S(2)}, u32[]{:S(2)}) collective-permute-start(f32[5,3456]{1,0:T(8,128)S(1)} %select_maximum_fusion), channel_id=1, source_target_pairs={{0,1},{1,0},{2,3},{3,2},{4,5},{5,4},{6,7},{7,6},{8,9},{9,8},{10,11... | collective-permute-start | bytes 207368 | tf_op jit(solution)/shard_map/ppermute | solution.py:196

commit v21 on v19

--- a/solution.py
+++ b/solution.py
@@ -21,15 +21,18 @@
 
 
 def score_kernel(*refs, scale):
-    p_ref, piece_refs = refs[0], refs[1:-5]
-    max_ref, sum_ref, r_scr, t_scr, s_scr = refs[-5:]
+    p_ref, piece_refs = refs[0], refs[1:-7]
+    max_ref, sum_ref, r_scr, t_scr, s_scr, pt_scr, pa_scr = refs[-7:]
     flat_len = p_ref.shape[1]
     t_scr[...] = jnp.concatenate([piece[...] for piece in piece_refs], axis=0).astype(jnp.float32).T
     for angle in range(ANGLES):
         picked = t_scr[pl.ds(angle, RADII, stride=ANGLES), :].astype(r_scr.dtype)
         r_scr[pl.ds(angle * RADII, RADII), :] = picked
         r_scr[pl.ds(flat_len + angle * RADII, RADII), :] = picked
-    images = p_ref[...]
+    pt_scr[...] = p_ref[...].astype(jnp.float32).T
+    for angle in range(ANGLES):
+        pa_scr[pl.ds(angle * RADII, RADII), :] = pt_scr[pl.ds(angle, RADII, stride=ANGLES), :]
+    images = pa_scr[...].T.astype(p_ref.dtype)
     half = ANGLES // 2
 
     def shift_scores(s, carry):
@@ -71,6 +74,8 @@
             pltpu.VMEM((2 * flat_len, ref_count), jnp.bfloat16),
             pltpu.VMEM((flat_len, ref_count), jnp.float32),
             pltpu.VMEM((ANGLES // 2, row_count, 2 * ref_count), jnp.float32),
+            pltpu.VMEM((flat_len, row_count), jnp.float32),
+            pltpu.VMEM((flat_len, row_count), jnp.float32),
         ],
     )(lhs, *pieces)
     return highest[0], summed[0]
@@ -129,8 +134,7 @@
     grp_size = lax.axis_size("grp")
     half_rows = row_count // grp_size
     grp_index = lax.axis_index("grp")
-    particle_rows = angle_major(particles)
-    own_rows = lax.dynamic_slice_in_dim(particle_rows, grp_index * half_rows, half_rows, 0)
+    own_rows = angle_major(lax.dynamic_slice_in_dim(particles, grp_index * half_rows, half_rows, 0))
     owner_count = lax.axis_size("loop")
     per_owner = references.shape[0] * grp_size
     capacity = max(2, row_count // owner_count)
@@ -154,7 +158,7 @@
     outgoing = outgoing.reshape(owner_count, capacity, flat_len + label_lanes)
     pieces, outgoing = staged_gather(references, "loop", outgoing)
     incoming = lax.all_to_all(outgoing, "loop", split_axis=0, concat_axis=0, tiled=True)
-    highest, summed = score_all(particle_rows, pieces)
+    highest, summed = score_all(particles, pieces)
     incoming, highest, summed = lax.optimization_barrier((incoming, highest, summed))
     incoming = incoming.reshape(slot_count, flat_len + label_lanes)
     labels_in = incoming[:, flat_len : flat_len + 3]

time: 64.6 us -> 64 us (level)
  waiting for transfers between devices: 8.81 us -> 5.78 us
  other arithmetic: 2.76 us -> 4.8 us
  local copies, waits for them, and re-layouts: 8.77 us -> 7.52 us
  starting transfers between devices: 25.9 us -> 27 us
    unnamed x21 -> x16, local copies, waits for them, and re-layouts: 3.27 us -> 0.04 us
    ppermute x9, waiting for transfers between devices: 7.85 us -> 4.82 us  [staged_gather(): parts.append(lax.ppermute(rows, axis, pairs))]
    dynamic_slice x1, local copies, waits for them, and re-layouts: 0.32 us -> 1.05 us  [local(): lax.dynamic_slice_in_dim(particles, grp_index * half_rows, half_rows, 0)]
    all_to_all x1, starting transfers between devices: 5.76 us -> 6.5 us  [local(): lax.all_to_all(outgoing, 'loop', split_axis=0, concat_axis=0, tiled=True)]
    concatenate x1, other arithmetic: 0.07 us -> 0.78 us  [staged_gather(): rows = jnp.concatenate(parts, axis=0)]
    another operation x2, other arithmetic: 0.02 us -> 0.69 us  [local(): jnp.stack([member_of, angles, weights], axis=1).astype(jnp.bfloat16)]
    select_n x1, other arithmetic: 0.01 us -> 0.67 us  [local(): owner_of = classes // per_owner]
    reshape x1 -> x2, local copies, waits for them, and re-layouts: 1.68 us -> 2.26 us  [angle_major(): rows.reshape(count, RADII, ANGLES).transpose(0, 2, 1)]
  transfers between devices with their start and end apart: 11 -> 11, of which waited for: 4 -> 3; matrix products, arithmetic and copies ran while one was open for 9% -> 12% of each run, Pallas kernels for 21% -> 22%
where the time goes in v21:
time: 64 us; the launch traced here: 63.6 us
  starting transfers between devices  27 us (42%)
  Pallas kernels  17.3 us (27%)
  local copies, waits for them, and re-layouts  7.52 us (12%)
  waiting for transfers between devices  5.78 us (9%)
  other arithmetic  4.8 us (8%)
  between operations  0.85 us (1%)
    ppermute x9, starting transfers between devices, staged_gather(): parts.append(lax.ppermute(rows, axis, pairs))  16.5 us
    pallas_call x1, Pallas kernels, score_all(): pl.pallas_call(functools.partial(score_kernel, scale=scale), out_shape=(j...  14 us
    all_to_all x1, starting transfers between devices, local(): lax.all_to_all(outgoing, 'loop', split_axis=0, concat_axis=0, tiled=True)  6.5 us
    ppermute x9, waiting for transfers between devices, staged_gather(): parts.append(lax.ppermute(rows, axis, pairs))  4.82 us
    ppermute x1, starting transfers between devices, local(): got = lax.ppermute(sent, 'grp', [(0, 1), (1, 0)])  4.03 us
    pallas_call x1, Pallas kernels, local(): pl.pallas_call(average_kernel, out_shape=jax.ShapeDtypeStruct((block, fla...  3.28 us
    reshape x2, local copies, waits for them, and re-layouts, angle_major(): rows.reshape(count, RADII, ANGLES).transpose(0, 2, 1)  2.26 us
  transfers between devices with their start and end apart: 11, of which 3 were waited for; matrix products, arithmetic and copies ran while one was open for 12% of the time, Pallas kernels for 22%

profile of v21, /device:TPU:1, one launch (start us, length us, event | category | flops | bytes accessed | tf_op | source)
XLA Modules:
  0.0 63.6 jit_solution(11664400533986730070)
XLA Ops:
  0.6 2.2 %collective-permute-start = (bf16[2,3456]{1,0:T(2,128)(2,1)}, bf16[2,3456]{1,0:T(2,128)(2,1)S(1)}, u32[]{:S(2)}, u32[]{:S(2)}) collective-permute-start(bf16[2,3456]{1,0:T(2,128)(2,1)} %param.6), channel_id=1, source_target_pairs={{0,2},{2,4},{4,6},{6,0},{8,10},{10,12},{12,14},{14,8},{16,18},{18,... | collective-permute-start | bytes 41480 | tf_op jit(solution)/shard_map/ppermute | solution.py:124
  2.8 2.6 %collective-permute-start.1 = (bf16[2,3456]{1,0:T(2,128)(2,1)}, bf16[2,3456]{1,0:T(2,128)(2,1)S(1)}, u32[]{:S(2)}, u32[]{:S(2)}) collective-permute-start(bf16[2,3456]{1,0:T(2,128)(2,1)} %param.6), channel_id=1, source_target_pairs={{0,4},{2,6},{4,0},{6,2},{8,12},{10,14},{12,8},{14,10},{16,20},{18,... | collective-permute-start | bytes 41480 | tf_op jit(solution)/shard_map/ppermute | solution.py:124
  5.4 1.1 %collective-permute-start.2 = (bf16[2,3456]{1,0:T(2,128)(2,1)}, bf16[2,3456]{1,0:T(2,128)(2,1)S(1)}, u32[]{:S(2)}, u32[]{:S(2)}) collective-permute-start(bf16[2,3456]{1,0:T(2,128)(2,1)} %param.6), channel_id=1, source_target_pairs={{0,6},{2,0},{4,2},{6,4},{8,14},{10,8},{12,10},{14,12},{16,22},{18,... | collective-permute-start | bytes 41480 | tf_op jit(solution)/shard_map/ppermute | solution.py:124
  6.5 0.7 %and_select_fusion.1 = (s32[64]{0:T(128)S(1)}, bf16[64,1]{0,1:T(2,128)(2,1)S(1)}) fusion(s32[64]{0:T(128)} %param.7), kind=kLoop, calls=%fused_computation.33 | loop fusion | flops 1280 | bytes 640 | tf_op jit(solution)/shard_map/jit(floor_divide)/jit(_where)/select_n | solution.py:142
  7.3 0.2 select_reduce_fusion
  7.5 1.1 %constant_dynamic-slice_fusion.3 = bf16[64,3456]{1,0:T(8,128)(2,1)S(1)} fusion(bf16[128,3456]{1,0:T(8,128)(2,1)} %refs_0_.1, s32[]{:T(128)S(6)} %select_n.33), kind=kLoop, calls=%fused_computation.37 | loop fusion | bytes 884740 | tf_op jit(solution)/shard_map/dynamic_slice | solution.py:137
  8.6 0.7 %convert_bitcast_fusion = (bf16[64,1]{0,1:T(2,128)(2,1)S(1)}, bf16[64,1]{0,1:T(2,128)(2,1)S(1)}) fusion(s32[64]{0:T(128)} %param.9, s32[64]{0:T(128)} %param.8), kind=kLoop, calls=%fused_computation.54 | loop fusion | flops 128 | bytes 768 | tf_op jit(solution)/shard_map/stack | solution.py:153
  9.3 0.8 %pad_maximum_fusion = bf16[8,3456]{1,0:T(8,128)(2,1)S(1)} fusion(bf16[2,3456]{1,0:T(2,128)(2,1)S(1)} %collective-permute-done.2, bf16[2,3456]{1,0:T(2,128)(2,1)S(1)} %collective-permute-done.1, bf16[2,3456]{1,0:T(2,128)(2,1)S(1)} %collective-permute-done, bf16[2,3456]{1,0:T(2,128)(2,1)} %param.6), kind=kLoop, calls=%fused_computation.19 | loop fusion | flops 221184 | bytes 110592 | tf_op jit(solution)/shard_map/concatenate | solution.py:125
  10.1 1.7 %collective-permute-start.3 = (bf16[8,3456]{1,0:T(8,128)(2,1)S(1)}, bf16[8,3456]{1,0:T(8,128)(2,1)S(1)}, u32[]{:S(2)}, u32[]{:S(2)}) collective-permute-start(bf16[8,3456]{1,0:T(8,128)(2,1)S(1)} %pad_maximum_fusion), channel_id=1, source_target_pairs={{0,8},{2,10},{4,12},{6,14},{8,16},{10,18},{12,20},{14,22},{16,24},... | collective-permute-start | bytes 165896 | tf_op jit(solution)/shard_map/ppermute | solution.py:124
  11.8 3.3 %collective-permute-start.4 = (bf16[8,3456]{1,0:T(8,128)(2,1)S(1)}, bf16[8,3456]{1,0:T(8,128)(2,1)S(1)}, u32[]{:S(2)}, u32[]{:S(2)}) collective-permute-start(bf16[8,3456]{1,0:T(8,128)(2,1)S(1)} %pad_maximum_fusion), channel_id=1, source_target_pairs={{0,16},{2,18},{4,20},{6,22},{8,24},{10,26},{12,28},{14,30},{16,0},... | collective-permute-start | bytes 165896 | tf_op jit(solution)/shard_map/ppermute | solution.py:124
  15.1 0.7 %collective-permute-start.5 = (bf16[8,3456]{1,0:T(8,128)(2,1)S(1)}, bf16[8,3456]{1,0:T(8,128)(2,1)S(1)}, u32[]{:S(2)}, u32[]{:S(2)}) collective-permute-start(bf16[8,3456]{1,0:T(8,128)(2,1)S(1)} %pad_maximum_fusion), channel_id=1, source_target_pairs={{0,24},{2,26},{4,28},{6,30},{8,0},{10,2},{12,4},{14,6},{16,8},{18,... | collective-permute-start | bytes 165896 | tf_op jit(solution)/shard_map/ppermute | solution.py:124
  15.8 1.4 %reshape.86 = bf16[64,48,72]{2,1,0:T(8,128)(2,1)S(1)} reshape(bf16[64,3456]{1,0:T(8,128)(2,1)S(1)} %constant_dynamic-slice_fusion.3) | data formatting | bytes 884736 | tf_op jit(solution)/shard_map/reshape | solution.py:20
  17.2 0.7 %copy.21 = bf16[64,72,48]{2,1,0:T(8,128)(2,1)S(1)} copy(bf16[64,72,48]{1,2,0:T(8,128)(2,1)S(1)} %bitcast.27) | data formatting | bytes 884736 | tf_op jit(solution)/shard_map/transpose | solution.py:20
  17.9 0.9 %reshape.87 = bf16[64,3456]{1,0:T(8,128)(2,1)S(1)} reshape(bf16[64,72,48]{2,1,0:T(8,128)(2,1)S(1)} %copy.21) | data formatting | bytes 884736 | tf_op jit(solution)/shard_map/reshape | solution.py:20
  19.1 1.3 %collective-permute-start.6 = (bf16[32,3456]{1,0:T(8,128)(2,1)S(1)}, bf16[32,3456]{1,0:T(8,128)(2,1)S(1)}, u32[]{:S(2)}, u32[]{:S(2)}) collective-permute-start(bf16[32,3456]{1,0:T(8,128)(2,1)S(1)} %concatenate.14.refs_1_), channel_id=1, source_target_pairs={{0,32},{2,34},{4,36},{6,38},{8,40},{10,42},{12,44},{14,46},{16,48}... | collective-permute-start | bytes 663560 | tf_op jit(solution)/shard_map/ppermute | solution.py:124
  20.4 2.5 %collective-permute-start.7 = (bf16[32,3456]{1,0:T(8,128)(2,1)S(1)}, bf16[32,3456]{1,0:T(8,128)(2,1)S(1)}, u32[]{:S(2)}, u32[]{:S(2)}) collective-permute-start(bf16[32,3456]{1,0:T(8,128)(2,1)S(1)} %concatenate.14.refs_1_), channel_id=1, source_target_pairs={{0,64},{2,66},{4,68},{6,70},{8,72},{10,74},{12,76},{14,78},{16,80}... | collective-permute-start | bytes 663560 | tf_op jit(solution)/shard_map/ppermute | solution.py:124
  22.9 1.2 %collective-permute-start.8 = (bf16[32,3456]{1,0:T(8,128)(2,1)S(1)}, bf16[32,3456]{1,0:T(8,128)(2,1)S(1)}, u32[]{:S(2)}, u32[]{:S(2)}) collective-permute-start(bf16[32,3456]{1,0:T(8,128)(2,1)S(1)} %concatenate.14.refs_1_), channel_id=1, source_target_pairs={{0,96},{2,98},{4,100},{6,102},{8,104},{10,106},{12,108},{14,110},{... | collective-permute-start | bytes 663560 | tf_op jit(solution)/shard_map/ppermute | solution.py:124
  24.0 0.4 convolution_convert_fusion
  24.4 1.3 %reshape.88 = bf16[64,2,3584]{2,1,0:T(2,128)(2,1)} reshape(bf16[128,3584]{1,0:T(8,128)(2,1)S(1)} %convolution_convert_fusion) | data formatting | bytes 1835008 | tf_op jit(solution)/shard_map/reshape | solution.py:158
  25.7 4.7 %collective-permute-done.7.refs_3_ = bf16[32,3456]{1,0:T(8,128)(2,1)S(1)} collective-permute-done((bf16[32,3456]{1,0:T(8,128)(2,1)S(1)}, bf16[32,3456]{1,0:T(8,128)(2,1)S(1)}, u32[]{:S(2)}, u32[]{:S(2)}) %collective-permute-start.7) | collective-permute-done | bytes 221216 | tf_op jit(solution)/shard_map/ppermute | solution.py:124
  30.4 6.5 %all-to-all-start = ((bf16[64,2,3584]{2,1,0:T(2,128)(2,1)}), bf16[64,2,3584]{2,1,0:T(2,128)(2,1)S(1)}, u32[]{:S(2)}, u32[]{:S(2)}) async-start(bf16[64,2,3584]{2,1,0:T(2,128)(2,1)} %reshape.88), calls=%async_computation | async-start | bytes 1835008 | tf_op jit(solution)/shard_map/all_to_all | solution.py:160
  37.0 14.0 %shard_map.68 = (f32[1,128]{1,0:T(1,128)}, f32[1,128]{1,0:T(1,128)}) custom-call(bf16[128,3456]{1,0:T(8,128)(2,1)} %refs_0_.1, bf16[32,3456]{1,0:T(8,128)(2,1)} %copy-done.1, bf16[32,3456]{1,0:T(8,128)(2,1)} %copy-done.2, bf16[32,3456]{1,0:T(8,128)(2,1)} %copy-done.3, bf16[32,3456]{1,0:T(8,128)(2,1)} %copy-done.4), custom_call_target="tpu_custom_call" | custom-call | tf_op jit(solution)/shard_map/pallas_call | solution.py:67
  51.0 0.3 reshape.89.x_ref
  51.4 0.2 slice_reduce_fusion.2
  51.6 0.7 %select_convert_fusion.w_ref = bf16[576,128]{1,0:T(8,128)(2,1)} fusion(f32[128]{0:T(128)S(1)} %get-tuple-element.23, pred[8,128]{1,0:T(8,128)(4,1)S(1)} %iota_compare_fusion.8, pred[72,128]{1,0:T(8,128)(4,1)S(1)} %iota_compare_fusion.6), kind=kLoop, calls=%fused_computation.7 | loop fusion | flops 147456 | bytes 158208 | tf_op jit(solution)/shard_map/convert_element_type | solution.py:175
  52.4 3.3 %shard_map.69 = f32[8,3456]{1,0:T(8,128)} custom-call(bf16[576,128]{1,0:T(8,128)(2,1)} %select_convert_fusion.w_ref, bf16[128,3584]{1,0:T(8,128)(2,1)} %copy-done), custom_call_target="tpu_custom_call" | custom-call | tf_op jit(solution)/shard_map/pallas_call | solution.py:177
  55.6 0.9 %slice.49 = f32[4,3456]{1,0:T(4,128)S(1)} slice(f32[8,3456]{1,0:T(8,128)} %shard_map.69), slice={[0:4], [0:3456]} | slice | bytes 110592 | tf_op jit(solution)/shard_map/slice | solution.py:182
  56.9 0.2 select_reduce_fusion.1
  57.3 4.0 %collective-permute-start.9 = (f32[5,3456]{1,0:T(8,128)S(1)}, f32[5,3456]{1,0:T(8,128)S(1)}, u32[]{:S(2)}, u32[]{:S(2)}) collective-permute-start(f32[5,3456]{1,0:T(8,128)S(1)} %select_maximum_fusion), channel_id=1, source_target_pairs={{0,1},{1,0},{2,3},{3,2},{4,5},{5,4},{6,7},{7,6},{8,9},{9,8},{10,11... | collective-permute-start | bytes 207368 | tf_op jit(solution)/shard_map/ppermute | solution.py:200
  61.3 1.0 %collective-permute-done.9 = f32[5,3456]{1,0:T(8,128)S(1)} collective-permute-done((f32[5,3456]{1,0:T(8,128)S(1)}, f32[5,3456]{1,0:T(8,128)S(1)}, u32[]{:S(2)}, u32[]{:S(2)}) %collective-permute-start.9) | collective-permute-done | bytes 69152 | tf_op jit(solution)/shard_map/ppermute | solution.py:200
  62.3 0.5 log_add_fusion
  62.9 0.7 %fusion.10 = f32[2,3456]{1,0:T(2,128)} fusion(f32[5,3456]{1,0:T(8,128)S(1)} %collective-permute-done.9, f32[4,3456]{1,0:T(4,128)S(1)} %reshape.91, s32[]{:T(128)S(6)} %select_n.38, f32[2]{0:T(128)S(1)} %fusion.15), kind=kLoop, calls=%fused_computation.27 | loop fusion | flops 13824 | bytes 82956 | tf_op jit(solution)/shard_map/div | solution.py:217
  (47 shorter events, 1.3 us)
Async XLA Ops:
  0.6 8.6 %collective-permute-start = (bf16[2,3456]{1,0:T(2,128)(2,1)}, bf16[2,3456]{1,0:T(2,128)(2,1)S(1)}, u32[]{:S(2)}, u32[]{:S(2)}) collective-permute-start(bf16[2,3456]{1,0:T(2,128)(2,1)} %param.6), channel_id=1, source_target_pairs={{0,2},{2,4},{4,6},{6,0},{8,10},{10,12},{12,14},{14,8},{16,18},{18,... | collective-permute-start | bytes 41480 | tf_op jit(solution)/shard_map/ppermute | solution.py:124
  2.8 6.5 %collective-permute-start.1 = (bf16[2,3456]{1,0:T(2,128)(2,1)}, bf16[2,3456]{1,0:T(2,128)(2,1)S(1)}, u32[]{:S(2)}, u32[]{:S(2)}) collective-permute-start(bf16[2,3456]{1,0:T(2,128)(2,1)} %param.6), channel_id=1, source_target_pairs={{0,4},{2,6},{4,0},{6,2},{8,12},{10,14},{12,8},{14,10},{16,20},{18,... | collective-permute-start | bytes 41480 | tf_op jit(solution)/shard_map/ppermute | solution.py:124
  5.4 3.8 %collective-permute-start.2 = (bf16[2,3456]{1,0:T(2,128)(2,1)}, bf16[2,3456]{1,0:T(2,128)(2,1)S(1)}, u32[]{:S(2)}, u32[]{:S(2)}) collective-permute-start(bf16[2,3456]{1,0:T(2,128)(2,1)} %param.6), channel_id=1, source_target_pairs={{0,6},{2,0},{4,2},{6,4},{8,14},{10,8},{12,10},{14,12},{16,22},{18,... | collective-permute-start | bytes 41480 | tf_op jit(solution)/shard_map/ppermute | solution.py:124
  10.1 8.8 %collective-permute-start.3 = (bf16[8,3456]{1,0:T(8,128)(2,1)S(1)}, bf16[8,3456]{1,0:T(8,128)(2,1)S(1)}, u32[]{:S(2)}, u32[]{:S(2)}) collective-permute-start(bf16[8,3456]{1,0:T(8,128)(2,1)S(1)} %pad_maximum_fusion), channel_id=1, source_target_pairs={{0,8},{2,10},{4,12},{6,14},{8,16},{10,18},{12,20},{14,22},{16,24},... | collective-permute-start | bytes 165896 | tf_op jit(solution)/shard_map/ppermute | solution.py:124
  11.8 7.1 %collective-permute-start.4 = (bf16[8,3456]{1,0:T(8,128)(2,1)S(1)}, bf16[8,3456]{1,0:T(8,128)(2,1)S(1)}, u32[]{:S(2)}, u32[]{:S(2)}) collective-permute-start(bf16[8,3456]{1,0:T(8,128)(2,1)S(1)} %pad_maximum_fusion), channel_id=1, source_target_pairs={{0,16},{2,18},{4,20},{6,22},{8,24},{10,26},{12,28},{14,30},{16,0},... | collective-permute-start | bytes 165896 | tf_op jit(solution)/shard_map/ppermute | solution.py:124
  15.1 3.9 %collective-permute-start.5 = (bf16[8,3456]{1,0:T(8,128)(2,1)S(1)}, bf16[8,3456]{1,0:T(8,128)(2,1)S(1)}, u32[]{:S(2)}, u32[]{:S(2)}) collective-permute-start(bf16[8,3456]{1,0:T(8,128)(2,1)S(1)} %pad_maximum_fusion), channel_id=1, source_target_pairs={{0,24},{2,26},{4,28},{6,30},{8,0},{10,2},{12,4},{14,6},{16,8},{18,... | collective-permute-start | bytes 165896 | tf_op jit(solution)/shard_map/ppermute | solution.py:124
  17.9 1.1 %copy-start.5 = (bf16[2,3456]{1,0:T(2,128)(2,1)S(1)}, bf16[2,3456]{1,0:T(2,128)(2,1)}, u32[]{:S(2)}) copy-start(bf16[2,3456]{1,0:T(2,128)(2,1)} %param.6) | copy-start | bytes 41476
  19.1 6.5 %copy-start.1 = (bf16[32,3456]{1,0:T(8,128)(2,1)}, bf16[32,3456]{1,0:T(8,128)(2,1)S(1)}, u32[]{:S(2)}) copy-start(bf16[32,3456]{1,0:T(8,128)(2,1)S(1)} %concatenate.14.refs_1_) | copy-start | bytes 663556
  19.1 6.5 %collective-permute-start.6 = (bf16[32,3456]{1,0:T(8,128)(2,1)S(1)}, bf16[32,3456]{1,0:T(8,128)(2,1)S(1)}, u32[]{:S(2)}, u32[]{:S(2)}) collective-permute-start(bf16[32,3456]{1,0:T(8,128)(2,1)S(1)} %concatenate.14.refs_1_), channel_id=1, source_target_pairs={{0,32},{2,34},{4,36},{6,38},{8,40},{10,42},{12,44},{14,46},{16,48}... | collective-permute-start | bytes 663560 | tf_op jit(solution)/shard_map/ppermute | solution.py:124
  20.4 10.0 %collective-permute-start.7 = (bf16[32,3456]{1,0:T(8,128)(2,1)S(1)}, bf16[32,3456]{1,0:T(8,128)(2,1)S(1)}, u32[]{:S(2)}, u32[]{:S(2)}) collective-permute-start(bf16[32,3456]{1,0:T(8,128)(2,1)S(1)} %concatenate.14.refs_1_), channel_id=1, source_target_pairs={{0,64},{2,66},{4,68},{6,70},{8,72},{10,74},{12,76},{14,78},{16,80}... | collective-permute-start | bytes 663560 | tf_op jit(solution)/shard_map/ppermute | solution.py:124
  22.9 7.6 %collective-permute-start.8 = (bf16[32,3456]{1,0:T(8,128)(2,1)S(1)}, bf16[32,3456]{1,0:T(8,128)(2,1)S(1)}, u32[]{:S(2)}, u32[]{:S(2)}) collective-permute-start(bf16[32,3456]{1,0:T(8,128)(2,1)S(1)} %concatenate.14.refs_1_), channel_id=1, source_target_pairs={{0,96},{2,98},{4,100},{6,102},{8,104},{10,106},{12,108},{14,110},{... | collective-permute-start | bytes 663560 | tf_op jit(solution)/shard_map/ppermute | solution.py:124
  25.7 11.3 %copy-start.2 = (bf16[32,3456]{1,0:T(8,128)(2,1)}, bf16[32,3456]{1,0:T(8,128)(2,1)S(1)}, u32[]{:S(2)}) copy-start(bf16[32,3456]{1,0:T(8,128)(2,1)S(1)} %collective-permute-done.6.refs_2_) | copy-start | bytes 663556
  30.4 6.5 %copy-start.3 = (bf16[32,3456]{1,0:T(8,128)(2,1)}, bf16[32,3456]{1,0:T(8,128)(2,1)S(1)}, u32[]{:S(2)}) copy-start(bf16[32,3456]{1,0:T(8,128)(2,1)S(1)} %collective-permute-done.7.refs_3_) | copy-start | bytes 663556
  30.4 6.5 %copy-start.4 = (bf16[32,3456]{1,0:T(8,128)(2,1)}, bf16[32,3456]{1,0:T(8,128)(2,1)S(1)}, u32[]{:S(2)}) copy-start(bf16[32,3456]{1,0:T(8,128)(2,1)S(1)} %collective-permute-done.8.refs_4_) | copy-start | bytes 663556
  30.4 20.6 %all-to-all-start = ((bf16[64,2,3584]{2,1,0:T(2,128)(2,1)}), bf16[64,2,3584]{2,1,0:T(2,128)(2,1)S(1)}, u32[]{:S(2)}, u32[]{:S(2)}) async-start(bf16[64,2,3584]{2,1,0:T(2,128)(2,1)} %reshape.88), calls=%async_computation | async-start | bytes 1835008 | tf_op jit(solution)/shard_map/all_to_all | solution.py:160
  51.3 1.0 %copy-start = (bf16[128,3584]{1,0:T(8,128)(2,1)}, bf16[128,3584]{1,0:T(8,128)(2,1)S(1)}, u32[]{:S(2)}) copy-start(bf16[128,3584]{1,0:T(8,128)(2,1)S(1)} %reshape.89.x_ref) | copy-start | bytes 2752516
  51.3 5.8 %copy-start.6 = (f32[1,128]{1,0:T(1,128)S(1)}, f32[1,128]{1,0:T(1,128)}, u32[]{:S(2)}) copy-start(f32[1,128]{1,0:T(1,128)} %get-tuple-element.17) | copy-start | bytes 1540
  51.4 5.8 %copy-start.7 = (f32[1,128]{1,0:T(1,128)S(1)}, f32[1,128]{1,0:T(1,128)}, u32[]{:S(2)}) copy-start(f32[1,128]{1,0:T(1,128)} %get-tuple-element.18) | copy-start | bytes 1540
  57.3 5.0 %collective-permute-start.9 = (f32[5,3456]{1,0:T(8,128)S(1)}, f32[5,3456]{1,0:T(8,128)S(1)}, u32[]{:S(2)}, u32[]{:S(2)}) collective-permute-start(f32[5,3456]{1,0:T(8,128)S(1)} %select_maximum_fusion), channel_id=1, source_target_pairs={{0,1},{1,0},{2,3},{3,2},{4,5},{5,4},{6,7},{7,6},{8,9},{9,8},{10,11... | collective-permute-start | bytes 207368 | tf_op jit(solution)/shard_map/ppermute | solution.py:200

commit v22 on v19

--- a/solution.py
+++ b/solution.py
@@ -45,7 +45,7 @@
         return jnp.maximum(carry, scores)
 
     first = jnp.full(s_scr.shape[1:], -jnp.inf, jnp.float32)
-    lane_max = lax.fori_loop(0, half, shift_scores, first, unroll=9)
+    lane_max = lax.fori_loop(0, half, shift_scores, first, unroll=12)
     highest = jnp.max(lane_max.T, axis=0, keepdims=True)
     highest_col = jnp.max(lane_max, axis=1, keepdims=True)
 

time: 64.6 us -> 64.9 us (level)
  no operation moved by 1% of the time
where the time goes in v22:
time: 64.9 us; the launch traced here: 64.5 us
  starting transfers between devices  26.1 us (40%)
  Pallas kernels  16.9 us (26%)
  waiting for transfers between devices  8.81 us (14%)
  local copies, waits for them, and re-layouts  8.77 us (14%)
  other arithmetic  2.76 us (4%)
  between operations  0.84 us (1%)
    ppermute x9, starting transfers between devices, staged_gather(): parts.append(lax.ppermute(rows, axis, pairs))  16.5 us
    pallas_call x1, Pallas kernels, score_all(): pl.pallas_call(functools.partial(score_kernel, scale=scale), out_shape=(j...  13.6 us
    ppermute x9, waiting for transfers between devices, staged_gather(): parts.append(lax.ppermute(rows, axis, pairs))  7.85 us
    all_to_all x1, starting transfers between devices, local(): lax.all_to_all(outgoing, 'loop', split_axis=0, concat_axis=0, tiled=True)  5.95 us
    ppermute x1, starting transfers between devices, local(): got = lax.ppermute(sent, 'grp', [(0, 1), (1, 0)])  3.63 us
    pallas_call x1, Pallas kernels, local(): pl.pallas_call(average_kernel, out_shape=jax.ShapeDtypeStruct((block, fla...  3.3 us
    unnamed x21, local copies, waits for them, and re-layouts  3.27 us
    reshape x1, local copies, waits for them, and re-layouts, angle_major(): rows.reshape(count, RADII, ANGLES).transpose(0, 2, 1)  1.68 us
  transfers between devices with their start and end apart: 11, of which 4 were waited for; matrix products, arithmetic and copies ran while one was open for 9% of the time, Pallas kernels for 21%

profile of v22, /device:TPU:1, one launch (start us, length us, event | category | flops | bytes accessed | tf_op | source)
XLA Modules:
  0.0 64.5 jit_solution(4494636200613698873)
XLA Ops:
  0.6 2.2 %collective-permute-start = (bf16[2,3456]{1,0:T(2,128)(2,1)}, bf16[2,3456]{1,0:T(2,128)(2,1)S(1)}, u32[]{:S(2)}, u32[]{:S(2)}) collective-permute-start(bf16[2,3456]{1,0:T(2,128)(2,1)} %param.6), channel_id=1, source_target_pairs={{0,2},{2,4},{4,6},{6,0},{8,10},{10,12},{12,14},{14,8},{16,18},{18,... | collective-permute-start | bytes 41480 | tf_op jit(solution)/shard_map/ppermute | solution.py:119
  2.8 2.6 %collective-permute-start.1 = (bf16[2,3456]{1,0:T(2,128)(2,1)}, bf16[2,3456]{1,0:T(2,128)(2,1)S(1)}, u32[]{:S(2)}, u32[]{:S(2)}) collective-permute-start(bf16[2,3456]{1,0:T(2,128)(2,1)} %param.6), channel_id=1, source_target_pairs={{0,4},{2,6},{4,0},{6,2},{8,12},{10,14},{12,8},{14,10},{16,20},{18,... | collective-permute-start | bytes 41480 | tf_op jit(solution)/shard_map/ppermute | solution.py:119
  5.4 1.1 %collective-permute-start.2 = (bf16[2,3456]{1,0:T(2,128)(2,1)}, bf16[2,3456]{1,0:T(2,128)(2,1)S(1)}, u32[]{:S(2)}, u32[]{:S(2)}) collective-permute-start(bf16[2,3456]{1,0:T(2,128)(2,1)} %param.6), channel_id=1, source_target_pairs={{0,6},{2,0},{4,2},{6,4},{8,14},{10,8},{12,10},{14,12},{16,22},{18,... | collective-permute-start | bytes 41480 | tf_op jit(solution)/shard_map/ppermute | solution.py:119
  6.5 1.9 %copy.16 = bf16[128,3456]{0,1:T(8,128)(2,1)S(1)} copy(bf16[128,3456]{1,0:T(8,128)(2,1)} %param.5) | data formatting | bytes 1769472 | tf_op args[0]
  8.5 0.5 copy-done.9
  9.3 0.2 select_reduce_fusion
  9.4 0.3 constant_dynamic-slice_fusion.3
  10.1 1.7 %collective-permute-start.3 = (bf16[8,3456]{1,0:T(8,128)(2,1)S(1)}, bf16[8,3456]{1,0:T(8,128)(2,1)S(1)}, u32[]{:S(2)}, u32[]{:S(2)}) collective-permute-start(bf16[8,3456]{1,0:T(8,128)(2,1)S(1)} %pad_maximum_fusion), channel_id=1, source_target_pairs={{0,8},{2,10},{4,12},{6,14},{8,16},{10,18},{12,20},{14,22},{16,24},... | collective-permute-start | bytes 165896 | tf_op jit(solution)/shard_map/ppermute | solution.py:119
  11.8 3.3 %collective-permute-start.4 = (bf16[8,3456]{1,0:T(8,128)(2,1)S(1)}, bf16[8,3456]{1,0:T(8,128)(2,1)S(1)}, u32[]{:S(2)}, u32[]{:S(2)}) collective-permute-start(bf16[8,3456]{1,0:T(8,128)(2,1)S(1)} %pad_maximum_fusion), channel_id=1, source_target_pairs={{0,16},{2,18},{4,20},{6,22},{8,24},{10,26},{12,28},{14,30},{16,0},... | collective-permute-start | bytes 165896 | tf_op jit(solution)/shard_map/ppermute | solution.py:119
  15.1 0.7 %collective-permute-start.5 = (bf16[8,3456]{1,0:T(8,128)(2,1)S(1)}, bf16[8,3456]{1,0:T(8,128)(2,1)S(1)}, u32[]{:S(2)}, u32[]{:S(2)}) collective-permute-start(bf16[8,3456]{1,0:T(8,128)(2,1)S(1)} %pad_maximum_fusion), channel_id=1, source_target_pairs={{0,24},{2,26},{4,28},{6,30},{8,0},{10,2},{12,4},{14,6},{16,8},{18,... | collective-permute-start | bytes 165896 | tf_op jit(solution)/shard_map/ppermute | solution.py:119
  15.8 1.5 %collective-permute-done.4 = bf16[8,3456]{1,0:T(8,128)(2,1)S(1)} collective-permute-done((bf16[8,3456]{1,0:T(8,128)(2,1)S(1)}, bf16[8,3456]{1,0:T(8,128)(2,1)S(1)}, u32[]{:S(2)}, u32[]{:S(2)}) %collective-permute-start.4) | collective-permute-done | bytes 55328 | tf_op jit(solution)/shard_map/ppermute | solution.py:119
  17.3 1.7 %collective-permute-done.5 = bf16[8,3456]{1,0:T(8,128)(2,1)S(1)} collective-permute-done((bf16[8,3456]{1,0:T(8,128)(2,1)S(1)}, bf16[8,3456]{1,0:T(8,128)(2,1)S(1)}, u32[]{:S(2)}, u32[]{:S(2)}) %collective-permute-start.5) | collective-permute-done | bytes 55328 | tf_op jit(solution)/shard_map/ppermute | solution.py:119
  19.1 1.3 %collective-permute-start.6 = (bf16[32,3456]{1,0:T(8,128)(2,1)S(1)}, bf16[32,3456]{1,0:T(8,128)(2,1)S(1)}, u32[]{:S(2)}, u32[]{:S(2)}) collective-permute-start(bf16[32,3456]{1,0:T(8,128)(2,1)S(1)} %concatenate.14.refs_1_), channel_id=1, source_target_pairs={{0,32},{2,34},{4,36},{6,38},{8,40},{10,42},{12,44},{14,46},{16,48}... | collective-permute-start | bytes 663560 | tf_op jit(solution)/shard_map/ppermute | solution.py:119
  20.4 2.5 %collective-permute-start.7 = (bf16[32,3456]{1,0:T(8,128)(2,1)S(1)}, bf16[32,3456]{1,0:T(8,128)(2,1)S(1)}, u32[]{:S(2)}, u32[]{:S(2)}) collective-permute-start(bf16[32,3456]{1,0:T(8,128)(2,1)S(1)} %concatenate.14.refs_1_), channel_id=1, source_target_pairs={{0,64},{2,66},{4,68},{6,70},{8,72},{10,74},{12,76},{14,78},{16,80}... | collective-permute-start | bytes 663560 | tf_op jit(solution)/shard_map/ppermute | solution.py:119
  22.8 1.2 %collective-permute-start.8 = (bf16[32,3456]{1,0:T(8,128)(2,1)S(1)}, bf16[32,3456]{1,0:T(8,128)(2,1)}, u32[]{:S(2)}, u32[]{:S(2)}) collective-permute-start(bf16[32,3456]{1,0:T(8,128)(2,1)S(1)} %concatenate.14.refs_1_), channel_id=1, source_target_pairs={{0,96},{2,98},{4,100},{6,102},{8,104},{10,106},{12,108},{14,110},{... | collective-permute-start | bytes 663560 | tf_op jit(solution)/shard_map/ppermute | solution.py:119
  24.0 0.4 convolution_convert_fusion
  24.4 1.3 %reshape.88 = bf16[64,2,3584]{2,1,0:T(2,128)(2,1)} reshape(bf16[128,3584]{1,0:T(8,128)(2,1)S(1)} %convolution_convert_fusion) | data formatting | bytes 1835008 | tf_op jit(solution)/shard_map/reshape | solution.py:154
  25.7 4.7 %collective-permute-done.7.refs_3_ = bf16[32,3456]{1,0:T(8,128)(2,1)S(1)} collective-permute-done((bf16[32,3456]{1,0:T(8,128)(2,1)S(1)}, bf16[32,3456]{1,0:T(8,128)(2,1)S(1)}, u32[]{:S(2)}, u32[]{:S(2)}) %collective-permute-start.7) | collective-permute-done | bytes 221216 | tf_op jit(solution)/shard_map/ppermute | solution.py:119
  30.4 0.7 %copy-done.3 = bf16[32,3456]{1,0:T(8,128)(2,1)} copy-done((bf16[32,3456]{1,0:T(8,128)(2,1)}, bf16[32,3456]{1,0:T(8,128)(2,1)S(1)}, u32[]{:S(2)}) %copy-start.3) | copy-done | bytes 221208
  31.1 5.9 %all-to-all-start = ((bf16[64,2,3584]{2,1,0:T(2,128)(2,1)}), bf16[64,2,3584]{2,1,0:T(2,128)(2,1)S(1)}, u32[]{:S(2)}, u32[]{:S(2)}) async-start(bf16[64,2,3584]{2,1,0:T(2,128)(2,1)} %reshape.88), calls=%async_computation | async-start | bytes 1835008 | tf_op jit(solution)/shard_map/all_to_all | solution.py:156
  37.0 1.7 %copy.18.refs_0_ = bf16[128,3456]{1,0:T(8,128)(2,1)} copy(bf16[128,3456]{0,1:T(8,128)(2,1)S(1)} %bitcast.31) | data formatting | bytes 1769472 | tf_op jit(solution)/shard_map/reshape | solution.py:20
  38.7 13.6 %shard_map.68 = (f32[1,128]{1,0:T(1,128)}, f32[1,128]{1,0:T(1,128)}) custom-call(bf16[128,3456]{1,0:T(8,128)(2,1)} %copy.18.refs_0_, bf16[32,3456]{1,0:T(8,128)(2,1)} %copy-done.1, bf16[32,3456]{1,0:T(8,128)(2,1)} %copy-done.2, bf16[32,3456]{1,0:T(8,128)(2,1)} %copy-done.3, bf16[32,3456]{1,0:T(8,128)(2,1)} %collective-permute-done.8.refs_4_), custom_call_target="tpu_custom_call" | custom-call | tf_op jit(solution)/shard_map/pallas_call | solution.py:64
  52.3 0.3 reshape.89.x_ref
  52.6 0.2 slice_reduce_fusion.2
  52.9 0.7 %select_convert_fusion.w_ref = bf16[576,128]{1,0:T(8,128)(2,1)} fusion(f32[128]{0:T(128)S(1)} %get-tuple-element.23, pred[8,128]{1,0:T(8,128)(4,1)S(1)} %iota_compare_fusion.8, pred[72,128]{1,0:T(8,128)(4,1)S(1)} %iota_compare_fusion.6), kind=kLoop, calls=%fused_computation.4 | loop fusion | flops 147456 | bytes 158208 | tf_op jit(solution)/shard_map/convert_element_type | solution.py:171
  53.6 3.3 %shard_map.69 = f32[8,3456]{1,0:T(8,128)} custom-call(bf16[576,128]{1,0:T(8,128)(2,1)} %select_convert_fusion.w_ref, bf16[128,3584]{1,0:T(8,128)(2,1)} %copy-done), custom_call_target="tpu_custom_call" | custom-call | tf_op jit(solution)/shard_map/pallas_call | solution.py:173
  56.9 0.9 %slice.49 = f32[4,3456]{1,0:T(4,128)S(1)} slice(f32[8,3456]{1,0:T(8,128)} %shard_map.69), slice={[0:4], [0:3456]} | slice | bytes 110592 | tf_op jit(solution)/shard_map/slice | solution.py:178
  58.2 0.2 select_reduce_fusion.1
  58.6 3.6 %collective-permute-start.9 = (f32[5,3456]{1,0:T(8,128)S(1)}, f32[5,3456]{1,0:T(8,128)S(1)}, u32[]{:S(2)}, u32[]{:S(2)}) collective-permute-start(f32[5,3456]{1,0:T(8,128)S(1)} %select_maximum_fusion), channel_id=1, source_target_pairs={{0,1},{1,0},{2,3},{3,2},{4,5},{5,4},{6,7},{7,6},{8,9},{9,8},{10,11... | collective-permute-start | bytes 207368 | tf_op jit(solution)/shard_map/ppermute | solution.py:196
  62.2 1.0 %collective-permute-done.9 = f32[5,3456]{1,0:T(8,128)S(1)} collective-permute-done((f32[5,3456]{1,0:T(8,128)S(1)}, f32[5,3456]{1,0:T(8,128)S(1)}, u32[]{:S(2)}, u32[]{:S(2)}) %collective-permute-start.9) | collective-permute-done | bytes 69152 | tf_op jit(solution)/shard_map/ppermute | solution.py:196
  63.2 0.5 log_add_fusion
  63.8 0.7 %fusion.11 = f32[2,3456]{1,0:T(2,128)} fusion(f32[5,3456]{1,0:T(8,128)S(1)} %collective-permute-done.9, f32[4,3456]{1,0:T(4,128)S(1)} %reshape.91, s32[]{:T(128)S(6)} %select_n.38, f32[2]{0:T(128)S(1)} %fusion.16), kind=kLoop, calls=%fused_computation.29 | loop fusion | flops 13824 | bytes 82956 | tf_op jit(solution)/shard_map/div | solution.py:213
  (50 shorter events, 1.5 us)
Async XLA Ops:
  0.6 9.3 %collective-permute-start = (bf16[2,3456]{1,0:T(2,128)(2,1)}, bf16[2,3456]{1,0:T(2,128)(2,1)S(1)}, u32[]{:S(2)}, u32[]{:S(2)}) collective-permute-start(bf16[2,3456]{1,0:T(2,128)(2,1)} %param.6), channel_id=1, source_target_pairs={{0,2},{2,4},{4,6},{6,0},{8,10},{10,12},{12,14},{14,8},{16,18},{18,... | collective-permute-start | bytes 41480 | tf_op jit(solution)/shard_map/ppermute | solution.py:119
  2.8 7.1 %collective-permute-start.1 = (bf16[2,3456]{1,0:T(2,128)(2,1)}, bf16[2,3456]{1,0:T(2,128)(2,1)S(1)}, u32[]{:S(2)}, u32[]{:S(2)}) collective-permute-start(bf16[2,3456]{1,0:T(2,128)(2,1)} %param.6), channel_id=1, source_target_pairs={{0,4},{2,6},{4,0},{6,2},{8,12},{10,14},{12,8},{14,10},{16,20},{18,... | collective-permute-start | bytes 41480 | tf_op jit(solution)/shard_map/ppermute | solution.py:119
  5.4 4.5 %collective-permute-start.2 = (bf16[2,3456]{1,0:T(2,128)(2,1)}, bf16[2,3456]{1,0:T(2,128)(2,1)S(1)}, u32[]{:S(2)}, u32[]{:S(2)}) collective-permute-start(bf16[2,3456]{1,0:T(2,128)(2,1)} %param.6), channel_id=1, source_target_pairs={{0,6},{2,0},{4,2},{6,4},{8,14},{10,8},{12,10},{14,12},{16,22},{18,... | collective-permute-start | bytes 41480 | tf_op jit(solution)/shard_map/ppermute | solution.py:119
  8.4 0.7 %copy-start.9 = (s32[64]{0:T(128)S(1)}, s32[64]{0:T(128)}, u32[]{:S(2)}) copy-start(s32[64]{0:T(128)} %param.7) | copy-start | bytes 772
  9.2 0.7 %copy-start.5 = (s32[64]{0:T(128)S(1)}, s32[64]{0:T(128)}, u32[]{:S(2)}) copy-start(s32[64]{0:T(128)} %param.9) | copy-start | bytes 772
  9.2 0.7 %copy-start.6 = (s32[64]{0:T(128)S(1)}, s32[64]{0:T(128)}, u32[]{:S(2)}) copy-start(s32[64]{0:T(128)} %param.8) | copy-start | bytes 772
  9.3 0.7 %copy-start.4 = (bf16[2,3456]{1,0:T(2,128)(2,1)S(1)}, bf16[2,3456]{1,0:T(2,128)(2,1)}, u32[]{:S(2)}) copy-start(bf16[2,3456]{1,0:T(2,128)(2,1)} %param.6) | copy-start | bytes 41476
  10.1 5.8 %collective-permute-start.3 = (bf16[8,3456]{1,0:T(8,128)(2,1)S(1)}, bf16[8,3456]{1,0:T(8,128)(2,1)S(1)}, u32[]{:S(2)}, u32[]{:S(2)}) collective-permute-start(bf16[8,3456]{1,0:T(8,128)(2,1)S(1)} %pad_maximum_fusion), channel_id=1, source_target_pairs={{0,8},{2,10},{4,12},{6,14},{8,16},{10,18},{12,20},{14,22},{16,24},... | collective-permute-start | bytes 165896 | tf_op jit(solution)/shard_map/ppermute | solution.py:119
  11.8 5.5 %collective-permute-start.4 = (bf16[8,3456]{1,0:T(8,128)(2,1)S(1)}, bf16[8,3456]{1,0:T(8,128)(2,1)S(1)}, u32[]{:S(2)}, u32[]{:S(2)}) collective-permute-start(bf16[8,3456]{1,0:T(8,128)(2,1)S(1)} %pad_maximum_fusion), channel_id=1, source_target_pairs={{0,16},{2,18},{4,20},{6,22},{8,24},{10,26},{12,28},{14,30},{16,0},... | collective-permute-start | bytes 165896 | tf_op jit(solution)/shard_map/ppermute | solution.py:119
  15.1 3.9 %collective-permute-start.5 = (bf16[8,3456]{1,0:T(8,128)(2,1)S(1)}, bf16[8,3456]{1,0:T(8,128)(2,1)S(1)}, u32[]{:S(2)}, u32[]{:S(2)}) collective-permute-start(bf16[8,3456]{1,0:T(8,128)(2,1)S(1)} %pad_maximum_fusion), channel_id=1, source_target_pairs={{0,24},{2,26},{4,28},{6,30},{8,0},{10,2},{12,4},{14,6},{16,8},{18,... | collective-permute-start | bytes 165896 | tf_op jit(solution)/shard_map/ppermute | solution.py:119
  19.1 5.3 %copy-start.1 = (bf16[32,3456]{1,0:T(8,128)(2,1)}, bf16[32,3456]{1,0:T(8,128)(2,1)S(1)}, u32[]{:S(2)}) copy-start(bf16[32,3456]{1,0:T(8,128)(2,1)S(1)} %concatenate.14.refs_1_) | copy-start | bytes 663556
  19.1 6.6 %collective-permute-start.6 = (bf16[32,3456]{1,0:T(8,128)(2,1)S(1)}, bf16[32,3456]{1,0:T(8,128)(2,1)S(1)}, u32[]{:S(2)}, u32[]{:S(2)}) collective-permute-start(bf16[32,3456]{1,0:T(8,128)(2,1)S(1)} %concatenate.14.refs_1_), channel_id=1, source_target_pairs={{0,32},{2,34},{4,36},{6,38},{8,40},{10,42},{12,44},{14,46},{16,48}... | collective-permute-start | bytes 663560 | tf_op jit(solution)/shard_map/ppermute | solution.py:119
  20.4 10.0 %collective-permute-start.7 = (bf16[32,3456]{1,0:T(8,128)(2,1)S(1)}, bf16[32,3456]{1,0:T(8,128)(2,1)S(1)}, u32[]{:S(2)}, u32[]{:S(2)}) collective-permute-start(bf16[32,3456]{1,0:T(8,128)(2,1)S(1)} %concatenate.14.refs_1_), channel_id=1, source_target_pairs={{0,64},{2,66},{4,68},{6,70},{8,72},{10,74},{12,76},{14,78},{16,80}... | collective-permute-start | bytes 663560 | tf_op jit(solution)/shard_map/ppermute | solution.py:119
  22.8 7.6 %collective-permute-start.8 = (bf16[32,3456]{1,0:T(8,128)(2,1)S(1)}, bf16[32,3456]{1,0:T(8,128)(2,1)}, u32[]{:S(2)}, u32[]{:S(2)}) collective-permute-start(bf16[32,3456]{1,0:T(8,128)(2,1)S(1)} %concatenate.14.refs_1_), channel_id=1, source_target_pairs={{0,96},{2,98},{4,100},{6,102},{8,104},{10,106},{12,108},{14,110},{... | collective-permute-start | bytes 663560 | tf_op jit(solution)/shard_map/ppermute | solution.py:119
  25.7 4.7 %copy-start.2 = (bf16[32,3456]{1,0:T(8,128)(2,1)}, bf16[32,3456]{1,0:T(8,128)(2,1)S(1)}, u32[]{:S(2)}) copy-start(bf16[32,3456]{1,0:T(8,128)(2,1)S(1)} %collective-permute-done.6.refs_2_) | copy-start | bytes 663556
  30.4 0.7 %copy-start.3 = (bf16[32,3456]{1,0:T(8,128)(2,1)}, bf16[32,3456]{1,0:T(8,128)(2,1)S(1)}, u32[]{:S(2)}) copy-start(bf16[32,3456]{1,0:T(8,128)(2,1)S(1)} %collective-permute-done.7.refs_3_) | copy-start | bytes 663556
  31.1 21.2 %all-to-all-start = ((bf16[64,2,3584]{2,1,0:T(2,128)(2,1)}), bf16[64,2,3584]{2,1,0:T(2,128)(2,1)S(1)}, u32[]{:S(2)}, u32[]{:S(2)}) async-start(bf16[64,2,3584]{2,1,0:T(2,128)(2,1)} %reshape.88), calls=%async_computation | async-start | bytes 1835008 | tf_op jit(solution)/shard_map/all_to_all | solution.py:156
  52.6 1.0 %copy-start = (bf16[128,3584]{1,0:T(8,128)(2,1)}, bf16[128,3584]{1,0:T(8,128)(2,1)S(1)}, u32[]{:S(2)}) copy-start(bf16[128,3584]{1,0:T(8,128)(2,1)S(1)} %reshape.89.x_ref) | copy-start | bytes 2752516
  53.6 4.9 %copy-start.7 = (f32[1,128]{1,0:T(1,128)S(1)}, f32[1,128]{1,0:T(1,128)}, u32[]{:S(2)}) copy-start(f32[1,128]{1,0:T(1,128)} %get-tuple-element.17) | copy-start | bytes 1540
  53.6 4.9 %copy-start.8 = (f32[1,128]{1,0:T(1,128)S(1)}, f32[1,128]{1,0:T(1,128)}, u32[]{:S(2)}) copy-start(f32[1,128]{1,0:T(1,128)} %get-tuple-element.18) | copy-start | bytes 1540
  58.6 4.6 %collective-permute-start.9 = (f32[5,3456]{1,0:T(8,128)S(1)}, f32[5,3456]{1,0:T(8,128)S(1)}, u32[]{:S(2)}, u32[]{:S(2)}) collective-permute-start(f32[5,3456]{1,0:T(8,128)S(1)} %select_maximum_fusion), channel_id=1, source_target_pairs={{0,1},{1,0},{2,3},{3,2},{4,5},{5,4},{6,7},{7,6},{8,9},{9,8},{10,11... | collective-permute-start | bytes 207368 | tf_op jit(solution)/shard_map/ppermute | solution.py:196

commit v23 on v19

--- a/solution.py
+++ b/solution.py
@@ -175,8 +175,7 @@
         out_shape=jax.ShapeDtypeStruct((block, flat_len), jnp.float32),
         scratch_shapes=[pltpu.VMEM((ANGLES * block, flat_len), jnp.float32)],
     )(by_angle, incoming)
-    partial_sums = partial_sums[:per_owner].reshape(per_owner, ANGLES, RADII).transpose(0, 2, 1)
-    partial_sums = partial_sums.reshape(per_owner, flat_len)
+    partial_sums = partial_sums[:per_owner]
     weighted = (member_grid[:per_owner, None] == member_in[None, :]).astype(jnp.float32) * weight_of[None, :]
     partial_weight = jnp.sum(weighted, axis=1)
     own_classes = references.shape[0]
@@ -211,6 +210,7 @@
         class_weight = lax.dynamic_slice_in_dim(partial_weight, grp_index * own_classes, own_classes, 0)
         stats = lax.dynamic_slice_in_dim(stats, grp_index * half_rows, half_rows, 2)
     class_average = class_sums / class_weight[:, None]
+    class_average = class_average.reshape(-1, ANGLES, RADII).transpose(0, 2, 1).reshape(-1, flat_len)
     highest = jnp.max(stats[:, 0], axis=0)
     summed = jnp.sum(stats[:, 1] * jnp.exp(stats[:, 0] - highest[None, :]), axis=0)
     log_evidence = highest + jnp.log(summed)

time: 64.6 us -> 64.6 us (level)
  no operation moved by 1% of the time
where the time goes in v23:
time: 64.6 us; the launch traced here: 64.2 us
  starting transfers between devices  25.9 us (40%)
  Pallas kernels  16.8 us (26%)
  local copies, waits for them, and re-layouts  9.35 us (14%)
  waiting for transfers between devices  8.81 us (14%)
  other arithmetic  2.15 us (3%)
  between operations  0.84 us (1%)
    ppermute x9, starting transfers between devices, staged_gather(): parts.append(lax.ppermute(rows, axis, pairs))  16.5 us
    pallas_call x1, Pallas kernels, score_all(): pl.pallas_call(functools.partial(score_kernel, scale=scale), out_shape=(j...  13.5 us
    ppermute x9, waiting for transfers between devices, staged_gather(): parts.append(lax.ppermute(rows, axis, pairs))  7.85 us
    all_to_all x1, starting transfers between devices, local(): lax.all_to_all(outgoing, 'loop', split_axis=0, concat_axis=0, tiled=True)  5.76 us
    ppermute x1, starting transfers between devices, local(): got = lax.ppermute(sent, 'grp', [(0, 1), (1, 0)])  3.63 us
    pallas_call x1, Pallas kernels, local(): pl.pallas_call(average_kernel, out_shape=jax.ShapeDtypeStruct((block, fla...  3.28 us
    unnamed x21, local copies, waits for them, and re-layouts  3.27 us
    reshape x1, local copies, waits for them, and re-layouts, angle_major(): rows.reshape(count, RADII, ANGLES).transpose(0, 2, 1)  1.68 us
  transfers between devices with their start and end apart: 11, of which 4 were waited for; matrix products, arithmetic and copies ran while one was open for 9% of the time, Pallas kernels for 21%

profile of v23, /device:TPU:1, one launch (start us, length us, event | category | flops | bytes accessed | tf_op | source)
XLA Modules:
  0.0 64.2 jit_solution(6202792285562014394)
XLA Ops:
  0.6 2.2 %collective-permute-start = (bf16[2,3456]{1,0:T(2,128)(2,1)}, bf16[2,3456]{1,0:T(2,128)(2,1)S(1)}, u32[]{:S(2)}, u32[]{:S(2)}) collective-permute-start(bf16[2,3456]{1,0:T(2,128)(2,1)} %param.6), channel_id=1, source_target_pairs={{0,2},{2,4},{4,6},{6,0},{8,10},{10,12},{12,14},{14,8},{16,18},{18,... | collective-permute-start | bytes 41480 | tf_op jit(solution)/shard_map/ppermute | solution.py:119
  2.8 2.6 %collective-permute-start.1 = (bf16[2,3456]{1,0:T(2,128)(2,1)}, bf16[2,3456]{1,0:T(2,128)(2,1)S(1)}, u32[]{:S(2)}, u32[]{:S(2)}) collective-permute-start(bf16[2,3456]{1,0:T(2,128)(2,1)} %param.6), channel_id=1, source_target_pairs={{0,4},{2,6},{4,0},{6,2},{8,12},{10,14},{12,8},{14,10},{16,20},{18,... | collective-permute-start | bytes 41480 | tf_op jit(solution)/shard_map/ppermute | solution.py:119
  5.4 1.1 %collective-permute-start.2 = (bf16[2,3456]{1,0:T(2,128)(2,1)}, bf16[2,3456]{1,0:T(2,128)(2,1)S(1)}, u32[]{:S(2)}, u32[]{:S(2)}) collective-permute-start(bf16[2,3456]{1,0:T(2,128)(2,1)} %param.6), channel_id=1, source_target_pairs={{0,6},{2,0},{4,2},{6,4},{8,14},{10,8},{12,10},{14,12},{16,22},{18,... | collective-permute-start | bytes 41480 | tf_op jit(solution)/shard_map/ppermute | solution.py:119
  6.5 1.9 %copy.19 = bf16[128,3456]{0,1:T(8,128)(2,1)S(1)} copy(bf16[128,3456]{1,0:T(8,128)(2,1)} %param.5) | data formatting | bytes 1769472 | tf_op args[0]
  8.5 0.5 copy-done.9
  9.3 0.2 select_reduce_fusion
  9.4 0.3 constant_dynamic-slice_fusion.3
  10.1 1.7 %collective-permute-start.3 = (bf16[8,3456]{1,0:T(8,128)(2,1)S(1)}, bf16[8,3456]{1,0:T(8,128)(2,1)S(1)}, u32[]{:S(2)}, u32[]{:S(2)}) collective-permute-start(bf16[8,3456]{1,0:T(8,128)(2,1)S(1)} %pad_maximum_fusion), channel_id=1, source_target_pairs={{0,8},{2,10},{4,12},{6,14},{8,16},{10,18},{12,20},{14,22},{16,24},... | collective-permute-start | bytes 165896 | tf_op jit(solution)/shard_map/ppermute | solution.py:119
  11.8 3.3 %collective-permute-start.4 = (bf16[8,3456]{1,0:T(8,128)(2,1)S(1)}, bf16[8,3456]{1,0:T(8,128)(2,1)S(1)}, u32[]{:S(2)}, u32[]{:S(2)}) collective-permute-start(bf16[8,3456]{1,0:T(8,128)(2,1)S(1)} %pad_maximum_fusion), channel_id=1, source_target_pairs={{0,16},{2,18},{4,20},{6,22},{8,24},{10,26},{12,28},{14,30},{16,0},... | collective-permute-start | bytes 165896 | tf_op jit(solution)/shard_map/ppermute | solution.py:119
  15.1 0.7 %collective-permute-start.5 = (bf16[8,3456]{1,0:T(8,128)(2,1)S(1)}, bf16[8,3456]{1,0:T(8,128)(2,1)S(1)}, u32[]{:S(2)}, u32[]{:S(2)}) collective-permute-start(bf16[8,3456]{1,0:T(8,128)(2,1)S(1)} %pad_maximum_fusion), channel_id=1, source_target_pairs={{0,24},{2,26},{4,28},{6,30},{8,0},{10,2},{12,4},{14,6},{16,8},{18,... | collective-permute-start | bytes 165896 | tf_op jit(solution)/shard_map/ppermute | solution.py:119
  15.8 1.5 %collective-permute-done.4 = bf16[8,3456]{1,0:T(8,128)(2,1)S(1)} collective-permute-done((bf16[8,3456]{1,0:T(8,128)(2,1)S(1)}, bf16[8,3456]{1,0:T(8,128)(2,1)S(1)}, u32[]{:S(2)}, u32[]{:S(2)}) %collective-permute-start.4) | collective-permute-done | bytes 55328 | tf_op jit(solution)/shard_map/ppermute | solution.py:119
  17.3 1.7 %collective-permute-done.5 = bf16[8,3456]{1,0:T(8,128)(2,1)S(1)} collective-permute-done((bf16[8,3456]{1,0:T(8,128)(2,1)S(1)}, bf16[8,3456]{1,0:T(8,128)(2,1)S(1)}, u32[]{:S(2)}, u32[]{:S(2)}) %collective-permute-start.5) | collective-permute-done | bytes 55328 | tf_op jit(solution)/shard_map/ppermute | solution.py:119
  19.1 1.3 %collective-permute-start.6 = (bf16[32,3456]{1,0:T(8,128)(2,1)S(1)}, bf16[32,3456]{1,0:T(8,128)(2,1)S(1)}, u32[]{:S(2)}, u32[]{:S(2)}) collective-permute-start(bf16[32,3456]{1,0:T(8,128)(2,1)S(1)} %concatenate.14.refs_1_), channel_id=1, source_target_pairs={{0,32},{2,34},{4,36},{6,38},{8,40},{10,42},{12,44},{14,46},{16,48}... | collective-permute-start | bytes 663560 | tf_op jit(solution)/shard_map/ppermute | solution.py:119
  20.4 2.5 %collective-permute-start.7 = (bf16[32,3456]{1,0:T(8,128)(2,1)S(1)}, bf16[32,3456]{1,0:T(8,128)(2,1)S(1)}, u32[]{:S(2)}, u32[]{:S(2)}) collective-permute-start(bf16[32,3456]{1,0:T(8,128)(2,1)S(1)} %concatenate.14.refs_1_), channel_id=1, source_target_pairs={{0,64},{2,66},{4,68},{6,70},{8,72},{10,74},{12,76},{14,78},{16,80}... | collective-permute-start | bytes 663560 | tf_op jit(solution)/shard_map/ppermute | solution.py:119
  22.8 1.2 %collective-permute-start.8 = (bf16[32,3456]{1,0:T(8,128)(2,1)S(1)}, bf16[32,3456]{1,0:T(8,128)(2,1)}, u32[]{:S(2)}, u32[]{:S(2)}) collective-permute-start(bf16[32,3456]{1,0:T(8,128)(2,1)S(1)} %concatenate.14.refs_1_), channel_id=1, source_target_pairs={{0,96},{2,98},{4,100},{6,102},{8,104},{10,106},{12,108},{14,110},{... | collective-permute-start | bytes 663560 | tf_op jit(solution)/shard_map/ppermute | solution.py:119
  24.0 0.4 convolution_convert_fusion
  24.4 1.3 %reshape.88 = bf16[64,2,3584]{2,1,0:T(2,128)(2,1)} reshape(bf16[128,3584]{1,0:T(8,128)(2,1)S(1)} %convolution_convert_fusion) | data formatting | bytes 1835008 | tf_op jit(solution)/shard_map/reshape | solution.py:154
  25.7 4.7 %collective-permute-done.7.refs_3_ = bf16[32,3456]{1,0:T(8,128)(2,1)S(1)} collective-permute-done((bf16[32,3456]{1,0:T(8,128)(2,1)S(1)}, bf16[32,3456]{1,0:T(8,128)(2,1)S(1)}, u32[]{:S(2)}, u32[]{:S(2)}) %collective-permute-start.7) | collective-permute-done | bytes 221216 | tf_op jit(solution)/shard_map/ppermute | solution.py:119
  30.4 0.7 %copy-done.3 = bf16[32,3456]{1,0:T(8,128)(2,1)} copy-done((bf16[32,3456]{1,0:T(8,128)(2,1)}, bf16[32,3456]{1,0:T(8,128)(2,1)S(1)}, u32[]{:S(2)}) %copy-start.3) | copy-done | bytes 221208
  31.1 5.8 %all-to-all-start = ((bf16[64,2,3584]{2,1,0:T(2,128)(2,1)}), bf16[64,2,3584]{2,1,0:T(2,128)(2,1)S(1)}, u32[]{:S(2)}, u32[]{:S(2)}) async-start(bf16[64,2,3584]{2,1,0:T(2,128)(2,1)} %reshape.88), calls=%async_computation | async-start | bytes 1835008 | tf_op jit(solution)/shard_map/all_to_all | solution.py:156
  36.8 1.7 %copy.21.refs_0_ = bf16[128,3456]{1,0:T(8,128)(2,1)} copy(bf16[128,3456]{0,1:T(8,128)(2,1)S(1)} %bitcast.31) | data formatting | bytes 1769472 | tf_op jit(solution)/shard_map/reshape | solution.py:20
  38.5 13.5 %shard_map.68 = (f32[1,128]{1,0:T(1,128)}, f32[1,128]{1,0:T(1,128)}) custom-call(bf16[128,3456]{1,0:T(8,128)(2,1)} %copy.21.refs_0_, bf16[32,3456]{1,0:T(8,128)(2,1)} %copy-done.1, bf16[32,3456]{1,0:T(8,128)(2,1)} %copy-done.2, bf16[32,3456]{1,0:T(8,128)(2,1)} %copy-done.3, bf16[32,3456]{1,0:T(8,128)(2,1)} %collective-permute-done.8.refs_4_), custom_call_target="tpu_custom_call" | custom-call | tf_op jit(solution)/shard_map/pallas_call | solution.py:64
  52.0 0.3 reshape.89.x_ref
  52.4 0.2 slice_reduce_fusion.2
  52.7 0.7 %select_convert_fusion.w_ref = bf16[576,128]{1,0:T(8,128)(2,1)} fusion(f32[128]{0:T(128)S(1)} %get-tuple-element.23, pred[8,128]{1,0:T(8,128)(4,1)S(1)} %iota_compare_fusion.8, pred[72,128]{1,0:T(8,128)(4,1)S(1)} %iota_compare_fusion.6), kind=kLoop, calls=%fused_computation.4 | loop fusion | flops 147456 | bytes 158208 | tf_op jit(solution)/shard_map/convert_element_type | solution.py:171
  53.4 3.3 %shard_map.69 = f32[8,3456]{1,0:T(8,128)} custom-call(bf16[576,128]{1,0:T(8,128)(2,1)} %select_convert_fusion.w_ref, bf16[128,3584]{1,0:T(8,128)(2,1)} %copy-done), custom_call_target="tpu_custom_call" | custom-call | tf_op jit(solution)/shard_map/pallas_call | solution.py:173
  56.7 0.9 %slice.49 = f32[4,3456]{1,0:T(4,128)S(1)} slice(f32[8,3456]{1,0:T(8,128)} %shard_map.69), slice={[0:4], [0:3456]} | slice | bytes 110592 | tf_op jit(solution)/shard_map/slice | solution.py:178
  57.6 0.2 select_reduce_fusion.1
  58.0 3.6 %collective-permute-start.9 = (f32[5,3456]{1,0:T(8,128)S(1)}, f32[5,3456]{1,0:T(8,128)S(1)}, u32[]{:S(2)}, u32[]{:S(2)}) collective-permute-start(f32[5,3456]{1,0:T(8,128)S(1)} %select_maximum_fusion), channel_id=1, source_target_pairs={{0,1},{1,0},{2,3},{3,2},{4,5},{5,4},{6,7},{7,6},{8,9},{9,8},{10,11... | collective-permute-start | bytes 207368 | tf_op jit(solution)/shard_map/ppermute | solution.py:195
  61.6 1.0 %collective-permute-done.9 = f32[5,3456]{1,0:T(8,128)S(1)} collective-permute-done((f32[5,3456]{1,0:T(8,128)S(1)}, f32[5,3456]{1,0:T(8,128)S(1)}, u32[]{:S(2)}, u32[]{:S(2)}) %collective-permute-start.9) | collective-permute-done | bytes 69152 | tf_op jit(solution)/shard_map/ppermute | solution.py:195
  62.9 0.7 %reshape.91 = f32[2,3456]{1,0:T(2,128)} reshape(f32[2,48,72]{2,1,0:T(8,128)S(1)} %copy.22) | data formatting | bytes 55296 | tf_op jit(solution)/shard_map/reshape | solution.py:213
  63.7 0.5 log_add_fusion
  (50 shorter events, 1.4 us)
Async XLA Ops:
  0.6 9.3 %collective-permute-start = (bf16[2,3456]{1,0:T(2,128)(2,1)}, bf16[2,3456]{1,0:T(2,128)(2,1)S(1)}, u32[]{:S(2)}, u32[]{:S(2)}) collective-permute-start(bf16[2,3456]{1,0:T(2,128)(2,1)} %param.6), channel_id=1, source_target_pairs={{0,2},{2,4},{4,6},{6,0},{8,10},{10,12},{12,14},{14,8},{16,18},{18,... | collective-permute-start | bytes 41480 | tf_op jit(solution)/shard_map/ppermute | solution.py:119
  2.8 7.1 %collective-permute-start.1 = (bf16[2,3456]{1,0:T(2,128)(2,1)}, bf16[2,3456]{1,0:T(2,128)(2,1)S(1)}, u32[]{:S(2)}, u32[]{:S(2)}) collective-permute-start(bf16[2,3456]{1,0:T(2,128)(2,1)} %param.6), channel_id=1, source_target_pairs={{0,4},{2,6},{4,0},{6,2},{8,12},{10,14},{12,8},{14,10},{16,20},{18,... | collective-permute-start | bytes 41480 | tf_op jit(solution)/shard_map/ppermute | solution.py:119
  5.4 4.5 %collective-permute-start.2 = (bf16[2,3456]{1,0:T(2,128)(2,1)}, bf16[2,3456]{1,0:T(2,128)(2,1)S(1)}, u32[]{:S(2)}, u32[]{:S(2)}) collective-permute-start(bf16[2,3456]{1,0:T(2,128)(2,1)} %param.6), channel_id=1, source_target_pairs={{0,6},{2,0},{4,2},{6,4},{8,14},{10,8},{12,10},{14,12},{16,22},{18,... | collective-permute-start | bytes 41480 | tf_op jit(solution)/shard_map/ppermute | solution.py:119
  8.4 0.7 %copy-start.9 = (s32[64]{0:T(128)S(1)}, s32[64]{0:T(128)}, u32[]{:S(2)}) copy-start(s32[64]{0:T(128)} %param.7) | copy-start | bytes 772
  9.2 0.7 %copy-start.5 = (s32[64]{0:T(128)S(1)}, s32[64]{0:T(128)}, u32[]{:S(2)}) copy-start(s32[64]{0:T(128)} %param.9) | copy-start | bytes 772
  9.2 0.7 %copy-start.6 = (s32[64]{0:T(128)S(1)}, s32[64]{0:T(128)}, u32[]{:S(2)}) copy-start(s32[64]{0:T(128)} %param.8) | copy-start | bytes 772
  9.3 0.7 %copy-start.4 = (bf16[2,3456]{1,0:T(2,128)(2,1)S(1)}, bf16[2,3456]{1,0:T(2,128)(2,1)}, u32[]{:S(2)}) copy-start(bf16[2,3456]{1,0:T(2,128)(2,1)} %param.6) | copy-start | bytes 41476
  10.1 5.8 %collective-permute-start.3 = (bf16[8,3456]{1,0:T(8,128)(2,1)S(1)}, bf16[8,3456]{1,0:T(8,128)(2,1)S(1)}, u32[]{:S(2)}, u32[]{:S(2)}) collective-permute-start(bf16[8,3456]{1,0:T(8,128)(2,1)S(1)} %pad_maximum_fusion), channel_id=1, source_target_pairs={{0,8},{2,10},{4,12},{6,14},{8,16},{10,18},{12,20},{14,22},{16,24},... | collective-permute-start | bytes 165896 | tf_op jit(solution)/shard_map/ppermute | solution.py:119
  11.8 5.5 %collective-permute-start.4 = (bf16[8,3456]{1,0:T(8,128)(2,1)S(1)}, bf16[8,3456]{1,0:T(8,128)(2,1)S(1)}, u32[]{:S(2)}, u32[]{:S(2)}) collective-permute-start(bf16[8,3456]{1,0:T(8,128)(2,1)S(1)} %pad_maximum_fusion), channel_id=1, source_target_pairs={{0,16},{2,18},{4,20},{6,22},{8,24},{10,26},{12,28},{14,30},{16,0},... | collective-permute-start | bytes 165896 | tf_op jit(solution)/shard_map/ppermute | solution.py:119
  15.1 3.9 %collective-permute-start.5 = (bf16[8,3456]{1,0:T(8,128)(2,1)S(1)}, bf16[8,3456]{1,0:T(8,128)(2,1)S(1)}, u32[]{:S(2)}, u32[]{:S(2)}) collective-permute-start(bf16[8,3456]{1,0:T(8,128)(2,1)S(1)} %pad_maximum_fusion), channel_id=1, source_target_pairs={{0,24},{2,26},{4,28},{6,30},{8,0},{10,2},{12,4},{14,6},{16,8},{18,... | collective-permute-start | bytes 165896 | tf_op jit(solution)/shard_map/ppermute | solution.py:119
  19.1 5.3 %copy-start.1 = (bf16[32,3456]{1,0:T(8,128)(2,1)}, bf16[32,3456]{1,0:T(8,128)(2,1)S(1)}, u32[]{:S(2)}) copy-start(bf16[32,3456]{1,0:T(8,128)(2,1)S(1)} %concatenate.14.refs_1_) | copy-start | bytes 663556
  19.1 6.6 %collective-permute-start.6 = (bf16[32,3456]{1,0:T(8,128)(2,1)S(1)}, bf16[32,3456]{1,0:T(8,128)(2,1)S(1)}, u32[]{:S(2)}, u32[]{:S(2)}) collective-permute-start(bf16[32,3456]{1,0:T(8,128)(2,1)S(1)} %concatenate.14.refs_1_), channel_id=1, source_target_pairs={{0,32},{2,34},{4,36},{6,38},{8,40},{10,42},{12,44},{14,46},{16,48}... | collective-permute-start | bytes 663560 | tf_op jit(solution)/shard_map/ppermute | solution.py:119
  20.4 10.0 %collective-permute-start.7 = (bf16[32,3456]{1,0:T(8,128)(2,1)S(1)}, bf16[32,3456]{1,0:T(8,128)(2,1)S(1)}, u32[]{:S(2)}, u32[]{:S(2)}) collective-permute-start(bf16[32,3456]{1,0:T(8,128)(2,1)S(1)} %concatenate.14.refs_1_), channel_id=1, source_target_pairs={{0,64},{2,66},{4,68},{6,70},{8,72},{10,74},{12,76},{14,78},{16,80}... | collective-permute-start | bytes 663560 | tf_op jit(solution)/shard_map/ppermute | solution.py:119
  22.8 7.6 %collective-permute-start.8 = (bf16[32,3456]{1,0:T(8,128)(2,1)S(1)}, bf16[32,3456]{1,0:T(8,128)(2,1)}, u32[]{:S(2)}, u32[]{:S(2)}) collective-permute-start(bf16[32,3456]{1,0:T(8,128)(2,1)S(1)} %concatenate.14.refs_1_), channel_id=1, source_target_pairs={{0,96},{2,98},{4,100},{6,102},{8,104},{10,106},{12,108},{14,110},{... | collective-permute-start | bytes 663560 | tf_op jit(solution)/shard_map/ppermute | solution.py:119
  25.7 4.7 %copy-start.2 = (bf16[32,3456]{1,0:T(8,128)(2,1)}, bf16[32,3456]{1,0:T(8,128)(2,1)S(1)}, u32[]{:S(2)}) copy-start(bf16[32,3456]{1,0:T(8,128)(2,1)S(1)} %collective-permute-done.6.refs_2_) | copy-start | bytes 663556
  30.4 0.7 %copy-start.3 = (bf16[32,3456]{1,0:T(8,128)(2,1)}, bf16[32,3456]{1,0:T(8,128)(2,1)S(1)}, u32[]{:S(2)}) copy-start(bf16[32,3456]{1,0:T(8,128)(2,1)S(1)} %collective-permute-done.7.refs_3_) | copy-start | bytes 663556
  31.1 20.9 %all-to-all-start = ((bf16[64,2,3584]{2,1,0:T(2,128)(2,1)}), bf16[64,2,3584]{2,1,0:T(2,128)(2,1)S(1)}, u32[]{:S(2)}, u32[]{:S(2)}) async-start(bf16[64,2,3584]{2,1,0:T(2,128)(2,1)} %reshape.88), calls=%async_computation | async-start | bytes 1835008 | tf_op jit(solution)/shard_map/all_to_all | solution.py:156
  52.3 1.0 %copy-start = (bf16[128,3584]{1,0:T(8,128)(2,1)}, bf16[128,3584]{1,0:T(8,128)(2,1)S(1)}, u32[]{:S(2)}) copy-start(bf16[128,3584]{1,0:T(8,128)(2,1)S(1)} %reshape.89.x_ref) | copy-start | bytes 2752516
  52.4 5.5 %copy-start.7 = (f32[1,128]{1,0:T(1,128)S(1)}, f32[1,128]{1,0:T(1,128)}, u32[]{:S(2)}) copy-start(f32[1,128]{1,0:T(1,128)} %get-tuple-element.17) | copy-start | bytes 1540
  52.4 5.5 %copy-start.8 = (f32[1,128]{1,0:T(1,128)S(1)}, f32[1,128]{1,0:T(1,128)}, u32[]{:S(2)}) copy-start(f32[1,128]{1,0:T(1,128)} %get-tuple-element.18) | copy-start | bytes 1540
  58.0 4.6 %collective-permute-start.9 = (f32[5,3456]{1,0:T(8,128)S(1)}, f32[5,3456]{1,0:T(8,128)S(1)}, u32[]{:S(2)}, u32[]{:S(2)}) collective-permute-start(f32[5,3456]{1,0:T(8,128)S(1)} %select_maximum_fusion), channel_id=1, source_target_pairs={{0,1},{1,0},{2,3},{3,2},{4,5},{5,4},{6,7},{7,6},{8,9},{9,8},{10,11... | collective-permute-start | bytes 207368 | tf_op jit(solution)/shard_map/ppermute | solution.py:195

commit v24 on v19

--- a/solution.py
+++ b/solution.py
@@ -52,7 +52,7 @@
     def shift_sum(s, carry):
         return carry + jnp.exp(s_scr[s] - highest_col)
 
-    lane_sum = lax.fori_loop(0, half, shift_sum, jnp.zeros(s_scr.shape[1:], jnp.float32), unroll=4)
+    lane_sum = lax.fori_loop(0, half, shift_sum, jnp.zeros(s_scr.shape[1:], jnp.float32), unroll=9)
     max_ref[...] = highest
     sum_ref[...] = jnp.sum(lane_sum.T, axis=0, keepdims=True)
 

time: 64.6 us -> 64.6 us (level)
  no operation moved by 1% of the time
where the time goes in v24:
time: 64.6 us; the launch traced here: 64.2 us
  starting transfers between devices  25.9 us (40%)
  Pallas kernels  16.7 us (26%)
  waiting for transfers between devices  8.81 us (14%)
  local copies, waits for them, and re-layouts  8.77 us (14%)
  other arithmetic  2.76 us (4%)
  between operations  0.84 us (1%)
    ppermute x9, starting transfers between devices, staged_gather(): parts.append(lax.ppermute(rows, axis, pairs))  16.5 us
    pallas_call x1, Pallas kernels, score_all(): pl.pallas_call(functools.partial(score_kernel, scale=scale), out_shape=(j...  13.4 us
    ppermute x9, waiting for transfers between devices, staged_gather(): parts.append(lax.ppermute(rows, axis, pairs))  7.85 us
    all_to_all x1, starting transfers between devices, local(): lax.all_to_all(outgoing, 'loop', split_axis=0, concat_axis=0, tiled=True)  5.76 us
    ppermute x1, starting transfers between devices, local(): got = lax.ppermute(sent, 'grp', [(0, 1), (1, 0)])  3.63 us
    pallas_call x1, Pallas kernels, local(): pl.pallas_call(average_kernel, out_shape=jax.ShapeDtypeStruct((block, fla...  3.3 us
    unnamed x21, local copies, waits for them, and re-layouts  3.27 us
    reshape x1, local copies, waits for them, and re-layouts, angle_major(): rows.reshape(count, RADII, ANGLES).transpose(0, 2, 1)  1.68 us
  transfers between devices with their start and end apart: 11, of which 4 were waited for; matrix products, arithmetic and copies ran while one was open for 9% of the time, Pallas kernels for 21%

profile of v24, /device:TPU:1, one launch (start us, length us, event | category | flops | bytes accessed | tf_op | source)
XLA Modules:
  0.0 64.2 jit_solution(11734863816514020748)
XLA Ops:
  0.6 2.2 %collective-permute-start = (bf16[2,3456]{1,0:T(2,128)(2,1)}, bf16[2,3456]{1,0:T(2,128)(2,1)S(1)}, u32[]{:S(2)}, u32[]{:S(2)}) collective-permute-start(bf16[2,3456]{1,0:T(2,128)(2,1)} %param.6), channel_id=1, source_target_pairs={{0,2},{2,4},{4,6},{6,0},{8,10},{10,12},{12,14},{14,8},{16,18},{18,... | collective-permute-start | bytes 41480 | tf_op jit(solution)/shard_map/ppermute | solution.py:119
  2.8 2.6 %collective-permute-start.1 = (bf16[2,3456]{1,0:T(2,128)(2,1)}, bf16[2,3456]{1,0:T(2,128)(2,1)S(1)}, u32[]{:S(2)}, u32[]{:S(2)}) collective-permute-start(bf16[2,3456]{1,0:T(2,128)(2,1)} %param.6), channel_id=1, source_target_pairs={{0,4},{2,6},{4,0},{6,2},{8,12},{10,14},{12,8},{14,10},{16,20},{18,... | collective-permute-start | bytes 41480 | tf_op jit(solution)/shard_map/ppermute | solution.py:119
  5.4 1.1 %collective-permute-start.2 = (bf16[2,3456]{1,0:T(2,128)(2,1)}, bf16[2,3456]{1,0:T(2,128)(2,1)S(1)}, u32[]{:S(2)}, u32[]{:S(2)}) collective-permute-start(bf16[2,3456]{1,0:T(2,128)(2,1)} %param.6), channel_id=1, source_target_pairs={{0,6},{2,0},{4,2},{6,4},{8,14},{10,8},{12,10},{14,12},{16,22},{18,... | collective-permute-start | bytes 41480 | tf_op jit(solution)/shard_map/ppermute | solution.py:119
  6.5 1.9 %copy.16 = bf16[128,3456]{0,1:T(8,128)(2,1)S(1)} copy(bf16[128,3456]{1,0:T(8,128)(2,1)} %param.5) | data formatting | bytes 1769472 | tf_op args[0]
  8.5 0.5 copy-done.9
  9.3 0.2 select_reduce_fusion
  9.4 0.3 constant_dynamic-slice_fusion.3
  10.1 1.7 %collective-permute-start.3 = (bf16[8,3456]{1,0:T(8,128)(2,1)S(1)}, bf16[8,3456]{1,0:T(8,128)(2,1)S(1)}, u32[]{:S(2)}, u32[]{:S(2)}) collective-permute-start(bf16[8,3456]{1,0:T(8,128)(2,1)S(1)} %pad_maximum_fusion), channel_id=1, source_target_pairs={{0,8},{2,10},{4,12},{6,14},{8,16},{10,18},{12,20},{14,22},{16,24},... | collective-permute-start | bytes 165896 | tf_op jit(solution)/shard_map/ppermute | solution.py:119
  11.8 3.3 %collective-permute-start.4 = (bf16[8,3456]{1,0:T(8,128)(2,1)S(1)}, bf16[8,3456]{1,0:T(8,128)(2,1)S(1)}, u32[]{:S(2)}, u32[]{:S(2)}) collective-permute-start(bf16[8,3456]{1,0:T(8,128)(2,1)S(1)} %pad_maximum_fusion), channel_id=1, source_target_pairs={{0,16},{2,18},{4,20},{6,22},{8,24},{10,26},{12,28},{14,30},{16,0},... | collective-permute-start | bytes 165896 | tf_op jit(solution)/shard_map/ppermute | solution.py:119
  15.1 0.7 %collective-permute-start.5 = (bf16[8,3456]{1,0:T(8,128)(2,1)S(1)}, bf16[8,3456]{1,0:T(8,128)(2,1)S(1)}, u32[]{:S(2)}, u32[]{:S(2)}) collective-permute-start(bf16[8,3456]{1,0:T(8,128)(2,1)S(1)} %pad_maximum_fusion), channel_id=1, source_target_pairs={{0,24},{2,26},{4,28},{6,30},{8,0},{10,2},{12,4},{14,6},{16,8},{18,... | collective-permute-start | bytes 165896 | tf_op jit(solution)/shard_map/ppermute | solution.py:119
  15.8 1.5 %collective-permute-done.4 = bf16[8,3456]{1,0:T(8,128)(2,1)S(1)} collective-permute-done((bf16[8,3456]{1,0:T(8,128)(2,1)S(1)}, bf16[8,3456]{1,0:T(8,128)(2,1)S(1)}, u32[]{:S(2)}, u32[]{:S(2)}) %collective-permute-start.4) | collective-permute-done | bytes 55328 | tf_op jit(solution)/shard_map/ppermute | solution.py:119
  17.3 1.7 %collective-permute-done.5 = bf16[8,3456]{1,0:T(8,128)(2,1)S(1)} collective-permute-done((bf16[8,3456]{1,0:T(8,128)(2,1)S(1)}, bf16[8,3456]{1,0:T(8,128)(2,1)S(1)}, u32[]{:S(2)}, u32[]{:S(2)}) %collective-permute-start.5) | collective-permute-done | bytes 55328 | tf_op jit(solution)/shard_map/ppermute | solution.py:119
  19.1 1.3 %collective-permute-start.6 = (bf16[32,3456]{1,0:T(8,128)(2,1)S(1)}, bf16[32,3456]{1,0:T(8,128)(2,1)S(1)}, u32[]{:S(2)}, u32[]{:S(2)}) collective-permute-start(bf16[32,3456]{1,0:T(8,128)(2,1)S(1)} %concatenate.14.refs_1_), channel_id=1, source_target_pairs={{0,32},{2,34},{4,36},{6,38},{8,40},{10,42},{12,44},{14,46},{16,48}... | collective-permute-start | bytes 663560 | tf_op jit(solution)/shard_map/ppermute | solution.py:119
  20.4 2.5 %collective-permute-start.7 = (bf16[32,3456]{1,0:T(8,128)(2,1)S(1)}, bf16[32,3456]{1,0:T(8,128)(2,1)S(1)}, u32[]{:S(2)}, u32[]{:S(2)}) collective-permute-start(bf16[32,3456]{1,0:T(8,128)(2,1)S(1)} %concatenate.14.refs_1_), channel_id=1, source_target_pairs={{0,64},{2,66},{4,68},{6,70},{8,72},{10,74},{12,76},{14,78},{16,80}... | collective-permute-start | bytes 663560 | tf_op jit(solution)/shard_map/ppermute | solution.py:119
  22.8 1.2 %collective-permute-start.8 = (bf16[32,3456]{1,0:T(8,128)(2,1)S(1)}, bf16[32,3456]{1,0:T(8,128)(2,1)}, u32[]{:S(2)}, u32[]{:S(2)}) collective-permute-start(bf16[32,3456]{1,0:T(8,128)(2,1)S(1)} %concatenate.14.refs_1_), channel_id=1, source_target_pairs={{0,96},{2,98},{4,100},{6,102},{8,104},{10,106},{12,108},{14,110},{... | collective-permute-start | bytes 663560 | tf_op jit(solution)/shard_map/ppermute | solution.py:119
  24.0 0.4 convolution_convert_fusion
  24.4 1.3 %reshape.88 = bf16[64,2,3584]{2,1,0:T(2,128)(2,1)} reshape(bf16[128,3584]{1,0:T(8,128)(2,1)S(1)} %convolution_convert_fusion) | data formatting | bytes 1835008 | tf_op jit(solution)/shard_map/reshape | solution.py:154
  25.7 4.7 %collective-permute-done.7.refs_3_ = bf16[32,3456]{1,0:T(8,128)(2,1)S(1)} collective-permute-done((bf16[32,3456]{1,0:T(8,128)(2,1)S(1)}, bf16[32,3456]{1,0:T(8,128)(2,1)S(1)}, u32[]{:S(2)}, u32[]{:S(2)}) %collective-permute-start.7) | collective-permute-done | bytes 221216 | tf_op jit(solution)/shard_map/ppermute | solution.py:119
  30.4 0.7 %copy-done.3 = bf16[32,3456]{1,0:T(8,128)(2,1)} copy-done((bf16[32,3456]{1,0:T(8,128)(2,1)}, bf16[32,3456]{1,0:T(8,128)(2,1)S(1)}, u32[]{:S(2)}) %copy-start.3) | copy-done | bytes 221208
  31.1 5.8 %all-to-all-start = ((bf16[64,2,3584]{2,1,0:T(2,128)(2,1)}), bf16[64,2,3584]{2,1,0:T(2,128)(2,1)S(1)}, u32[]{:S(2)}, u32[]{:S(2)}) async-start(bf16[64,2,3584]{2,1,0:T(2,128)(2,1)} %reshape.88), calls=%async_computation | async-start | bytes 1835008 | tf_op jit(solution)/shard_map/all_to_all | solution.py:156
  36.8 1.7 %copy.18.refs_0_ = bf16[128,3456]{1,0:T(8,128)(2,1)} copy(bf16[128,3456]{0,1:T(8,128)(2,1)S(1)} %bitcast.31) | data formatting | bytes 1769472 | tf_op jit(solution)/shard_map/reshape | solution.py:20
  38.5 13.4 %shard_map.68 = (f32[1,128]{1,0:T(1,128)}, f32[1,128]{1,0:T(1,128)}) custom-call(bf16[128,3456]{1,0:T(8,128)(2,1)} %copy.18.refs_0_, bf16[32,3456]{1,0:T(8,128)(2,1)} %copy-done.1, bf16[32,3456]{1,0:T(8,128)(2,1)} %copy-done.2, bf16[32,3456]{1,0:T(8,128)(2,1)} %copy-done.3, bf16[32,3456]{1,0:T(8,128)(2,1)} %collective-permute-done.8.refs_4_), custom_call_target="tpu_custom_call" | custom-call | tf_op jit(solution)/shard_map/pallas_call | solution.py:64
  51.9 0.3 reshape.89.x_ref
  52.3 0.2 slice_reduce_fusion.2
  52.6 0.7 %select_convert_fusion.w_ref = bf16[576,128]{1,0:T(8,128)(2,1)} fusion(f32[128]{0:T(128)S(1)} %get-tuple-element.23, pred[8,128]{1,0:T(8,128)(4,1)S(1)} %iota_compare_fusion.8, pred[72,128]{1,0:T(8,128)(4,1)S(1)} %iota_compare_fusion.6), kind=kLoop, calls=%fused_computation.4 | loop fusion | flops 147456 | bytes 158208 | tf_op jit(solution)/shard_map/convert_element_type | solution.py:171
  53.3 3.3 %shard_map.69 = f32[8,3456]{1,0:T(8,128)} custom-call(bf16[576,128]{1,0:T(8,128)(2,1)} %select_convert_fusion.w_ref, bf16[128,3584]{1,0:T(8,128)(2,1)} %copy-done), custom_call_target="tpu_custom_call" | custom-call | tf_op jit(solution)/shard_map/pallas_call | solution.py:173
  56.6 0.9 %slice.49 = f32[4,3456]{1,0:T(4,128)S(1)} slice(f32[8,3456]{1,0:T(8,128)} %shard_map.69), slice={[0:4], [0:3456]} | slice | bytes 110592 | tf_op jit(solution)/shard_map/slice | solution.py:178
  57.9 0.2 select_reduce_fusion.1
  58.3 3.6 %collective-permute-start.9 = (f32[5,3456]{1,0:T(8,128)S(1)}, f32[5,3456]{1,0:T(8,128)S(1)}, u32[]{:S(2)}, u32[]{:S(2)}) collective-permute-start(f32[5,3456]{1,0:T(8,128)S(1)} %select_maximum_fusion), channel_id=1, source_target_pairs={{0,1},{1,0},{2,3},{3,2},{4,5},{5,4},{6,7},{7,6},{8,9},{9,8},{10,11... | collective-permute-start | bytes 207368 | tf_op jit(solution)/shard_map/ppermute | solution.py:196
  61.9 1.0 %collective-permute-done.9 = f32[5,3456]{1,0:T(8,128)S(1)} collective-permute-done((f32[5,3456]{1,0:T(8,128)S(1)}, f32[5,3456]{1,0:T(8,128)S(1)}, u32[]{:S(2)}, u32[]{:S(2)}) %collective-permute-start.9) | collective-permute-done | bytes 69152 | tf_op jit(solution)/shard_map/ppermute | solution.py:196
  62.9 0.5 log_add_fusion
  63.5 0.7 %fusion.11 = f32[2,3456]{1,0:T(2,128)} fusion(f32[5,3456]{1,0:T(8,128)S(1)} %collective-permute-done.9, f32[4,3456]{1,0:T(4,128)S(1)} %reshape.91, s32[]{:T(128)S(6)} %select_n.38, f32[2]{0:T(128)S(1)} %fusion.16), kind=kLoop, calls=%fused_computation.29 | loop fusion | flops 13824 | bytes 82956 | tf_op jit(solution)/shard_map/div | solution.py:213
  (50 shorter events, 1.5 us)
Async XLA Ops:
  0.6 9.3 %collective-permute-start = (bf16[2,3456]{1,0:T(2,128)(2,1)}, bf16[2,3456]{1,0:T(2,128)(2,1)S(1)}, u32[]{:S(2)}, u32[]{:S(2)}) collective-permute-start(bf16[2,3456]{1,0:T(2,128)(2,1)} %param.6), channel_id=1, source_target_pairs={{0,2},{2,4},{4,6},{6,0},{8,10},{10,12},{12,14},{14,8},{16,18},{18,... | collective-permute-start | bytes 41480 | tf_op jit(solution)/shard_map/ppermute | solution.py:119
  2.8 7.1 %collective-permute-start.1 = (bf16[2,3456]{1,0:T(2,128)(2,1)}, bf16[2,3456]{1,0:T(2,128)(2,1)S(1)}, u32[]{:S(2)}, u32[]{:S(2)}) collective-permute-start(bf16[2,3456]{1,0:T(2,128)(2,1)} %param.6), channel_id=1, source_target_pairs={{0,4},{2,6},{4,0},{6,2},{8,12},{10,14},{12,8},{14,10},{16,20},{18,... | collective-permute-start | bytes 41480 | tf_op jit(solution)/shard_map/ppermute | solution.py:119
  5.4 4.5 %collective-permute-start.2 = (bf16[2,3456]{1,0:T(2,128)(2,1)}, bf16[2,3456]{1,0:T(2,128)(2,1)S(1)}, u32[]{:S(2)}, u32[]{:S(2)}) collective-permute-start(bf16[2,3456]{1,0:T(2,128)(2,1)} %param.6), channel_id=1, source_target_pairs={{0,6},{2,0},{4,2},{6,4},{8,14},{10,8},{12,10},{14,12},{16,22},{18,... | collective-permute-start | bytes 41480 | tf_op jit(solution)/shard_map/ppermute | solution.py:119
  8.4 0.7 %copy-start.9 = (s32[64]{0:T(128)S(1)}, s32[64]{0:T(128)}, u32[]{:S(2)}) copy-start(s32[64]{0:T(128)} %param.7) | copy-start | bytes 772
  9.2 0.7 %copy-start.5 = (s32[64]{0:T(128)S(1)}, s32[64]{0:T(128)}, u32[]{:S(2)}) copy-start(s32[64]{0:T(128)} %param.9) | copy-start | bytes 772
  9.2 0.7 %copy-start.6 = (s32[64]{0:T(128)S(1)}, s32[64]{0:T(128)}, u32[]{:S(2)}) copy-start(s32[64]{0:T(128)} %param.8) | copy-start | bytes 772
  9.3 0.7 %copy-start.4 = (bf16[2,3456]{1,0:T(2,128)(2,1)S(1)}, bf16[2,3456]{1,0:T(2,128)(2,1)}, u32[]{:S(2)}) copy-start(bf16[2,3456]{1,0:T(2,128)(2,1)} %param.6) | copy-start | bytes 41476
  10.1 5.8 %collective-permute-start.3 = (bf16[8,3456]{1,0:T(8,128)(2,1)S(1)}, bf16[8,3456]{1,0:T(8,128)(2,1)S(1)}, u32[]{:S(2)}, u32[]{:S(2)}) collective-permute-start(bf16[8,3456]{1,0:T(8,128)(2,1)S(1)} %pad_maximum_fusion), channel_id=1, source_target_pairs={{0,8},{2,10},{4,12},{6,14},{8,16},{10,18},{12,20},{14,22},{16,24},... | collective-permute-start | bytes 165896 | tf_op jit(solution)/shard_map/ppermute | solution.py:119
  11.8 5.5 %collective-permute-start.4 = (bf16[8,3456]{1,0:T(8,128)(2,1)S(1)}, bf16[8,3456]{1,0:T(8,128)(2,1)S(1)}, u32[]{:S(2)}, u32[]{:S(2)}) collective-permute-start(bf16[8,3456]{1,0:T(8,128)(2,1)S(1)} %pad_maximum_fusion), channel_id=1, source_target_pairs={{0,16},{2,18},{4,20},{6,22},{8,24},{10,26},{12,28},{14,30},{16,0},... | collective-permute-start | bytes 165896 | tf_op jit(solution)/shard_map/ppermute | solution.py:119
  15.1 3.9 %collective-permute-start.5 = (bf16[8,3456]{1,0:T(8,128)(2,1)S(1)}, bf16[8,3456]{1,0:T(8,128)(2,1)S(1)}, u32[]{:S(2)}, u32[]{:S(2)}) collective-permute-start(bf16[8,3456]{1,0:T(8,128)(2,1)S(1)} %pad_maximum_fusion), channel_id=1, source_target_pairs={{0,24},{2,26},{4,28},{6,30},{8,0},{10,2},{12,4},{14,6},{16,8},{18,... | collective-permute-start | bytes 165896 | tf_op jit(solution)/shard_map/ppermute | solution.py:119
  19.1 5.3 %copy-start.1 = (bf16[32,3456]{1,0:T(8,128)(2,1)}, bf16[32,3456]{1,0:T(8,128)(2,1)S(1)}, u32[]{:S(2)}) copy-start(bf16[32,3456]{1,0:T(8,128)(2,1)S(1)} %concatenate.14.refs_1_) | copy-start | bytes 663556
  19.1 6.6 %collective-permute-start.6 = (bf16[32,3456]{1,0:T(8,128)(2,1)S(1)}, bf16[32,3456]{1,0:T(8,128)(2,1)S(1)}, u32[]{:S(2)}, u32[]{:S(2)}) collective-permute-start(bf16[32,3456]{1,0:T(8,128)(2,1)S(1)} %concatenate.14.refs_1_), channel_id=1, source_target_pairs={{0,32},{2,34},{4,36},{6,38},{8,40},{10,42},{12,44},{14,46},{16,48}... | collective-permute-start | bytes 663560 | tf_op jit(solution)/shard_map/ppermute | solution.py:119
  20.4 10.0 %collective-permute-start.7 = (bf16[32,3456]{1,0:T(8,128)(2,1)S(1)}, bf16[32,3456]{1,0:T(8,128)(2,1)S(1)}, u32[]{:S(2)}, u32[]{:S(2)}) collective-permute-start(bf16[32,3456]{1,0:T(8,128)(2,1)S(1)} %concatenate.14.refs_1_), channel_id=1, source_target_pairs={{0,64},{2,66},{4,68},{6,70},{8,72},{10,74},{12,76},{14,78},{16,80}... | collective-permute-start | bytes 663560 | tf_op jit(solution)/shard_map/ppermute | solution.py:119
  22.8 7.6 %collective-permute-start.8 = (bf16[32,3456]{1,0:T(8,128)(2,1)S(1)}, bf16[32,3456]{1,0:T(8,128)(2,1)}, u32[]{:S(2)}, u32[]{:S(2)}) collective-permute-start(bf16[32,3456]{1,0:T(8,128)(2,1)S(1)} %concatenate.14.refs_1_), channel_id=1, source_target_pairs={{0,96},{2,98},{4,100},{6,102},{8,104},{10,106},{12,108},{14,110},{... | collective-permute-start | bytes 663560 | tf_op jit(solution)/shard_map/ppermute | solution.py:119
  25.7 4.7 %copy-start.2 = (bf16[32,3456]{1,0:T(8,128)(2,1)}, bf16[32,3456]{1,0:T(8,128)(2,1)S(1)}, u32[]{:S(2)}) copy-start(bf16[32,3456]{1,0:T(8,128)(2,1)S(1)} %collective-permute-done.6.refs_2_) | copy-start | bytes 663556
  30.4 0.7 %copy-start.3 = (bf16[32,3456]{1,0:T(8,128)(2,1)}, bf16[32,3456]{1,0:T(8,128)(2,1)S(1)}, u32[]{:S(2)}) copy-start(bf16[32,3456]{1,0:T(8,128)(2,1)S(1)} %collective-permute-done.7.refs_3_) | copy-start | bytes 663556
  31.1 20.9 %all-to-all-start = ((bf16[64,2,3584]{2,1,0:T(2,128)(2,1)}), bf16[64,2,3584]{2,1,0:T(2,128)(2,1)S(1)}, u32[]{:S(2)}, u32[]{:S(2)}) async-start(bf16[64,2,3584]{2,1,0:T(2,128)(2,1)} %reshape.88), calls=%async_computation | async-start | bytes 1835008 | tf_op jit(solution)/shard_map/all_to_all | solution.py:156
  52.3 1.0 %copy-start = (bf16[128,3584]{1,0:T(8,128)(2,1)}, bf16[128,3584]{1,0:T(8,128)(2,1)S(1)}, u32[]{:S(2)}) copy-start(bf16[128,3584]{1,0:T(8,128)(2,1)S(1)} %reshape.89.x_ref) | copy-start | bytes 2752516
  53.3 4.9 %copy-start.7 = (f32[1,128]{1,0:T(1,128)S(1)}, f32[1,128]{1,0:T(1,128)}, u32[]{:S(2)}) copy-start(f32[1,128]{1,0:T(1,128)} %get-tuple-element.17) | copy-start | bytes 1540
  53.3 4.9 %copy-start.8 = (f32[1,128]{1,0:T(1,128)S(1)}, f32[1,128]{1,0:T(1,128)}, u32[]{:S(2)}) copy-start(f32[1,128]{1,0:T(1,128)} %get-tuple-element.18) | copy-start | bytes 1540
  58.3 4.6 %collective-permute-start.9 = (f32[5,3456]{1,0:T(8,128)S(1)}, f32[5,3456]{1,0:T(8,128)S(1)}, u32[]{:S(2)}, u32[]{:S(2)}) collective-permute-start(f32[5,3456]{1,0:T(8,128)S(1)} %select_maximum_fusion), channel_id=1, source_target_pairs={{0,1},{1,0},{2,3},{3,2},{4,5},{5,4},{6,7},{7,6},{8,9},{9,8},{10,11... | collective-permute-start | bytes 207368 | tf_op jit(solution)/shard_map/ppermute | solution.py:196
